TPU v7x, 32 devices: a whole 2x2x4 slice. The times are simulated.
32 devices in a mesh: groups: 2 (over x), rows: 8 (over z, y), cols: 2 (over core).
Axes of the slice: x: 2, y: 2, z: 4, core: 2. Of those that a mesh axis runs over, the one named last changes fastest.
Arguments:
- radiance: float32 [224, 512, 256], P(None, ('groups', 'rows'), 'cols'), parts along dimension 1, may hold values from -6 to 6
- decorrelation: float32 [224, 224], replicated, may hold values from -0.375 to 0.375
Outputs:
- coefficients: float32 [224, 512, 256], P(None, ('groups', 'rows'), 'cols'), parts along dimension 1
There are 2 independent parts, one for each index of `groups`. A program takes and returns all parts, laid end to end along the dimension named above; an argument that names none is the same for every part. Nothing has to cross between parts.
All inputs are finite; a program needn't handle non-finite values.
Results may differ from a plain program's by a relative error of at most 0.00005.
Values sent between devices are 32-bit elements; how exact they have to be, the bound alone decides.
No kernel may reach another device: no remote copies, remote signals or barrier semaphores. Data moves between devices by JAX's collectives and lax.ppermute only.
A program may use at most 128 MiB of HBM per device.

v0:
```python
import jax
import jax.numpy as jnp
from jax import lax
from jax.sharding import PartitionSpec as P

LEVELS = 3


alpha_one = -1.586134342059924
beta_one = -0.052980118572961
alpha_two = 0.882911075530934
beta_two = 0.443506852043971
scale_k = 1.230174104914001


def shifted(x, axis, by):
    size = lax.axis_size(axis)
    pairs = [(i, i + by) for i in range(size) if 0 <= i + by < size]
    return lax.ppermute(x, axis, pairs)


def split_axis(x, dim):
    shape = x.shape[:dim] + (x.shape[dim] // 2, 2) + x.shape[dim + 1 :]
    paired = x.reshape(shape)
    return (
        lax.index_in_dim(paired, 0, dim + 1, keepdims=False),
        lax.index_in_dim(paired, 1, dim + 1, keepdims=False),
    )


def join_axis(even_part, odd_part, dim):
    stacked = jnp.stack([even_part, odd_part], axis=dim + 1)
    shape = even_part.shape[:dim] + (even_part.shape[dim] * 2,) + even_part.shape[dim + 1 :]
    return stacked.reshape(shape)


def lift_axis(x, dim, axis):
    a1, b1, a2, b2 = alpha_one, beta_one, alpha_two, beta_two
    even, odd = split_axis(x, dim)
    m = even.shape[dim]

    def sl(v, lo, hi):
        return lax.slice_in_dim(v, lo, hi, axis=dim)

    def cat(parts):
        return jnp.concatenate(parts, axis=dim)

    s_first, s_second, d_first = sl(even, 0, 1), sl(even, 1, 2), sl(odd, 0, 1)
    s_pen, s_last = sl(even, m - 2, m - 1), sl(even, m - 1, m)
    d_pen, d_last = sl(odd, m - 2, m - 1), sl(odd, m - 1, m)

    to_next = cat([d_last + a1 * s_last, s_last + b1 * (d_pen + a1 * (s_pen + s_last))])
    to_prev = cat([s_first, s_first + b1 * (d_first + a1 * (s_first + s_second))])
    from_prev = shifted(to_next, axis, 1)
    from_next = shifted(to_prev, axis, -1)
    a_in, b_in = sl(from_prev, 0, 1), sl(from_prev, 1, 2)
    s_in, c_in = sl(from_next, 0, 1), sl(from_next, 1, 2)

    at_first = lax.axis_index(axis) == 0
    at_last = lax.axis_index(axis) == lax.axis_size(axis) - 1

    s_after = jnp.where(at_last, s_last, s_in)
    d1 = odd + a1 * (even + cat([sl(even, 1, m), s_after]))
    d1_before = jnp.where(at_first, sl(d1, 0, 1), a_in + a1 * s_first)
    s1 = even + b1 * (cat([d1_before, sl(d1, 0, m - 1)]) + d1)
    s1_after = jnp.where(at_last, sl(s1, m - 1, m), c_in + b1 * sl(d1, m - 1, m))
    d2 = d1 + a2 * (s1 + cat([sl(s1, 1, m), s1_after]))
    s1_before = b_in + b1 * d1_before
    d2_before = jnp.where(
        at_first, sl(d2, 0, 1), d1_before + a2 * (s1_before + sl(s1, 0, 1))
    )
    s2 = s1 + b2 * (cat([d2_before, sl(d2, 0, m - 1)]) + d2)
    return join_axis(s2 / scale_k, d2 * scale_k, dim)


def decompose(level_array, remaining):
    if remaining == 0:
        return level_array
    lifted = lift_axis(lift_axis(level_array, 0, "rows"), 1, "cols")
    height_here, width_here, band_count = lifted.shape
    blocks = lifted.reshape(height_here // 2, 2, width_here // 2, 2, band_count)
    inner_part = decompose(blocks[:, 0, :, 0], remaining - 1)
    return blocks.at[:, 0, :, 0].set(inner_part).reshape(height_here, width_here, band_count)


def on_device(radiance, decorrelation):
    mixed = jnp.einsum(
        "crw,bc->rwb",
        radiance,
        decorrelation,
        precision=lax.Precision.HIGHEST,
        preferred_element_type=jnp.float32,
    )
    return jnp.transpose(decompose(mixed, LEVELS), (2, 0, 1))


def solution(mesh):
    placed = (P(None, ("groups", "rows"), "cols"), P())
    return jax.shard_map(
        on_device,
        mesh=mesh,
        in_specs=placed,
        out_specs=P(None, ("groups", "rows"), "cols"),
        check_vma=False,
    )
```

profile of v0, /device:TPU:11, one launch (start us, length us, event | category | flops | bytes accessed | tf_op | source)
XLA Modules:
  0.0 120.9 jit_solution(8493749507223106722)
XLA Ops:
  0.0 0.9 copy-done
  0.9 7.7 %fusion = f32[32,128,224]{1,2,0:T(8,128)S(1)} fusion(f32[224,32,128]{2,1,0:T(8,128)} %param.8, f32[224,224]{1,0:T(8,128)S(1)} %copy-done), kind=kOutput, calls=%fused_computation.2 | convolution fusion | flops 2466250752 | bytes 7540736 | tf_op jit(solution)/shard_map/crw,bc->rwb/dot_general | solution.py:87
  8.6 1.8 %copy-done.2 = f32[32,128,224]{1,2,0:T(8,128)} copy-done((f32[32,128,224]{1,2,0:T(8,128)}, f32[32,128,224]{1,2,0:T(8,128)S(1)}, u32[]{:S(2)}) %copy-start.2) | copy-done | bytes 3670040
  10.5 3.0 %collective-permute-start = (f32[2,128,224]{1,2,0:T(8,128)S(1)}, f32[2,128,224]{1,2,0:T(8,128)S(1)}, u32[]{:S(2)}, u32[]{:S(2)}) collective-permute-start(f32[2,128,224]{1,2,0:T(8,128)S(1)} %pad_maximum_fusion.6), channel_id=1, source_target_pairs={{2,0},{4,2},{6,4},{8,6},{10,8},{12,10},{14,12},{3,1},{5,3},{7,5},{... | collective-permute-start | bytes 688136 | tf_op jit(solution)/shard_map/ppermute | solution.py:19
  13.6 2.4 %collective-permute-start.1 = (f32[2,128,224]{1,2,0:T(8,128)S(1)}, f32[2,128,224]{1,2,0:T(8,128)S(1)}, u32[]{:S(2)}, u32[]{:S(2)}) collective-permute-start(f32[2,128,224]{1,2,0:T(8,128)S(1)} %pad_maximum_fusion.7), channel_id=1, source_target_pairs={{0,2},{2,4},{4,6},{6,8},{8,10},{10,12},{12,14},{1,3},{3,5},{5,7},{... | collective-permute-start | bytes 688136 | tf_op jit(solution)/shard_map/ppermute | solution.py:19
  16.1 2.0 %slice_bitcast_fusion.2 = (f32[15,1,128,224]{2,3,0,1:T(8,128)S(1)}, f32[15,128,224]{1,2,0:T(8,128)S(1)}) fusion(f32[16,2,128,224]{2,3,1,0:T(8,128)} %bitcast.521), kind=kLoop, calls=%fused_computation.56 | loop fusion | bytes 5160960 | tf_op jit(solution)/shard_map/slice | solution.py:43
  18.1 0.8 collective-permute-done
  18.9 0.3 fusion.20
  19.2 0.4 slice_bitcast_fusion.44
  19.7 5.2 %collective-permute-done.1 = f32[2,128,224]{1,2,0:T(8,128)S(1)} collective-permute-done((f32[2,128,224]{1,2,0:T(8,128)S(1)}, f32[2,128,224]{1,2,0:T(8,128)S(1)}, u32[]{:S(2)}, u32[]{:S(2)}) %collective-permute-start.1) | collective-permute-done | bytes 229408 | tf_op jit(solution)/shard_map/ppermute | solution.py:19
  24.8 0.4 fusion.27
  25.2 0.4 fusion.181
  25.7 0.3 fusion.29
  26.0 0.1 slice_bitcast_fusion.1
  26.1 1.2 fusion.32
  27.4 2.1 %pad_maximum_fusion.1 = f32[16,2,128,224]{2,3,1,0:T(8,128)} fusion(f32[16,1,128,224]{2,3,1,0:T(8,128)S(1)} %get-tuple-element.44, f32[16,1,128,224]{2,3,1,0:T(8,128)S(1)} %get-tuple-element.43), kind=kLoop, calls=%fused_computation.1 | loop fusion | flops 917504 | bytes 7340032 | tf_op jit(solution)/shard_map/stack | solution.py:32
  29.5 5.1 %copy.276 = f32[16,2,128,224]{3,2,1,0:T(8,128)} copy(f32[16,2,128,224]{2,3,1,0:T(8,128)} %pad_maximum_fusion.1) | data formatting | bytes 7340032 | tf_op jit(solution)/shard_map/stack | solution.py:32
  34.6 5.9 %reshape_reshape.12 = f32[32,64,2,224]{3,2,1,0:T(2,128)} reshape(f32[16,2,128,224]{3,2,1,0:T(8,128)} %copy.276) | data formatting | bytes 7340032 | tf_op jit(solution)/shard_map/reshape;reshape | solution.py:24
  40.5 7.8 %fusion.179 = (f32[32,64,1,224]{3,2,1,0:T(1,128)S(1)}, f32[32,64,1,224]{3,2,1,0:T(1,128)S(1)}) fusion(f32[32,64,2,224]{3,2,1,0:T(2,128)} %reshape_reshape.12), kind=kLoop, calls=%fused_computation.356 | loop fusion | bytes 7340032 | tf_op jit(solution)/shard_map/slice | solution.py:27
  48.3 0.5 copy_bitcast_fusion
  48.8 0.5 slice_bitcast_fusion.47
  49.3 0.2 slice_add_fusion.13
  49.6 3.2 %collective-permute-start.2 = (f32[32,2,224]{2,1,0:T(2,128)S(1)}, f32[32,2,224]{2,1,0:T(2,128)S(1)}, u32[]{:S(2)}, u32[]{:S(2)}) collective-permute-start(f32[32,2,224]{2,1,0:T(2,128)S(1)} %pad_maximum_fusion.10), channel_id=1, source_target_pairs={{1,0},{3,2},{5,4},{7,6},{9,8},{11,10},{13,12},{15,14},{17,16},{19,... | collective-permute-start | bytes 172040 | tf_op jit(solution)/shard_map/ppermute | solution.py:19
  52.9 1.5 %collective-permute-start.3 = (f32[32,2,224]{2,1,0:T(2,128)S(1)}, f32[32,2,224]{2,1,0:T(2,128)S(1)}, u32[]{:S(2)}, u32[]{:S(2)}) collective-permute-start(f32[32,2,224]{2,1,0:T(2,128)S(1)} %pad_maximum_fusion.11), channel_id=1, source_target_pairs={{0,1},{2,3},{4,5},{6,7},{8,9},{10,11},{12,13},{14,15},{16,17},{18,... | collective-permute-start | bytes 172040 | tf_op jit(solution)/shard_map/ppermute | solution.py:19
  54.5 0.8 fusion.3
  55.3 0.5 slice_bitcast_fusion.46
  55.8 0.3 collective-permute-done.3
  56.1 0.9 fusion.10
  57.0 0.5 fusion.180
  57.6 0.8 fusion.12
  58.4 0.2 slice_bitcast_fusion
  58.7 2.2 %fusion.16 = (f32[32,64,1,224]{3,1,2,0:T(8,128)S(1)}, f32[32,64,1,224]{3,1,2,0:T(8,128)S(1)}) fusion(f32[32,63,1,224]{3,1,0,2:T(8,128)S(1)} %slice_bitcast_fusion, f32[32,1,1,224]{3,1,0,2:T(1,128)S(1)} %fusion.137, f32[32,1,1,224]{3,1,2,0:T(1,128)S(1)} %bitcast.571, f32[32,63,1,224]{3,1,2,0:T(8,128)S(1)} %get-tuple-element.60, ...), kind=kLoop, calls=%fused_computation.25 | loop fusion | flops 8257536 | bytes 14680064 | tf_op jit(solution)/shard_map/div | solution.py:73
  61.2 3.2 %collective-permute-start.4 = (f32[2,64,224]{2,1,0:T(8,128)S(1)}, f32[2,64,224]{2,1,0:T(8,128)S(1)}, u32[]{:S(2)}, u32[]{:S(2)}) collective-permute-start(f32[2,64,224]{2,1,0:T(8,128)S(1)} %pad_maximum_fusion.8), channel_id=1, source_target_pairs={{2,0},{4,2},{6,4},{8,6},{10,8},{12,10},{14,12},{3,1},{5,3},{7,5},{... | collective-permute-start | bytes 344072 | tf_op jit(solution)/shard_map/ppermute | solution.py:19
  64.4 2.1 %collective-permute-start.5 = (f32[2,64,224]{2,1,0:T(8,128)S(1)}, f32[2,64,224]{2,1,0:T(8,128)S(1)}, u32[]{:S(2)}, u32[]{:S(2)}) collective-permute-start(f32[2,64,224]{2,1,0:T(8,128)S(1)} %pad_maximum_fusion.9), channel_id=1, source_target_pairs={{0,2},{2,4},{4,6},{6,8},{8,10},{10,12},{12,14},{1,3},{3,5},{5,7},{... | collective-permute-start | bytes 344072 | tf_op jit(solution)/shard_map/ppermute | solution.py:19
  66.5 2.4 %pad_maximum_fusion = f32[16,2,64,2,224]{4,2,1,0,3:T(8,128)} fusion(f32[16,2,64,1,224]{4,2,1,0,3:T(8,128)S(1)} %bitcast.538, f32[16,2,64,1,224]{4,2,1,0,3:T(8,128)S(1)} %bitcast.537), kind=kLoop, calls=%fused_computation | loop fusion | flops 917504 | bytes 7340032 | tf_op jit(solution)/shard_map/stack | solution.py:32
  69.1 2.3 %collective-permute-done.5 = f32[2,64,224]{2,1,0:T(8,128)S(1)} collective-permute-done((f32[2,64,224]{2,1,0:T(8,128)S(1)}, f32[2,64,224]{2,1,0:T(8,128)S(1)}, u32[]{:S(2)}, u32[]{:S(2)}) %collective-permute-start.5) | collective-permute-done | bytes 114720 | tf_op jit(solution)/shard_map/ppermute | solution.py:19
  71.8 0.3 fusion.48
  72.3 0.6 reshape_reshape.13
  72.9 1.1 fusion.182
  74.4 3.8 %collective-permute-start.6 = (f32[16,2,224]{2,1,0:T(2,128)S(1)}, f32[16,2,224]{2,1,0:T(2,128)S(1)}, u32[]{:S(2)}, u32[]{:S(2)}) collective-permute-start(f32[16,2,224]{2,1,0:T(2,128)S(1)} %pad_maximum_fusion.14), channel_id=1, source_target_pairs={{1,0},{3,2},{5,4},{7,6},{9,8},{11,10},{13,12},{15,14},{17,16},{19,... | collective-permute-start | bytes 86024 | tf_op jit(solution)/shard_map/ppermute | solution.py:19
  78.3 1.3 %collective-permute-start.7 = (f32[16,2,224]{2,1,0:T(2,128)S(1)}, f32[16,2,224]{2,1,0:T(2,128)S(1)}, u32[]{:S(2)}, u32[]{:S(2)}) collective-permute-start(f32[16,2,224]{2,1,0:T(2,128)S(1)} %pad_maximum_fusion.15), channel_id=1, source_target_pairs={{0,1},{2,3},{4,5},{6,7},{8,9},{10,11},{12,13},{14,15},{16,17},{18,... | collective-permute-start | bytes 86024 | tf_op jit(solution)/shard_map/ppermute | solution.py:19
  79.6 0.2 fusion.52
  79.9 1.5 %collective-permute-done.7 = f32[16,2,224]{2,1,0:T(2,128)S(1)} collective-permute-done((f32[16,2,224]{2,1,0:T(2,128)S(1)}, f32[16,2,224]{2,1,0:T(2,128)S(1)}, u32[]{:S(2)}, u32[]{:S(2)}) %collective-permute-start.7) | collective-permute-done | bytes 28704 | tf_op jit(solution)/shard_map/ppermute | solution.py:19
  81.4 0.2 fusion.59
  81.7 0.1 fusion.61
  82.0 0.5 fusion.65
  82.6 2.6 %collective-permute-start.8 = (f32[2,32,224]{2,1,0:T(8,128)S(1)}, f32[2,32,224]{2,1,0:T(8,128)S(1)}, u32[]{:S(2)}, u32[]{:S(2)}) collective-permute-start(f32[2,32,224]{2,1,0:T(8,128)S(1)} %pad_maximum_fusion.12), channel_id=1, source_target_pairs={{2,0},{4,2},{6,4},{8,6},{10,8},{12,10},{14,12},{3,1},{5,3},{7,5},{... | collective-permute-start | bytes 172040 | tf_op jit(solution)/shard_map/ppermute | solution.py:19
  85.2 2.7 %collective-permute-start.9 = (f32[2,32,224]{2,1,0:T(8,128)S(1)}, f32[2,32,224]{2,1,0:T(8,128)S(1)}, u32[]{:S(2)}, u32[]{:S(2)}) collective-permute-start(f32[2,32,224]{2,1,0:T(8,128)S(1)} %pad_maximum_fusion.13), channel_id=1, source_target_pairs={{0,2},{2,4},{4,6},{6,8},{8,10},{10,12},{12,14},{1,3},{3,5},{5,7},{... | collective-permute-start | bytes 172040 | tf_op jit(solution)/shard_map/ppermute | solution.py:19
  88.0 0.1 collective-permute-done.8
  88.1 3.0 %collective-permute-done.9 = f32[2,32,224]{2,1,0:T(8,128)S(1)} collective-permute-done((f32[2,32,224]{2,1,0:T(8,128)S(1)}, f32[2,32,224]{2,1,0:T(8,128)S(1)}, u32[]{:S(2)}, u32[]{:S(2)}) %collective-permute-start.9) | collective-permute-done | bytes 57376 | tf_op jit(solution)/shard_map/ppermute | solution.py:19
  91.5 0.1 reshape_reshape.14
  91.6 0.2 fusion.185
  92.0 3.5 %collective-permute-start.10 = (f32[8,2,224]{2,1,0:T(2,128)S(1)}, f32[8,2,224]{2,1,0:T(2,128)S(1)}, u32[]{:S(2)}, u32[]{:S(2)}) collective-permute-start(f32[8,2,224]{2,1,0:T(2,128)S(1)} %pad_maximum_fusion.16), channel_id=1, source_target_pairs={{1,0},{3,2},{5,4},{7,6},{9,8},{11,10},{13,12},{15,14},{17,16},{19,... | collective-permute-start | bytes 43016 | tf_op jit(solution)/shard_map/ppermute | solution.py:19
  95.5 1.6 %collective-permute-start.11 = (f32[8,2,224]{2,1,0:T(2,128)S(1)}, f32[8,2,224]{2,1,0:T(2,128)S(1)}, u32[]{:S(2)}, u32[]{:S(2)}) collective-permute-start(f32[8,2,224]{2,1,0:T(2,128)S(1)} %pad_maximum_fusion.17), channel_id=1, source_target_pairs={{0,1},{2,3},{4,5},{6,7},{8,9},{10,11},{12,13},{14,15},{16,17},{18,... | collective-permute-start | bytes 43016 | tf_op jit(solution)/shard_map/ppermute | solution.py:19
  97.2 1.4 %collective-permute-done.11 = f32[8,2,224]{2,1,0:T(2,128)S(1)} collective-permute-done((f32[8,2,224]{2,1,0:T(2,128)S(1)}, f32[8,2,224]{2,1,0:T(2,128)S(1)}, u32[]{:S(2)}, u32[]{:S(2)}) %collective-permute-start.11) | collective-permute-done | bytes 14368 | tf_op jit(solution)/shard_map/ppermute | solution.py:19
  98.8 0.2 fusion.98
  99.0 0.2 copy.330
  99.2 0.2 reshape.672
  99.5 0.8 copy.332
  100.3 0.7 reshape.673
  101.0 1.1 bitcast_dynamic-update-slice_fusion
  102.1 7.5 %copy.334 = f32[16,2,64,2,224]{4,3,2,1,0:T(2,128)} copy(f32[16,2,64,2,224]{4,2,1,0,3:T(8,128)} %bitcast_dynamic-update-slice_fusion) | data formatting | bytes 7340032 | tf_op jit(solution)/shard_map/scatter | solution.py:83
  109.6 6.1 %reshape.674 = f32[32,128,224]{2,1,0:T(8,128)} reshape(f32[16,2,64,2,224]{4,3,2,1,0:T(2,128)} %copy.334) | data formatting | bytes 7340032 | tf_op jit(solution)/shard_map/reshape | solution.py:83
  115.7 5.1 %copy.335 = f32[224,32,128]{2,1,0:T(8,128)} copy(f32[224,32,128]{0,2,1:T(8,128)} %bitcast.535) | data formatting | bytes 7340032 | tf_op jit(solution)/shard_map/transpose | solution.py:94
  (94 shorter events, 3.3 us)
Async XLA Ops:
  0.0 0.9 copy-start
  8.6 1.8 %copy-start.2 = (f32[32,128,224]{1,2,0:T(8,128)}, f32[32,128,224]{1,2,0:T(8,128)S(1)}, u32[]{:S(2)}) copy-start(f32[32,128,224]{1,2,0:T(8,128)S(1)} %fusion) | copy-start | bytes 11010052
  10.5 8.4 %collective-permute-start = (f32[2,128,224]{1,2,0:T(8,128)S(1)}, f32[2,128,224]{1,2,0:T(8,128)S(1)}, u32[]{:S(2)}, u32[]{:S(2)}) collective-permute-start(f32[2,128,224]{1,2,0:T(8,128)S(1)} %pad_maximum_fusion.6), channel_id=1, source_target_pairs={{2,0},{4,2},{6,4},{8,6},{10,8},{12,10},{14,12},{3,1},{5,3},{7,5},{... | collective-permute-start | bytes 688136 | tf_op jit(solution)/shard_map/ppermute | solution.py:19
  13.6 11.2 %collective-permute-start.1 = (f32[2,128,224]{1,2,0:T(8,128)S(1)}, f32[2,128,224]{1,2,0:T(8,128)S(1)}, u32[]{:S(2)}, u32[]{:S(2)}) collective-permute-start(f32[2,128,224]{1,2,0:T(8,128)S(1)} %pad_maximum_fusion.7), channel_id=1, source_target_pairs={{0,2},{2,4},{4,6},{6,8},{8,10},{10,12},{12,14},{1,3},{3,5},{5,7},{... | collective-permute-start | bytes 688136 | tf_op jit(solution)/shard_map/ppermute | solution.py:19
  16.1 2.8 %copy-start.3 = (f32[32,128,224]{1,2,0:T(8,128)S(1)}, f32[32,128,224]{1,2,0:T(8,128)}, u32[]{:S(2)}) copy-start(f32[32,128,224]{1,2,0:T(8,128)} %copy-done.2) | copy-start | bytes 11010052
  49.6 4.8 %collective-permute-start.2 = (f32[32,2,224]{2,1,0:T(2,128)S(1)}, f32[32,2,224]{2,1,0:T(2,128)S(1)}, u32[]{:S(2)}, u32[]{:S(2)}) collective-permute-start(f32[32,2,224]{2,1,0:T(2,128)S(1)} %pad_maximum_fusion.10), channel_id=1, source_target_pairs={{1,0},{3,2},{5,4},{7,6},{9,8},{11,10},{13,12},{15,14},{17,16},{19,... | collective-permute-start | bytes 172040 | tf_op jit(solution)/shard_map/ppermute | solution.py:19
  52.9 3.1 %collective-permute-start.3 = (f32[32,2,224]{2,1,0:T(2,128)S(1)}, f32[32,2,224]{2,1,0:T(2,128)S(1)}, u32[]{:S(2)}, u32[]{:S(2)}) collective-permute-start(f32[32,2,224]{2,1,0:T(2,128)S(1)} %pad_maximum_fusion.11), channel_id=1, source_target_pairs={{0,1},{2,3},{4,5},{6,7},{8,9},{10,11},{12,13},{14,15},{16,17},{18,... | collective-permute-start | bytes 172040 | tf_op jit(solution)/shard_map/ppermute | solution.py:19
  61.2 7.7 %collective-permute-start.4 = (f32[2,64,224]{2,1,0:T(8,128)S(1)}, f32[2,64,224]{2,1,0:T(8,128)S(1)}, u32[]{:S(2)}, u32[]{:S(2)}) collective-permute-start(f32[2,64,224]{2,1,0:T(8,128)S(1)} %pad_maximum_fusion.8), channel_id=1, source_target_pairs={{2,0},{4,2},{6,4},{8,6},{10,8},{12,10},{14,12},{3,1},{5,3},{7,5},{... | collective-permute-start | bytes 344072 | tf_op jit(solution)/shard_map/ppermute | solution.py:19
  64.4 7.0 %collective-permute-start.5 = (f32[2,64,224]{2,1,0:T(8,128)S(1)}, f32[2,64,224]{2,1,0:T(8,128)S(1)}, u32[]{:S(2)}, u32[]{:S(2)}) collective-permute-start(f32[2,64,224]{2,1,0:T(8,128)S(1)} %pad_maximum_fusion.9), channel_id=1, source_target_pairs={{0,2},{2,4},{4,6},{6,8},{8,10},{10,12},{12,14},{1,3},{3,5},{5,7},{... | collective-permute-start | bytes 344072 | tf_op jit(solution)/shard_map/ppermute | solution.py:19
  74.4 5.2 %collective-permute-start.6 = (f32[16,2,224]{2,1,0:T(2,128)S(1)}, f32[16,2,224]{2,1,0:T(2,128)S(1)}, u32[]{:S(2)}, u32[]{:S(2)}) collective-permute-start(f32[16,2,224]{2,1,0:T(2,128)S(1)} %pad_maximum_fusion.14), channel_id=1, source_target_pairs={{1,0},{3,2},{5,4},{7,6},{9,8},{11,10},{13,12},{15,14},{17,16},{19,... | collective-permute-start | bytes 86024 | tf_op jit(solution)/shard_map/ppermute | solution.py:19
  78.3 3.1 %collective-permute-start.7 = (f32[16,2,224]{2,1,0:T(2,128)S(1)}, f32[16,2,224]{2,1,0:T(2,128)S(1)}, u32[]{:S(2)}, u32[]{:S(2)}) collective-permute-start(f32[16,2,224]{2,1,0:T(2,128)S(1)} %pad_maximum_fusion.15), channel_id=1, source_target_pairs={{0,1},{2,3},{4,5},{6,7},{8,9},{10,11},{12,13},{14,15},{16,17},{18,... | collective-permute-start | bytes 86024 | tf_op jit(solution)/shard_map/ppermute | solution.py:19
  82.6 5.4 %collective-permute-start.8 = (f32[2,32,224]{2,1,0:T(8,128)S(1)}, f32[2,32,224]{2,1,0:T(8,128)S(1)}, u32[]{:S(2)}, u32[]{:S(2)}) collective-permute-start(f32[2,32,224]{2,1,0:T(8,128)S(1)} %pad_maximum_fusion.12), channel_id=1, source_target_pairs={{2,0},{4,2},{6,4},{8,6},{10,8},{12,10},{14,12},{3,1},{5,3},{7,5},{... | collective-permute-start | bytes 172040 | tf_op jit(solution)/shard_map/ppermute | solution.py:19
  85.2 5.9 %collective-permute-start.9 = (f32[2,32,224]{2,1,0:T(8,128)S(1)}, f32[2,32,224]{2,1,0:T(8,128)S(1)}, u32[]{:S(2)}, u32[]{:S(2)}) collective-permute-start(f32[2,32,224]{2,1,0:T(8,128)S(1)} %pad_maximum_fusion.13), channel_id=1, source_target_pairs={{0,2},{2,4},{4,6},{6,8},{8,10},{10,12},{12,14},{1,3},{3,5},{5,7},{... | collective-permute-start | bytes 172040 | tf_op jit(solution)/shard_map/ppermute | solution.py:19
  92.0 5.1 %collective-permute-start.10 = (f32[8,2,224]{2,1,0:T(2,128)S(1)}, f32[8,2,224]{2,1,0:T(2,128)S(1)}, u32[]{:S(2)}, u32[]{:S(2)}) collective-permute-start(f32[8,2,224]{2,1,0:T(2,128)S(1)} %pad_maximum_fusion.16), channel_id=1, source_target_pairs={{1,0},{3,2},{5,4},{7,6},{9,8},{11,10},{13,12},{15,14},{17,16},{19,... | collective-permute-start | bytes 43016 | tf_op jit(solution)/shard_map/ppermute | solution.py:19
  95.5 3.1 %collective-permute-start.11 = (f32[8,2,224]{2,1,0:T(2,128)S(1)}, f32[8,2,224]{2,1,0:T(2,128)S(1)}, u32[]{:S(2)}, u32[]{:S(2)}) collective-permute-start(f32[8,2,224]{2,1,0:T(2,128)S(1)} %pad_maximum_fusion.17), channel_id=1, source_target_pairs={{0,1},{2,3},{4,5},{6,7},{8,9},{10,11},{12,13},{14,15},{16,17},{18,... | collective-permute-start | bytes 43016 | tf_op jit(solution)/shard_map/ppermute | solution.py:19
  115.7 5.1 %copy-start.1 = (f32[224,224]{1,0:T(8,128)S(1)}, f32[224,224]{1,0:T(8,128)}, u32[]{:S(2)}) copy-start(f32[224,224]{1,0:T(8,128)} %param.9) | copy-start | bytes 602116
where the time goes:
time: 122 us; the launch traced here: 121 us
  local copies, waits for them, and re-layouts  51.7 us (42%)
  starting transfers between devices  30.9 us (25%)
  other arithmetic  15.1 us (12%)
  waiting for transfers between devices  14.6 us (12%)
  matrix products  7.67 us (6%)
    ppermute x12, starting transfers between devices, shifted(): return lax.ppermute(x, axis, pairs)  30.9 us
    ppermute x12, waiting for transfers between devices, shifted(): return lax.ppermute(x, axis, pairs)  14.6 us
    scatter x6, local copies, waits for them, and re-layouts, decompose(): blocks.at[:, 0, :, 0].set(inner_part)  9.67 us
    slice x3, local copies, waits for them, and re-layouts, split_axis(): lax.index_in_dim(paired, 1, dim + 1, keepdims=False)  9.13 us
    dot_general x1, matrix products, on_device(): jnp.einsum('crw,bc->rwb', radiance, decorrelation, precision=lax.Precisio...  7.67 us
    another operation x3, local copies, waits for them, and re-layouts, split_axis(): paired = x.reshape(shape)  6.68 us
    reshape x1, local copies, waits for them, and re-layouts, decompose(): blocks.at[:, 0, :, 0].set(inner_part)  6.11 us
    another operation x3, local copies, waits for them, and re-layouts, join_axis(): stacked = jnp.stack([even_part, odd_part], axis=dim + 1)  5.22 us
  transfers between devices with their start and end apart: 12, of which 8 were waited for; matrix products, arithmetic and copies ran while one was open for 6% of the time, Pallas kernels for 0%

commit v1 on v0

--- a/solution.py
+++ b/solution.py
@@ -73,28 +73,66 @@
     return join_axis(s2 / scale_k, d2 * scale_k, dim)
 
 
+def lift_local(x, dim):
+    even, odd = split_axis(x, dim)
+    m = even.shape[dim]
+
+    def sl(v, lo, hi):
+        return lax.slice_in_dim(v, lo, hi, axis=dim)
+
+    def cat(parts):
+        return jnp.concatenate(parts, axis=dim)
+
+    for a, b in ((alpha_one, beta_one), (alpha_two, beta_two)):
+        odd = odd + a * (even + cat([sl(even, 1, m), sl(even, m - 1, m)]))
+        even = even + b * (cat([sl(odd, 0, 1), sl(odd, 0, m - 1)]) + odd)
+    return join_axis(even / scale_k, odd * scale_k, dim)
+
+
 def decompose(level_array, remaining):
     if remaining == 0:
         return level_array
-    lifted = lift_axis(lift_axis(level_array, 0, "rows"), 1, "cols")
+    lifted = lift_local(lift_axis(level_array, 0, "rows"), 1)
     height_here, width_here, band_count = lifted.shape
     blocks = lifted.reshape(height_here // 2, 2, width_here // 2, 2, band_count)
     inner_part = decompose(blocks[:, 0, :, 0], remaining - 1)
     return blocks.at[:, 0, :, 0].set(inner_part).reshape(height_here, width_here, band_count)
 
 
+HALO = 32
+
+
+def with_column_halo(radiance):
+    width = radiance.shape[2]
+    right_of_left = shifted(radiance[:, :, :HALO], "cols", -1)
+    left_of_right = shifted(radiance[:, :, width - HALO :], "cols", 1)
+    on_left = lax.axis_index("cols") == 0
+    return jnp.where(
+        on_left,
+        jnp.concatenate([radiance, right_of_left], axis=2),
+        jnp.concatenate([left_of_right, radiance], axis=2),
+    )
+
+
 def on_device(radiance, decorrelation):
+    width = radiance.shape[2]
+    extended = with_column_halo(radiance)
     mixed = jnp.einsum(
         "crw,bc->rwb",
-        radiance,
+        extended,
         decorrelation,
         precision=lax.Precision.HIGHEST,
         preferred_element_type=jnp.float32,
     )
-    return jnp.transpose(decompose(mixed, LEVELS), (2, 0, 1))
+    coeffs = decompose(mixed, LEVELS)
+    own = jnp.where(
+        lax.axis_index("cols") == 0, coeffs[:, :width], coeffs[:, HALO : HALO + width]
+    )
+    return jnp.transpose(own, (2, 0, 1))
 
 
 def solution(mesh):
+    assert mesh.shape["cols"] == 2
     placed = (P(None, ("groups", "rows"), "cols"), P())
     return jax.shard_map(
         on_device,

time: 122 us -> 177 us (1.45)
  the two profiles are of different devices: /device:TPU:11 before, /device:TPU:0 now
where the time goes in v1:
time: 177 us
  local copies, waits for them, and re-layouts  75.6 us (43%)
  other arithmetic  31.1 us (18%)
  matrix products  28.4 us (16%)
  starting transfers between devices  22.5 us (13%)
  waiting for transfers between devices  17.9 us (10%)
    dot_general x1, matrix products, on_device(): jnp.einsum('crw,bc->rwb', extended, decorrelation, precision=lax.Precisio...  28.4 us
    ppermute x8, starting transfers between devices, shifted(): return lax.ppermute(x, axis, pairs)  22.5 us
    ppermute x8, waiting for transfers between devices, shifted(): return lax.ppermute(x, axis, pairs)  17.9 us
    scatter x5, local copies, waits for them, and re-layouts, decompose(): blocks.at[:, 0, :, 0].set(inner_part)  12.5 us
    slice x3, local copies, waits for them, and re-layouts, split_axis(): lax.index_in_dim(paired, 1, dim + 1, keepdims=False)  12.3 us
    another operation x3, local copies, waits for them, and re-layouts, split_axis(): paired = x.reshape(shape)  8.45 us
    unnamed x13, local copies, waits for them, and re-layouts  7.75 us
    reshape x1, local copies, waits for them, and re-layouts, decompose(): blocks.at[:, 0, :, 0].set(inner_part)  7.59 us
  transfers between devices with their start and end apart: 8, of which 6 were waited for; matrix products, arithmetic and copies ran while one was open for 6% of the time, Pallas kernels for 0%

profile of v1, /device:TPU:0, one launch (start us, length us, event | category | flops | bytes accessed | tf_op | source)
XLA Modules:
  0.0 176.5 jit_solution(14829497171255984151)
XLA Ops:
  0.0 7.3 %fusion.157 = (f32[224,32,32]{2,1,0:T(8,128)}, f32[224,32,32]{2,1,0:T(8,128)}) fusion(f32[224,32,128]{2,1,0:T(8,128)} %param.8), kind=kLoop, calls=%fused_computation.298 | loop fusion | bytes 3670016 | tf_op jit(solution)/shard_map/slice | solution.py:108
  7.3 3.2 %copy.330 = f32[224,32,32]{0,2,1:T(8,128)S(1)} copy(f32[224,32,32]{2,1,0:T(8,128)} %get-tuple-element.52) | data formatting | bytes 1835008
  10.4 2.4 %collective-permute-start.1 = (f32[224,32,32]{0,2,1:T(8,128)S(1)}, f32[224,32,32]{0,2,1:T(8,128)S(1)}, u32[]{:S(2)}, u32[]{:S(2)}) collective-permute-start(f32[224,32,32]{0,2,1:T(8,128)S(1)} %copy.330), channel_id=1, source_target_pairs={{0,1},{2,3},{4,5},{6,7},{8,9},{10,11},{12,13},{14,15},{16,17},{18,... | collective-permute-start | bytes 2752520 | tf_op jit(solution)/shard_map/ppermute | solution.py:19
  12.9 3.2 %copy.329 = f32[224,32,32]{0,2,1:T(8,128)S(1)} copy(f32[224,32,32]{2,1,0:T(8,128)} %get-tuple-element.53) | data formatting | bytes 1835008
  16.0 1.3 collective-permute-start
  17.4 3.3 %copy.265 = f32[224,32,32]{2,1,0:T(8,128)} copy(f32[224,32,32]{0,2,1:T(8,128)S(1)} %collective-permute-done.1) | data formatting | bytes 1835008 | tf_op jit(solution)/shard_map/ppermute | solution.py:19
  20.7 4.1 %copy.263 = f32[224,32,32]{2,1,0:T(8,128)} copy(f32[224,32,32]{0,2,1:T(8,128)} %collective-permute-done) | data formatting | bytes 1835008 | tf_op jit(solution)/shard_map/ppermute | solution.py:19
  24.8 6.7 %maximum_select_fusion = f32[224,32,160]{2,1,0:T(8,128)S(1)} fusion(f32[224,32,32]{2,1,0:T(8,128)} %copy.263, f32[224,32,128]{2,1,0:T(8,128)} %param.8, f32[224,32,32]{2,1,0:T(8,128)} %copy.265, pred[]{:T(512)S(6)} %eq.6), kind=kLoop, calls=%fused_computation | loop fusion | flops 3440640 | bytes 10092545 | tf_op jit(solution)/shard_map/jit(_where)/select_n | solution.py:110
  31.6 28.4 %fusion = f32[32,160,224]{2,1,0:T(8,128)S(1)} fusion(f32[224,32,160]{2,1,0:T(8,128)S(1)} %maximum_select_fusion, f32[224,224]{1,0:T(8,128)S(1)} %copy-done), kind=kOutput, calls=%fused_computation.1 | convolution fusion | flops 3082813440 | bytes 9375744 | tf_op jit(solution)/shard_map/crw,bc->rwb/dot_general | solution.py:120
  60.2 1.3 collective-permute-start.2
  61.5 4.9 %collective-permute-start.3 = (f32[2,160,224]{2,1,0:T(8,128)S(1)}, f32[2,160,224]{2,1,0:T(8,128)S(1)}, u32[]{:S(2)}, u32[]{:S(2)}) collective-permute-start(f32[2,160,224]{2,1,0:T(8,128)S(1)} %pad_maximum_fusion.5), channel_id=1, source_target_pairs={{0,2},{2,4},{4,6},{6,8},{8,10},{10,12},{12,14},{1,3},{3,5},{5,7},{... | collective-permute-start | bytes 860168 | tf_op jit(solution)/shard_map/ppermute | solution.py:19
  66.4 0.6 fusion.156
  67.0 4.6 %collective-permute-done.2 = f32[2,160,224]{2,1,0:T(8,128)S(1)} collective-permute-done((f32[2,160,224]{2,1,0:T(8,128)S(1)}, f32[2,160,224]{2,1,0:T(8,128)S(1)}, u32[]{:S(2)}, u32[]{:S(2)}) %collective-permute-start.2) | collective-permute-done | bytes 286752 | tf_op jit(solution)/shard_map/ppermute | solution.py:19
  71.7 0.6 fusion.4
  72.3 0.6 slice_bitcast_fusion.54
  72.9 7.4 %collective-permute-done.3 = f32[2,160,224]{2,1,0:T(8,128)S(1)} collective-permute-done((f32[2,160,224]{2,1,0:T(8,128)S(1)}, f32[2,160,224]{2,1,0:T(8,128)S(1)}, u32[]{:S(2)}, u32[]{:S(2)}) %collective-permute-start.3) | collective-permute-done | bytes 286752 | tf_op jit(solution)/shard_map/ppermute | solution.py:19
  80.4 0.6 fusion.10
  80.9 0.6 fusion.160
  81.6 0.6 fusion.12
  82.2 0.2 slice_bitcast_fusion.1
  82.5 2.1 %fusion.16 = (f32[16,1,160,224]{3,2,1,0:T(8,128)S(1)}, f32[16,1,160,224]{3,2,1,0:T(8,128)S(1)}) fusion(f32[15,1,160,224]{3,2,0,1:T(8,128)S(1)} %slice_bitcast_fusion.1, f32[1,1,160,224]{3,2,0,1:T(8,128)S(1)} %fusion.72, f32[1,1,160,224]{3,2,1,0:T(8,128)S(1)} %bitcast.507, f32[15,1,160,224]{3,2,1,0:T(8,128)S(1)} %get-tuple-element.71, ...), kind=kLoop, calls=%fused_computation.27 | loop fusion | flops 10321920 | bytes 18350080 | tf_op jit(solution)/shard_map/div | solution.py:73
  84.6 2.7 %pad_maximum_fusion = f32[16,2,160,224]{3,2,1,0:T(8,128)} fusion(f32[16,1,160,224]{3,2,1,0:T(8,128)S(1)} %get-tuple-element.44, f32[16,1,160,224]{3,2,1,0:T(8,128)S(1)} %get-tuple-element.43), kind=kLoop, calls=%fused_computation.3 | loop fusion | flops 1146880 | bytes 9175040 | tf_op jit(solution)/shard_map/stack | solution.py:32
  87.3 7.5 %reshape_reshape.12 = f32[32,80,2,224]{3,2,1,0:T(2,128)} reshape(f32[16,2,160,224]{3,2,1,0:T(8,128)} %pad_maximum_fusion) | data formatting | bytes 9175040 | tf_op jit(solution)/shard_map/reshape;reshape | solution.py:24
  94.8 11.0 %fusion.155 = (f32[32,80,1,224]{3,2,1,0:T(1,128)}, f32[32,80,1,224]{3,2,1,0:T(1,128)S(1)}) fusion(f32[32,80,2,224]{3,2,1,0:T(2,128)} %reshape_reshape.12), kind=kLoop, calls=%fused_computation.296 | loop fusion | bytes 9175040 | tf_op jit(solution)/shard_map/slice | solution.py:27
  105.8 0.2 copy.408
  106.0 0.7 slice_bitcast_fusion.58
  106.7 1.0 copy-done.2
  107.8 0.8 fusion.20
  108.6 0.8 slice_bitcast_fusion.57
  109.5 0.9 fusion.27
  110.5 0.8 fusion.158
  111.3 0.8 fusion.29
  112.1 0.2 slice_bitcast_fusion
  112.3 2.9 %fusion.33 = (f32[32,80,1,224]{3,1,2,0:T(8,128)S(1)}, f32[32,80,1,224]{3,1,2,0:T(8,128)S(1)}) fusion(f32[32,79,1,224]{3,1,0,2:T(8,128)S(1)} %slice_bitcast_fusion, f32[32,1,1,224]{3,1,0,2:T(1,128)S(1)} %slice_bitcast_fusion.31, f32[32,1,1,224]{3,1,2,0:T(1,128)S(1)} %get-tuple-element.61, f32[32,79,1,224]{3,1,2,0:T(8,128)S(1)} %get-tuple-element.59, ...), kind=kLoop, calls=%fused_computation.51 | loop fusion | flops 10321920 | bytes 18350080 | tf_op jit(solution)/shard_map/div | solution.py:89
  115.5 1.3 collective-permute-start.4
  116.8 5.0 %collective-permute-start.5 = (f32[2,80,224]{2,1,0:T(8,128)S(1)}, f32[2,80,224]{2,1,0:T(8,128)S(1)}, u32[]{:S(2)}, u32[]{:S(2)}) collective-permute-start(f32[2,80,224]{2,1,0:T(8,128)S(1)} %pad_maximum_fusion.9), channel_id=1, source_target_pairs={{0,2},{2,4},{4,6},{6,8},{8,10},{10,12},{12,14},{1,3},{3,5},{5,7},{... | collective-permute-start | bytes 430088 | tf_op jit(solution)/shard_map/ppermute | solution.py:19
  121.9 2.8 %pad_maximum_fusion.1 = f32[16,2,80,2,224]{4,2,1,0,3:T(8,128)} fusion(f32[16,2,80,1,224]{4,2,1,0,3:T(8,128)S(1)} %bitcast.491, f32[16,2,80,1,224]{4,2,1,0,3:T(8,128)S(1)} %bitcast.488), kind=kLoop, calls=%fused_computation.4 | loop fusion | flops 1146880 | bytes 9175040 | tf_op jit(solution)/shard_map/stack | solution.py:32
  124.9 3.2 %collective-permute-done.5 = f32[2,80,224]{2,1,0:T(8,128)S(1)} collective-permute-done((f32[2,80,224]{2,1,0:T(8,128)S(1)}, f32[2,80,224]{2,1,0:T(8,128)S(1)}, u32[]{:S(2)}, u32[]{:S(2)}) %collective-permute-start.5) | collective-permute-done | bytes 143392 | tf_op jit(solution)/shard_map/ppermute | solution.py:19
  128.5 0.4 fusion.48
  129.1 0.8 reshape_reshape.13
  130.0 1.0 fusion.161
  131.2 0.2 fusion.52
  131.5 0.2 fusion.59
  131.8 0.1 fusion.61
  132.0 0.5 fusion.65
  132.8 1.3 collective-permute-start.6
  134.1 5.0 %collective-permute-start.7 = (f32[2,40,224]{2,1,0:T(8,128)S(1)}, f32[2,40,224]{2,1,0:T(8,128)S(1)}, u32[]{:S(2)}, u32[]{:S(2)}) collective-permute-start(f32[2,40,224]{2,1,0:T(8,128)S(1)} %pad_maximum_fusion.11), channel_id=1, source_target_pairs={{0,2},{2,4},{4,6},{6,8},{8,10},{10,12},{12,14},{1,3},{3,5},{5,7},{... | collective-permute-start | bytes 215048 | tf_op jit(solution)/shard_map/ppermute | solution.py:19
  139.1 0.7 collective-permute-done.6
  139.9 1.9 %collective-permute-done.7 = f32[2,40,224]{2,1,0:T(8,128)S(1)} collective-permute-done((f32[2,40,224]{2,1,0:T(8,128)S(1)}, f32[2,40,224]{2,1,0:T(8,128)S(1)}, u32[]{:S(2)}, u32[]{:S(2)}) %collective-permute-start.7) | collective-permute-done | bytes 71712 | tf_op jit(solution)/shard_map/ppermute | solution.py:19
  142.1 0.2 reshape_reshape.14
  142.3 0.3 fusion.165
  143.0 0.2 fusion.116
  143.1 0.2 copy.314
  143.3 0.2 copy.315
  143.5 0.3 pad_maximum_fusion.7
  143.8 1.3 scatter.10
  145.1 0.2 reshape.672
  145.3 1.0 copy.317
  146.4 0.9 reshape.673
  147.3 1.2 bitcast_dynamic-update-slice_fusion
  148.4 9.0 %copy.319 = f32[16,2,80,2,224]{4,3,2,1,0:T(2,128)} copy(f32[16,2,80,2,224]{4,2,1,0,3:T(8,128)} %bitcast_dynamic-update-slice_fusion) | data formatting | bytes 9175040 | tf_op jit(solution)/shard_map/scatter | solution.py:99
  157.5 7.6 %reshape.674 = f32[32,160,224]{2,1,0:T(8,128)} reshape(f32[16,2,80,2,224]{4,3,2,1,0:T(2,128)} %copy.319) | data formatting | bytes 9175040 | tf_op jit(solution)/shard_map/reshape | solution.py:99
  165.0 6.2 %fusion.2 = f32[224,32,128]{0,2,1:T(8,128)} fusion(f32[32,160,224]{2,1,0:T(8,128)} %reshape.674, pred[]{:T(512)S(6)} %eq.6), kind=kLoop, calls=%fused_computation.6 | loop fusion | flops 917504 | bytes 11010049 | tf_op jit(solution)/shard_map/transpose | solution.py:131
  171.2 5.1 %copy.320 = f32[224,32,128]{2,1,0:T(8,128)} copy(f32[224,32,128]{0,2,1:T(8,128)} %fusion.2) | data formatting | bytes 7340032 | tf_op jit(solution)/shard_map/transpose | solution.py:131
  (81 shorter events, 3.0 us)
Async XLA Ops:
  0.0 31.5 %copy-start = (f32[224,224]{1,0:T(8,128)S(1)}, f32[224,224]{1,0:T(8,128)}, u32[]{:S(2)}) copy-start(f32[224,224]{1,0:T(8,128)} %param.9) | copy-start | bytes 602116
  10.4 6.9 %collective-permute-start.1 = (f32[224,32,32]{0,2,1:T(8,128)S(1)}, f32[224,32,32]{0,2,1:T(8,128)S(1)}, u32[]{:S(2)}, u32[]{:S(2)}) collective-permute-start(f32[224,32,32]{0,2,1:T(8,128)S(1)} %copy.330), channel_id=1, source_target_pairs={{0,1},{2,3},{4,5},{6,7},{8,9},{10,11},{12,13},{14,15},{16,17},{18,... | collective-permute-start | bytes 2752520 | tf_op jit(solution)/shard_map/ppermute | solution.py:19
  16.0 4.7 %collective-permute-start = (f32[224,32,32]{0,2,1:T(8,128)S(1)}, f32[224,32,32]{0,2,1:T(8,128)}, u32[]{:S(2)}, u32[]{:S(2)}) collective-permute-start(f32[224,32,32]{0,2,1:T(8,128)S(1)} %copy.329), channel_id=1, source_target_pairs={{1,0},{3,2},{5,4},{7,6},{9,8},{11,10},{13,12},{15,14},{17,16},{19,... | collective-permute-start | bytes 2752520 | tf_op jit(solution)/shard_map/ppermute | solution.py:19
  60.2 11.5 %collective-permute-start.2 = (f32[2,160,224]{2,1,0:T(8,128)S(1)}, f32[2,160,224]{2,1,0:T(8,128)S(1)}, u32[]{:S(2)}, u32[]{:S(2)}) collective-permute-start(f32[2,160,224]{2,1,0:T(8,128)S(1)} %pad_maximum_fusion.4), channel_id=1, source_target_pairs={{2,0},{4,2},{6,4},{8,6},{10,8},{12,10},{14,12},{3,1},{5,3},{7,5},{... | collective-permute-start | bytes 860168 | tf_op jit(solution)/shard_map/ppermute | solution.py:19
  61.5 18.8 %collective-permute-start.3 = (f32[2,160,224]{2,1,0:T(8,128)S(1)}, f32[2,160,224]{2,1,0:T(8,128)S(1)}, u32[]{:S(2)}, u32[]{:S(2)}) collective-permute-start(f32[2,160,224]{2,1,0:T(8,128)S(1)} %pad_maximum_fusion.5), channel_id=1, source_target_pairs={{0,2},{2,4},{4,6},{6,8},{8,10},{10,12},{12,14},{1,3},{3,5},{5,7},{... | collective-permute-start | bytes 860168 | tf_op jit(solution)/shard_map/ppermute | solution.py:19
  106.0 1.7 copy-start.2
  115.5 9.1 %collective-permute-start.4 = (f32[2,80,224]{2,1,0:T(8,128)S(1)}, f32[2,80,224]{2,1,0:T(8,128)S(1)}, u32[]{:S(2)}, u32[]{:S(2)}) collective-permute-start(f32[2,80,224]{2,1,0:T(8,128)S(1)} %pad_maximum_fusion.8), channel_id=1, source_target_pairs={{2,0},{4,2},{6,4},{8,6},{10,8},{12,10},{14,12},{3,1},{5,3},{7,5},{... | collective-permute-start | bytes 430088 | tf_op jit(solution)/shard_map/ppermute | solution.py:19
  116.8 11.2 %collective-permute-start.5 = (f32[2,80,224]{2,1,0:T(8,128)S(1)}, f32[2,80,224]{2,1,0:T(8,128)S(1)}, u32[]{:S(2)}, u32[]{:S(2)}) collective-permute-start(f32[2,80,224]{2,1,0:T(8,128)S(1)} %pad_maximum_fusion.9), channel_id=1, source_target_pairs={{0,2},{2,4},{4,6},{6,8},{8,10},{10,12},{12,14},{1,3},{3,5},{5,7},{... | collective-permute-start | bytes 430088 | tf_op jit(solution)/shard_map/ppermute | solution.py:19
  132.8 7.0 %collective-permute-start.6 = (f32[2,40,224]{2,1,0:T(8,128)S(1)}, f32[2,40,224]{2,1,0:T(8,128)S(1)}, u32[]{:S(2)}, u32[]{:S(2)}) collective-permute-start(f32[2,40,224]{2,1,0:T(8,128)S(1)} %pad_maximum_fusion.10), channel_id=1, source_target_pairs={{2,0},{4,2},{6,4},{8,6},{10,8},{12,10},{14,12},{3,1},{5,3},{7,5},{... | collective-permute-start | bytes 215048 | tf_op jit(solution)/shard_map/ppermute | solution.py:19
  134.1 7.7 %collective-permute-start.7 = (f32[2,40,224]{2,1,0:T(8,128)S(1)}, f32[2,40,224]{2,1,0:T(8,128)S(1)}, u32[]{:S(2)}, u32[]{:S(2)}) collective-permute-start(f32[2,40,224]{2,1,0:T(8,128)S(1)} %pad_maximum_fusion.11), channel_id=1, source_target_pairs={{0,2},{2,4},{4,6},{6,8},{8,10},{10,12},{12,14},{1,3},{3,5},{5,7},{... | collective-permute-start | bytes 215048 | tf_op jit(solution)/shard_map/ppermute | solution.py:19
  165.0 11.3 %copy-start.1 = (f32[224,224]{1,0:T(8,128)S(1)}, f32[224,224]{1,0:T(8,128)}, u32[]{:S(2)}) copy-start(f32[224,224]{1,0:T(8,128)} %param.9) | copy-start | bytes 602116

commit v2 on v0

v2 whole, which is shorter than its diff:
```python
import functools

import jax
import jax.numpy as jnp
from jax import lax
from jax.experimental import pallas as pl
from jax.experimental.pallas import tpu as pltpu
from jax.sharding import PartitionSpec as P

LEVELS = 3
HALO = 32
EDGE = 4


alpha_one = -1.586134342059924
beta_one = -0.052980118572961
alpha_two = 0.882911075530934
beta_two = 0.443506852043971
scale_k = 1.230174104914001


def shifted(x, axis, by):
    size = lax.axis_size(axis)
    pairs = [(i, i + by) for i in range(size) if 0 <= i + by < size]
    return lax.ppermute(x, axis, pairs)


def level_kernel(x_ref, top_ref, bot_ref, *rest, stride):
    if stride == 1:
        out_ref, ll_ref, ext, half = rest
    else:
        prev_ref, out_ref, ll_ref, ext, half = rest
        out_ref[...] = prev_ref[...]
    rows, width, bands = x_ref.shape
    hr, hw = rows // 2, width // 2
    a1, b1, a2, b2 = alpha_one, beta_one, alpha_two, beta_two

    ext[0:EDGE] = top_ref[...]
    ext[EDGE : EDGE + rows] = x_ref[...]
    ext[EDGE + rows : 2 * EDGE + rows] = bot_ref[...]
    n = hr + EDGE
    pairs = ext[...].reshape(n, 2, width, bands)
    s = pairs[:, 0]
    d = pairs[:, 1]

    def nxt0(v):
        return jnp.concatenate([v[1:], v[-1:]], axis=0)

    def prv0(v):
        return jnp.concatenate([v[:1], v[:-1]], axis=0)

    d = d + a1 * (s + nxt0(s))
    s = s + b1 * (prv0(d) + d)
    d = d + a2 * (s + nxt0(s))
    s = s + b2 * (prv0(d) + d)
    lo = EDGE // 2
    half[0] = s[lo : lo + hr] / scale_k
    half[1] = d[lo : lo + hr] * scale_k

    col = lax.broadcasted_iota(jnp.int32, (hr, hw, bands), 1)

    def nxt1(v):
        return jnp.where(col == hw - 1, v, pltpu.roll(v, hw - 1, 1))

    def prv1(v):
        return jnp.where(col == 0, v, pltpu.roll(v, 1, 1))

    for pr in range(2):
        e = half[pr, :, pl.ds(0, hw, stride=2), :]
        o = half[pr, :, pl.ds(1, hw, stride=2), :]
        o = o + a1 * (e + nxt1(e))
        e = e + b1 * (prv1(o) + o)
        o = o + a2 * (e + nxt1(e))
        e = e + b2 * (prv1(o) + o)
        e = e / scale_k
        o = o * scale_k
        step = 2 * stride
        out_ref[pl.ds(pr * stride, hr, stride=step), pl.ds(0, hw, stride=step), :] = e
        out_ref[pl.ds(pr * stride, hr, stride=step), pl.ds(stride, hw, stride=step), :] = o
        if pr == 0:
            ll_ref[...] = e


def run_level(x, top, bot, out, stride):
    rows, width, bands = x.shape
    vm = pl.BlockSpec(memory_space=pltpu.VMEM)
    ins = [x, top, bot]
    aliases = {}
    if out is not None:
        ins.append(out)
        aliases = {3: 0}
        out_shape = out.shape
    else:
        out_shape = x.shape
    return pl.pallas_call(
        functools.partial(level_kernel, stride=stride),
        out_shape=(
            jax.ShapeDtypeStruct(out_shape, jnp.float32),
            jax.ShapeDtypeStruct((rows // 2, width // 2, bands), jnp.float32),
        ),
        in_specs=[vm] * len(ins),
        out_specs=(vm, vm),
        scratch_shapes=[
            pltpu.VMEM((rows + 2 * EDGE, width, bands), jnp.float32),
            pltpu.VMEM((2, rows // 2, width, bands), jnp.float32),
        ],
        input_output_aliases=aliases,
        compiler_params=pltpu.CompilerParams(vmem_limit_bytes=100 * 1024 * 1024),
    )(*ins)


def row_halos(x):
    rows = x.shape[0]
    from_prev = shifted(x[rows - EDGE :], "rows", 1)
    from_next = shifted(x[:EDGE], "rows", -1)
    at_first = lax.axis_index("rows") == 0
    at_last = lax.axis_index("rows") == lax.axis_size("rows") - 1
    top = jnp.where(at_first, x[EDGE:0:-1], from_prev)
    bot = jnp.where(at_last, x[rows - 2 : rows - 2 - EDGE : -1], from_next)
    return top, bot


LANES = 128


def band_blocks(decorrelation):
    bands = decorrelation.shape[0]
    count = -(-bands // LANES)
    padded = jnp.pad(decorrelation, ((0, count * LANES - bands), (0, 0)))
    return [padded[i * LANES : (i + 1) * LANES] for i in range(count)]


def mix(radiance, decorrelation):
    return jnp.einsum(
        "crw,bc->rwb",
        radiance,
        decorrelation,
        precision=lax.Precision.HIGHEST,
        preferred_element_type=jnp.float32,
    )


def on_device(radiance, decorrelation):
    width = radiance.shape[2]
    on_left = lax.axis_index("cols") == 0
    right_of_left = shifted(radiance[:, :, :HALO], "cols", -1)
    left_of_right = shifted(radiance[:, :, width - HALO :], "cols", 1)
    halo_in = jnp.where(on_left, right_of_left, left_of_right)
    parts = []
    for block in band_blocks(decorrelation):
        own = mix(radiance, block)
        halo = mix(halo_in, block)
        level = jnp.where(
            on_left,
            jnp.concatenate([own, halo], axis=1),
            jnp.concatenate([halo, own], axis=1),
        )
        out = None
        for lvl in range(LEVELS):
            top, bot = row_halos(level)
            out, level = run_level(level, top, bot, out, 2**lvl)
        coeffs = jnp.where(on_left, out[:, :width], out[:, HALO : HALO + width])
        parts.append(jnp.transpose(coeffs, (2, 0, 1)))
    return jnp.concatenate(parts, axis=0)[: radiance.shape[0]]


def solution(mesh):
    assert mesh.shape["cols"] == 2
    placed = (P(None, ("groups", "rows"), "cols"), P())
    return jax.shard_map(
        on_device,
        mesh=mesh,
        in_specs=placed,
        out_specs=P(None, ("groups", "rows"), "cols"),
        check_vma=False,
    )
```

time: 122 us -> 169 us (1.39)
  the two profiles are of different devices: /device:TPU:11 before, /device:TPU:0 now
where the time goes in v2:
time: 169 us; the launch traced here: 167 us
  starting transfers between devices  47.7 us (28%)
  local copies, waits for them, and re-layouts  32 us (19%)
  Pallas kernels  29.9 us (18%)
  other arithmetic  27.5 us (16%)
  matrix products  20.7 us (12%)
  waiting for transfers between devices  9.54 us (6%)
    ppermute x14, starting transfers between devices, shifted(): return lax.ppermute(x, axis, pairs)  47.7 us
    pallas_call x6, Pallas kernels, run_level(): pl.pallas_call(functools.partial(level_kernel, stride=stride), out_shape=...  29.9 us
    dot_general x4, matrix products, mix(): jnp.einsum('crw,bc->rwb', radiance, decorrelation, precision=lax.Precisio...  20.7 us
    select_n x6, other arithmetic, row_halos(): bot = jnp.where(at_last, x[rows - 2:rows - 2 - EDGE:-1], from_next)  10 us
    unnamed x15, local copies, waits for them, and re-layouts  10 us
    slice x6, local copies, waits for them, and re-layouts, row_halos(): bot = jnp.where(at_last, x[rows - 2:rows - 2 - EDGE:-1], from_next)  9.68 us
    ppermute x14, waiting for transfers between devices, shifted(): return lax.ppermute(x, axis, pairs)  9.54 us
    select_n x6, other arithmetic, row_halos(): top = jnp.where(at_first, x[EDGE:0:-1], from_prev)  7.89 us
  transfers between devices with their start and end apart: 14, of which 1 were waited for; matrix products, arithmetic and copies ran while one was open for 32% of the time, Pallas kernels for 16%

profile of v2, /device:TPU:0, one launch (start us, length us, event | category | flops | bytes accessed | tf_op | source)
XLA Modules:
  0.0 167.4 jit_solution(8074785238026519338)
XLA Ops:
  0.0 7.2 %fusion.14 = (f32[224,32,32]{2,1,0:T(8,128)}, f32[224,32,32]{2,1,0:T(8,128)}) fusion(f32[224,32,128]{2,1,0:T(8,128)} %param.2), kind=kLoop, calls=%fused_computation.30 | loop fusion | bytes 3670016 | tf_op jit(solution)/shard_map/slice | solution.py:147
  7.2 3.2 %copy.21 = f32[224,32,32]{0,2,1:T(8,128)S(1)} copy(f32[224,32,32]{2,1,0:T(8,128)} %get-tuple-element.26) | data formatting | bytes 1835008
  10.4 1.3 collective-permute-start
  11.7 4.0 %copy.22 = f32[224,32,32]{0,2,1:T(8,128)} copy(f32[224,32,32]{2,1,0:T(8,128)} %get-tuple-element.25) | data formatting | bytes 1835008
  15.7 3.3 %collective-permute-start.1 = (f32[224,32,32]{0,2,1:T(8,128)}, f32[224,32,32]{0,2,1:T(8,128)S(1)}, u32[]{:S(2)}, u32[]{:S(2)}) collective-permute-start(f32[224,32,32]{0,2,1:T(8,128)} %copy.22), channel_id=1, source_target_pairs={{0,1},{2,3},{4,5},{6,7},{8,9},{10,11},{12,13},{14,15},{16,17},{18,... | collective-permute-start | bytes 2752520 | tf_op jit(solution)/shard_map/ppermute | solution.py:25
  19.0 1.1 copy.14
  20.1 0.0 copy-start
  20.1 10.2 %fusion.4 = f32[32,128,128]{2,1,0:T(8,128)S(1)} fusion(f32[224,32,128]{2,1,0:T(8,128)} %param.2, f32[224,224]{0,1:T(8,128)S(1)} %copy.14), kind=kOutput, calls=%fused_computation.9 | convolution fusion | flops 1409286144 | bytes 5967872 | tf_op jit(solution)/shard_map/crw,bc->rwb/dot_general | solution.py:134
  30.4 8.4 %fusion.2 = f32[32,128,128]{2,1,0:T(8,128)S(1)} fusion(f32[224,32,128]{2,1,0:T(8,128)S(1)} %copy-done, f32[224,224]{0,1:T(8,128)S(1)} %copy.14), kind=kOutput, calls=%fused_computation.3 | convolution fusion | flops 1409286144 | bytes 5881856 | tf_op jit(solution)/shard_map/crw,bc->rwb/dot_general | solution.py:134
  38.8 0.0 collective-permute-done.1
  38.8 1.0 fusion.7
  39.8 1.0 fusion.8
  40.8 0.7 maximum_select_fusion
  41.5 0.0 copy-start.1
  41.5 1.5 copy-done.2
  43.1 1.0 fusion.15
  44.1 1.3 collective-permute-start.3
  45.4 5.5 %collective-permute-start.2 = (f32[4,160,128]{2,1,0:T(8,128)}, f32[4,160,128]{2,1,0:T(8,128)S(1)}, u32[]{:S(2)}, u32[]{:S(2)}) collective-permute-start(f32[4,160,128]{2,1,0:T(8,128)} %get-tuple-element.29), channel_id=1, source_target_pairs={{0,2},{2,4},{4,6},{6,8},{8,10},{10,12},{12,14},{1,3},{3,5},{5,7},{... | collective-permute-start | bytes 983048 | tf_op jit(solution)/shard_map/ppermute | solution.py:25
  50.9 1.1 fusion.16
  52.0 1.3 collective-permute-start.9
  53.3 6.2 %collective-permute-start.8 = (f32[4,160,128]{2,1,0:T(8,128)}, f32[4,160,128]{2,1,0:T(8,128)}, u32[]{:S(2)}, u32[]{:S(2)}) collective-permute-start(f32[4,160,128]{2,1,0:T(8,128)} %get-tuple-element.33), channel_id=1, source_target_pairs={{0,2},{2,4},{4,6},{6,8},{8,10},{10,12},{12,14},{1,3},{3,5},{5,7},{... | collective-permute-start | bytes 983048 | tf_op jit(solution)/shard_map/ppermute | solution.py:25
  59.5 1.8 %reverse_select_fusion.2.bot_ref = f32[4,160,128]{2,1,0:T(8,128)} fusion(f32[4,160,128]{2,1,0:T(8,128)} %collective-permute-done.3, f32[4,160,128]{2,1,0:T(8,128)S(1)} %get-tuple-element.27, pred[]{:T(512)S(6)} %eq.8), kind=kLoop, calls=%fused_computation.15 | loop fusion | flops 81920 | bytes 983041 | tf_op jit(solution)/shard_map/jit(_where)/select_n | solution.py:119
  61.2 9.5 %collective-permute-done.2 = f32[4,160,128]{2,1,0:T(8,128)S(1)} collective-permute-done((f32[4,160,128]{2,1,0:T(8,128)}, f32[4,160,128]{2,1,0:T(8,128)S(1)}, u32[]{:S(2)}, u32[]{:S(2)}) %collective-permute-start.2) | collective-permute-done | bytes 327712 | tf_op jit(solution)/shard_map/ppermute | solution.py:25
  70.7 0.8 reverse_select_fusion.3.top_ref
  71.5 6.7 %shard_map.28 = (f32[32,160,128]{2,1,0:T(8,128)}, f32[16,80,128]{2,1,0:T(8,128)}) custom-call(f32[32,160,128]{2,1,0:T(8,128)} %copy-done.2, f32[4,160,128]{2,1,0:T(8,128)} %reverse_select_fusion.3.top_ref, f32[4,160,128]{2,1,0:T(8,128)} %reverse_select_fusion.2.bot_ref), custom_call_target="tpu_custom_call" | custom-call | tf_op jit(solution)/shard_map/pallas_call | solution.py:95
  78.2 2.0 %fusion.17 = (f32[4,80,128]{2,1,0:T(8,128)}, f32[4,80,128]{2,1,0:T(8,128)}, f32[4,80,128]{2,1,0:T(8,128)}, f32[4,80,128]{2,1,0:T(8,128)}) fusion(f32[16,80,128]{2,1,0:T(8,128)} %get-tuple-element.15.x_ref), kind=kLoop, calls=%fused_computation.33 | loop fusion | bytes 1310720 | tf_op jit(solution)/shard_map/slice | solution.py:119
  80.2 1.3 collective-permute-start.5
  81.5 5.6 %collective-permute-start.4 = (f32[4,80,128]{2,1,0:T(8,128)}, f32[4,80,128]{2,1,0:T(8,128)}, u32[]{:S(2)}, u32[]{:S(2)}) collective-permute-start(f32[4,80,128]{2,1,0:T(8,128)} %get-tuple-element.37), channel_id=1, source_target_pairs={{0,2},{2,4},{4,6},{6,8},{8,10},{10,12},{12,14},{1,3},{3,5},{5,7},{... | collective-permute-start | bytes 491528 | tf_op jit(solution)/shard_map/ppermute | solution.py:25
  87.1 0.0 collective-permute-done.9
  87.1 1.8 %reverse_select_fusion.bot_ref = f32[4,160,128]{2,1,0:T(8,128)} fusion(f32[4,160,128]{2,1,0:T(8,128)} %collective-permute-done.9, f32[4,160,128]{2,1,0:T(8,128)} %get-tuple-element.31, pred[]{:T(512)S(6)} %eq.8), kind=kLoop, calls=%fused_computation.13 | loop fusion | flops 81920 | bytes 983041 | tf_op jit(solution)/shard_map/jit(_where)/select_n | solution.py:119
  88.9 0.0 collective-permute-done.8
  88.9 1.7 %reverse_select_fusion.1.top_ref = f32[4,160,128]{2,1,0:T(8,128)} fusion(f32[4,160,128]{2,1,0:T(8,128)} %collective-permute-done.8, f32[4,160,128]{2,1,0:T(8,128)} %get-tuple-element.34, pred[]{:T(512)S(6)} %eq.7), kind=kLoop, calls=%fused_computation.14 | loop fusion | flops 81920 | bytes 983041 | tf_op jit(solution)/shard_map/jit(_where)/select_n | solution.py:118
  90.7 6.7 %shard_map.31 = (f32[32,160,128]{2,1,0:T(8,128)}, f32[16,80,128]{2,1,0:T(8,128)}) custom-call(f32[32,160,128]{2,1,0:T(8,128)} %copy-done.1, f32[4,160,128]{2,1,0:T(8,128)} %reverse_select_fusion.1.top_ref, f32[4,160,128]{2,1,0:T(8,128)} %reverse_select_fusion.bot_ref), custom_call_target="tpu_custom_call" | custom-call | tf_op jit(solution)/shard_map/pallas_call | solution.py:95
  97.4 2.0 %fusion.18 = (f32[4,80,128]{2,1,0:T(8,128)}, f32[4,80,128]{2,1,0:T(8,128)}, f32[4,80,128]{2,1,0:T(8,128)}, f32[4,80,128]{2,1,0:T(8,128)}) fusion(f32[16,80,128]{2,1,0:T(8,128)} %get-tuple-element.20.x_ref), kind=kLoop, calls=%fused_computation.34 | loop fusion | bytes 1310720 | tf_op jit(solution)/shard_map/slice | solution.py:119
  99.4 1.3 collective-permute-start.11
  100.7 7.0 %collective-permute-start.10 = (f32[4,80,128]{2,1,0:T(8,128)}, f32[4,80,128]{2,1,0:T(8,128)}, u32[]{:S(2)}, u32[]{:S(2)}) collective-permute-start(f32[4,80,128]{2,1,0:T(8,128)} %get-tuple-element.41), channel_id=1, source_target_pairs={{0,2},{2,4},{4,6},{6,8},{8,10},{10,12},{12,14},{1,3},{3,5},{5,7},{... | collective-permute-start | bytes 491528 | tf_op jit(solution)/shard_map/ppermute | solution.py:25
  107.7 1.7 %reverse_select_fusion.6.bot_ref = f32[4,80,128]{2,1,0:T(8,128)} fusion(f32[4,80,128]{2,1,0:T(8,128)} %collective-permute-done.5, f32[4,80,128]{2,1,0:T(8,128)} %get-tuple-element.35, pred[]{:T(512)S(6)} %eq.8), kind=kLoop, calls=%fused_computation.20 | loop fusion | flops 40960 | bytes 491521 | tf_op jit(solution)/shard_map/jit(_where)/select_n | solution.py:119
  109.4 0.0 collective-permute-done.4
  109.4 1.6 reverse_select_fusion.7.top_ref
  111.0 4.4 %shard_map.29 = (f32[32,160,128]{2,1,0:T(8,128)}, f32[8,40,128]{2,1,0:T(8,128)}) custom-call(f32[16,80,128]{2,1,0:T(8,128)} %get-tuple-element.15.x_ref, f32[4,80,128]{2,1,0:T(8,128)} %reverse_select_fusion.7.top_ref, f32[4,80,128]{2,1,0:T(8,128)} %reverse_select_fusion.6.bot_ref, ...), custom_call_target="tpu_custom_call", output_to_operand_aliasing={{0}: (3, {})} | custom-call | tf_op jit(solution)/shard_map/pallas_call | solution.py:95
  115.4 1.8 %fusion.19 = (f32[4,40,128]{2,1,0:T(8,128)}, f32[4,40,128]{2,1,0:T(8,128)}, f32[4,40,128]{2,1,0:T(8,128)}, f32[4,40,128]{2,1,0:T(8,128)}) fusion(f32[8,40,128]{2,1,0:T(8,128)} %get-tuple-element.17.x_ref), kind=kLoop, calls=%fused_computation.35 | loop fusion | bytes 655360 | tf_op jit(solution)/shard_map/slice | solution.py:119
  117.2 1.3 collective-permute-start.7
  118.5 5.5 %collective-permute-start.6 = (f32[4,40,128]{2,1,0:T(8,128)}, f32[4,40,128]{2,1,0:T(8,128)}, u32[]{:S(2)}, u32[]{:S(2)}) collective-permute-start(f32[4,40,128]{2,1,0:T(8,128)} %get-tuple-element.45), channel_id=1, source_target_pairs={{0,2},{2,4},{4,6},{6,8},{8,10},{10,12},{12,14},{1,3},{3,5},{5,7},{... | collective-permute-start | bytes 245768 | tf_op jit(solution)/shard_map/ppermute | solution.py:25
  124.0 0.0 collective-permute-done.11
  124.0 1.7 reverse_select_fusion.4.bot_ref
  125.7 1.6 reverse_select_fusion.5.top_ref
  127.3 4.5 %shard_map.32 = (f32[32,160,128]{2,1,0:T(8,128)}, f32[8,40,128]{2,1,0:T(8,128)}) custom-call(f32[16,80,128]{2,1,0:T(8,128)} %get-tuple-element.20.x_ref, f32[4,80,128]{2,1,0:T(8,128)} %reverse_select_fusion.5.top_ref, f32[4,80,128]{2,1,0:T(8,128)} %reverse_select_fusion.4.bot_ref, ...), custom_call_target="tpu_custom_call", output_to_operand_aliasing={{0}: (3, {})} | custom-call | tf_op jit(solution)/shard_map/pallas_call | solution.py:95
  131.7 1.8 %fusion.20 = (f32[4,40,128]{2,1,0:T(8,128)}, f32[4,40,128]{2,1,0:T(8,128)}, f32[4,40,128]{2,1,0:T(8,128)}, f32[4,40,128]{2,1,0:T(8,128)}) fusion(f32[8,40,128]{2,1,0:T(8,128)} %get-tuple-element.22.x_ref), kind=kLoop, calls=%fused_computation.36 | loop fusion | bytes 655360 | tf_op jit(solution)/shard_map/slice | solution.py:119
  133.5 1.3 collective-permute-start.13
  134.8 5.5 %collective-permute-start.12 = (f32[4,40,128]{2,1,0:T(8,128)}, f32[4,40,128]{2,1,0:T(8,128)}, u32[]{:S(2)}, u32[]{:S(2)}) collective-permute-start(f32[4,40,128]{2,1,0:T(8,128)} %get-tuple-element.49), channel_id=1, source_target_pairs={{0,2},{2,4},{4,6},{6,8},{8,10},{10,12},{12,14},{1,3},{3,5},{5,7},{... | collective-permute-start | bytes 245768 | tf_op jit(solution)/shard_map/ppermute | solution.py:25
  140.3 0.0 collective-permute-done.7
  140.3 1.6 reverse_select_fusion.10.bot_ref
  141.9 1.5 reverse_select_fusion.11.top_ref
  143.4 3.8 %shard_map.30 = (f32[32,160,128]{2,1,0:T(8,128)}, f32[4,20,128]{2,1,0:T(8,128)}) custom-call(f32[8,40,128]{2,1,0:T(8,128)} %get-tuple-element.17.x_ref, f32[4,40,128]{2,1,0:T(8,128)} %reverse_select_fusion.11.top_ref, f32[4,40,128]{2,1,0:T(8,128)} %reverse_select_fusion.10.bot_ref, ...), custom_call_target="tpu_custom_call", output_to_operand_aliasing={{0}: (3, {})} | custom-call | tf_op jit(solution)/shard_map/pallas_call | solution.py:95
  147.2 3.9 %select_bitcast_fusion.1 = f32[128,32,128]{0,2,1:T(8,128)} fusion(f32[32,160,128]{2,1,0:T(8,128)} %get-tuple-element.19, pred[]{:T(512)S(6)} %eq.6), kind=kLoop, calls=%fused_computation.8 | loop fusion | flops 524288 | bytes 6291457 | tf_op jit(solution)/shard_map/transpose | solution.py:163
  151.2 0.0 collective-permute-done.13
  151.2 1.5 reverse_select_fusion.8.bot_ref
  152.7 0.0 collective-permute-done.12
  152.7 0.6 reverse_select_fusion.9.top_ref
  153.4 3.8 %shard_map.33 = (f32[32,160,128]{2,1,0:T(8,128)}, f32[4,20,128]{2,1,0:T(8,128)}) custom-call(f32[8,40,128]{2,1,0:T(8,128)} %get-tuple-element.22.x_ref, f32[4,40,128]{2,1,0:T(8,128)} %reverse_select_fusion.9.top_ref, f32[4,40,128]{2,1,0:T(8,128)} %reverse_select_fusion.8.bot_ref, ...), custom_call_target="tpu_custom_call", output_to_operand_aliasing={{0}: (3, {})} | custom-call | tf_op jit(solution)/shard_map/pallas_call | solution.py:95
  157.2 2.6 %select_bitcast_fusion = f32[128,32,128]{0,2,1:T(8,128)S(1)} fusion(f32[32,160,128]{2,1,0:T(8,128)} %get-tuple-element.24, pred[]{:T(512)S(6)} %eq.6), kind=kLoop, calls=%fused_computation.7 | loop fusion | flops 524288 | bytes 6291457 | tf_op jit(solution)/shard_map/transpose | solution.py:163
  159.8 0.2 copy-done.3
  160.0 2.3 %pad_maximum_fusion = f32[224,32,128]{0,2,1:T(8,128)} fusion(f32[128,32,128]{0,2,1:T(8,128)S(1)} %select_bitcast_fusion, f32[128,32,128]{0,2,1:T(8,128)S(1)} %copy-done.3), kind=kLoop, calls=%fused_computation | loop fusion | flops 917504 | bytes 7864320 | tf_op jit(solution)/shard_map/concatenate | solution.py:164
  162.3 5.1 %copy.20 = f32[224,32,128]{2,1,0:T(8,128)} copy(f32[224,32,128]{0,2,1:T(8,128)} %pad_maximum_fusion) | data formatting | bytes 7340032 | tf_op jit(solution)/shard_map/slice | solution.py:164
  (13 shorter events, 0.0 us)
Async XLA Ops:
  10.4 28.4 %collective-permute-start = (f32[224,32,32]{0,2,1:T(8,128)S(1)}, f32[224,32,32]{0,2,1:T(8,128)S(1)}, u32[]{:S(2)}, u32[]{:S(2)}) collective-permute-start(f32[224,32,32]{0,2,1:T(8,128)S(1)} %copy.21), channel_id=1, source_target_pairs={{1,0},{3,2},{5,4},{7,6},{9,8},{11,10},{13,12},{15,14},{17,16},{19,... | collective-permute-start | bytes 2752520 | tf_op jit(solution)/shard_map/ppermute | solution.py:25
  15.7 23.1 %collective-permute-start.1 = (f32[224,32,32]{0,2,1:T(8,128)}, f32[224,32,32]{0,2,1:T(8,128)S(1)}, u32[]{:S(2)}, u32[]{:S(2)}) collective-permute-start(f32[224,32,32]{0,2,1:T(8,128)} %copy.22), channel_id=1, source_target_pairs={{0,1},{2,3},{4,5},{6,7},{8,9},{10,11},{12,13},{14,15},{16,17},{18,... | collective-permute-start | bytes 2752520 | tf_op jit(solution)/shard_map/ppermute | solution.py:25
  20.1 10.3 %copy-start = (f32[224,32,128]{2,1,0:T(8,128)S(1)}, f32[224,32,128]{2,1,0:T(8,128)}, u32[]{:S(2)}) copy-start(f32[224,32,128]{2,1,0:T(8,128)} %param.2) | copy-start | bytes 11010052
  41.5 1.5 copy-start.2
  41.5 10.4 %copy-start.1 = (f32[32,160,128]{2,1,0:T(8,128)}, f32[32,160,128]{2,1,0:T(8,128)S(1)}, u32[]{:S(2)}) copy-start(f32[32,160,128]{2,1,0:T(8,128)S(1)} %get-tuple-element.52.x_ref) | copy-start | bytes 7864324
  44.1 15.4 %collective-permute-start.3 = (f32[4,160,128]{2,1,0:T(8,128)}, f32[4,160,128]{2,1,0:T(8,128)}, u32[]{:S(2)}, u32[]{:S(2)}) collective-permute-start(f32[4,160,128]{2,1,0:T(8,128)} %get-tuple-element.28), channel_id=1, source_target_pairs={{2,0},{4,2},{6,4},{8,6},{10,8},{12,10},{14,12},{3,1},{5,3},{7,5},{... | collective-permute-start | bytes 983048 | tf_op jit(solution)/shard_map/ppermute | solution.py:25
  45.4 25.4 %collective-permute-start.2 = (f32[4,160,128]{2,1,0:T(8,128)}, f32[4,160,128]{2,1,0:T(8,128)S(1)}, u32[]{:S(2)}, u32[]{:S(2)}) collective-permute-start(f32[4,160,128]{2,1,0:T(8,128)} %get-tuple-element.29), channel_id=1, source_target_pairs={{0,2},{2,4},{4,6},{6,8},{8,10},{10,12},{12,14},{1,3},{3,5},{5,7},{... | collective-permute-start | bytes 983048 | tf_op jit(solution)/shard_map/ppermute | solution.py:25
  52.0 35.1 %collective-permute-start.9 = (f32[4,160,128]{2,1,0:T(8,128)}, f32[4,160,128]{2,1,0:T(8,128)}, u32[]{:S(2)}, u32[]{:S(2)}) collective-permute-start(f32[4,160,128]{2,1,0:T(8,128)} %get-tuple-element.32), channel_id=1, source_target_pairs={{2,0},{4,2},{6,4},{8,6},{10,8},{12,10},{14,12},{3,1},{5,3},{7,5},{... | collective-permute-start | bytes 983048 | tf_op jit(solution)/shard_map/ppermute | solution.py:25
  53.3 35.7 %collective-permute-start.8 = (f32[4,160,128]{2,1,0:T(8,128)}, f32[4,160,128]{2,1,0:T(8,128)}, u32[]{:S(2)}, u32[]{:S(2)}) collective-permute-start(f32[4,160,128]{2,1,0:T(8,128)} %get-tuple-element.33), channel_id=1, source_target_pairs={{0,2},{2,4},{4,6},{6,8},{8,10},{10,12},{12,14},{1,3},{3,5},{5,7},{... | collective-permute-start | bytes 983048 | tf_op jit(solution)/shard_map/ppermute | solution.py:25
  80.2 27.5 %collective-permute-start.5 = (f32[4,80,128]{2,1,0:T(8,128)}, f32[4,80,128]{2,1,0:T(8,128)}, u32[]{:S(2)}, u32[]{:S(2)}) collective-permute-start(f32[4,80,128]{2,1,0:T(8,128)} %get-tuple-element.36), channel_id=1, source_target_pairs={{2,0},{4,2},{6,4},{8,6},{10,8},{12,10},{14,12},{3,1},{5,3},{7,5},{... | collective-permute-start | bytes 491528 | tf_op jit(solution)/shard_map/ppermute | solution.py:25
  81.5 27.9 %collective-permute-start.4 = (f32[4,80,128]{2,1,0:T(8,128)}, f32[4,80,128]{2,1,0:T(8,128)}, u32[]{:S(2)}, u32[]{:S(2)}) collective-permute-start(f32[4,80,128]{2,1,0:T(8,128)} %get-tuple-element.37), channel_id=1, source_target_pairs={{0,2},{2,4},{4,6},{6,8},{8,10},{10,12},{12,14},{1,3},{3,5},{5,7},{... | collective-permute-start | bytes 491528 | tf_op jit(solution)/shard_map/ppermute | solution.py:25
  99.4 24.6 %collective-permute-start.11 = (f32[4,80,128]{2,1,0:T(8,128)}, f32[4,80,128]{2,1,0:T(8,128)}, u32[]{:S(2)}, u32[]{:S(2)}) collective-permute-start(f32[4,80,128]{2,1,0:T(8,128)} %get-tuple-element.40), channel_id=1, source_target_pairs={{2,0},{4,2},{6,4},{8,6},{10,8},{12,10},{14,12},{3,1},{5,3},{7,5},{... | collective-permute-start | bytes 491528 | tf_op jit(solution)/shard_map/ppermute | solution.py:25
  100.7 25.0 %collective-permute-start.10 = (f32[4,80,128]{2,1,0:T(8,128)}, f32[4,80,128]{2,1,0:T(8,128)}, u32[]{:S(2)}, u32[]{:S(2)}) collective-permute-start(f32[4,80,128]{2,1,0:T(8,128)} %get-tuple-element.41), channel_id=1, source_target_pairs={{0,2},{2,4},{4,6},{6,8},{8,10},{10,12},{12,14},{1,3},{3,5},{5,7},{... | collective-permute-start | bytes 491528 | tf_op jit(solution)/shard_map/ppermute | solution.py:25
  117.2 23.2 %collective-permute-start.7 = (f32[4,40,128]{2,1,0:T(8,128)}, f32[4,40,128]{2,1,0:T(8,128)}, u32[]{:S(2)}, u32[]{:S(2)}) collective-permute-start(f32[4,40,128]{2,1,0:T(8,128)} %get-tuple-element.44), channel_id=1, source_target_pairs={{2,0},{4,2},{6,4},{8,6},{10,8},{12,10},{14,12},{3,1},{5,3},{7,5},{... | collective-permute-start | bytes 245768 | tf_op jit(solution)/shard_map/ppermute | solution.py:25
  118.5 23.4 %collective-permute-start.6 = (f32[4,40,128]{2,1,0:T(8,128)}, f32[4,40,128]{2,1,0:T(8,128)}, u32[]{:S(2)}, u32[]{:S(2)}) collective-permute-start(f32[4,40,128]{2,1,0:T(8,128)} %get-tuple-element.45), channel_id=1, source_target_pairs={{0,2},{2,4},{4,6},{6,8},{8,10},{10,12},{12,14},{1,3},{3,5},{5,7},{... | collective-permute-start | bytes 245768 | tf_op jit(solution)/shard_map/ppermute | solution.py:25
  133.5 17.7 %collective-permute-start.13 = (f32[4,40,128]{2,1,0:T(8,128)}, f32[4,40,128]{2,1,0:T(8,128)}, u32[]{:S(2)}, u32[]{:S(2)}) collective-permute-start(f32[4,40,128]{2,1,0:T(8,128)} %get-tuple-element.48), channel_id=1, source_target_pairs={{2,0},{4,2},{6,4},{8,6},{10,8},{12,10},{14,12},{3,1},{5,3},{7,5},{... | collective-permute-start | bytes 245768 | tf_op jit(solution)/shard_map/ppermute | solution.py:25
  134.8 17.9 %collective-permute-start.12 = (f32[4,40,128]{2,1,0:T(8,128)}, f32[4,40,128]{2,1,0:T(8,128)}, u32[]{:S(2)}, u32[]{:S(2)}) collective-permute-start(f32[4,40,128]{2,1,0:T(8,128)} %get-tuple-element.49), channel_id=1, source_target_pairs={{0,2},{2,4},{4,6},{6,8},{8,10},{10,12},{12,14},{1,3},{3,5},{5,7},{... | collective-permute-start | bytes 245768 | tf_op jit(solution)/shard_map/ppermute | solution.py:25
  147.2 3.9 %copy-start.5 = (f32[4,40,128]{2,1,0:T(8,128)S(1)}, f32[4,40,128]{2,1,0:T(8,128)}, u32[]{:S(2)}) copy-start(f32[4,40,128]{2,1,0:T(8,128)} %get-tuple-element.47) | copy-start | bytes 245764
  147.2 5.5 %copy-start.4 = (f32[4,40,128]{2,1,0:T(8,128)S(1)}, f32[4,40,128]{2,1,0:T(8,128)}, u32[]{:S(2)}) copy-start(f32[4,40,128]{2,1,0:T(8,128)} %get-tuple-element.50) | copy-start | bytes 245764
  157.2 2.9 %copy-start.3 = (f32[128,32,128]{0,2,1:T(8,128)S(1)}, f32[128,32,128]{0,2,1:T(8,128)}, u32[]{:S(2)}) copy-start(f32[128,32,128]{0,2,1:T(8,128)} %select_bitcast_fusion.1) | copy-start | bytes 6291460

commit v3 on v2

v3 whole, which is shorter than its diff:
```python
import functools

import jax
import jax.numpy as jnp
from jax import lax
from jax.experimental import pallas as pl
from jax.experimental.pallas import tpu as pltpu
from jax.sharding import PartitionSpec as P

LEVELS = 3
HALO = 32
EDGE = 4
LANES = 128


alpha_one = -1.586134342059924
beta_one = -0.052980118572961
alpha_two = 0.882911075530934
beta_two = 0.443506852043971
scale_k = 1.230174104914001


def shifted(x, axis, by):
    size = lax.axis_size(axis)
    pairs = [(i, i + by) for i in range(size) if 0 <= i + by < size]
    return lax.ppermute(x, axis, pairs)


def fill_rows(ext, flags, top, bot, rows):
    first = flags[1] == 1
    last = flags[2] == 1

    @pl.when(first)
    def _():
        ext[0:EDGE] = jnp.concatenate(
            [ext[2 * EDGE - k : 2 * EDGE - k + 1] for k in range(EDGE)], axis=0
        )

    @pl.when(jnp.logical_not(first))
    def _():
        ext[0:EDGE] = top

    base = EDGE + rows

    @pl.when(last)
    def _():
        ext[base : base + EDGE] = jnp.concatenate(
            [ext[base - 2 - k : base - 1 - k] for k in range(EDGE)], axis=0
        )

    @pl.when(jnp.logical_not(last))
    def _():
        ext[base : base + EDGE] = bot


def lift_block(ext, half, out_ref, ll_ref, rows, width, stride):
    hr, hw = rows // 2, width // 2
    a1, b1, a2, b2 = alpha_one, beta_one, alpha_two, beta_two
    n = hr + EDGE
    pairs = ext[...].reshape(n, 2, width, LANES)
    s = pairs[:, 0]
    d = pairs[:, 1]

    def nxt0(v):
        return jnp.concatenate([v[1:], v[-1:]], axis=0)

    def prv0(v):
        return jnp.concatenate([v[:1], v[:-1]], axis=0)

    d = d + a1 * (s + nxt0(s))
    s = s + b1 * (prv0(d) + d)
    d = d + a2 * (s + nxt0(s))
    s = s + b2 * (prv0(d) + d)
    lo = EDGE // 2
    half[0] = s[lo : lo + hr] / scale_k
    half[1] = d[lo : lo + hr] * scale_k

    col = lax.broadcasted_iota(jnp.int32, (hr, hw, LANES), 1)

    def nxt1(v):
        return jnp.where(col == hw - 1, v, pltpu.roll(v, hw - 1, 1))

    def prv1(v):
        return jnp.where(col == 0, v, pltpu.roll(v, 1, 1))

    step = 2 * stride
    for pr in range(2):
        e = half[pr, :, pl.ds(0, hw, stride=2), :]
        o = half[pr, :, pl.ds(1, hw, stride=2), :]
        o = o + a1 * (e + nxt1(e))
        e = e + b1 * (prv1(o) + o)
        o = o + a2 * (e + nxt1(e))
        e = e + b2 * (prv1(o) + o)
        e = e / scale_k
        o = o * scale_k
        out_ref[pl.ds(pr * stride, hr, stride=step), pl.ds(0, hw, stride=step), :] = e
        out_ref[pl.ds(pr * stride, hr, stride=step), pl.ds(stride, hw, stride=step), :] = o
        if pr == 0:
            ll_ref[...] = e


def first_kernel(flags, own, halo, top_own, top_halo, bot_own, bot_halo, out_ref, ll_ref, ext, half):
    rows, width = own.shape[0], own.shape[1] + halo.shape[1]
    h = halo.shape[1]
    on_left = flags[0] == 1

    @pl.when(on_left)
    def _():
        ext[EDGE : EDGE + rows, 0 : width - h] = own[...]
        ext[EDGE : EDGE + rows, width - h : width] = halo[...]

    @pl.when(jnp.logical_not(on_left))
    def _():
        ext[EDGE : EDGE + rows, 0:h] = halo[...]
        ext[EDGE : EDGE + rows, h:width] = own[...]

    top = jnp.where(on_left, jnp.concatenate([top_own[...], top_halo[...]], axis=1),
                    jnp.concatenate([top_halo[...], top_own[...]], axis=1))
    bot = jnp.where(on_left, jnp.concatenate([bot_own[...], bot_halo[...]], axis=1),
                    jnp.concatenate([bot_halo[...], bot_own[...]], axis=1))
    fill_rows(ext, flags, top, bot, rows)
    lift_block(ext, half, out_ref, ll_ref, rows, width, 1)


def next_kernel(flags, x_ref, top_ref, bot_ref, prev_ref, out_ref, ll_ref, ext, half, *, stride):
    rows, width = x_ref.shape[0], x_ref.shape[1]
    out_ref[...] = prev_ref[...]
    ext[EDGE : EDGE + rows] = x_ref[...]
    fill_rows(ext, flags, top_ref[...], bot_ref[...], rows)
    lift_block(ext, half, out_ref, ll_ref, rows, width, stride)


def spec(shape):
    return pl.BlockSpec(shape[:-1] + (LANES,), lambda h, f: (0,) * (len(shape) - 1) + (h,))


def level_call(kernel, flags, arrays, out_shape, rows, width, aliases):
    bands = arrays[0].shape[-1]
    ll_shape = (rows // 2, width // 2, bands)
    grid_spec = pltpu.PrefetchScalarGridSpec(
        num_scalar_prefetch=1,
        grid=(bands // LANES,),
        in_specs=[spec(a.shape) for a in arrays],
        out_specs=(spec(out_shape), spec(ll_shape)),
        scratch_shapes=[
            pltpu.VMEM((rows + 2 * EDGE, width, LANES), jnp.float32),
            pltpu.VMEM((2, rows // 2, width, LANES), jnp.float32),
        ],
    )
    return pl.pallas_call(
        kernel,
        grid_spec=grid_spec,
        out_shape=(
            jax.ShapeDtypeStruct(out_shape, jnp.float32),
            jax.ShapeDtypeStruct(ll_shape, jnp.float32),
        ),
        input_output_aliases=aliases,
        compiler_params=pltpu.CompilerParams(vmem_limit_bytes=100 * 1024 * 1024),
    )(flags, *arrays)


def edge_rows(x):
    rows = x.shape[0]
    return shifted(x[rows - EDGE :], "rows", 1), shifted(x[:EDGE], "rows", -1)


def on_device(radiance, decorrelation):
    bands, rows, width = radiance.shape
    padded_bands = -(-bands // LANES) * LANES
    on_left = lax.axis_index("cols") == 0
    flags = jnp.stack(
        [
            on_left,
            lax.axis_index("rows") == 0,
            lax.axis_index("rows") == lax.axis_size("rows") - 1,
        ]
    ).astype(jnp.int32)
    right_of_left = shifted(radiance[:, :, :HALO], "cols", -1)
    left_of_right = shifted(radiance[:, :, width - HALO :], "cols", 1)
    halo_in = jnp.where(on_left, right_of_left, left_of_right)
    weights = jnp.pad(decorrelation, ((0, padded_bands - bands), (0, 0)))

    def mix(x):
        return jnp.einsum("crw,bc->rwb", x, weights, precision=lax.Precision.HIGHEST,
                          preferred_element_type=jnp.float32)

    own = mix(radiance)
    halo = mix(halo_in)
    top_own, bot_own = edge_rows(own)
    top_halo, bot_halo = edge_rows(halo)
    ext_width = width + HALO
    out_shape = (rows, ext_width, padded_bands)
    out, level = level_call(
        first_kernel, flags, [own, halo, top_own, top_halo, bot_own, bot_halo],
        out_shape, rows, ext_width, {})
    for lvl in range(1, LEVELS):
        top, bot = edge_rows(level)
        r, w = level.shape[0], level.shape[1]
        out, level = level_call(
            functools.partial(next_kernel, stride=2**lvl), flags,
            [level, top, bot, out], out_shape, r, w, {4: 0})
    coeffs = jnp.where(on_left, out[:, :width], out[:, HALO : HALO + width])
    return jnp.transpose(coeffs, (2, 0, 1))[:bands]


def solution(mesh):
    assert mesh.shape["cols"] == 2
    placed = (P(None, ("groups", "rows"), "cols"), P())
    return jax.shard_map(
        on_device,
        mesh=mesh,
        in_specs=placed,
        out_specs=P(None, ("groups", "rows"), "cols"),
        check_vma=False,
    )
```

time: 169 us -> 136 us (0.80)
  waiting for transfers between devices: 9.54 us -> 35.9 us
  other arithmetic: 27.5 us -> 6.92 us
  starting transfers between devices: 47.7 us -> 30.2 us
  matrix products: 20.7 us -> 11.4 us
  Pallas kernels: 29.9 us -> 23 us
  local copies, waits for them, and re-layouts: 32 us -> 27.5 us
    ppermute x14 -> x10, waiting for transfers between devices: 9.54 us -> 35.9 us  [shifted(): return lax.ppermute(x, axis, pairs)]
    select_n x13 -> x0, other arithmetic: 18.6 us -> none  [the longest x6 10 us: row_halos(): bot = jnp.where(at_last, x[rows - 2:rows - 2 - EDGE:-1], from_next)]
    ppermute x14 -> x10, starting transfers between devices: 47.7 us -> 30.2 us  [shifted(): return lax.ppermute(x, axis, pairs)]
    dot_general x4 -> x2, matrix products: 20.7 us -> 11.4 us  [mix(): jnp.einsum('crw,bc->rwb', x, weights, precision=lax.Precision.HIGHEST, pr...]
    pallas_call x6 -> x3, Pallas kernels: 29.9 us -> 23 us  [level_call(): pl.pallas_call(kernel, grid_spec=grid_spec, out_shape=(jax.ShapeDtypeStru...]
    slice x7 -> x5, local copies, waits for them, and re-layouts: 14.8 us -> 8.34 us  [the longest x1 5.1 us: on_device(): return jnp.transpose(coeffs, (2, 0, 1))[:bands]]
    concatenate x1 -> x0, other arithmetic: 2.28 us -> none  [on_device(): return jnp.concatenate(parts, axis=0)[:radiance.shape[0]]]
    unnamed x15 -> x9, local copies, waits for them, and re-layouts: 10 us -> 11.9 us
  transfers between devices with their start and end apart: 14 -> 10, of which waited for: 1 -> 5; matrix products, arithmetic and copies ran while one was open for 32% -> 13% of each run, Pallas kernels for 16% -> 0%
where the time goes in v3:
time: 136 us; the launch traced here: 135 us
  waiting for transfers between devices  35.9 us (26%)
  starting transfers between devices  30.2 us (22%)
  local copies, waits for them, and re-layouts  27.5 us (20%)
  Pallas kernels  23 us (17%)
  matrix products  11.4 us (8%)
  other arithmetic  6.92 us (5%)
    ppermute x10, waiting for transfers between devices, shifted(): return lax.ppermute(x, axis, pairs)  35.9 us
    ppermute x10, starting transfers between devices, shifted(): return lax.ppermute(x, axis, pairs)  30.2 us
    pallas_call x3, Pallas kernels, level_call(): pl.pallas_call(kernel, grid_spec=grid_spec, out_shape=(jax.ShapeDtypeStru...  23 us
    unnamed x9, local copies, waits for them, and re-layouts  11.9 us
    dot_general x2, matrix products, mix(): jnp.einsum('crw,bc->rwb', x, weights, precision=lax.Precision.HIGHEST, pr...  11.4 us
    slice x1, local copies, waits for them, and re-layouts, on_device(): left_of_right = shifted(radiance[:, :, width - HALO:], 'cols', 1)  7.21 us
    transpose x1, other arithmetic, on_device(): return jnp.transpose(coeffs, (2, 0, 1))[:bands]  6.25 us
    slice x1, local copies, waits for them, and re-layouts, on_device(): return jnp.transpose(coeffs, (2, 0, 1))[:bands]  5.1 us
  transfers between devices with their start and end apart: 10, of which 5 were waited for; matrix products, arithmetic and copies ran while one was open for 13% of the time, Pallas kernels for 0%

profile of v3, /device:TPU:0, one launch (start us, length us, event | category | flops | bytes accessed | tf_op | source)
XLA Modules:
  0.0 135.0 jit_solution(9968597300621952675)
XLA Ops:
  0.0 7.2 %fusion.15 = (f32[224,32,32]{2,1,0:T(8,128)}, f32[224,32,32]{2,1,0:T(8,128)}) fusion(f32[224,32,128]{2,1,0:T(8,128)} %param.2), kind=kLoop, calls=%fused_computation.15 | loop fusion | bytes 3670016 | tf_op jit(solution)/shard_map/slice | solution.py:179
  7.2 3.2 %copy.17 = f32[224,32,32]{0,2,1:T(8,128)S(1)} copy(f32[224,32,32]{2,1,0:T(8,128)} %get-tuple-element.18) | data formatting | bytes 1835008
  10.4 1.3 collective-permute-start
  11.7 4.0 %copy.18 = f32[224,32,32]{0,2,1:T(8,128)} copy(f32[224,32,32]{2,1,0:T(8,128)} %get-tuple-element.17) | data formatting | bytes 1835008
  15.7 3.1 %collective-permute-start.1 = (f32[224,32,32]{0,2,1:T(8,128)}, f32[224,32,32]{0,2,1:T(8,128)S(1)}, u32[]{:S(2)}, u32[]{:S(2)}) collective-permute-start(f32[224,32,32]{0,2,1:T(8,128)} %copy.18), channel_id=1, source_target_pairs={{0,1},{2,3},{4,5},{6,7},{8,9},{10,11},{12,13},{14,15},{16,17},{18,... | collective-permute-start | bytes 2752520 | tf_op jit(solution)/shard_map/ppermute | solution.py:26
  18.8 1.1 copy.10
  19.9 10.4 %fusion.2.own = f32[32,128,256]{2,1,0:T(8,128)S(1)} fusion(f32[224,32,128]{2,1,0:T(8,128)} %param.2, f32[224,224]{0,1:T(8,128)S(1)} %copy.10), kind=kOutput, calls=%fused_computation.3 | convolution fusion | flops 2818572288 | bytes 8065024 | tf_op jit(solution)/shard_map/crw,bc->rwb/dot_general | solution.py:184
  30.3 0.0 copy-start
  30.3 2.0 %copy-done = f32[32,128,256]{2,1,0:T(8,128)} copy-done((f32[32,128,256]{2,1,0:T(8,128)}, f32[32,128,256]{2,1,0:T(8,128)S(1)}, u32[]{:S(2)}) %copy-start) | copy-done | bytes 4194328
  32.3 1.1 fusion.14
  33.4 5.8 %collective-permute-start.2 = (f32[4,128,256]{2,1,0:T(8,128)}, f32[4,128,256]{2,1,0:T(8,128)}, u32[]{:S(2)}, u32[]{:S(2)}) collective-permute-start(f32[4,128,256]{2,1,0:T(8,128)} %get-tuple-element.16), channel_id=1, source_target_pairs={{0,2},{2,4},{4,6},{6,8},{8,10},{10,12},{12,14},{1,3},{3,5},{5,7},{... | collective-permute-start | bytes 1572872 | tf_op jit(solution)/shard_map/ppermute | solution.py:26
  39.3 1.3 collective-permute-start.4
  40.6 0.0 collective-permute-done
  40.6 0.0 collective-permute-done.1
  40.6 1.0 fusion.5.halo
  41.6 0.0 copy-start.1
  41.6 1.0 copy-done.1
  42.6 4.6 %collective-permute-start.3 = (f32[4,32,256]{2,1,0:T(8,128)S(1)}, f32[4,32,256]{2,1,0:T(8,128)S(1)}, u32[]{:S(2)}, u32[]{:S(2)}) collective-permute-start(f32[4,32,256]{2,1,0:T(8,128)S(1)} %get-tuple-element.22), channel_id=1, source_target_pairs={{0,2},{2,4},{4,6},{6,8},{8,10},{10,12},{12,14},{1,3},{3,5},{5,7},{... | collective-permute-start | bytes 393224 | tf_op jit(solution)/shard_map/ppermute | solution.py:26
  47.1 1.3 collective-permute-start.5
  48.5 0.7 add_convert_fusion.flags
  49.1 15.6 %collective-permute-done.2.top_own = f32[4,128,256]{2,1,0:T(8,128)} collective-permute-done((f32[4,128,256]{2,1,0:T(8,128)}, f32[4,128,256]{2,1,0:T(8,128)}, u32[]{:S(2)}, u32[]{:S(2)}) %collective-permute-start.2) | collective-permute-done | bytes 524320 | tf_op jit(solution)/shard_map/ppermute | solution.py:26
  64.7 0.0 collective-permute-done.4.bot_own
  64.7 1.3 collective-permute-done.3.top_halo
  66.0 0.0 copy-start.2
  66.0 0.6 copy-done.2
  66.7 0.0 collective-permute-done.5.bot_halo
  66.7 11.3 %shard_map.28 = (f32[32,160,256]{2,1,0:T(8,128)}, f32[16,80,256]{2,1,0:T(8,128)}) custom-call(s32[3]{0:T(128)} %add_convert_fusion.flags, f32[32,128,256]{2,1,0:T(8,128)} %copy-done, f32[32,32,256]{2,1,0:T(8,128)} %copy-done.1, f32[4,128,256]{2,1,0:T(8,128)} %collective-permute-done.2.top_own, f32[4,32,256]{2,1,0:T(8,128)} %copy-done.2, ...), custom_call_target="tpu_custom_call" | custom-call | tf_op jit(solution)/shard_map/pallas_call | solution.py:150
  78.0 1.1 fusion.16
  79.1 5.1 %collective-permute-start.6 = (f32[4,80,256]{2,1,0:T(8,128)S(1)}, f32[4,80,256]{2,1,0:T(8,128)}, u32[]{:S(2)}, u32[]{:S(2)}) collective-permute-start(f32[4,80,256]{2,1,0:T(8,128)S(1)} %get-tuple-element.20), channel_id=1, source_target_pairs={{0,2},{2,4},{4,6},{6,8},{8,10},{10,12},{12,14},{1,3},{3,5},{5,7},{... | collective-permute-start | bytes 983048 | tf_op jit(solution)/shard_map/ppermute | solution.py:26
  84.2 1.3 collective-permute-start.7
  85.5 10.6 %collective-permute-done.6.top_ref = f32[4,80,256]{2,1,0:T(8,128)} collective-permute-done((f32[4,80,256]{2,1,0:T(8,128)S(1)}, f32[4,80,256]{2,1,0:T(8,128)}, u32[]{:S(2)}, u32[]{:S(2)}) %collective-permute-start.6) | collective-permute-done | bytes 327712 | tf_op jit(solution)/shard_map/ppermute | solution.py:26
  96.1 0.0 collective-permute-done.7.bot_ref
  96.1 6.3 %shard_map.29 = (f32[32,160,256]{2,1,0:T(8,128)}, f32[8,40,256]{2,1,0:T(8,128)}) custom-call(s32[3]{0:T(128)} %add_convert_fusion.flags, f32[16,80,256]{2,1,0:T(8,128)} %get-tuple-element.10.x_ref, f32[4,80,256]{2,1,0:T(8,128)} %collective-permute-done.6.top_ref, f32[4,80,256]{2,1,0:T(8,128)} %collective-permute-done.7.bot_ref, ...), custom_call_target="tpu_custom_call", output_to_operand_aliasing={{0}: (4, {})} | custom-call | tf_op jit(solution)/shard_map/pallas_call | solution.py:150
  102.4 1.0 fusion.18
  103.4 5.2 %collective-permute-start.8 = (f32[4,40,256]{2,1,0:T(8,128)S(1)}, f32[4,40,256]{2,1,0:T(8,128)}, u32[]{:S(2)}, u32[]{:S(2)}) collective-permute-start(f32[4,40,256]{2,1,0:T(8,128)S(1)} %get-tuple-element.24), channel_id=1, source_target_pairs={{0,2},{2,4},{4,6},{6,8},{8,10},{10,12},{12,14},{1,3},{3,5},{5,7},{... | collective-permute-start | bytes 491528 | tf_op jit(solution)/shard_map/ppermute | solution.py:26
  108.6 1.3 collective-permute-start.9
  109.9 0.9 collective-permute-done.8.top_ref
  110.7 7.6 %collective-permute-done.9.bot_ref = f32[4,40,256]{2,1,0:T(8,128)} collective-permute-done((f32[4,40,256]{2,1,0:T(8,128)S(1)}, f32[4,40,256]{2,1,0:T(8,128)}, u32[]{:S(2)}, u32[]{:S(2)}) %collective-permute-start.9) | collective-permute-done | bytes 163872 | tf_op jit(solution)/shard_map/ppermute | solution.py:26
  118.3 5.4 %shard_map.30 = (f32[32,160,256]{2,1,0:T(8,128)}, f32[4,20,256]{2,1,0:T(8,128)}) custom-call(s32[3]{0:T(128)} %add_convert_fusion.flags, f32[8,40,256]{2,1,0:T(8,128)} %get-tuple-element.12.x_ref, f32[4,40,256]{2,1,0:T(8,128)} %collective-permute-done.8.top_ref, f32[4,40,256]{2,1,0:T(8,128)} %collective-permute-done.9.bot_ref, ...), custom_call_target="tpu_custom_call", output_to_operand_aliasing={{0}: (4, {})} | custom-call | tf_op jit(solution)/shard_map/pallas_call | solution.py:150
  123.7 6.2 %select_bitcast_fusion = f32[256,32,128]{0,2,1:T(8,128)} fusion(f32[32,160,256]{2,1,0:T(8,128)} %get-tuple-element.14, pred[]{:T(512)} %eq.9), kind=kLoop, calls=%fused_computation | loop fusion | flops 1048576 | bytes 12582913 | tf_op jit(solution)/shard_map/transpose | solution.py:203
  129.9 5.1 %copy.15 = f32[224,32,128]{2,1,0:T(8,128)} copy(f32[224,32,128]{0,2,1:T(8,128)} %bitcast.13) | data formatting | bytes 7340032 | tf_op jit(solution)/shard_map/slice | solution.py:203
  (1 shorter events, 0.0 us)
Async XLA Ops:
  10.4 30.2 %collective-permute-start = (f32[224,32,32]{0,2,1:T(8,128)S(1)}, f32[224,32,32]{0,2,1:T(8,128)S(1)}, u32[]{:S(2)}, u32[]{:S(2)}) collective-permute-start(f32[224,32,32]{0,2,1:T(8,128)S(1)} %copy.17), channel_id=1, source_target_pairs={{1,0},{3,2},{5,4},{7,6},{9,8},{11,10},{13,12},{15,14},{17,16},{19,... | collective-permute-start | bytes 2752520 | tf_op jit(solution)/shard_map/ppermute | solution.py:26
  15.7 24.9 %collective-permute-start.1 = (f32[224,32,32]{0,2,1:T(8,128)}, f32[224,32,32]{0,2,1:T(8,128)S(1)}, u32[]{:S(2)}, u32[]{:S(2)}) collective-permute-start(f32[224,32,32]{0,2,1:T(8,128)} %copy.18), channel_id=1, source_target_pairs={{0,1},{2,3},{4,5},{6,7},{8,9},{10,11},{12,13},{14,15},{16,17},{18,... | collective-permute-start | bytes 2752520 | tf_op jit(solution)/shard_map/ppermute | solution.py:26
  30.3 2.0 %copy-start = (f32[32,128,256]{2,1,0:T(8,128)}, f32[32,128,256]{2,1,0:T(8,128)S(1)}, u32[]{:S(2)}) copy-start(f32[32,128,256]{2,1,0:T(8,128)S(1)} %fusion.2.own) | copy-start | bytes 12582916
  33.4 31.3 %collective-permute-start.2 = (f32[4,128,256]{2,1,0:T(8,128)}, f32[4,128,256]{2,1,0:T(8,128)}, u32[]{:S(2)}, u32[]{:S(2)}) collective-permute-start(f32[4,128,256]{2,1,0:T(8,128)} %get-tuple-element.16), channel_id=1, source_target_pairs={{0,2},{2,4},{4,6},{6,8},{8,10},{10,12},{12,14},{1,3},{3,5},{5,7},{... | collective-permute-start | bytes 1572872 | tf_op jit(solution)/shard_map/ppermute | solution.py:26
  39.3 25.4 %collective-permute-start.4 = (f32[4,128,256]{2,1,0:T(8,128)}, f32[4,128,256]{2,1,0:T(8,128)}, u32[]{:S(2)}, u32[]{:S(2)}) collective-permute-start(f32[4,128,256]{2,1,0:T(8,128)} %get-tuple-element.15), channel_id=1, source_target_pairs={{2,0},{4,2},{6,4},{8,6},{10,8},{12,10},{14,12},{3,1},{5,3},{7,5},{... | collective-permute-start | bytes 1572872 | tf_op jit(solution)/shard_map/ppermute | solution.py:26
  41.6 1.0 copy-start.1
  42.6 23.4 %collective-permute-start.3 = (f32[4,32,256]{2,1,0:T(8,128)S(1)}, f32[4,32,256]{2,1,0:T(8,128)S(1)}, u32[]{:S(2)}, u32[]{:S(2)}) collective-permute-start(f32[4,32,256]{2,1,0:T(8,128)S(1)} %get-tuple-element.22), channel_id=1, source_target_pairs={{0,2},{2,4},{4,6},{6,8},{8,10},{10,12},{12,14},{1,3},{3,5},{5,7},{... | collective-permute-start | bytes 393224 | tf_op jit(solution)/shard_map/ppermute | solution.py:26
  47.1 19.5 %collective-permute-start.5 = (f32[4,32,256]{2,1,0:T(8,128)S(1)}, f32[4,32,256]{2,1,0:T(8,128)}, u32[]{:S(2)}, u32[]{:S(2)}) collective-permute-start(f32[4,32,256]{2,1,0:T(8,128)S(1)} %get-tuple-element.21), channel_id=1, source_target_pairs={{2,0},{4,2},{6,4},{8,6},{10,8},{12,10},{14,12},{3,1},{5,3},{7,5},{... | collective-permute-start | bytes 393224 | tf_op jit(solution)/shard_map/ppermute | solution.py:26
  66.0 0.7 copy-start.2
  79.1 17.0 %collective-permute-start.6 = (f32[4,80,256]{2,1,0:T(8,128)S(1)}, f32[4,80,256]{2,1,0:T(8,128)}, u32[]{:S(2)}, u32[]{:S(2)}) collective-permute-start(f32[4,80,256]{2,1,0:T(8,128)S(1)} %get-tuple-element.20), channel_id=1, source_target_pairs={{0,2},{2,4},{4,6},{6,8},{8,10},{10,12},{12,14},{1,3},{3,5},{5,7},{... | collective-permute-start | bytes 983048 | tf_op jit(solution)/shard_map/ppermute | solution.py:26
  84.2 11.9 %collective-permute-start.7 = (f32[4,80,256]{2,1,0:T(8,128)S(1)}, f32[4,80,256]{2,1,0:T(8,128)}, u32[]{:S(2)}, u32[]{:S(2)}) collective-permute-start(f32[4,80,256]{2,1,0:T(8,128)S(1)} %get-tuple-element.19), channel_id=1, source_target_pairs={{2,0},{4,2},{6,4},{8,6},{10,8},{12,10},{14,12},{3,1},{5,3},{7,5},{... | collective-permute-start | bytes 983048 | tf_op jit(solution)/shard_map/ppermute | solution.py:26
  103.4 7.3 %collective-permute-start.8 = (f32[4,40,256]{2,1,0:T(8,128)S(1)}, f32[4,40,256]{2,1,0:T(8,128)}, u32[]{:S(2)}, u32[]{:S(2)}) collective-permute-start(f32[4,40,256]{2,1,0:T(8,128)S(1)} %get-tuple-element.24), channel_id=1, source_target_pairs={{0,2},{2,4},{4,6},{6,8},{8,10},{10,12},{12,14},{1,3},{3,5},{5,7},{... | collective-permute-start | bytes 491528 | tf_op jit(solution)/shard_map/ppermute | solution.py:26
  108.6 9.7 %collective-permute-start.9 = (f32[4,40,256]{2,1,0:T(8,128)S(1)}, f32[4,40,256]{2,1,0:T(8,128)}, u32[]{:S(2)}, u32[]{:S(2)}) collective-permute-start(f32[4,40,256]{2,1,0:T(8,128)S(1)} %get-tuple-element.23), channel_id=1, source_target_pairs={{2,0},{4,2},{6,4},{8,6},{10,8},{12,10},{14,12},{3,1},{5,3},{7,5},{... | collective-permute-start | bytes 491528 | tf_op jit(solution)/shard_map/ppermute | solution.py:26

commit v4 on v3

--- a/solution.py
+++ b/solution.py
@@ -26,9 +26,27 @@
     return lax.ppermute(x, axis, pairs)
 
 
-def fill_rows(ext, flags, top, bot, rows):
+def partials(x, axis):
+    a1, b1 = alpha_one, beta_one
+    n = x.shape[axis]
+
+    def row(i):
+        return lax.slice_in_dim(x, i, i + 1, axis=axis)
+
+    s_pen, d_pen, s_last, d_last = row(n - 4), row(n - 3), row(n - 2), row(n - 1)
+    s0, d0, s1 = row(0), row(1), row(2)
+    to_next = jnp.concatenate(
+        [s_last + b1 * (d_pen + a1 * (s_pen + s_last)), d_last + a1 * s_last], axis=axis
+    )
+    to_prev = jnp.concatenate([s0, d0 + a1 * (s0 + s1)], axis=axis)
+    return to_next, to_prev
+
+
+def fill_rows(ext, flags, from_prev, from_next, rows):
+    a1 = alpha_one
     first = flags[1] == 1
     last = flags[2] == 1
+    base = EDGE + rows
 
     @pl.when(first)
     def _():
@@ -38,9 +56,8 @@
 
     @pl.when(jnp.logical_not(first))
     def _():
-        ext[0:EDGE] = top
-
-    base = EDGE + rows
+        b, a = from_prev[0:1], from_prev[1:2]
+        ext[0:EDGE] = jnp.concatenate([jnp.zeros_like(b), -a1 * b, b, a - a1 * b], axis=0)
 
     @pl.when(last)
     def _():
@@ -50,10 +67,12 @@
 
     @pl.when(jnp.logical_not(last))
     def _():
-        ext[base : base + EDGE] = bot
-
-
-def lift_block(ext, half, out_ref, ll_ref, rows, width, stride):
+        s, dp = from_next[0:1], from_next[1:2]
+        z = jnp.zeros_like(s)
+        ext[base : base + EDGE] = jnp.concatenate([s, dp - a1 * s, z, z], axis=0)
+
+
+def lift_block(ext, half, out_ref, ll_ref, tn_ref, tp_ref, rows, width, stride):
     hr, hw = rows // 2, width // 2
     a1, b1, a2, b2 = alpha_one, beta_one, alpha_two, beta_two
     n = hr + EDGE
@@ -97,11 +116,15 @@
         out_ref[pl.ds(pr * stride, hr, stride=step), pl.ds(stride, hw, stride=step), :] = o
         if pr == 0:
             ll_ref[...] = e
-
-
-def first_kernel(flags, own, halo, top_own, top_halo, bot_own, bot_halo, out_ref, ll_ref, ext, half):
-    rows, width = own.shape[0], own.shape[1] + halo.shape[1]
-    h = halo.shape[1]
+            to_next, to_prev = partials(e, 0)
+            tn_ref[...] = to_next
+            tp_ref[...] = to_prev
+
+
+def first_kernel(flags, own, halo, prev_own, prev_halo, next_own, next_halo,
+                 out_ref, ll_ref, tn_ref, tp_ref, ext, half):
+    rows, h = own.shape[0], halo.shape[1]
+    width = own.shape[1] + h
     on_left = flags[0] == 1
 
     @pl.when(on_left)
@@ -114,20 +137,21 @@
         ext[EDGE : EDGE + rows, 0:h] = halo[...]
         ext[EDGE : EDGE + rows, h:width] = own[...]
 
-    top = jnp.where(on_left, jnp.concatenate([top_own[...], top_halo[...]], axis=1),
-                    jnp.concatenate([top_halo[...], top_own[...]], axis=1))
-    bot = jnp.where(on_left, jnp.concatenate([bot_own[...], bot_halo[...]], axis=1),
-                    jnp.concatenate([bot_halo[...], bot_own[...]], axis=1))
-    fill_rows(ext, flags, top, bot, rows)
-    lift_block(ext, half, out_ref, ll_ref, rows, width, 1)
-
-
-def next_kernel(flags, x_ref, top_ref, bot_ref, prev_ref, out_ref, ll_ref, ext, half, *, stride):
+    def joined(o, hh):
+        return jnp.where(on_left, jnp.concatenate([o[...], hh[...]], axis=1),
+                         jnp.concatenate([hh[...], o[...]], axis=1))
+
+    fill_rows(ext, flags, joined(prev_own, prev_halo), joined(next_own, next_halo), rows)
+    lift_block(ext, half, out_ref, ll_ref, tn_ref, tp_ref, rows, width, 1)
+
+
+def next_kernel(flags, x_ref, from_prev, from_next, prev_out,
+                out_ref, ll_ref, tn_ref, tp_ref, ext, half, *, stride):
     rows, width = x_ref.shape[0], x_ref.shape[1]
-    out_ref[...] = prev_ref[...]
+    out_ref[...] = prev_out[...]
     ext[EDGE : EDGE + rows] = x_ref[...]
-    fill_rows(ext, flags, top_ref[...], bot_ref[...], rows)
-    lift_block(ext, half, out_ref, ll_ref, rows, width, stride)
+    fill_rows(ext, flags, from_prev[...], from_next[...], rows)
+    lift_block(ext, half, out_ref, ll_ref, tn_ref, tp_ref, rows, width, stride)
 
 
 def spec(shape):
@@ -137,11 +161,13 @@
 def level_call(kernel, flags, arrays, out_shape, rows, width, aliases):
     bands = arrays[0].shape[-1]
     ll_shape = (rows // 2, width // 2, bands)
+    edge_shape = (2, width // 2, bands)
+    outs = (out_shape, ll_shape, edge_shape, edge_shape)
     grid_spec = pltpu.PrefetchScalarGridSpec(
         num_scalar_prefetch=1,
         grid=(bands // LANES,),
         in_specs=[spec(a.shape) for a in arrays],
-        out_specs=(spec(out_shape), spec(ll_shape)),
+        out_specs=tuple(spec(o) for o in outs),
         scratch_shapes=[
             pltpu.VMEM((rows + 2 * EDGE, width, LANES), jnp.float32),
             pltpu.VMEM((2, rows // 2, width, LANES), jnp.float32),
@@ -150,18 +176,25 @@
     return pl.pallas_call(
         kernel,
         grid_spec=grid_spec,
-        out_shape=(
-            jax.ShapeDtypeStruct(out_shape, jnp.float32),
-            jax.ShapeDtypeStruct(ll_shape, jnp.float32),
-        ),
+        out_shape=tuple(jax.ShapeDtypeStruct(o, jnp.float32) for o in outs),
         input_output_aliases=aliases,
         compiler_params=pltpu.CompilerParams(vmem_limit_bytes=100 * 1024 * 1024),
     )(flags, *arrays)
 
 
-def edge_rows(x):
-    rows = x.shape[0]
-    return shifted(x[rows - EDGE :], "rows", 1), shifted(x[:EDGE], "rows", -1)
+def to_core_mate(x):
+    return lax.ppermute(x, "cols", [(0, 1), (1, 0)])
+
+
+def diagonal(x, by):
+    rows = lax.axis_size("rows")
+    pairs = [
+        (r * 2 + c, (r + by) * 2 + 1 - c)
+        for r in range(rows)
+        for c in range(2)
+        if 0 <= r + by < rows
+    ]
+    return lax.ppermute(x, ("rows", "cols"), pairs)
 
 
 def on_device(radiance, decorrelation):
@@ -175,30 +208,36 @@
             lax.axis_index("rows") == lax.axis_size("rows") - 1,
         ]
     ).astype(jnp.int32)
-    right_of_left = shifted(radiance[:, :, :HALO], "cols", -1)
-    left_of_right = shifted(radiance[:, :, width - HALO :], "cols", 1)
-    halo_in = jnp.where(on_left, right_of_left, left_of_right)
     weights = jnp.pad(decorrelation, ((0, padded_bands - bands), (0, 0)))
+
+    def facing(x):
+        return jnp.where(on_left, x[..., width - HALO :], x[..., :HALO])
+
+    rad_next, rad_prev = partials(radiance, 1)
+    p_own = shifted(rad_next, "rows", 1)
+    n_own = shifted(rad_prev, "rows", -1)
+    p_halo = diagonal(facing(rad_next), 1)
+    n_halo = diagonal(facing(rad_prev), -1)
 
     def mix(x):
         return jnp.einsum("crw,bc->rwb", x, weights, precision=lax.Precision.HIGHEST,
                           preferred_element_type=jnp.float32)
 
     own = mix(radiance)
-    halo = mix(halo_in)
-    top_own, bot_own = edge_rows(own)
-    top_halo, bot_halo = edge_rows(halo)
+    halo = to_core_mate(jnp.where(on_left, own[:, width - HALO :], own[:, :HALO]))
     ext_width = width + HALO
     out_shape = (rows, ext_width, padded_bands)
-    out, level = level_call(
-        first_kernel, flags, [own, halo, top_own, top_halo, bot_own, bot_halo],
+    out, level, tn, tp = level_call(
+        first_kernel, flags,
+        [own, halo, mix(p_own), mix(p_halo), mix(n_own), mix(n_halo)],
         out_shape, rows, ext_width, {})
     for lvl in range(1, LEVELS):
-        top, bot = edge_rows(level)
+        from_prev = shifted(tn, "rows", 1)
+        from_next = shifted(tp, "rows", -1)
         r, w = level.shape[0], level.shape[1]
-        out, level = level_call(
+        out, level, tn, tp = level_call(
             functools.partial(next_kernel, stride=2**lvl), flags,
-            [level, top, bot, out], out_shape, r, w, {4: 0})
+            [level, from_prev, from_next, out], out_shape, r, w, {4: 0})
     coeffs = jnp.where(on_left, out[:, :width], out[:, HALO : HALO + width])
     return jnp.transpose(coeffs, (2, 0, 1))[:bands]
 

time: 136 us -> 95.5 us (0.70)
  waiting for transfers between devices: 35.9 us -> 13.1 us
  local copies, waits for them, and re-layouts: 27.5 us -> 11.4 us
  starting transfers between devices: 30.2 us -> 24.5 us
  matrix products: 11.4 us -> 15.3 us
    ppermute x10 -> x6, waiting for transfers between devices: 35.9 us -> 13.1 us  [shifted(): return lax.ppermute(x, axis, pairs)]
    ppermute x10 -> x6, starting transfers between devices: 30.2 us -> 19.6 us  [shifted(): return lax.ppermute(x, axis, pairs)]
    slice x5 -> x0, local copies, waits for them, and re-layouts: 10.5 us -> none  [the longest x1 7.21 us: on_device(): left_of_right = shifted(radiance[:, :, width - HALO:], 'cols', 1)]
    unnamed x9 -> x6, local copies, waits for them, and re-layouts: 11.9 us -> 6.35 us
    ppermute x0 -> x3, starting transfers between devices: none -> 4.9 us  [the longest x2 3.88 us: diagonal(): return lax.ppermute(x, ('rows', 'cols'), pairs)]
    dot_general x2 -> x5, matrix products: 11.4 us -> 15.3 us  [mix(): jnp.einsum('crw,bc->rwb', x, weights, precision=lax.Precision.HIGHEST, pr...]
  transfers between devices with their start and end apart: 10 -> 9, of which waited for: 5 -> 4; matrix products, arithmetic and copies ran while one was open for 13% -> 17% of each run, Pallas kernels for 0% -> 0%
where the time goes in v4:
time: 95.5 us; the launch traced here: 95 us
  starting transfers between devices  24.5 us (26%)
  Pallas kernels  23.1 us (24%)
  matrix products  15.3 us (16%)
  waiting for transfers between devices  13.1 us (14%)
  local copies, waits for them, and re-layouts  11.4 us (12%)
  other arithmetic  7.44 us (8%)
    pallas_call x3, Pallas kernels, level_call(): pl.pallas_call(kernel, grid_spec=grid_spec, out_shape=tuple((jax.ShapeDty...  23.1 us
    ppermute x6, starting transfers between devices, shifted(): return lax.ppermute(x, axis, pairs)  19.6 us
    dot_general x5, matrix products, mix(): jnp.einsum('crw,bc->rwb', x, weights, precision=lax.Precision.HIGHEST, pr...  15.3 us
    ppermute x6, waiting for transfers between devices, shifted(): return lax.ppermute(x, axis, pairs)  13.1 us
    unnamed x6, local copies, waits for them, and re-layouts  6.35 us
    transpose x1, other arithmetic, on_device(): return jnp.transpose(coeffs, (2, 0, 1))[:bands]  6.24 us
    slice x1, local copies, waits for them, and re-layouts, on_device(): return jnp.transpose(coeffs, (2, 0, 1))[:bands]  5.1 us
    ppermute x2, starting transfers between devices, diagonal(): return lax.ppermute(x, ('rows', 'cols'), pairs)  3.88 us
  transfers between devices with their start and end apart: 9, of which 4 were waited for; matrix products, arithmetic and copies ran while one was open for 17% of the time, Pallas kernels for 0%

profile of v4, /device:TPU:0, one launch (start us, length us, event | category | flops | bytes accessed | tf_op | source)
XLA Modules:
  0.0 95.0 jit_solution(9389896060076514127)
XLA Ops:
  0.0 0.0 copy-start.1
  0.0 4.2 %copy.6 = f32[224,32,128]{2,0,1:T(8,128)S(1)} copy(f32[224,32,128]{2,1,0:T(8,128)} %param.2) | data formatting | bytes 7340032 | tf_op args[0]
  4.2 0.1 fusion.32
  4.3 4.9 %collective-permute-start.1 = (f32[224,2,128]{2,0,1:T(8,128)S(1)}, f32[224,2,128]{2,0,1:T(8,128)S(1)}, u32[]{:S(2)}, u32[]{:S(2)}) collective-permute-start(f32[224,2,128]{2,0,1:T(8,128)S(1)} %pad_maximum_fusion), channel_id=1, source_target_pairs={{0,2},{2,4},{4,6},{6,8},{8,10},{10,12},{12,14},{1,3},{3,5},{5,7},{... | collective-permute-start | bytes 688136 | tf_op jit(solution)/shard_map/ppermute | solution.py:26
  9.2 0.1 fusion.4
  9.3 2.6 %collective-permute-start.2 = (f32[224,2,32]{2,0,1:T(8,128)S(1)}, f32[224,2,32]{2,0,1:T(8,128)S(1)}, u32[]{:S(2)}, u32[]{:S(2)}) collective-permute-start(f32[224,2,32]{2,0,1:T(8,128)S(1)} %fusion.4), channel_id=1, source_target_pairs={{0,3},{1,2},{2,5},{3,4},{4,7},{5,6},{6,9},{7,8},{8,11},{9,10},{10,... | collective-permute-start | bytes 172040 | tf_op jit(solution)/shard_map/ppermute | solution.py:197
  11.9 0.1 fusion.1
  12.1 1.3 %collective-permute-start.4 = (f32[224,2,32]{2,0,1:T(8,128)S(1)}, f32[224,2,32]{2,0,1:T(8,128)S(1)}, u32[]{:S(2)}, u32[]{:S(2)}) collective-permute-start(f32[224,2,32]{2,0,1:T(8,128)S(1)} %fusion.1), channel_id=1, source_target_pairs={{2,1},{3,0},{4,3},{5,2},{6,5},{7,4},{8,7},{9,6},{10,9},{11,8},{12,... | collective-permute-start | bytes 172040 | tf_op jit(solution)/shard_map/ppermute | solution.py:197
  13.4 1.5 %collective-permute-start.3 = (f32[224,2,128]{2,0,1:T(8,128)S(1)}, f32[224,2,128]{2,0,1:T(8,128)S(1)}, u32[]{:S(2)}, u32[]{:S(2)}) collective-permute-start(f32[224,2,128]{2,0,1:T(8,128)S(1)} %pad_maximum_fusion.1), channel_id=1, source_target_pairs={{2,0},{4,2},{6,4},{8,6},{10,8},{12,10},{14,12},{3,1},{5,3},{7,5},{... | collective-permute-start | bytes 688136 | tf_op jit(solution)/shard_map/ppermute | solution.py:26
  14.9 0.0 copy-done.1
  14.9 0.1 copy.5
  15.0 10.4 %convolution_bitcast_fusion.own = f32[32,128,256]{2,1,0:T(8,128)S(1)} fusion(f32[224,224]{0,1:T(8,128)S(1)} %copy.5, f32[224,32,128]{2,1,0:T(8,128)} %param.2), kind=kOutput, calls=%fused_computation.1 | convolution fusion | flops 2818572288 | bytes 8065024 | tf_op jit(solution)/shard_map/crw,bc->rwb/dot_general | solution.py:223
  25.4 0.0 copy-start
  25.4 2.0 %copy-done = f32[32,128,256]{2,1,0:T(8,128)} copy-done((f32[32,128,256]{2,1,0:T(8,128)}, f32[32,128,256]{2,1,0:T(8,128)S(1)}, u32[]{:S(2)}) %copy-start) | copy-done | bytes 4194328
  27.4 0.2 slice_select_fusion
  27.6 1.0 %collective-permute-start = (f32[32,32,256]{2,1,0:T(8,128)S(1)}, f32[32,32,256]{2,1,0:T(8,128)}, u32[]{:S(2)}, u32[]{:S(2)}) collective-permute-start(f32[32,32,256]{2,1,0:T(8,128)S(1)} %slice_select_fusion), channel_id=1, source_target_pairs={{0,1},{1,0},{2,3},{3,2},{4,5},{5,4},{6,7},{7,6},{8,9},{9,8},{10,11... | collective-permute-start | bytes 3145736 | tf_op jit(solution)/shard_map/ppermute | solution.py:186
  28.6 0.7 add_convert_fusion.flags
  29.3 0.0 collective-permute-done.2
  29.3 1.2 %fusion.10.prev_halo = f32[2,32,256]{2,1,0:T(8,128)} fusion(f32[224,2,32]{2,0,1:T(8,128)S(1)} %collective-permute-done.2, f32[224,224]{0,1:T(8,128)S(1)} %copy.5), kind=kOutput, calls=%fused_computation.23 | convolution fusion | flops 44040192 | bytes 323584 | tf_op jit(solution)/shard_map/crw,bc->rwb/dot_general | solution.py:223
  30.5 0.0 collective-permute-done.4
  30.5 1.2 %fusion.6.next_halo = f32[2,32,256]{2,1,0:T(8,128)} fusion(f32[224,2,32]{2,0,1:T(8,128)S(1)} %collective-permute-done.4, f32[224,224]{0,1:T(8,128)S(1)} %copy.5), kind=kOutput, calls=%fused_computation.19 | convolution fusion | flops 44040192 | bytes 323584 | tf_op jit(solution)/shard_map/crw,bc->rwb/dot_general | solution.py:223
  31.6 0.0 collective-permute-done.1
  31.6 1.3 %fusion.12.prev_own = f32[2,128,256]{2,1,0:T(8,128)} fusion(f32[224,2,128]{2,0,1:T(8,128)S(1)} %collective-permute-done.1, f32[224,224]{0,1:T(8,128)S(1)} %copy.5), kind=kOutput, calls=%fused_computation.25 | convolution fusion | flops 176160768 | bytes 692224 | tf_op jit(solution)/shard_map/crw,bc->rwb/dot_general | solution.py:223
  32.9 0.0 collective-permute-done.3
  32.9 1.3 %fusion.8.next_own = f32[2,128,256]{2,1,0:T(8,128)} fusion(f32[224,2,128]{2,0,1:T(8,128)S(1)} %collective-permute-done.3, f32[224,224]{0,1:T(8,128)S(1)} %copy.5), kind=kOutput, calls=%fused_computation.21 | convolution fusion | flops 176160768 | bytes 692224 | tf_op jit(solution)/shard_map/crw,bc->rwb/dot_general | solution.py:223
  34.3 0.0 collective-permute-done.halo
  34.3 11.5 %shard_map.28 = (f32[32,160,256]{2,1,0:T(8,128)}, f32[16,80,256]{2,1,0:T(8,128)}, f32[2,80,256]{2,1,0:T(8,128)}, f32[2,80,256]{2,1,0:T(8,128)}) custom-call(s32[3]{0:T(128)} %add_convert_fusion.flags, f32[32,128,256]{2,1,0:T(8,128)} %copy-done, f32[32,32,256]{2,1,0:T(8,128)} %collective-permute-done.halo, f32[2,128,256]{2,1,0:T(8,128)} %fusion.12.prev_own, ...), custom_call_target="tpu_custom_call" | custom-call | tf_op jit(solution)/shard_map/pallas_call | solution.py:176
  45.8 5.5 %collective-permute-start.5 = (f32[2,80,256]{2,1,0:T(8,128)}, f32[2,80,256]{2,1,0:T(8,128)}, u32[]{:S(2)}, u32[]{:S(2)}) collective-permute-start(f32[2,80,256]{2,1,0:T(8,128)} %get-tuple-element.15), channel_id=1, source_target_pairs={{0,2},{2,4},{4,6},{6,8},{8,10},{10,12},{12,14},{1,3},{3,5},{5,7},{... | collective-permute-start | bytes 491528 | tf_op jit(solution)/shard_map/ppermute | solution.py:26
  51.3 1.3 %collective-permute-start.6 = (f32[2,80,256]{2,1,0:T(8,128)}, f32[2,80,256]{2,1,0:T(8,128)}, u32[]{:S(2)}, u32[]{:S(2)}) collective-permute-start(f32[2,80,256]{2,1,0:T(8,128)} %get-tuple-element.16), channel_id=1, source_target_pairs={{2,0},{4,2},{6,4},{8,6},{10,8},{12,10},{14,12},{3,1},{5,3},{7,5},{... | collective-permute-start | bytes 491528 | tf_op jit(solution)/shard_map/ppermute | solution.py:26
  52.6 2.4 %collective-permute-done.5.from_prev = f32[2,80,256]{2,1,0:T(8,128)} collective-permute-done((f32[2,80,256]{2,1,0:T(8,128)}, f32[2,80,256]{2,1,0:T(8,128)}, u32[]{:S(2)}, u32[]{:S(2)}) %collective-permute-start.5) | collective-permute-done | bytes 163872 | tf_op jit(solution)/shard_map/ppermute | solution.py:26
  55.0 5.3 %collective-permute-done.6.from_next = f32[2,80,256]{2,1,0:T(8,128)} collective-permute-done((f32[2,80,256]{2,1,0:T(8,128)}, f32[2,80,256]{2,1,0:T(8,128)}, u32[]{:S(2)}, u32[]{:S(2)}) %collective-permute-start.6) | collective-permute-done | bytes 163872 | tf_op jit(solution)/shard_map/ppermute | solution.py:26
  60.3 6.2 %shard_map.29 = (f32[32,160,256]{2,1,0:T(8,128)}, f32[8,40,256]{2,1,0:T(8,128)}, f32[2,40,256]{2,1,0:T(8,128)}, f32[2,40,256]{2,1,0:T(8,128)}) custom-call(s32[3]{0:T(128)} %add_convert_fusion.flags, f32[16,80,256]{2,1,0:T(8,128)} %get-tuple-element.14.x_ref, f32[2,80,256]{2,1,0:T(8,128)} %collective-permute-done.5.from_prev, ...), custom_call_target="tpu_custom_call", output_to_operand_aliasing={{0}: (4, {})} | custom-call | tf_op jit(solution)/shard_map/pallas_call | solution.py:176
  66.5 5.2 %collective-permute-start.7 = (f32[2,40,256]{2,1,0:T(8,128)}, f32[2,40,256]{2,1,0:T(8,128)}, u32[]{:S(2)}, u32[]{:S(2)}) collective-permute-start(f32[2,40,256]{2,1,0:T(8,128)} %get-tuple-element.19), channel_id=1, source_target_pairs={{0,2},{2,4},{4,6},{6,8},{8,10},{10,12},{12,14},{1,3},{3,5},{5,7},{... | collective-permute-start | bytes 245768 | tf_op jit(solution)/shard_map/ppermute | solution.py:26
  71.7 1.3 %collective-permute-start.8 = (f32[2,40,256]{2,1,0:T(8,128)}, f32[2,40,256]{2,1,0:T(8,128)}, u32[]{:S(2)}, u32[]{:S(2)}) collective-permute-start(f32[2,40,256]{2,1,0:T(8,128)} %get-tuple-element.20), channel_id=1, source_target_pairs={{2,0},{4,2},{6,4},{8,6},{10,8},{12,10},{14,12},{3,1},{5,3},{7,5},{... | collective-permute-start | bytes 245768 | tf_op jit(solution)/shard_map/ppermute | solution.py:26
  73.0 0.4 collective-permute-done.7.from_prev
  73.4 4.9 %collective-permute-done.8.from_next = f32[2,40,256]{2,1,0:T(8,128)} collective-permute-done((f32[2,40,256]{2,1,0:T(8,128)}, f32[2,40,256]{2,1,0:T(8,128)}, u32[]{:S(2)}, u32[]{:S(2)}) %collective-permute-start.8) | collective-permute-done | bytes 81952 | tf_op jit(solution)/shard_map/ppermute | solution.py:26
  78.3 5.4 %shard_map.30 = (f32[32,160,256]{2,1,0:T(8,128)}, f32[4,20,256]{2,1,0:T(8,128)}, f32[2,20,256]{2,1,0:T(8,128)}, f32[2,20,256]{2,1,0:T(8,128)}) custom-call(s32[3]{0:T(128)} %add_convert_fusion.flags, f32[8,40,256]{2,1,0:T(8,128)} %get-tuple-element.18.x_ref, f32[2,40,256]{2,1,0:T(8,128)} %collective-permute-done.7.from_prev, ...), custom_call_target="tpu_custom_call", output_to_operand_aliasing={{0}: (4, {})} | custom-call | tf_op jit(solution)/shard_map/pallas_call | solution.py:176
  83.7 6.2 %select_bitcast_fusion = f32[256,32,128]{0,2,1:T(8,128)} fusion(f32[32,160,256]{2,1,0:T(8,128)} %get-tuple-element.22, pred[]{:T(512)} %eq.9), kind=kLoop, calls=%fused_computation | loop fusion | flops 1048576 | bytes 12582913 | tf_op jit(solution)/shard_map/transpose | solution.py:242
  89.9 5.1 %copy.16 = f32[224,32,128]{2,1,0:T(8,128)} copy(f32[224,32,128]{0,2,1:T(8,128)} %bitcast.23) | data formatting | bytes 7340032 | tf_op jit(solution)/shard_map/slice | solution.py:242
  (2 shorter events, 0.0 us)
Async XLA Ops:
  0.0 14.9 %copy-start.1 = (f32[224,224]{1,0:T(8,128)S(1)}, f32[224,224]{1,0:T(8,128)}, u32[]{:S(2)}) copy-start(f32[224,224]{1,0:T(8,128)} %param.3) | copy-start | bytes 602116
  4.3 27.3 %collective-permute-start.1 = (f32[224,2,128]{2,0,1:T(8,128)S(1)}, f32[224,2,128]{2,0,1:T(8,128)S(1)}, u32[]{:S(2)}, u32[]{:S(2)}) collective-permute-start(f32[224,2,128]{2,0,1:T(8,128)S(1)} %pad_maximum_fusion), channel_id=1, source_target_pairs={{0,2},{2,4},{4,6},{6,8},{8,10},{10,12},{12,14},{1,3},{3,5},{5,7},{... | collective-permute-start | bytes 688136 | tf_op jit(solution)/shard_map/ppermute | solution.py:26
  9.3 20.0 %collective-permute-start.2 = (f32[224,2,32]{2,0,1:T(8,128)S(1)}, f32[224,2,32]{2,0,1:T(8,128)S(1)}, u32[]{:S(2)}, u32[]{:S(2)}) collective-permute-start(f32[224,2,32]{2,0,1:T(8,128)S(1)} %fusion.4), channel_id=1, source_target_pairs={{0,3},{1,2},{2,5},{3,4},{4,7},{5,6},{6,9},{7,8},{8,11},{9,10},{10,... | collective-permute-start | bytes 172040 | tf_op jit(solution)/shard_map/ppermute | solution.py:197
  12.1 18.4 %collective-permute-start.4 = (f32[224,2,32]{2,0,1:T(8,128)S(1)}, f32[224,2,32]{2,0,1:T(8,128)S(1)}, u32[]{:S(2)}, u32[]{:S(2)}) collective-permute-start(f32[224,2,32]{2,0,1:T(8,128)S(1)} %fusion.1), channel_id=1, source_target_pairs={{2,1},{3,0},{4,3},{5,2},{6,5},{7,4},{8,7},{9,6},{10,9},{11,8},{12,... | collective-permute-start | bytes 172040 | tf_op jit(solution)/shard_map/ppermute | solution.py:197
  13.4 19.6 %collective-permute-start.3 = (f32[224,2,128]{2,0,1:T(8,128)S(1)}, f32[224,2,128]{2,0,1:T(8,128)S(1)}, u32[]{:S(2)}, u32[]{:S(2)}) collective-permute-start(f32[224,2,128]{2,0,1:T(8,128)S(1)} %pad_maximum_fusion.1), channel_id=1, source_target_pairs={{2,0},{4,2},{6,4},{8,6},{10,8},{12,10},{14,12},{3,1},{5,3},{7,5},{... | collective-permute-start | bytes 688136 | tf_op jit(solution)/shard_map/ppermute | solution.py:26
  25.4 2.0 %copy-start = (f32[32,128,256]{2,1,0:T(8,128)}, f32[32,128,256]{2,1,0:T(8,128)S(1)}, u32[]{:S(2)}) copy-start(f32[32,128,256]{2,1,0:T(8,128)S(1)} %convolution_bitcast_fusion.own) | copy-start | bytes 12582916
  27.6 6.7 %collective-permute-start = (f32[32,32,256]{2,1,0:T(8,128)S(1)}, f32[32,32,256]{2,1,0:T(8,128)}, u32[]{:S(2)}, u32[]{:S(2)}) collective-permute-start(f32[32,32,256]{2,1,0:T(8,128)S(1)} %slice_select_fusion), channel_id=1, source_target_pairs={{0,1},{1,0},{2,3},{3,2},{4,5},{5,4},{6,7},{7,6},{8,9},{9,8},{10,11... | collective-permute-start | bytes 3145736 | tf_op jit(solution)/shard_map/ppermute | solution.py:186
  45.8 9.2 %collective-permute-start.5 = (f32[2,80,256]{2,1,0:T(8,128)}, f32[2,80,256]{2,1,0:T(8,128)}, u32[]{:S(2)}, u32[]{:S(2)}) collective-permute-start(f32[2,80,256]{2,1,0:T(8,128)} %get-tuple-element.15), channel_id=1, source_target_pairs={{0,2},{2,4},{4,6},{6,8},{8,10},{10,12},{12,14},{1,3},{3,5},{5,7},{... | collective-permute-start | bytes 491528 | tf_op jit(solution)/shard_map/ppermute | solution.py:26
  51.3 9.0 %collective-permute-start.6 = (f32[2,80,256]{2,1,0:T(8,128)}, f32[2,80,256]{2,1,0:T(8,128)}, u32[]{:S(2)}, u32[]{:S(2)}) collective-permute-start(f32[2,80,256]{2,1,0:T(8,128)} %get-tuple-element.16), channel_id=1, source_target_pairs={{2,0},{4,2},{6,4},{8,6},{10,8},{12,10},{14,12},{3,1},{5,3},{7,5},{... | collective-permute-start | bytes 491528 | tf_op jit(solution)/shard_map/ppermute | solution.py:26
  66.5 6.9 %collective-permute-start.7 = (f32[2,40,256]{2,1,0:T(8,128)}, f32[2,40,256]{2,1,0:T(8,128)}, u32[]{:S(2)}, u32[]{:S(2)}) collective-permute-start(f32[2,40,256]{2,1,0:T(8,128)} %get-tuple-element.19), channel_id=1, source_target_pairs={{0,2},{2,4},{4,6},{6,8},{8,10},{10,12},{12,14},{1,3},{3,5},{5,7},{... | collective-permute-start | bytes 245768 | tf_op jit(solution)/shard_map/ppermute | solution.py:26
  71.7 6.6 %collective-permute-start.8 = (f32[2,40,256]{2,1,0:T(8,128)}, f32[2,40,256]{2,1,0:T(8,128)}, u32[]{:S(2)}, u32[]{:S(2)}) collective-permute-start(f32[2,40,256]{2,1,0:T(8,128)} %get-tuple-element.20), channel_id=1, source_target_pairs={{2,0},{4,2},{6,4},{8,6},{10,8},{12,10},{14,12},{3,1},{5,3},{7,5},{... | collective-permute-start | bytes 245768 | tf_op jit(solution)/shard_map/ppermute | solution.py:26

commit v5 on v4

--- a/solution.py
+++ b/solution.py
@@ -72,7 +72,7 @@
         ext[base : base + EDGE] = jnp.concatenate([s, dp - a1 * s, z, z], axis=0)
 
 
-def lift_block(ext, half, out_ref, ll_ref, tn_ref, tp_ref, rows, width, stride):
+def lift_block(flags, ext, half, out_ref, ll_ref, tn_ref, tp_ref, rows, width, stride):
     hr, hw = rows // 2, width // 2
     a1, b1, a2, b2 = alpha_one, beta_one, alpha_two, beta_two
     n = hr + EDGE
@@ -103,6 +103,22 @@
         return jnp.where(col == 0, v, pltpu.roll(v, 1, 1))
 
     step = 2 * stride
+    own_hw = out_ref.shape[1] // step
+    on_left = flags[0] == 1
+
+    def store(pr, e, o):
+        rows_at = pl.ds(pr * stride, hr, stride=step)
+
+        @pl.when(on_left)
+        def _():
+            out_ref[rows_at, pl.ds(0, own_hw, stride=step), :] = e[:, :own_hw]
+            out_ref[rows_at, pl.ds(stride, own_hw, stride=step), :] = o[:, :own_hw]
+
+        @pl.when(jnp.logical_not(on_left))
+        def _():
+            out_ref[rows_at, pl.ds(0, own_hw, stride=step), :] = e[:, hw - own_hw :]
+            out_ref[rows_at, pl.ds(stride, own_hw, stride=step), :] = o[:, hw - own_hw :]
+
     for pr in range(2):
         e = half[pr, :, pl.ds(0, hw, stride=2), :]
         o = half[pr, :, pl.ds(1, hw, stride=2), :]
@@ -112,8 +128,7 @@
         e = e + b2 * (prv1(o) + o)
         e = e / scale_k
         o = o * scale_k
-        out_ref[pl.ds(pr * stride, hr, stride=step), pl.ds(0, hw, stride=step), :] = e
-        out_ref[pl.ds(pr * stride, hr, stride=step), pl.ds(stride, hw, stride=step), :] = o
+        store(pr, e, o)
         if pr == 0:
             ll_ref[...] = e
             to_next, to_prev = partials(e, 0)
@@ -142,7 +157,7 @@
                          jnp.concatenate([hh[...], o[...]], axis=1))
 
     fill_rows(ext, flags, joined(prev_own, prev_halo), joined(next_own, next_halo), rows)
-    lift_block(ext, half, out_ref, ll_ref, tn_ref, tp_ref, rows, width, 1)
+    lift_block(flags, ext, half, out_ref, ll_ref, tn_ref, tp_ref, rows, width, 1)
 
 
 def next_kernel(flags, x_ref, from_prev, from_next, prev_out,
@@ -151,7 +166,7 @@
     out_ref[...] = prev_out[...]
     ext[EDGE : EDGE + rows] = x_ref[...]
     fill_rows(ext, flags, from_prev[...], from_next[...], rows)
-    lift_block(ext, half, out_ref, ll_ref, tn_ref, tp_ref, rows, width, stride)
+    lift_block(flags, ext, half, out_ref, ll_ref, tn_ref, tp_ref, rows, width, stride)
 
 
 def spec(shape):
@@ -211,25 +226,27 @@
     weights = jnp.pad(decorrelation, ((0, padded_bands - bands), (0, 0)))
 
     def facing(x):
-        return jnp.where(on_left, x[..., width - HALO :], x[..., :HALO])
-
-    rad_next, rad_prev = partials(radiance, 1)
-    p_own = shifted(rad_next, "rows", 1)
-    n_own = shifted(rad_prev, "rows", -1)
-    p_halo = diagonal(facing(rad_next), 1)
-    n_halo = diagonal(facing(rad_prev), -1)
+        return jnp.where(on_left, x[:, width - HALO :], x[:, :HALO])
 
     def mix(x):
         return jnp.einsum("crw,bc->rwb", x, weights, precision=lax.Precision.HIGHEST,
                           preferred_element_type=jnp.float32)
 
+    rad_next, rad_prev = partials(radiance, 1)
+    mixed_parts = mix(jnp.concatenate([rad_next, rad_prev], axis=1))
+    mixed_next, mixed_prev = mixed_parts[:2], mixed_parts[2:]
+    p_own = shifted(mixed_next, "rows", 1)
+    n_own = shifted(mixed_prev, "rows", -1)
+    p_halo = diagonal(facing(mixed_next), 1)
+    n_halo = diagonal(facing(mixed_prev), -1)
+
     own = mix(radiance)
-    halo = to_core_mate(jnp.where(on_left, own[:, width - HALO :], own[:, :HALO]))
+    halo = to_core_mate(facing(own))
     ext_width = width + HALO
-    out_shape = (rows, ext_width, padded_bands)
+    out_shape = (rows, width, padded_bands)
     out, level, tn, tp = level_call(
         first_kernel, flags,
-        [own, halo, mix(p_own), mix(p_halo), mix(n_own), mix(n_halo)],
+        [own, halo, p_own, p_halo, n_own, n_halo],
         out_shape, rows, ext_width, {})
     for lvl in range(1, LEVELS):
         from_prev = shifted(tn, "rows", 1)
@@ -238,8 +255,7 @@
         out, level, tn, tp = level_call(
             functools.partial(next_kernel, stride=2**lvl), flags,
             [level, from_prev, from_next, out], out_shape, r, w, {4: 0})
-    coeffs = jnp.where(on_left, out[:, :width], out[:, HALO : HALO + width])
-    return jnp.transpose(coeffs, (2, 0, 1))[:bands]
+    return jnp.transpose(out, (2, 0, 1))[:bands]
 
 
 def solution(mesh):

time: 95.5 us -> 89.4 us (0.936)
  other arithmetic: 7.44 us -> 0.82 us
  waiting for transfers between devices: 13.1 us -> 18.9 us
  matrix products: 15.3 us -> 11.5 us
  Pallas kernels: 23.1 us -> 22.1 us
    ppermute x2, waiting for transfers between devices: 0.01 us -> 6.69 us  [diagonal(): return lax.ppermute(x, ('rows', 'cols'), pairs)]
    transpose x1 -> x0, other arithmetic: 6.24 us -> none  [on_device(): return jnp.transpose(coeffs, (2, 0, 1))[:bands]]
    dot_general x5 -> x2, matrix products: 15.3 us -> 11.5 us  [mix(): jnp.einsum('crw,bc->rwb', x, weights, precision=lax.Precision.HIGHEST, pr...]
    ppermute x2, starting transfers between devices: 3.88 us -> 5.58 us  [diagonal(): return lax.ppermute(x, ('rows', 'cols'), pairs)]
    ppermute x6, starting transfers between devices: 19.6 us -> 18.4 us  [shifted(): return lax.ppermute(x, axis, pairs)]
    unnamed x6 -> x10, local copies, waits for them, and re-layouts: 6.35 us -> 5.79 us
    slice x1 -> x2, local copies, waits for them, and re-layouts: 5.1 us -> 5.14 us  [the longest x1 5.1 us: on_device(): return jnp.transpose(out, (2, 0, 1))[:bands]]
  transfers between devices with their start and end apart: 9 -> 9, of which waited for: 4 -> 5; matrix products, arithmetic and copies ran while one was open for 17% -> 4% of each run, Pallas kernels for 0% -> 0%
where the time goes in v5:
time: 89.4 us; the launch traced here: 88.9 us
  starting transfers between devices  24.5 us (27%)
  Pallas kernels  22.1 us (25%)
  waiting for transfers between devices  18.9 us (21%)
  matrix products  11.5 us (13%)
  local copies, waits for them, and re-layouts  10.9 us (12%)
    pallas_call x3, Pallas kernels, level_call(): pl.pallas_call(kernel, grid_spec=grid_spec, out_shape=tuple((jax.ShapeDty...  22.1 us
    ppermute x6, starting transfers between devices, shifted(): return lax.ppermute(x, axis, pairs)  18.4 us
    ppermute x6, waiting for transfers between devices, shifted(): return lax.ppermute(x, axis, pairs)  12.2 us
    dot_general x2, matrix products, mix(): jnp.einsum('crw,bc->rwb', x, weights, precision=lax.Precision.HIGHEST, pr...  11.5 us
    ppermute x2, waiting for transfers between devices, diagonal(): return lax.ppermute(x, ('rows', 'cols'), pairs)  6.69 us
    unnamed x10, local copies, waits for them, and re-layouts  5.79 us
    ppermute x2, starting transfers between devices, diagonal(): return lax.ppermute(x, ('rows', 'cols'), pairs)  5.58 us
    slice x1, local copies, waits for them, and re-layouts, on_device(): return jnp.transpose(out, (2, 0, 1))[:bands]  5.1 us
  transfers between devices with their start and end apart: 9, of which 5 were waited for; matrix products, arithmetic and copies ran while one was open for 4% of the time, Pallas kernels for 0%

profile of v5, /device:TPU:0, one launch (start us, length us, event | category | flops | bytes accessed | tf_op | source)
XLA Modules:
  0.0 88.9 jit_solution(10833191561464380361)
XLA Ops:
  0.0 1.1 %copy.5 = f32[224,224]{0,1:T(8,128)S(1)} copy(f32[224,224]{1,0:T(8,128)} %param.3) | data formatting | bytes 401408 | tf_op args[1]
  1.1 0.0 copy-start.1
  1.1 10.5 %convolution_bitcast_fusion.own = f32[32,128,256]{2,1,0:T(8,128)S(1)} fusion(f32[224,224]{0,1:T(8,128)S(1)} %copy.5, f32[224,32,128]{2,1,0:T(8,128)} %param.2), kind=kOutput, calls=%fused_computation | convolution fusion | flops 2818572288 | bytes 8065024 | tf_op jit(solution)/shard_map/crw,bc->rwb/dot_general | solution.py:232
  11.6 0.0 copy-start
  11.6 2.0 %copy-done = f32[32,128,256]{2,1,0:T(8,128)} copy-done((f32[32,128,256]{2,1,0:T(8,128)}, f32[32,128,256]{2,1,0:T(8,128)S(1)}, u32[]{:S(2)}) %copy-start) | copy-done | bytes 4194328
  13.6 0.1 slice_select_fusion
  13.7 0.5 collective-permute-start
  14.2 0.0 copy-done.1
  14.3 2.1 %copy.6 = f32[224,32,128]{2,0,1:T(8,128)S(1)} copy(f32[224,32,128]{2,1,0:T(8,128)S(1)} %copy-done.1) | data formatting | bytes 7340032 | tf_op args[0]
  16.4 0.1 fusion.17
  16.4 1.0 %fusion = f32[4,128,256]{2,1,0:T(8,128)S(1)} fusion(f32[224,1,128]{2,0,1:T(8,128)S(1)} %get-tuple-element.24, f32[224,1,128]{2,0,1:T(8,128)S(1)} %get-tuple-element.25, f32[224,1,128]{2,0,1:T(8,128)S(1)} %get-tuple-element.26, f32[224,1,128]{2,0,1:T(8,128)S(1)} %get-tuple-element.23, f32[224,224]{0,1:T(8,128)S(1)} %copy.5), kind=kOutput, calls=%fused_computation.2 | convolution fusion | flops 352665600 | bytes 1183744 | tf_op jit(solution)/shard_map/crw,bc->rwb/dot_general | solution.py:232
  17.5 1.3 %collective-permute-start.3 = (f32[2,128,256]{2,1,0:T(8,128)S(1)}, f32[2,128,256]{2,1,0:T(8,128)}, u32[]{:S(2)}, u32[]{:S(2)}) collective-permute-start(f32[2,128,256]{2,1,0:T(8,128)S(1)} %get-tuple-element.29), channel_id=1, source_target_pairs={{2,0},{4,2},{6,4},{8,6},{10,8},{12,10},{14,12},{3,1},{5,3},{7,5},{... | collective-permute-start | bytes 786440 | tf_op jit(solution)/shard_map/ppermute | solution.py:26
  18.8 5.8 %collective-permute-start.1 = (f32[2,128,256]{2,1,0:T(8,128)S(1)}, f32[2,128,256]{2,1,0:T(8,128)}, u32[]{:S(2)}, u32[]{:S(2)}) collective-permute-start(f32[2,128,256]{2,1,0:T(8,128)S(1)} %get-tuple-element.30), channel_id=1, source_target_pairs={{0,2},{2,4},{4,6},{6,8},{8,10},{10,12},{12,14},{1,3},{3,5},{5,7},{... | collective-permute-start | bytes 786440 | tf_op jit(solution)/shard_map/ppermute | solution.py:26
  24.6 1.3 %collective-permute-start.4 = (f32[2,32,256]{2,1,0:T(8,128)S(1)}, f32[2,32,256]{2,1,0:T(8,128)S(1)}, u32[]{:S(2)}, u32[]{:S(2)}) collective-permute-start(f32[2,32,256]{2,1,0:T(8,128)S(1)} %get-tuple-element.27), channel_id=1, source_target_pairs={{2,1},{3,0},{4,3},{5,2},{6,5},{7,4},{8,7},{9,6},{10,9},{11,8},{12,... | collective-permute-start | bytes 196616 | tf_op jit(solution)/shard_map/ppermute | solution.py:212
  25.9 4.3 %collective-permute-start.2 = (f32[2,32,256]{2,1,0:T(8,128)S(1)}, f32[2,32,256]{2,1,0:T(8,128)S(1)}, u32[]{:S(2)}, u32[]{:S(2)}) collective-permute-start(f32[2,32,256]{2,1,0:T(8,128)S(1)} %get-tuple-element.28), channel_id=1, source_target_pairs={{0,3},{1,2},{2,5},{3,4},{4,7},{5,6},{6,9},{7,8},{8,11},{9,10},{10,... | collective-permute-start | bytes 196616 | tf_op jit(solution)/shard_map/ppermute | solution.py:212
  30.2 0.6 add_convert_fusion.flags
  30.8 0.0 collective-permute-done.4.next_halo
  30.8 0.0 copy-start.2
  30.8 6.7 %collective-permute-done.2.prev_halo = f32[2,32,256]{2,1,0:T(8,128)S(1)} collective-permute-done((f32[2,32,256]{2,1,0:T(8,128)S(1)}, f32[2,32,256]{2,1,0:T(8,128)S(1)}, u32[]{:S(2)}, u32[]{:S(2)}) %collective-permute-start.2) | collective-permute-done | bytes 65568 | tf_op jit(solution)/shard_map/ppermute | solution.py:212
  37.5 0.0 copy-start.3
  37.5 0.0 collective-permute-done.3.next_own
  37.5 0.0 collective-permute-done.1.prev_own
  37.5 0.0 copy-done.2
  37.5 0.6 copy-done.3
  38.1 0.0 collective-permute-done.halo
  38.2 11.5 %shard_map.28 = (f32[32,128,256]{2,1,0:T(8,128)}, f32[16,80,256]{2,1,0:T(8,128)}, f32[2,80,256]{2,1,0:T(8,128)}, f32[2,80,256]{2,1,0:T(8,128)}) custom-call(s32[3]{0:T(128)} %add_convert_fusion.flags, f32[32,128,256]{2,1,0:T(8,128)} %copy-done, f32[32,32,256]{2,1,0:T(8,128)} %collective-permute-done.halo, f32[2,128,256]{2,1,0:T(8,128)} %collective-permute-done.1.prev_own, ...), custom_call_target="tpu_custom_call" | custom-call | tf_op jit(solution)/shard_map/pallas_call | solution.py:191
  49.6 5.0 %collective-permute-start.5 = (f32[2,80,256]{2,1,0:T(8,128)}, f32[2,80,256]{2,1,0:T(8,128)}, u32[]{:S(2)}, u32[]{:S(2)}) collective-permute-start(f32[2,80,256]{2,1,0:T(8,128)} %get-tuple-element.15), channel_id=1, source_target_pairs={{0,2},{2,4},{4,6},{6,8},{8,10},{10,12},{12,14},{1,3},{3,5},{5,7},{... | collective-permute-start | bytes 491528 | tf_op jit(solution)/shard_map/ppermute | solution.py:26
  54.6 1.3 %collective-permute-start.6 = (f32[2,80,256]{2,1,0:T(8,128)}, f32[2,80,256]{2,1,0:T(8,128)}, u32[]{:S(2)}, u32[]{:S(2)}) collective-permute-start(f32[2,80,256]{2,1,0:T(8,128)} %get-tuple-element.16), channel_id=1, source_target_pairs={{2,0},{4,2},{6,4},{8,6},{10,8},{12,10},{14,12},{3,1},{5,3},{7,5},{... | collective-permute-start | bytes 491528 | tf_op jit(solution)/shard_map/ppermute | solution.py:26
  55.9 5.6 %collective-permute-done.5.from_prev = f32[2,80,256]{2,1,0:T(8,128)} collective-permute-done((f32[2,80,256]{2,1,0:T(8,128)}, f32[2,80,256]{2,1,0:T(8,128)}, u32[]{:S(2)}, u32[]{:S(2)}) %collective-permute-start.5) | collective-permute-done | bytes 163872 | tf_op jit(solution)/shard_map/ppermute | solution.py:26
  61.5 1.2 %collective-permute-done.6.from_next = f32[2,80,256]{2,1,0:T(8,128)} collective-permute-done((f32[2,80,256]{2,1,0:T(8,128)}, f32[2,80,256]{2,1,0:T(8,128)}, u32[]{:S(2)}, u32[]{:S(2)}) %collective-permute-start.6) | collective-permute-done | bytes 163872 | tf_op jit(solution)/shard_map/ppermute | solution.py:26
  62.7 5.8 %shard_map.29 = (f32[32,128,256]{2,1,0:T(8,128)}, f32[8,40,256]{2,1,0:T(8,128)}, f32[2,40,256]{2,1,0:T(8,128)}, f32[2,40,256]{2,1,0:T(8,128)}) custom-call(s32[3]{0:T(128)} %add_convert_fusion.flags, f32[16,80,256]{2,1,0:T(8,128)} %get-tuple-element.14.x_ref, f32[2,80,256]{2,1,0:T(8,128)} %collective-permute-done.5.from_prev, ...), custom_call_target="tpu_custom_call", output_to_operand_aliasing={{0}: (4, {})} | custom-call | tf_op jit(solution)/shard_map/pallas_call | solution.py:191
  68.5 3.8 %collective-permute-start.7 = (f32[2,40,256]{2,1,0:T(8,128)}, f32[2,40,256]{2,1,0:T(8,128)}, u32[]{:S(2)}, u32[]{:S(2)}) collective-permute-start(f32[2,40,256]{2,1,0:T(8,128)} %get-tuple-element.19), channel_id=1, source_target_pairs={{0,2},{2,4},{4,6},{6,8},{8,10},{10,12},{12,14},{1,3},{3,5},{5,7},{... | collective-permute-start | bytes 245768 | tf_op jit(solution)/shard_map/ppermute | solution.py:26
  72.3 1.3 %collective-permute-start.8 = (f32[2,40,256]{2,1,0:T(8,128)}, f32[2,40,256]{2,1,0:T(8,128)}, u32[]{:S(2)}, u32[]{:S(2)}) collective-permute-start(f32[2,40,256]{2,1,0:T(8,128)} %get-tuple-element.20), channel_id=1, source_target_pairs={{2,0},{4,2},{6,4},{8,6},{10,8},{12,10},{14,12},{3,1},{5,3},{7,5},{... | collective-permute-start | bytes 245768 | tf_op jit(solution)/shard_map/ppermute | solution.py:26
  73.6 0.4 collective-permute-done.7.from_prev
  74.0 4.9 %collective-permute-done.8.from_next = f32[2,40,256]{2,1,0:T(8,128)} collective-permute-done((f32[2,40,256]{2,1,0:T(8,128)}, f32[2,40,256]{2,1,0:T(8,128)}, u32[]{:S(2)}, u32[]{:S(2)}) %collective-permute-start.8) | collective-permute-done | bytes 81952 | tf_op jit(solution)/shard_map/ppermute | solution.py:26
  78.9 4.9 %shard_map.30 = (f32[32,128,256]{2,1,0:T(8,128)}, f32[4,20,256]{2,1,0:T(8,128)}, f32[2,20,256]{2,1,0:T(8,128)}, f32[2,20,256]{2,1,0:T(8,128)}) custom-call(s32[3]{0:T(128)} %add_convert_fusion.flags, f32[8,40,256]{2,1,0:T(8,128)} %get-tuple-element.18.x_ref, f32[2,40,256]{2,1,0:T(8,128)} %collective-permute-done.7.from_prev, ...), custom_call_target="tpu_custom_call", output_to_operand_aliasing={{0}: (4, {})} | custom-call | tf_op jit(solution)/shard_map/pallas_call | solution.py:191
  83.8 5.1 %copy.14 = f32[224,32,128]{2,1,0:T(8,128)} copy(f32[224,32,128]{0,2,1:T(8,128)} %bitcast.12) | data formatting | bytes 7340032 | tf_op jit(solution)/shard_map/slice | solution.py:258
  (2 shorter events, 0.1 us)
Async XLA Ops:
  1.1 13.2 %copy-start.1 = (f32[224,32,128]{2,1,0:T(8,128)S(1)}, f32[224,32,128]{2,1,0:T(8,128)}, u32[]{:S(2)}) copy-start(f32[224,32,128]{2,1,0:T(8,128)} %param.2) | copy-start | bytes 11010052
  11.6 2.0 %copy-start = (f32[32,128,256]{2,1,0:T(8,128)}, f32[32,128,256]{2,1,0:T(8,128)S(1)}, u32[]{:S(2)}) copy-start(f32[32,128,256]{2,1,0:T(8,128)S(1)} %convolution_bitcast_fusion.own) | copy-start | bytes 12582916
  13.7 24.4 %collective-permute-start = (f32[32,32,256]{2,1,0:T(8,128)S(1)}, f32[32,32,256]{2,1,0:T(8,128)}, u32[]{:S(2)}, u32[]{:S(2)}) collective-permute-start(f32[32,32,256]{2,1,0:T(8,128)S(1)} %slice_select_fusion), channel_id=1, source_target_pairs={{0,1},{1,0},{2,3},{3,2},{4,5},{5,4},{6,7},{7,6},{8,9},{9,8},{10,11... | collective-permute-start | bytes 3145736 | tf_op jit(solution)/shard_map/ppermute | solution.py:201
  17.5 20.0 %collective-permute-start.3 = (f32[2,128,256]{2,1,0:T(8,128)S(1)}, f32[2,128,256]{2,1,0:T(8,128)}, u32[]{:S(2)}, u32[]{:S(2)}) collective-permute-start(f32[2,128,256]{2,1,0:T(8,128)S(1)} %get-tuple-element.29), channel_id=1, source_target_pairs={{2,0},{4,2},{6,4},{8,6},{10,8},{12,10},{14,12},{3,1},{5,3},{7,5},{... | collective-permute-start | bytes 786440 | tf_op jit(solution)/shard_map/ppermute | solution.py:26
  18.8 18.7 %collective-permute-start.1 = (f32[2,128,256]{2,1,0:T(8,128)S(1)}, f32[2,128,256]{2,1,0:T(8,128)}, u32[]{:S(2)}, u32[]{:S(2)}) collective-permute-start(f32[2,128,256]{2,1,0:T(8,128)S(1)} %get-tuple-element.30), channel_id=1, source_target_pairs={{0,2},{2,4},{4,6},{6,8},{8,10},{10,12},{12,14},{1,3},{3,5},{5,7},{... | collective-permute-start | bytes 786440 | tf_op jit(solution)/shard_map/ppermute | solution.py:26
  24.6 6.2 %collective-permute-start.4 = (f32[2,32,256]{2,1,0:T(8,128)S(1)}, f32[2,32,256]{2,1,0:T(8,128)S(1)}, u32[]{:S(2)}, u32[]{:S(2)}) collective-permute-start(f32[2,32,256]{2,1,0:T(8,128)S(1)} %get-tuple-element.27), channel_id=1, source_target_pairs={{2,1},{3,0},{4,3},{5,2},{6,5},{7,4},{8,7},{9,6},{10,9},{11,8},{12,... | collective-permute-start | bytes 196616 | tf_op jit(solution)/shard_map/ppermute | solution.py:212
  25.9 11.6 %collective-permute-start.2 = (f32[2,32,256]{2,1,0:T(8,128)S(1)}, f32[2,32,256]{2,1,0:T(8,128)S(1)}, u32[]{:S(2)}, u32[]{:S(2)}) collective-permute-start(f32[2,32,256]{2,1,0:T(8,128)S(1)} %get-tuple-element.28), channel_id=1, source_target_pairs={{0,3},{1,2},{2,5},{3,4},{4,7},{5,6},{6,9},{7,8},{8,11},{9,10},{10,... | collective-permute-start | bytes 196616 | tf_op jit(solution)/shard_map/ppermute | solution.py:212
  30.8 6.7 %copy-start.2 = (f32[2,32,256]{2,1,0:T(8,128)}, f32[2,32,256]{2,1,0:T(8,128)S(1)}, u32[]{:S(2)}) copy-start(f32[2,32,256]{2,1,0:T(8,128)S(1)} %collective-permute-done.4.next_halo) | copy-start | bytes 196612
  37.5 0.6 copy-start.3
  49.6 11.9 %collective-permute-start.5 = (f32[2,80,256]{2,1,0:T(8,128)}, f32[2,80,256]{2,1,0:T(8,128)}, u32[]{:S(2)}, u32[]{:S(2)}) collective-permute-start(f32[2,80,256]{2,1,0:T(8,128)} %get-tuple-element.15), channel_id=1, source_target_pairs={{0,2},{2,4},{4,6},{6,8},{8,10},{10,12},{12,14},{1,3},{3,5},{5,7},{... | collective-permute-start | bytes 491528 | tf_op jit(solution)/shard_map/ppermute | solution.py:26
  54.6 8.1 %collective-permute-start.6 = (f32[2,80,256]{2,1,0:T(8,128)}, f32[2,80,256]{2,1,0:T(8,128)}, u32[]{:S(2)}, u32[]{:S(2)}) collective-permute-start(f32[2,80,256]{2,1,0:T(8,128)} %get-tuple-element.16), channel_id=1, source_target_pairs={{2,0},{4,2},{6,4},{8,6},{10,8},{12,10},{14,12},{3,1},{5,3},{7,5},{... | collective-permute-start | bytes 491528 | tf_op jit(solution)/shard_map/ppermute | solution.py:26
  68.5 5.5 %collective-permute-start.7 = (f32[2,40,256]{2,1,0:T(8,128)}, f32[2,40,256]{2,1,0:T(8,128)}, u32[]{:S(2)}, u32[]{:S(2)}) collective-permute-start(f32[2,40,256]{2,1,0:T(8,128)} %get-tuple-element.19), channel_id=1, source_target_pairs={{0,2},{2,4},{4,6},{6,8},{8,10},{10,12},{12,14},{1,3},{3,5},{5,7},{... | collective-permute-start | bytes 245768 | tf_op jit(solution)/shard_map/ppermute | solution.py:26
  72.3 6.6 %collective-permute-start.8 = (f32[2,40,256]{2,1,0:T(8,128)}, f32[2,40,256]{2,1,0:T(8,128)}, u32[]{:S(2)}, u32[]{:S(2)}) collective-permute-start(f32[2,40,256]{2,1,0:T(8,128)} %get-tuple-element.20), channel_id=1, source_target_pairs={{2,0},{4,2},{6,4},{8,6},{10,8},{12,10},{14,12},{3,1},{5,3},{7,5},{... | collective-permute-start | bytes 245768 | tf_op jit(solution)/shard_map/ppermute | solution.py:26

commit v6 on v5

--- a/solution.py
+++ b/solution.py
@@ -226,22 +226,26 @@
     weights = jnp.pad(decorrelation, ((0, padded_bands - bands), (0, 0)))
 
     def facing(x):
-        return jnp.where(on_left, x[:, width - HALO :], x[:, :HALO])
+        return jnp.where(on_left, x[..., width - HALO :], x[..., :HALO])
 
     def mix(x):
         return jnp.einsum("crw,bc->rwb", x, weights, precision=lax.Precision.HIGHEST,
                           preferred_element_type=jnp.float32)
 
     rad_next, rad_prev = partials(radiance, 1)
-    mixed_parts = mix(jnp.concatenate([rad_next, rad_prev], axis=1))
-    mixed_next, mixed_prev = mixed_parts[:2], mixed_parts[2:]
-    p_own = shifted(mixed_next, "rows", 1)
-    n_own = shifted(mixed_prev, "rows", -1)
-    p_halo = diagonal(facing(mixed_next), 1)
-    n_halo = diagonal(facing(mixed_prev), -1)
+    got_own = jnp.concatenate(
+        [shifted(rad_next, "rows", 1), shifted(rad_prev, "rows", -1)], axis=1
+    )
+    got_halo = jnp.concatenate(
+        [diagonal(facing(rad_next), 1), diagonal(facing(rad_prev), -1)], axis=1
+    )
+    mixed_own = mix(got_own)
+    mixed_halo = mix(got_halo)
+    p_own, n_own = mixed_own[:2], mixed_own[2:]
+    p_halo, n_halo = mixed_halo[:2], mixed_halo[2:]
 
     own = mix(radiance)
-    halo = to_core_mate(facing(own))
+    halo = to_core_mate(jnp.where(on_left, own[:, width - HALO :], own[:, :HALO]))
     ext_width = width + HALO
     out_shape = (rows, width, padded_bands)
     out, level, tn, tp = level_call(

time: 89.4 us -> 96.2 us (1.076)
  local copies, waits for them, and re-layouts: 10.9 us -> 16 us
  waiting for transfers between devices: 18.9 us -> 16.6 us
  starting transfers between devices: 24.5 us -> 26.6 us
  other arithmetic: 0.82 us -> 2.49 us
    ppermute x2, waiting for transfers between devices: 6.69 us -> 3.72 us  [diagonal(): return lax.ppermute(x, ('rows', 'cols'), pairs)]
    ppermute x0 -> x2, local copies, waits for them, and re-layouts: none -> 2.07 us  [diagonal(): return lax.ppermute(x, ('rows', 'cols'), pairs)]
    select_n x2 -> x3, other arithmetic: 0.17 us -> 1.82 us  [the longest x2 1.64 us: facing(): return jnp.where(on_left, x[..., width - HALO:], x[..., :HALO])]
    unnamed x10 -> x8, local copies, waits for them, and re-layouts: 5.79 us -> 7.34 us
    slice x1 -> x2, local copies, waits for them, and re-layouts: 0.04 us -> 1.51 us  [the longest x1 0.85 us: on_device(): p_own, n_own = (mixed_own[:2], mixed_own[2:])]
    ppermute x6, starting transfers between devices: 18.4 us -> 19.5 us  [shifted(): return lax.ppermute(x, axis, pairs)]
    ppermute x2, starting transfers between devices: 5.58 us -> 6.59 us  [diagonal(): return lax.ppermute(x, ('rows', 'cols'), pairs)]
    dot_general x2 -> x3, matrix products: 11.5 us -> 11.7 us  [mix(): jnp.einsum('crw,bc->rwb', x, weights, precision=lax.Precision.HIGHEST, pr...]
  transfers between devices with their start and end apart: 9 -> 9, of which waited for: 5 -> 5; matrix products, arithmetic and copies ran while one was open for 4% -> 19% of each run, Pallas kernels for 0% -> 0%
where the time goes in v6:
time: 96.2 us; the launch traced here: 95.7 us
  starting transfers between devices  26.6 us (28%)
  Pallas kernels  22.2 us (23%)
  waiting for transfers between devices  16.6 us (17%)
  local copies, waits for them, and re-layouts  16 us (17%)
  matrix products  11.7 us (12%)
  other arithmetic  2.49 us (3%)
    pallas_call x3, Pallas kernels, level_call(): pl.pallas_call(kernel, grid_spec=grid_spec, out_shape=tuple((jax.ShapeDty...  22.2 us
    ppermute x6, starting transfers between devices, shifted(): return lax.ppermute(x, axis, pairs)  19.5 us
    ppermute x6, waiting for transfers between devices, shifted(): return lax.ppermute(x, axis, pairs)  12.8 us
    dot_general x3, matrix products, mix(): jnp.einsum('crw,bc->rwb', x, weights, precision=lax.Precision.HIGHEST, pr...  11.7 us
    unnamed x8, local copies, waits for them, and re-layouts  7.34 us
    ppermute x2, starting transfers between devices, diagonal(): return lax.ppermute(x, ('rows', 'cols'), pairs)  6.59 us
    slice x1, local copies, waits for them, and re-layouts, on_device(): return jnp.transpose(out, (2, 0, 1))[:bands]  5.1 us
    ppermute x2, waiting for transfers between devices, diagonal(): return lax.ppermute(x, ('rows', 'cols'), pairs)  3.72 us
  transfers between devices with their start and end apart: 9, of which 5 were waited for; matrix products, arithmetic and copies ran while one was open for 19% of the time, Pallas kernels for 0%

profile of v6, /device:TPU:0, one launch (start us, length us, event | category | flops | bytes accessed | tf_op | source)
XLA Modules:
  0.0 95.7 jit_solution(8957214294578690954)
XLA Ops:
  0.0 0.0 copy-start.2
  0.0 4.2 %copy.17 = f32[224,32,128]{2,0,1:T(8,128)S(1)} copy(f32[224,32,128]{2,1,0:T(8,128)} %param.2) | data formatting | bytes 7340032 | tf_op args[0]
  4.2 0.1 fusion.25
  4.3 1.3 %collective-permute-start.2 = (f32[224,2,128]{2,0,1:T(8,128)S(1)}, f32[224,2,128]{2,0,1:T(8,128)S(1)}, u32[]{:S(2)}, u32[]{:S(2)}) collective-permute-start(f32[224,2,128]{2,0,1:T(8,128)S(1)} %pad_maximum_fusion.1), channel_id=1, source_target_pairs={{2,0},{4,2},{6,4},{8,6},{10,8},{12,10},{14,12},{3,1},{5,3},{7,5},{... | collective-permute-start | bytes 688136 | tf_op jit(solution)/shard_map/ppermute | solution.py:26
  5.6 0.8 fusion.5
  6.4 1.3 %collective-permute-start.4 = (f32[224,2,32]{2,0,1:T(8,128)}, f32[224,2,32]{2,0,1:T(8,128)}, u32[]{:S(2)}, u32[]{:S(2)}) collective-permute-start(f32[224,2,32]{2,0,1:T(8,128)} %fusion.5), channel_id=1, source_target_pairs={{2,1},{3,0},{4,3},{5,2},{6,5},{7,4},{8,7},{9,6},{10,9},{11,8},{12,... | collective-permute-start | bytes 172040 | tf_op jit(solution)/shard_map/ppermute | solution.py:212
  7.7 0.0 copy-done.2
  7.7 0.1 copy.16
  7.8 10.4 %convolution_bitcast_fusion.own = f32[32,128,256]{2,1,0:T(8,128)S(1)} fusion(f32[224,224]{0,1:T(8,128)S(1)} %copy.16, f32[224,32,128]{2,1,0:T(8,128)} %param.2), kind=kOutput, calls=%fused_computation | convolution fusion | flops 2818572288 | bytes 8065024 | tf_op jit(solution)/shard_map/crw,bc->rwb/dot_general | solution.py:232
  18.2 0.0 copy-start
  18.2 2.0 %copy-done = f32[32,128,256]{2,1,0:T(8,128)} copy-done((f32[32,128,256]{2,1,0:T(8,128)}, f32[32,128,256]{2,1,0:T(8,128)S(1)}, u32[]{:S(2)}) %copy-start) | copy-done | bytes 4194328
  20.2 0.2 slice_select_fusion
  20.4 0.5 collective-permute-start
  20.9 5.7 %collective-permute-start.1 = (f32[224,2,128]{2,0,1:T(8,128)S(1)}, f32[224,2,128]{2,0,1:T(8,128)S(1)}, u32[]{:S(2)}, u32[]{:S(2)}) collective-permute-start(f32[224,2,128]{2,0,1:T(8,128)S(1)} %pad_maximum_fusion), channel_id=1, source_target_pairs={{0,2},{2,4},{4,6},{6,8},{8,10},{10,12},{12,14},{1,3},{3,5},{5,7},{... | collective-permute-start | bytes 688136 | tf_op jit(solution)/shard_map/ppermute | solution.py:26
  26.6 0.8 fusion.8
  27.5 5.3 %collective-permute-start.3 = (f32[224,2,32]{2,0,1:T(8,128)}, f32[224,2,32]{2,0,1:T(8,128)}, u32[]{:S(2)}, u32[]{:S(2)}) collective-permute-start(f32[224,2,32]{2,0,1:T(8,128)} %fusion.8), channel_id=1, source_target_pairs={{0,3},{1,2},{2,5},{3,4},{4,7},{5,6},{6,9},{7,8},{8,11},{9,10},{10,... | collective-permute-start | bytes 172040 | tf_op jit(solution)/shard_map/ppermute | solution.py:212
  32.8 0.6 add_convert_fusion.flags
  33.4 0.0 collective-permute-done.4
  33.4 1.0 %copy.26 = f32[224,2,32]{0,2,1:T(8,128)S(1)} copy(f32[224,2,32]{2,0,1:T(8,128)} %collective-permute-done.4) | data formatting | bytes 114688 | tf_op jit(solution)/shard_map/ppermute | solution.py:212
  34.4 3.7 %collective-permute-done.3 = f32[224,2,32]{2,0,1:T(8,128)} collective-permute-done((f32[224,2,32]{2,0,1:T(8,128)}, f32[224,2,32]{2,0,1:T(8,128)}, u32[]{:S(2)}, u32[]{:S(2)}) %collective-permute-start.3) | collective-permute-done | bytes 57376 | tf_op jit(solution)/shard_map/ppermute | solution.py:212
  38.1 1.0 %copy.25 = f32[224,2,32]{0,2,1:T(8,128)S(1)} copy(f32[224,2,32]{2,0,1:T(8,128)} %collective-permute-done.3) | data formatting | bytes 114688 | tf_op jit(solution)/shard_map/ppermute | solution.py:212
  39.2 0.3 fusion.10
  39.5 0.7 fusion.33
  40.1 0.0 collective-permute-done.2
  40.1 0.0 collective-permute-done.1
  40.1 1.0 %fusion = f32[4,128,256]{2,1,0:T(8,128)S(1)} fusion(f32[224,2,128]{2,0,1:T(8,128)S(1)} %collective-permute-done.2, f32[224,2,128]{2,0,1:T(8,128)S(1)} %collective-permute-done.1, f32[224,224]{0,1:T(8,128)S(1)} %copy.16), kind=kOutput, calls=%fused_computation.2 | convolution fusion | flops 352436224 | bytes 1183744 | tf_op jit(solution)/shard_map/crw,bc->rwb/dot_general | solution.py:232
  41.1 0.9 fusion.32
  42.0 0.0 collective-permute-done.halo
  42.0 0.0 copy-start.1
  42.0 1.1 %copy-done.1 = f32[32,32,256]{2,1,0:T(8,128)} copy-done((f32[32,32,256]{2,1,0:T(8,128)}, f32[32,32,256]{2,1,0:T(8,128)S(1)}, u32[]{:S(2)}) %copy-start.1) | copy-done | bytes 1048600
  43.0 11.5 %shard_map.28 = (f32[32,128,256]{2,1,0:T(8,128)}, f32[16,80,256]{2,1,0:T(8,128)}, f32[2,80,256]{2,1,0:T(8,128)}, f32[2,80,256]{2,1,0:T(8,128)}) custom-call(s32[3]{0:T(128)} %add_convert_fusion.flags, f32[32,128,256]{2,1,0:T(8,128)} %copy-done, f32[32,32,256]{2,1,0:T(8,128)} %copy-done.1, f32[2,128,256]{2,1,0:T(8,128)} %get-tuple-element.28.prev_own, ...), custom_call_target="tpu_custom_call" | custom-call | tf_op jit(solution)/shard_map/pallas_call | solution.py:191
  54.5 4.8 %collective-permute-start.5 = (f32[2,80,256]{2,1,0:T(8,128)}, f32[2,80,256]{2,1,0:T(8,128)}, u32[]{:S(2)}, u32[]{:S(2)}) collective-permute-start(f32[2,80,256]{2,1,0:T(8,128)} %get-tuple-element.15), channel_id=1, source_target_pairs={{0,2},{2,4},{4,6},{6,8},{8,10},{10,12},{12,14},{1,3},{3,5},{5,7},{... | collective-permute-start | bytes 491528 | tf_op jit(solution)/shard_map/ppermute | solution.py:26
  59.3 1.3 %collective-permute-start.6 = (f32[2,80,256]{2,1,0:T(8,128)}, f32[2,80,256]{2,1,0:T(8,128)}, u32[]{:S(2)}, u32[]{:S(2)}) collective-permute-start(f32[2,80,256]{2,1,0:T(8,128)} %get-tuple-element.16), channel_id=1, source_target_pairs={{2,0},{4,2},{6,4},{8,6},{10,8},{12,10},{14,12},{3,1},{5,3},{7,5},{... | collective-permute-start | bytes 491528 | tf_op jit(solution)/shard_map/ppermute | solution.py:26
  60.6 2.1 %collective-permute-done.5.from_prev = f32[2,80,256]{2,1,0:T(8,128)} collective-permute-done((f32[2,80,256]{2,1,0:T(8,128)}, f32[2,80,256]{2,1,0:T(8,128)}, u32[]{:S(2)}, u32[]{:S(2)}) %collective-permute-start.5) | collective-permute-done | bytes 163872 | tf_op jit(solution)/shard_map/ppermute | solution.py:26
  62.7 5.4 %collective-permute-done.6.from_next = f32[2,80,256]{2,1,0:T(8,128)} collective-permute-done((f32[2,80,256]{2,1,0:T(8,128)}, f32[2,80,256]{2,1,0:T(8,128)}, u32[]{:S(2)}, u32[]{:S(2)}) %collective-permute-start.6) | collective-permute-done | bytes 163872 | tf_op jit(solution)/shard_map/ppermute | solution.py:26
  68.1 5.8 %shard_map.29 = (f32[32,128,256]{2,1,0:T(8,128)}, f32[8,40,256]{2,1,0:T(8,128)}, f32[2,40,256]{2,1,0:T(8,128)}, f32[2,40,256]{2,1,0:T(8,128)}) custom-call(s32[3]{0:T(128)} %add_convert_fusion.flags, f32[16,80,256]{2,1,0:T(8,128)} %get-tuple-element.14.x_ref, f32[2,80,256]{2,1,0:T(8,128)} %collective-permute-done.5.from_prev, ...), custom_call_target="tpu_custom_call", output_to_operand_aliasing={{0}: (4, {})} | custom-call | tf_op jit(solution)/shard_map/pallas_call | solution.py:191
  73.9 5.2 %collective-permute-start.7 = (f32[2,40,256]{2,1,0:T(8,128)}, f32[2,40,256]{2,1,0:T(8,128)}, u32[]{:S(2)}, u32[]{:S(2)}) collective-permute-start(f32[2,40,256]{2,1,0:T(8,128)} %get-tuple-element.19), channel_id=1, source_target_pairs={{0,2},{2,4},{4,6},{6,8},{8,10},{10,12},{12,14},{1,3},{3,5},{5,7},{... | collective-permute-start | bytes 245768 | tf_op jit(solution)/shard_map/ppermute | solution.py:26
  79.0 1.3 %collective-permute-start.8 = (f32[2,40,256]{2,1,0:T(8,128)}, f32[2,40,256]{2,1,0:T(8,128)}, u32[]{:S(2)}, u32[]{:S(2)}) collective-permute-start(f32[2,40,256]{2,1,0:T(8,128)} %get-tuple-element.20), channel_id=1, source_target_pairs={{2,0},{4,2},{6,4},{8,6},{10,8},{12,10},{14,12},{3,1},{5,3},{7,5},{... | collective-permute-start | bytes 245768 | tf_op jit(solution)/shard_map/ppermute | solution.py:26
  80.3 0.4 collective-permute-done.7.from_prev
  80.8 4.9 %collective-permute-done.8.from_next = f32[2,40,256]{2,1,0:T(8,128)} collective-permute-done((f32[2,40,256]{2,1,0:T(8,128)}, f32[2,40,256]{2,1,0:T(8,128)}, u32[]{:S(2)}, u32[]{:S(2)}) %collective-permute-start.8) | collective-permute-done | bytes 81952 | tf_op jit(solution)/shard_map/ppermute | solution.py:26
  85.7 4.9 %shard_map.30 = (f32[32,128,256]{2,1,0:T(8,128)}, f32[4,20,256]{2,1,0:T(8,128)}, f32[2,20,256]{2,1,0:T(8,128)}, f32[2,20,256]{2,1,0:T(8,128)}) custom-call(s32[3]{0:T(128)} %add_convert_fusion.flags, f32[8,40,256]{2,1,0:T(8,128)} %get-tuple-element.18.x_ref, f32[2,40,256]{2,1,0:T(8,128)} %collective-permute-done.7.from_prev, ...), custom_call_target="tpu_custom_call", output_to_operand_aliasing={{0}: (4, {})} | custom-call | tf_op jit(solution)/shard_map/pallas_call | solution.py:191
  90.6 5.1 %copy.27 = f32[224,32,128]{2,1,0:T(8,128)} copy(f32[224,32,128]{0,2,1:T(8,128)} %bitcast.14) | data formatting | bytes 7340032 | tf_op jit(solution)/shard_map/slice | solution.py:262
  (2 shorter events, 0.0 us)
Async XLA Ops:
  0.0 7.7 %copy-start.2 = (f32[224,224]{1,0:T(8,128)S(1)}, f32[224,224]{1,0:T(8,128)}, u32[]{:S(2)}) copy-start(f32[224,224]{1,0:T(8,128)} %param.3) | copy-start | bytes 602116
  4.3 35.8 %collective-permute-start.2 = (f32[224,2,128]{2,0,1:T(8,128)S(1)}, f32[224,2,128]{2,0,1:T(8,128)S(1)}, u32[]{:S(2)}, u32[]{:S(2)}) collective-permute-start(f32[224,2,128]{2,0,1:T(8,128)S(1)} %pad_maximum_fusion.1), channel_id=1, source_target_pairs={{2,0},{4,2},{6,4},{8,6},{10,8},{12,10},{14,12},{3,1},{5,3},{7,5},{... | collective-permute-start | bytes 688136 | tf_op jit(solution)/shard_map/ppermute | solution.py:26
  6.4 26.9 %collective-permute-start.4 = (f32[224,2,32]{2,0,1:T(8,128)}, f32[224,2,32]{2,0,1:T(8,128)}, u32[]{:S(2)}, u32[]{:S(2)}) collective-permute-start(f32[224,2,32]{2,0,1:T(8,128)} %fusion.5), channel_id=1, source_target_pairs={{2,1},{3,0},{4,3},{5,2},{6,5},{7,4},{8,7},{9,6},{10,9},{11,8},{12,... | collective-permute-start | bytes 172040 | tf_op jit(solution)/shard_map/ppermute | solution.py:212
  18.2 2.0 %copy-start = (f32[32,128,256]{2,1,0:T(8,128)}, f32[32,128,256]{2,1,0:T(8,128)S(1)}, u32[]{:S(2)}) copy-start(f32[32,128,256]{2,1,0:T(8,128)S(1)} %convolution_bitcast_fusion.own) | copy-start | bytes 12582916
  20.4 21.6 %collective-permute-start = (f32[32,32,256]{2,1,0:T(8,128)S(1)}, f32[32,32,256]{2,1,0:T(8,128)S(1)}, u32[]{:S(2)}, u32[]{:S(2)}) collective-permute-start(f32[32,32,256]{2,1,0:T(8,128)S(1)} %slice_select_fusion), channel_id=1, source_target_pairs={{0,1},{1,0},{2,3},{3,2},{4,5},{5,4},{6,7},{7,6},{8,9},{9,8},{10,11... | collective-permute-start | bytes 3145736 | tf_op jit(solution)/shard_map/ppermute | solution.py:201
  20.9 19.2 %collective-permute-start.1 = (f32[224,2,128]{2,0,1:T(8,128)S(1)}, f32[224,2,128]{2,0,1:T(8,128)S(1)}, u32[]{:S(2)}, u32[]{:S(2)}) collective-permute-start(f32[224,2,128]{2,0,1:T(8,128)S(1)} %pad_maximum_fusion), channel_id=1, source_target_pairs={{0,2},{2,4},{4,6},{6,8},{8,10},{10,12},{12,14},{1,3},{3,5},{5,7},{... | collective-permute-start | bytes 688136 | tf_op jit(solution)/shard_map/ppermute | solution.py:26
  27.5 10.7 %collective-permute-start.3 = (f32[224,2,32]{2,0,1:T(8,128)}, f32[224,2,32]{2,0,1:T(8,128)}, u32[]{:S(2)}, u32[]{:S(2)}) collective-permute-start(f32[224,2,32]{2,0,1:T(8,128)} %fusion.8), channel_id=1, source_target_pairs={{0,3},{1,2},{2,5},{3,4},{4,7},{5,6},{6,9},{7,8},{8,11},{9,10},{10,... | collective-permute-start | bytes 172040 | tf_op jit(solution)/shard_map/ppermute | solution.py:212
  42.0 1.1 %copy-start.1 = (f32[32,32,256]{2,1,0:T(8,128)}, f32[32,32,256]{2,1,0:T(8,128)S(1)}, u32[]{:S(2)}) copy-start(f32[32,32,256]{2,1,0:T(8,128)S(1)} %collective-permute-done.halo) | copy-start | bytes 3145732
  54.5 8.2 %collective-permute-start.5 = (f32[2,80,256]{2,1,0:T(8,128)}, f32[2,80,256]{2,1,0:T(8,128)}, u32[]{:S(2)}, u32[]{:S(2)}) collective-permute-start(f32[2,80,256]{2,1,0:T(8,128)} %get-tuple-element.15), channel_id=1, source_target_pairs={{0,2},{2,4},{4,6},{6,8},{8,10},{10,12},{12,14},{1,3},{3,5},{5,7},{... | collective-permute-start | bytes 491528 | tf_op jit(solution)/shard_map/ppermute | solution.py:26
  59.3 8.8 %collective-permute-start.6 = (f32[2,80,256]{2,1,0:T(8,128)}, f32[2,80,256]{2,1,0:T(8,128)}, u32[]{:S(2)}, u32[]{:S(2)}) collective-permute-start(f32[2,80,256]{2,1,0:T(8,128)} %get-tuple-element.16), channel_id=1, source_target_pairs={{2,0},{4,2},{6,4},{8,6},{10,8},{12,10},{14,12},{3,1},{5,3},{7,5},{... | collective-permute-start | bytes 491528 | tf_op jit(solution)/shard_map/ppermute | solution.py:26
  73.9 6.9 %collective-permute-start.7 = (f32[2,40,256]{2,1,0:T(8,128)}, f32[2,40,256]{2,1,0:T(8,128)}, u32[]{:S(2)}, u32[]{:S(2)}) collective-permute-start(f32[2,40,256]{2,1,0:T(8,128)} %get-tuple-element.19), channel_id=1, source_target_pairs={{0,2},{2,4},{4,6},{6,8},{8,10},{10,12},{12,14},{1,3},{3,5},{5,7},{... | collective-permute-start | bytes 245768 | tf_op jit(solution)/shard_map/ppermute | solution.py:26
  79.0 6.6 %collective-permute-start.8 = (f32[2,40,256]{2,1,0:T(8,128)}, f32[2,40,256]{2,1,0:T(8,128)}, u32[]{:S(2)}, u32[]{:S(2)}) collective-permute-start(f32[2,40,256]{2,1,0:T(8,128)} %get-tuple-element.20), channel_id=1, source_target_pairs={{2,0},{4,2},{6,4},{8,6},{10,8},{12,10},{14,12},{3,1},{5,3},{7,5},{... | collective-permute-start | bytes 245768 | tf_op jit(solution)/shard_map/ppermute | solution.py:26

commit v7 on v5

--- a/solution.py
+++ b/solution.py
@@ -229,7 +229,7 @@
         return jnp.where(on_left, x[:, width - HALO :], x[:, :HALO])
 
     def mix(x):
-        return jnp.einsum("crw,bc->rwb", x, weights, precision=lax.Precision.HIGHEST,
+        return jnp.einsum("crw,bc->rwb", x, weights, precision=lax.Precision.HIGH,
                           preferred_element_type=jnp.float32)
 
     rad_next, rad_prev = partials(radiance, 1)

time: 89.4 us -> 85.4 us (0.955)
  matrix products: 11.5 us -> 7.59 us
    dot_general x2, matrix products: 11.5 us -> 7.59 us  [mix(): jnp.einsum('crw,bc->rwb', x, weights, precision=lax.Precision.HIGH, prefe...]
where the time goes in v7:
time: 85.4 us; the launch traced here: 85 us
  starting transfers between devices  24.7 us (29%)
  Pallas kernels  22.1 us (26%)
  waiting for transfers between devices  18.7 us (22%)
  local copies, waits for them, and re-layouts  10.9 us (13%)
  matrix products  7.59 us (9%)
    pallas_call x3, Pallas kernels, level_call(): pl.pallas_call(kernel, grid_spec=grid_spec, out_shape=tuple((jax.ShapeDty...  22.1 us
    ppermute x6, starting transfers between devices, shifted(): return lax.ppermute(x, axis, pairs)  18.4 us
    ppermute x6, waiting for transfers between devices, shifted(): return lax.ppermute(x, axis, pairs)  12.2 us
    dot_general x2, matrix products, mix(): jnp.einsum('crw,bc->rwb', x, weights, precision=lax.Precision.HIGH, prefe...  7.59 us
    ppermute x2, waiting for transfers between devices, diagonal(): return lax.ppermute(x, ('rows', 'cols'), pairs)  6.51 us
    unnamed x10, local copies, waits for them, and re-layouts  5.79 us
    ppermute x2, starting transfers between devices, diagonal(): return lax.ppermute(x, ('rows', 'cols'), pairs)  5.76 us
    slice x1, local copies, waits for them, and re-layouts, on_device(): return jnp.transpose(out, (2, 0, 1))[:bands]  5.1 us
  transfers between devices with their start and end apart: 9, of which 5 were waited for; matrix products, arithmetic and copies ran while one was open for 4% of the time, Pallas kernels for 0%

profile of v7, /device:TPU:0, one launch (start us, length us, event | category | flops | bytes accessed | tf_op | source)
XLA Modules:
  0.0 85.0 jit_solution(15901092295212222999)
XLA Ops:
  0.0 1.1 %copy.5 = f32[224,224]{0,1:T(8,128)S(1)} copy(f32[224,224]{1,0:T(8,128)} %param.3) | data formatting | bytes 401408 | tf_op args[1]
  1.1 0.0 copy-start.1
  1.1 7.0 %convolution_bitcast_fusion.own = f32[32,128,256]{2,1,0:T(8,128)S(1)} fusion(f32[224,224]{0,1:T(8,128)S(1)} %copy.5, f32[224,32,128]{2,1,0:T(8,128)} %param.2), kind=kOutput, calls=%fused_computation | convolution fusion | flops 1409286144 | bytes 8065024 | tf_op jit(solution)/shard_map/crw,bc->rwb/dot_general | solution.py:232
  8.1 0.0 copy-start
  8.1 2.0 %copy-done = f32[32,128,256]{2,1,0:T(8,128)} copy-done((f32[32,128,256]{2,1,0:T(8,128)}, f32[32,128,256]{2,1,0:T(8,128)S(1)}, u32[]{:S(2)}) %copy-start) | copy-done | bytes 4194328
  10.1 0.1 slice_select_fusion
  10.2 0.5 collective-permute-start
  10.7 0.0 copy-done.1
  10.7 2.1 %copy.6 = f32[224,32,128]{2,0,1:T(8,128)S(1)} copy(f32[224,32,128]{2,1,0:T(8,128)S(1)} %copy-done.1) | data formatting | bytes 7340032 | tf_op args[0]
  12.9 0.1 fusion.17
  12.9 0.6 fusion
  13.6 1.3 %collective-permute-start.3 = (f32[2,128,256]{2,1,0:T(8,128)S(1)}, f32[2,128,256]{2,1,0:T(8,128)}, u32[]{:S(2)}, u32[]{:S(2)}) collective-permute-start(f32[2,128,256]{2,1,0:T(8,128)S(1)} %get-tuple-element.29), channel_id=1, source_target_pairs={{2,0},{4,2},{6,4},{8,6},{10,8},{12,10},{14,12},{3,1},{5,3},{7,5},{... | collective-permute-start | bytes 786440 | tf_op jit(solution)/shard_map/ppermute | solution.py:26
  14.9 5.8 %collective-permute-start.1 = (f32[2,128,256]{2,1,0:T(8,128)S(1)}, f32[2,128,256]{2,1,0:T(8,128)}, u32[]{:S(2)}, u32[]{:S(2)}) collective-permute-start(f32[2,128,256]{2,1,0:T(8,128)S(1)} %get-tuple-element.30), channel_id=1, source_target_pairs={{0,2},{2,4},{4,6},{6,8},{8,10},{10,12},{12,14},{1,3},{3,5},{5,7},{... | collective-permute-start | bytes 786440 | tf_op jit(solution)/shard_map/ppermute | solution.py:26
  20.7 1.3 %collective-permute-start.4 = (f32[2,32,256]{2,1,0:T(8,128)S(1)}, f32[2,32,256]{2,1,0:T(8,128)S(1)}, u32[]{:S(2)}, u32[]{:S(2)}) collective-permute-start(f32[2,32,256]{2,1,0:T(8,128)S(1)} %get-tuple-element.27), channel_id=1, source_target_pairs={{2,1},{3,0},{4,3},{5,2},{6,5},{7,4},{8,7},{9,6},{10,9},{11,8},{12,... | collective-permute-start | bytes 196616 | tf_op jit(solution)/shard_map/ppermute | solution.py:212
  22.0 4.5 %collective-permute-start.2 = (f32[2,32,256]{2,1,0:T(8,128)S(1)}, f32[2,32,256]{2,1,0:T(8,128)S(1)}, u32[]{:S(2)}, u32[]{:S(2)}) collective-permute-start(f32[2,32,256]{2,1,0:T(8,128)S(1)} %get-tuple-element.28), channel_id=1, source_target_pairs={{0,3},{1,2},{2,5},{3,4},{4,7},{5,6},{6,9},{7,8},{8,11},{9,10},{10,... | collective-permute-start | bytes 196616 | tf_op jit(solution)/shard_map/ppermute | solution.py:212
  26.5 0.6 add_convert_fusion.flags
  27.1 0.0 collective-permute-done.4.next_halo
  27.1 0.0 copy-start.2
  27.1 6.5 %collective-permute-done.2.prev_halo = f32[2,32,256]{2,1,0:T(8,128)S(1)} collective-permute-done((f32[2,32,256]{2,1,0:T(8,128)S(1)}, f32[2,32,256]{2,1,0:T(8,128)S(1)}, u32[]{:S(2)}, u32[]{:S(2)}) %collective-permute-start.2) | collective-permute-done | bytes 65568 | tf_op jit(solution)/shard_map/ppermute | solution.py:212
  33.6 0.0 copy-start.3
  33.6 0.0 collective-permute-done.3.next_own
  33.6 0.0 collective-permute-done.1.prev_own
  33.6 0.0 copy-done.2
  33.6 0.6 copy-done.3
  34.2 0.0 collective-permute-done.halo
  34.2 11.5 %shard_map.28 = (f32[32,128,256]{2,1,0:T(8,128)}, f32[16,80,256]{2,1,0:T(8,128)}, f32[2,80,256]{2,1,0:T(8,128)}, f32[2,80,256]{2,1,0:T(8,128)}) custom-call(s32[3]{0:T(128)} %add_convert_fusion.flags, f32[32,128,256]{2,1,0:T(8,128)} %copy-done, f32[32,32,256]{2,1,0:T(8,128)} %collective-permute-done.halo, f32[2,128,256]{2,1,0:T(8,128)} %collective-permute-done.1.prev_own, ...), custom_call_target="tpu_custom_call" | custom-call | tf_op jit(solution)/shard_map/pallas_call | solution.py:191
  45.7 5.0 %collective-permute-start.5 = (f32[2,80,256]{2,1,0:T(8,128)}, f32[2,80,256]{2,1,0:T(8,128)}, u32[]{:S(2)}, u32[]{:S(2)}) collective-permute-start(f32[2,80,256]{2,1,0:T(8,128)} %get-tuple-element.15), channel_id=1, source_target_pairs={{0,2},{2,4},{4,6},{6,8},{8,10},{10,12},{12,14},{1,3},{3,5},{5,7},{... | collective-permute-start | bytes 491528 | tf_op jit(solution)/shard_map/ppermute | solution.py:26
  50.7 1.3 %collective-permute-start.6 = (f32[2,80,256]{2,1,0:T(8,128)}, f32[2,80,256]{2,1,0:T(8,128)}, u32[]{:S(2)}, u32[]{:S(2)}) collective-permute-start(f32[2,80,256]{2,1,0:T(8,128)} %get-tuple-element.16), channel_id=1, source_target_pairs={{2,0},{4,2},{6,4},{8,6},{10,8},{12,10},{14,12},{3,1},{5,3},{7,5},{... | collective-permute-start | bytes 491528 | tf_op jit(solution)/shard_map/ppermute | solution.py:26
  52.0 5.6 %collective-permute-done.5.from_prev = f32[2,80,256]{2,1,0:T(8,128)} collective-permute-done((f32[2,80,256]{2,1,0:T(8,128)}, f32[2,80,256]{2,1,0:T(8,128)}, u32[]{:S(2)}, u32[]{:S(2)}) %collective-permute-start.5) | collective-permute-done | bytes 163872 | tf_op jit(solution)/shard_map/ppermute | solution.py:26
  57.6 1.2 %collective-permute-done.6.from_next = f32[2,80,256]{2,1,0:T(8,128)} collective-permute-done((f32[2,80,256]{2,1,0:T(8,128)}, f32[2,80,256]{2,1,0:T(8,128)}, u32[]{:S(2)}, u32[]{:S(2)}) %collective-permute-start.6) | collective-permute-done | bytes 163872 | tf_op jit(solution)/shard_map/ppermute | solution.py:26
  58.8 5.8 %shard_map.29 = (f32[32,128,256]{2,1,0:T(8,128)}, f32[8,40,256]{2,1,0:T(8,128)}, f32[2,40,256]{2,1,0:T(8,128)}, f32[2,40,256]{2,1,0:T(8,128)}) custom-call(s32[3]{0:T(128)} %add_convert_fusion.flags, f32[16,80,256]{2,1,0:T(8,128)} %get-tuple-element.14.x_ref, f32[2,80,256]{2,1,0:T(8,128)} %collective-permute-done.5.from_prev, ...), custom_call_target="tpu_custom_call", output_to_operand_aliasing={{0}: (4, {})} | custom-call | tf_op jit(solution)/shard_map/pallas_call | solution.py:191
  64.6 3.8 %collective-permute-start.7 = (f32[2,40,256]{2,1,0:T(8,128)}, f32[2,40,256]{2,1,0:T(8,128)}, u32[]{:S(2)}, u32[]{:S(2)}) collective-permute-start(f32[2,40,256]{2,1,0:T(8,128)} %get-tuple-element.19), channel_id=1, source_target_pairs={{0,2},{2,4},{4,6},{6,8},{8,10},{10,12},{12,14},{1,3},{3,5},{5,7},{... | collective-permute-start | bytes 245768 | tf_op jit(solution)/shard_map/ppermute | solution.py:26
  68.4 1.3 %collective-permute-start.8 = (f32[2,40,256]{2,1,0:T(8,128)}, f32[2,40,256]{2,1,0:T(8,128)}, u32[]{:S(2)}, u32[]{:S(2)}) collective-permute-start(f32[2,40,256]{2,1,0:T(8,128)} %get-tuple-element.20), channel_id=1, source_target_pairs={{2,0},{4,2},{6,4},{8,6},{10,8},{12,10},{14,12},{3,1},{5,3},{7,5},{... | collective-permute-start | bytes 245768 | tf_op jit(solution)/shard_map/ppermute | solution.py:26
  69.6 0.4 collective-permute-done.7.from_prev
  70.1 4.9 %collective-permute-done.8.from_next = f32[2,40,256]{2,1,0:T(8,128)} collective-permute-done((f32[2,40,256]{2,1,0:T(8,128)}, f32[2,40,256]{2,1,0:T(8,128)}, u32[]{:S(2)}, u32[]{:S(2)}) %collective-permute-start.8) | collective-permute-done | bytes 81952 | tf_op jit(solution)/shard_map/ppermute | solution.py:26
  75.0 4.9 %shard_map.30 = (f32[32,128,256]{2,1,0:T(8,128)}, f32[4,20,256]{2,1,0:T(8,128)}, f32[2,20,256]{2,1,0:T(8,128)}, f32[2,20,256]{2,1,0:T(8,128)}) custom-call(s32[3]{0:T(128)} %add_convert_fusion.flags, f32[8,40,256]{2,1,0:T(8,128)} %get-tuple-element.18.x_ref, f32[2,40,256]{2,1,0:T(8,128)} %collective-permute-done.7.from_prev, ...), custom_call_target="tpu_custom_call", output_to_operand_aliasing={{0}: (4, {})} | custom-call | tf_op jit(solution)/shard_map/pallas_call | solution.py:191
  79.9 5.1 %copy.14 = f32[224,32,128]{2,1,0:T(8,128)} copy(f32[224,32,128]{0,2,1:T(8,128)} %bitcast.12) | data formatting | bytes 7340032 | tf_op jit(solution)/shard_map/slice | solution.py:258
  (2 shorter events, 0.1 us)
Async XLA Ops:
  1.1 9.7 %copy-start.1 = (f32[224,32,128]{2,1,0:T(8,128)S(1)}, f32[224,32,128]{2,1,0:T(8,128)}, u32[]{:S(2)}) copy-start(f32[224,32,128]{2,1,0:T(8,128)} %param.2) | copy-start | bytes 11010052
  8.1 2.0 %copy-start = (f32[32,128,256]{2,1,0:T(8,128)}, f32[32,128,256]{2,1,0:T(8,128)S(1)}, u32[]{:S(2)}) copy-start(f32[32,128,256]{2,1,0:T(8,128)S(1)} %convolution_bitcast_fusion.own) | copy-start | bytes 12582916
  10.2 24.0 %collective-permute-start = (f32[32,32,256]{2,1,0:T(8,128)S(1)}, f32[32,32,256]{2,1,0:T(8,128)}, u32[]{:S(2)}, u32[]{:S(2)}) collective-permute-start(f32[32,32,256]{2,1,0:T(8,128)S(1)} %slice_select_fusion), channel_id=1, source_target_pairs={{0,1},{1,0},{2,3},{3,2},{4,5},{5,4},{6,7},{7,6},{8,9},{9,8},{10,11... | collective-permute-start | bytes 3145736 | tf_op jit(solution)/shard_map/ppermute | solution.py:201
  13.6 20.0 %collective-permute-start.3 = (f32[2,128,256]{2,1,0:T(8,128)S(1)}, f32[2,128,256]{2,1,0:T(8,128)}, u32[]{:S(2)}, u32[]{:S(2)}) collective-permute-start(f32[2,128,256]{2,1,0:T(8,128)S(1)} %get-tuple-element.29), channel_id=1, source_target_pairs={{2,0},{4,2},{6,4},{8,6},{10,8},{12,10},{14,12},{3,1},{5,3},{7,5},{... | collective-permute-start | bytes 786440 | tf_op jit(solution)/shard_map/ppermute | solution.py:26
  14.9 18.7 %collective-permute-start.1 = (f32[2,128,256]{2,1,0:T(8,128)S(1)}, f32[2,128,256]{2,1,0:T(8,128)}, u32[]{:S(2)}, u32[]{:S(2)}) collective-permute-start(f32[2,128,256]{2,1,0:T(8,128)S(1)} %get-tuple-element.30), channel_id=1, source_target_pairs={{0,2},{2,4},{4,6},{6,8},{8,10},{10,12},{12,14},{1,3},{3,5},{5,7},{... | collective-permute-start | bytes 786440 | tf_op jit(solution)/shard_map/ppermute | solution.py:26
  20.7 6.4 %collective-permute-start.4 = (f32[2,32,256]{2,1,0:T(8,128)S(1)}, f32[2,32,256]{2,1,0:T(8,128)S(1)}, u32[]{:S(2)}, u32[]{:S(2)}) collective-permute-start(f32[2,32,256]{2,1,0:T(8,128)S(1)} %get-tuple-element.27), channel_id=1, source_target_pairs={{2,1},{3,0},{4,3},{5,2},{6,5},{7,4},{8,7},{9,6},{10,9},{11,8},{12,... | collective-permute-start | bytes 196616 | tf_op jit(solution)/shard_map/ppermute | solution.py:212
  22.0 11.6 %collective-permute-start.2 = (f32[2,32,256]{2,1,0:T(8,128)S(1)}, f32[2,32,256]{2,1,0:T(8,128)S(1)}, u32[]{:S(2)}, u32[]{:S(2)}) collective-permute-start(f32[2,32,256]{2,1,0:T(8,128)S(1)} %get-tuple-element.28), channel_id=1, source_target_pairs={{0,3},{1,2},{2,5},{3,4},{4,7},{5,6},{6,9},{7,8},{8,11},{9,10},{10,... | collective-permute-start | bytes 196616 | tf_op jit(solution)/shard_map/ppermute | solution.py:212
  27.1 6.5 %copy-start.2 = (f32[2,32,256]{2,1,0:T(8,128)}, f32[2,32,256]{2,1,0:T(8,128)S(1)}, u32[]{:S(2)}) copy-start(f32[2,32,256]{2,1,0:T(8,128)S(1)} %collective-permute-done.4.next_halo) | copy-start | bytes 196612
  33.6 0.6 copy-start.3
  45.7 11.9 %collective-permute-start.5 = (f32[2,80,256]{2,1,0:T(8,128)}, f32[2,80,256]{2,1,0:T(8,128)}, u32[]{:S(2)}, u32[]{:S(2)}) collective-permute-start(f32[2,80,256]{2,1,0:T(8,128)} %get-tuple-element.15), channel_id=1, source_target_pairs={{0,2},{2,4},{4,6},{6,8},{8,10},{10,12},{12,14},{1,3},{3,5},{5,7},{... | collective-permute-start | bytes 491528 | tf_op jit(solution)/shard_map/ppermute | solution.py:26
  50.7 8.1 %collective-permute-start.6 = (f32[2,80,256]{2,1,0:T(8,128)}, f32[2,80,256]{2,1,0:T(8,128)}, u32[]{:S(2)}, u32[]{:S(2)}) collective-permute-start(f32[2,80,256]{2,1,0:T(8,128)} %get-tuple-element.16), channel_id=1, source_target_pairs={{2,0},{4,2},{6,4},{8,6},{10,8},{12,10},{14,12},{3,1},{5,3},{7,5},{... | collective-permute-start | bytes 491528 | tf_op jit(solution)/shard_map/ppermute | solution.py:26
  64.6 5.5 %collective-permute-start.7 = (f32[2,40,256]{2,1,0:T(8,128)}, f32[2,40,256]{2,1,0:T(8,128)}, u32[]{:S(2)}, u32[]{:S(2)}) collective-permute-start(f32[2,40,256]{2,1,0:T(8,128)} %get-tuple-element.19), channel_id=1, source_target_pairs={{0,2},{2,4},{4,6},{6,8},{8,10},{10,12},{12,14},{1,3},{3,5},{5,7},{... | collective-permute-start | bytes 245768 | tf_op jit(solution)/shard_map/ppermute | solution.py:26
  68.4 6.6 %collective-permute-start.8 = (f32[2,40,256]{2,1,0:T(8,128)}, f32[2,40,256]{2,1,0:T(8,128)}, u32[]{:S(2)}, u32[]{:S(2)}) collective-permute-start(f32[2,40,256]{2,1,0:T(8,128)} %get-tuple-element.20), channel_id=1, source_target_pairs={{2,0},{4,2},{6,4},{8,6},{10,8},{12,10},{14,12},{3,1},{5,3},{7,5},{... | collective-permute-start | bytes 245768 | tf_op jit(solution)/shard_map/ppermute | solution.py:26

commit v8 on v5

--- a/solution.py
+++ b/solution.py
@@ -167,6 +167,17 @@
     ext[EDGE : EDGE + rows] = x_ref[...]
     fill_rows(ext, flags, from_prev[...], from_next[...], rows)
     lift_block(flags, ext, half, out_ref, ll_ref, tn_ref, tp_ref, rows, width, stride)
+
+
+def last_kernel(flags, x_ref, from_prev, from_next, prev_out,
+                final_ref, ext, half, full, ll, tn, tp, *, stride):
+    rows, width = x_ref.shape[0], x_ref.shape[1]
+    full[...] = prev_out[...]
+    ext[EDGE : EDGE + rows] = x_ref[...]
+    fill_rows(ext, flags, from_prev[...], from_next[...], rows)
+    lift_block(flags, ext, half, full, ll, tn, tp, rows, width, stride)
+    for r in range(full.shape[0]):
+        final_ref[:, r, :] = full[r].T
 
 
 def spec(shape):
@@ -248,14 +259,42 @@
         first_kernel, flags,
         [own, halo, p_own, p_halo, n_own, n_halo],
         out_shape, rows, ext_width, {})
-    for lvl in range(1, LEVELS):
+    for lvl in range(1, LEVELS - 1):
         from_prev = shifted(tn, "rows", 1)
         from_next = shifted(tp, "rows", -1)
         r, w = level.shape[0], level.shape[1]
         out, level, tn, tp = level_call(
             functools.partial(next_kernel, stride=2**lvl), flags,
             [level, from_prev, from_next, out], out_shape, r, w, {4: 0})
-    return jnp.transpose(out, (2, 0, 1))[:bands]
+    from_prev = shifted(tn, "rows", 1)
+    from_next = shifted(tp, "rows", -1)
+    return last_call(flags, [level, from_prev, from_next, out], bands, 2 ** (LEVELS - 1))
+
+
+def last_call(flags, arrays, bands, stride):
+    level, out = arrays[0], arrays[3]
+    rows, width = level.shape[0], level.shape[1]
+    final_shape = (bands, out.shape[0], out.shape[1])
+    grid_spec = pltpu.PrefetchScalarGridSpec(
+        num_scalar_prefetch=1,
+        grid=(out.shape[-1] // LANES,),
+        in_specs=[spec(a.shape) for a in arrays],
+        out_specs=pl.BlockSpec((LANES,) + final_shape[1:], lambda h, f: (h, 0, 0)),
+        scratch_shapes=[
+            pltpu.VMEM((rows + 2 * EDGE, width, LANES), jnp.float32),
+            pltpu.VMEM((2, rows // 2, width, LANES), jnp.float32),
+            pltpu.VMEM(out.shape[:-1] + (LANES,), jnp.float32),
+            pltpu.VMEM((rows // 2, width // 2, LANES), jnp.float32),
+            pltpu.VMEM((2, width // 2, LANES), jnp.float32),
+            pltpu.VMEM((2, width // 2, LANES), jnp.float32),
+        ],
+    )
+    return pl.pallas_call(
+        functools.partial(last_kernel, stride=stride),
+        grid_spec=grid_spec,
+        out_shape=jax.ShapeDtypeStruct(final_shape, jnp.float32),
+        compiler_params=pltpu.CompilerParams(vmem_limit_bytes=100 * 1024 * 1024),
+    )(flags, *arrays)
 
 
 def solution(mesh):

time: 89.4 us -> 86.4 us (0.966)
  local copies, waits for them, and re-layouts: 10.9 us -> 5.81 us
  Pallas kernels: 22.1 us -> 24.3 us
    pallas_call x0 -> x1, Pallas kernels: none -> 7.05 us  [last_call(): pl.pallas_call(functools.partial(last_kernel, stride=stride), grid_spec=g...]
    slice x1 -> x0, local copies, waits for them, and re-layouts: 5.1 us -> none  [on_device(): return jnp.transpose(out, (2, 0, 1))[:bands]]
    pallas_call x3 -> x2, Pallas kernels: 22.1 us -> 17.3 us  [level_call(): pl.pallas_call(kernel, grid_spec=grid_spec, out_shape=tuple((jax.ShapeDty...]
where the time goes in v8:
time: 86.4 us; the launch traced here: 86 us
  starting transfers between devices  24.5 us (28%)
  Pallas kernels  24.3 us (28%)
  waiting for transfers between devices  18.9 us (22%)
  matrix products  11.5 us (13%)
  local copies, waits for them, and re-layouts  5.81 us (7%)
    ppermute x6, starting transfers between devices, shifted(): return lax.ppermute(x, axis, pairs)  18.4 us
    pallas_call x2, Pallas kernels, level_call(): pl.pallas_call(kernel, grid_spec=grid_spec, out_shape=tuple((jax.ShapeDty...  17.3 us
    ppermute x6, waiting for transfers between devices, shifted(): return lax.ppermute(x, axis, pairs)  12.2 us
    dot_general x2, matrix products, mix(): jnp.einsum('crw,bc->rwb', x, weights, precision=lax.Precision.HIGHEST, pr...  11.5 us
    pallas_call x1, Pallas kernels, last_call(): pl.pallas_call(functools.partial(last_kernel, stride=stride), grid_spec=g...  7.05 us
    ppermute x2, waiting for transfers between devices, diagonal(): return lax.ppermute(x, ('rows', 'cols'), pairs)  6.71 us
    unnamed x10, local copies, waits for them, and re-layouts  5.77 us
    ppermute x2, starting transfers between devices, diagonal(): return lax.ppermute(x, ('rows', 'cols'), pairs)  5.57 us
  transfers between devices with their start and end apart: 9, of which 5 were waited for; matrix products, arithmetic and copies ran while one was open for 4% of the time, Pallas kernels for 0%

profile of v8, /device:TPU:0, one launch (start us, length us, event | category | flops | bytes accessed | tf_op | source)
XLA Modules:
  0.0 86.0 jit_solution(11897391191765479163)
XLA Ops:
  0.0 1.1 %copy.4 = f32[224,224]{0,1:T(8,128)S(1)} copy(f32[224,224]{1,0:T(8,128)} %param.3) | data formatting | bytes 401408 | tf_op args[1]
  1.1 0.0 copy-start.1
  1.1 10.5 %convolution_bitcast_fusion.own = f32[32,128,256]{2,1,0:T(8,128)S(1)} fusion(f32[224,224]{0,1:T(8,128)S(1)} %copy.4, f32[224,32,128]{2,1,0:T(8,128)} %param.2), kind=kOutput, calls=%fused_computation | convolution fusion | flops 2818572288 | bytes 8065024 | tf_op jit(solution)/shard_map/crw,bc->rwb/dot_general | solution.py:243
  11.6 0.0 copy-start
  11.6 2.0 %copy-done = f32[32,128,256]{2,1,0:T(8,128)} copy-done((f32[32,128,256]{2,1,0:T(8,128)}, f32[32,128,256]{2,1,0:T(8,128)S(1)}, u32[]{:S(2)}) %copy-start) | copy-done | bytes 4194328
  13.6 0.2 slice_select_fusion
  13.8 0.5 collective-permute-start
  14.3 0.0 copy-done.1
  14.3 2.1 %copy.5 = f32[224,32,128]{2,0,1:T(8,128)S(1)} copy(f32[224,32,128]{2,1,0:T(8,128)S(1)} %copy-done.1) | data formatting | bytes 7340032 | tf_op args[0]
  16.4 0.1 fusion.17
  16.5 1.0 %fusion = f32[4,128,256]{2,1,0:T(8,128)S(1)} fusion(f32[224,1,128]{2,0,1:T(8,128)S(1)} %get-tuple-element.22, f32[224,1,128]{2,0,1:T(8,128)S(1)} %get-tuple-element.23, f32[224,1,128]{2,0,1:T(8,128)S(1)} %get-tuple-element.24, f32[224,1,128]{2,0,1:T(8,128)S(1)} %get-tuple-element.21, f32[224,224]{0,1:T(8,128)S(1)} %copy.4), kind=kOutput, calls=%fused_computation.2 | convolution fusion | flops 352665600 | bytes 1183744 | tf_op jit(solution)/shard_map/crw,bc->rwb/dot_general | solution.py:243
  17.6 1.3 %collective-permute-start.3 = (f32[2,128,256]{2,1,0:T(8,128)S(1)}, f32[2,128,256]{2,1,0:T(8,128)}, u32[]{:S(2)}, u32[]{:S(2)}) collective-permute-start(f32[2,128,256]{2,1,0:T(8,128)S(1)} %get-tuple-element.27), channel_id=1, source_target_pairs={{2,0},{4,2},{6,4},{8,6},{10,8},{12,10},{14,12},{3,1},{5,3},{7,5},{... | collective-permute-start | bytes 786440 | tf_op jit(solution)/shard_map/ppermute | solution.py:26
  18.9 5.8 %collective-permute-start.1 = (f32[2,128,256]{2,1,0:T(8,128)S(1)}, f32[2,128,256]{2,1,0:T(8,128)}, u32[]{:S(2)}, u32[]{:S(2)}) collective-permute-start(f32[2,128,256]{2,1,0:T(8,128)S(1)} %get-tuple-element.28), channel_id=1, source_target_pairs={{0,2},{2,4},{4,6},{6,8},{8,10},{10,12},{12,14},{1,3},{3,5},{5,7},{... | collective-permute-start | bytes 786440 | tf_op jit(solution)/shard_map/ppermute | solution.py:26
  24.7 1.3 %collective-permute-start.4 = (f32[2,32,256]{2,1,0:T(8,128)S(1)}, f32[2,32,256]{2,1,0:T(8,128)S(1)}, u32[]{:S(2)}, u32[]{:S(2)}) collective-permute-start(f32[2,32,256]{2,1,0:T(8,128)S(1)} %get-tuple-element.25), channel_id=1, source_target_pairs={{2,1},{3,0},{4,3},{5,2},{6,5},{7,4},{8,7},{9,6},{10,9},{11,8},{12,... | collective-permute-start | bytes 196616 | tf_op jit(solution)/shard_map/ppermute | solution.py:223
  26.0 4.3 %collective-permute-start.2 = (f32[2,32,256]{2,1,0:T(8,128)S(1)}, f32[2,32,256]{2,1,0:T(8,128)S(1)}, u32[]{:S(2)}, u32[]{:S(2)}) collective-permute-start(f32[2,32,256]{2,1,0:T(8,128)S(1)} %get-tuple-element.26), channel_id=1, source_target_pairs={{0,3},{1,2},{2,5},{3,4},{4,7},{5,6},{6,9},{7,8},{8,11},{9,10},{10,... | collective-permute-start | bytes 196616 | tf_op jit(solution)/shard_map/ppermute | solution.py:223
  30.3 0.6 add_convert_fusion.flags
  30.9 0.0 collective-permute-done.4.next_halo
  30.9 0.0 copy-start.2
  30.9 6.7 %collective-permute-done.2.prev_halo = f32[2,32,256]{2,1,0:T(8,128)S(1)} collective-permute-done((f32[2,32,256]{2,1,0:T(8,128)S(1)}, f32[2,32,256]{2,1,0:T(8,128)S(1)}, u32[]{:S(2)}, u32[]{:S(2)}) %collective-permute-start.2) | collective-permute-done | bytes 65568 | tf_op jit(solution)/shard_map/ppermute | solution.py:223
  37.6 0.0 copy-start.3
  37.6 0.0 collective-permute-done.3.next_own
  37.6 0.0 collective-permute-done.1.prev_own
  37.6 0.0 copy-done.2
  37.6 0.6 copy-done.3
  38.2 0.0 collective-permute-done.halo
  38.2 11.5 %shard_map.28 = (f32[32,128,256]{2,1,0:T(8,128)}, f32[16,80,256]{2,1,0:T(8,128)}, f32[2,80,256]{2,1,0:T(8,128)}, f32[2,80,256]{2,1,0:T(8,128)}) custom-call(s32[3]{0:T(128)} %add_convert_fusion.flags, f32[32,128,256]{2,1,0:T(8,128)} %copy-done, f32[32,32,256]{2,1,0:T(8,128)} %collective-permute-done.halo, f32[2,128,256]{2,1,0:T(8,128)} %collective-permute-done.1.prev_own, ...), custom_call_target="tpu_custom_call" | custom-call | tf_op jit(solution)/shard_map/pallas_call | solution.py:202
  49.7 5.0 %collective-permute-start.5 = (f32[2,80,256]{2,1,0:T(8,128)}, f32[2,80,256]{2,1,0:T(8,128)}, u32[]{:S(2)}, u32[]{:S(2)}) collective-permute-start(f32[2,80,256]{2,1,0:T(8,128)} %get-tuple-element.14), channel_id=1, source_target_pairs={{0,2},{2,4},{4,6},{6,8},{8,10},{10,12},{12,14},{1,3},{3,5},{5,7},{... | collective-permute-start | bytes 491528 | tf_op jit(solution)/shard_map/ppermute | solution.py:26
  54.7 1.3 %collective-permute-start.6 = (f32[2,80,256]{2,1,0:T(8,128)}, f32[2,80,256]{2,1,0:T(8,128)}, u32[]{:S(2)}, u32[]{:S(2)}) collective-permute-start(f32[2,80,256]{2,1,0:T(8,128)} %get-tuple-element.15), channel_id=1, source_target_pairs={{2,0},{4,2},{6,4},{8,6},{10,8},{12,10},{14,12},{3,1},{5,3},{7,5},{... | collective-permute-start | bytes 491528 | tf_op jit(solution)/shard_map/ppermute | solution.py:26
  55.9 5.6 %collective-permute-done.5.from_prev = f32[2,80,256]{2,1,0:T(8,128)} collective-permute-done((f32[2,80,256]{2,1,0:T(8,128)}, f32[2,80,256]{2,1,0:T(8,128)}, u32[]{:S(2)}, u32[]{:S(2)}) %collective-permute-start.5) | collective-permute-done | bytes 163872 | tf_op jit(solution)/shard_map/ppermute | solution.py:26
  61.6 1.2 %collective-permute-done.6.from_next = f32[2,80,256]{2,1,0:T(8,128)} collective-permute-done((f32[2,80,256]{2,1,0:T(8,128)}, f32[2,80,256]{2,1,0:T(8,128)}, u32[]{:S(2)}, u32[]{:S(2)}) %collective-permute-start.6) | collective-permute-done | bytes 163872 | tf_op jit(solution)/shard_map/ppermute | solution.py:26
  62.8 5.8 %shard_map.29 = (f32[32,128,256]{2,1,0:T(8,128)}, f32[8,40,256]{2,1,0:T(8,128)}, f32[2,40,256]{2,1,0:T(8,128)}, f32[2,40,256]{2,1,0:T(8,128)}) custom-call(s32[3]{0:T(128)} %add_convert_fusion.flags, f32[16,80,256]{2,1,0:T(8,128)} %get-tuple-element.13.x_ref, f32[2,80,256]{2,1,0:T(8,128)} %collective-permute-done.5.from_prev, ...), custom_call_target="tpu_custom_call", output_to_operand_aliasing={{0}: (4, {})} | custom-call | tf_op jit(solution)/shard_map/pallas_call | solution.py:202
  68.6 3.8 %collective-permute-start.7 = (f32[2,40,256]{2,1,0:T(8,128)}, f32[2,40,256]{2,1,0:T(8,128)}, u32[]{:S(2)}, u32[]{:S(2)}) collective-permute-start(f32[2,40,256]{2,1,0:T(8,128)} %get-tuple-element.18), channel_id=1, source_target_pairs={{0,2},{2,4},{4,6},{6,8},{8,10},{10,12},{12,14},{1,3},{3,5},{5,7},{... | collective-permute-start | bytes 245768 | tf_op jit(solution)/shard_map/ppermute | solution.py:26
  72.3 1.3 %collective-permute-start.8 = (f32[2,40,256]{2,1,0:T(8,128)}, f32[2,40,256]{2,1,0:T(8,128)}, u32[]{:S(2)}, u32[]{:S(2)}) collective-permute-start(f32[2,40,256]{2,1,0:T(8,128)} %get-tuple-element.19), channel_id=1, source_target_pairs={{2,0},{4,2},{6,4},{8,6},{10,8},{12,10},{14,12},{3,1},{5,3},{7,5},{... | collective-permute-start | bytes 245768 | tf_op jit(solution)/shard_map/ppermute | solution.py:26
  73.6 0.4 collective-permute-done.7.from_prev
  74.1 4.9 %collective-permute-done.8.from_next = f32[2,40,256]{2,1,0:T(8,128)} collective-permute-done((f32[2,40,256]{2,1,0:T(8,128)}, f32[2,40,256]{2,1,0:T(8,128)}, u32[]{:S(2)}, u32[]{:S(2)}) %collective-permute-start.8) | collective-permute-done | bytes 81952 | tf_op jit(solution)/shard_map/ppermute | solution.py:26
  79.0 7.0 %shard_map.30 = f32[224,32,128]{2,1,0:T(8,128)} custom-call(s32[3]{0:T(128)} %add_convert_fusion.flags, f32[8,40,256]{2,1,0:T(8,128)} %get-tuple-element.17.x_ref, f32[2,40,256]{2,1,0:T(8,128)} %collective-permute-done.7.from_prev, f32[2,40,256]{2,1,0:T(8,128)} %collective-permute-done.8.from_next, f32[32,128,256]{2,1,0:T(8,128)} %get-tuple-element.20.prev_out), custom_call_target="tpu_custom_call" | custom-call | tf_op jit(solution)/shard_map/pallas_call | solution.py:292
  (2 shorter events, 0.1 us)
Async XLA Ops:
  1.1 13.2 %copy-start.1 = (f32[224,32,128]{2,1,0:T(8,128)S(1)}, f32[224,32,128]{2,1,0:T(8,128)}, u32[]{:S(2)}) copy-start(f32[224,32,128]{2,1,0:T(8,128)} %param.2) | copy-start | bytes 11010052
  11.6 2.0 %copy-start = (f32[32,128,256]{2,1,0:T(8,128)}, f32[32,128,256]{2,1,0:T(8,128)S(1)}, u32[]{:S(2)}) copy-start(f32[32,128,256]{2,1,0:T(8,128)S(1)} %convolution_bitcast_fusion.own) | copy-start | bytes 12582916
  13.8 24.4 %collective-permute-start = (f32[32,32,256]{2,1,0:T(8,128)S(1)}, f32[32,32,256]{2,1,0:T(8,128)}, u32[]{:S(2)}, u32[]{:S(2)}) collective-permute-start(f32[32,32,256]{2,1,0:T(8,128)S(1)} %slice_select_fusion), channel_id=1, source_target_pairs={{0,1},{1,0},{2,3},{3,2},{4,5},{5,4},{6,7},{7,6},{8,9},{9,8},{10,11... | collective-permute-start | bytes 3145736 | tf_op jit(solution)/shard_map/ppermute | solution.py:212
  17.6 20.0 %collective-permute-start.3 = (f32[2,128,256]{2,1,0:T(8,128)S(1)}, f32[2,128,256]{2,1,0:T(8,128)}, u32[]{:S(2)}, u32[]{:S(2)}) collective-permute-start(f32[2,128,256]{2,1,0:T(8,128)S(1)} %get-tuple-element.27), channel_id=1, source_target_pairs={{2,0},{4,2},{6,4},{8,6},{10,8},{12,10},{14,12},{3,1},{5,3},{7,5},{... | collective-permute-start | bytes 786440 | tf_op jit(solution)/shard_map/ppermute | solution.py:26
  18.9 18.7 %collective-permute-start.1 = (f32[2,128,256]{2,1,0:T(8,128)S(1)}, f32[2,128,256]{2,1,0:T(8,128)}, u32[]{:S(2)}, u32[]{:S(2)}) collective-permute-start(f32[2,128,256]{2,1,0:T(8,128)S(1)} %get-tuple-element.28), channel_id=1, source_target_pairs={{0,2},{2,4},{4,6},{6,8},{8,10},{10,12},{12,14},{1,3},{3,5},{5,7},{... | collective-permute-start | bytes 786440 | tf_op jit(solution)/shard_map/ppermute | solution.py:26
  24.7 6.2 %collective-permute-start.4 = (f32[2,32,256]{2,1,0:T(8,128)S(1)}, f32[2,32,256]{2,1,0:T(8,128)S(1)}, u32[]{:S(2)}, u32[]{:S(2)}) collective-permute-start(f32[2,32,256]{2,1,0:T(8,128)S(1)} %get-tuple-element.25), channel_id=1, source_target_pairs={{2,1},{3,0},{4,3},{5,2},{6,5},{7,4},{8,7},{9,6},{10,9},{11,8},{12,... | collective-permute-start | bytes 196616 | tf_op jit(solution)/shard_map/ppermute | solution.py:223
  26.0 11.6 %collective-permute-start.2 = (f32[2,32,256]{2,1,0:T(8,128)S(1)}, f32[2,32,256]{2,1,0:T(8,128)S(1)}, u32[]{:S(2)}, u32[]{:S(2)}) collective-permute-start(f32[2,32,256]{2,1,0:T(8,128)S(1)} %get-tuple-element.26), channel_id=1, source_target_pairs={{0,3},{1,2},{2,5},{3,4},{4,7},{5,6},{6,9},{7,8},{8,11},{9,10},{10,... | collective-permute-start | bytes 196616 | tf_op jit(solution)/shard_map/ppermute | solution.py:223
  30.9 6.7 %copy-start.2 = (f32[2,32,256]{2,1,0:T(8,128)}, f32[2,32,256]{2,1,0:T(8,128)S(1)}, u32[]{:S(2)}) copy-start(f32[2,32,256]{2,1,0:T(8,128)S(1)} %collective-permute-done.4.next_halo) | copy-start | bytes 196612
  37.6 0.6 copy-start.3
  49.7 11.9 %collective-permute-start.5 = (f32[2,80,256]{2,1,0:T(8,128)}, f32[2,80,256]{2,1,0:T(8,128)}, u32[]{:S(2)}, u32[]{:S(2)}) collective-permute-start(f32[2,80,256]{2,1,0:T(8,128)} %get-tuple-element.14), channel_id=1, source_target_pairs={{0,2},{2,4},{4,6},{6,8},{8,10},{10,12},{12,14},{1,3},{3,5},{5,7},{... | collective-permute-start | bytes 491528 | tf_op jit(solution)/shard_map/ppermute | solution.py:26
  54.7 8.1 %collective-permute-start.6 = (f32[2,80,256]{2,1,0:T(8,128)}, f32[2,80,256]{2,1,0:T(8,128)}, u32[]{:S(2)}, u32[]{:S(2)}) collective-permute-start(f32[2,80,256]{2,1,0:T(8,128)} %get-tuple-element.15), channel_id=1, source_target_pairs={{2,0},{4,2},{6,4},{8,6},{10,8},{12,10},{14,12},{3,1},{5,3},{7,5},{... | collective-permute-start | bytes 491528 | tf_op jit(solution)/shard_map/ppermute | solution.py:26
  68.6 5.5 %collective-permute-start.7 = (f32[2,40,256]{2,1,0:T(8,128)}, f32[2,40,256]{2,1,0:T(8,128)}, u32[]{:S(2)}, u32[]{:S(2)}) collective-permute-start(f32[2,40,256]{2,1,0:T(8,128)} %get-tuple-element.18), channel_id=1, source_target_pairs={{0,2},{2,4},{4,6},{6,8},{8,10},{10,12},{12,14},{1,3},{3,5},{5,7},{... | collective-permute-start | bytes 245768 | tf_op jit(solution)/shard_map/ppermute | solution.py:26
  72.3 6.6 %collective-permute-start.8 = (f32[2,40,256]{2,1,0:T(8,128)}, f32[2,40,256]{2,1,0:T(8,128)}, u32[]{:S(2)}, u32[]{:S(2)}) collective-permute-start(f32[2,40,256]{2,1,0:T(8,128)} %get-tuple-element.19), channel_id=1, source_target_pairs={{2,0},{4,2},{6,4},{8,6},{10,8},{12,10},{14,12},{3,1},{5,3},{7,5},{... | collective-permute-start | bytes 245768 | tf_op jit(solution)/shard_map/ppermute | solution.py:26

commit v9 on v8

--- a/solution.py
+++ b/solution.py
@@ -208,6 +208,32 @@
     )(flags, *arrays)
 
 
+def mix_kernel(w_ref, x_ref, o_ref):
+    w = w_ref[...]
+    for j in range(x_ref.shape[1]):
+        y = jnp.dot(w, x_ref[:, j, :], precision=lax.Precision.HIGHEST,
+                    preferred_element_type=jnp.float32)
+        o_ref[j] = y.T
+
+
+def mix_block(weights, x):
+    c, rows, width = x.shape
+    b = weights.shape[0]
+    vm = pl.BlockSpec(memory_space=pltpu.VMEM)
+    return pl.pallas_call(
+        mix_kernel,
+        out_shape=jax.ShapeDtypeStruct((rows, width, b), jnp.float32),
+        in_specs=[vm, vm],
+        out_specs=vm,
+        cost_estimate=pl.CostEstimate(
+            flops=12 * b * c * rows * width,
+            transcendentals=0,
+            bytes_accessed=4 * (c * rows * width + b * c + b * rows * width),
+        ),
+        compiler_params=pltpu.CompilerParams(vmem_limit_bytes=100 * 1024 * 1024),
+    )(weights, x)
+
+
 def to_core_mate(x):
     return lax.ppermute(x, "cols", [(0, 1), (1, 0)])
 
@@ -251,7 +277,7 @@
     p_halo = diagonal(facing(mixed_next), 1)
     n_halo = diagonal(facing(mixed_prev), -1)
 
-    own = mix(radiance)
+    own = mix_block(weights, radiance)
     halo = to_core_mate(facing(own))
     ext_width = width + HALO
     out_shape = (rows, width, padded_bands)

time: 86.4 us -> 89.9 us (1.041)
  Pallas kernels: 24.3 us -> 36.5 us
  matrix products: 11.5 us -> 1.01 us
  other arithmetic: 0.84 us -> 2.39 us
    pallas_call x0 -> x1, Pallas kernels: none -> 12.2 us  [mix_block(): pl.pallas_call(mix_kernel, out_shape=jax.ShapeDtypeStruct((rows, width, b...]
    dot_general x2 -> x1, matrix products: 11.5 us -> 1.01 us  [mix(): jnp.einsum('crw,bc->rwb', x, weights, precision=lax.Precision.HIGHEST, pr...]
    unnamed x10 -> x6, local copies, waits for them, and re-layouts: 5.77 us -> 0.62 us
    slice x0 -> x1, local copies, waits for them, and re-layouts: none -> 3.82 us  [row(): return lax.slice_in_dim(x, i, i + 1, axis=axis)]
    pad x0 -> x1, local copies, waits for them, and re-layouts: none -> 1.66 us  [on_device(): weights = jnp.pad(decorrelation, ((0, padded_bands - bands), (0, 0)))]
    select_n x2, other arithmetic: 0.2 us -> 1.76 us  [facing(): return jnp.where(on_left, x[:, width - HALO:], x[:, :HALO])]
  transfers between devices with their start and end apart: 9 -> 9, of which waited for: 5 -> 5; matrix products, arithmetic and copies ran while one was open for 4% -> 6% of each run, Pallas kernels for 0% -> 0%
where the time goes in v9:
time: 89.9 us; the launch traced here: 89.5 us
  Pallas kernels  36.5 us (41%)
  starting transfers between devices  24.7 us (27%)
  waiting for transfers between devices  18.7 us (21%)
  local copies, waits for them, and re-layouts  6.13 us (7%)
  other arithmetic  2.39 us (3%)
  matrix products  1.01 us (1%)
    ppermute x6, starting transfers between devices, shifted(): return lax.ppermute(x, axis, pairs)  18.4 us
    pallas_call x2, Pallas kernels, level_call(): pl.pallas_call(kernel, grid_spec=grid_spec, out_shape=tuple((jax.ShapeDty...  17.3 us
    ppermute x6, waiting for transfers between devices, shifted(): return lax.ppermute(x, axis, pairs)  12.2 us
    pallas_call x1, Pallas kernels, mix_block(): pl.pallas_call(mix_kernel, out_shape=jax.ShapeDtypeStruct((rows, width, b...  12.2 us
    pallas_call x1, Pallas kernels, last_call(): pl.pallas_call(functools.partial(last_kernel, stride=stride), grid_spec=g...  7.05 us
    ppermute x2, waiting for transfers between devices, diagonal(): return lax.ppermute(x, ('rows', 'cols'), pairs)  6.53 us
    ppermute x2, starting transfers between devices, diagonal(): return lax.ppermute(x, ('rows', 'cols'), pairs)  5.76 us
    slice x1, local copies, waits for them, and re-layouts, row(): return lax.slice_in_dim(x, i, i + 1, axis=axis)  3.82 us
  transfers between devices with their start and end apart: 9, of which 5 were waited for; matrix products, arithmetic and copies ran while one was open for 6% of the time, Pallas kernels for 0%

profile of v9, /device:TPU:0, one launch (start us, length us, event | category | flops | bytes accessed | tf_op | source)
XLA Modules:
  0.0 89.5 jit_solution(14129675523275769832)
XLA Ops:
  0.0 1.7 %pad.4.w_ref = f32[256,224]{1,0:T(8,128)} pad(f32[224,224]{1,0:T(8,128)} %param.3, f32[]{:T(128)} %constant.15.clone.1), padding=0_32x0_0 | pad | bytes 430084 | tf_op jit(solution)/shard_map/jit(_pad)/pad | solution.py:263
  1.7 12.2 %shard_map.28.own = f32[32,128,256]{2,1,0:T(8,128)} custom-call(f32[256,224]{1,0:T(8,128)} %pad.4.w_ref, f32[224,32,128]{2,1,0:T(8,128)} %x_ref.1), custom_call_target="tpu_custom_call" | custom-call | flops 2818572288 | bytes 8093696 | tf_op jit(solution)/shard_map/pallas_call | solution.py:223
  13.8 0.0 copy-start
  13.8 1.7 %slice_select_fusion = f32[32,32,256]{2,1,0:T(8,128)S(1)} fusion(f32[32,128,256]{2,1,0:T(8,128)} %shard_map.28.own, pred[]{:T(512)} %eq.9), kind=kLoop, calls=%fused_computation | loop fusion | flops 262144 | bytes 3145729 | tf_op jit(solution)/shard_map/jit(_where)/select_n | solution.py:266
  15.6 0.5 collective-permute-start
  16.1 3.8 %fusion.12 = (f32[224,1,128]{2,1,0:T(1,128)S(1)}, f32[224,1,128]{2,1,0:T(1,128)S(1)}, f32[224,1,128]{2,1,0:T(1,128)S(1)}, f32[224,1,128]{2,1,0:T(1,128)S(1)}, f3...) fusion(f32[224,32,128]{2,1,0:T(8,128)} %x_ref.1), kind=kLoop, calls=%fused_computation.19 | loop fusion | bytes 1605632 | tf_op jit(solution)/shard_map/slice | solution.py:34
  19.9 0.1 multiply_add_fusion.2
  20.0 0.0 copy-done
  20.0 1.0 %fusion = f32[4,128,256]{2,1,0:T(8,128)S(1)} fusion(f32[224,1,128]{2,0,1:T(8,128)S(1)} %get-tuple-element.34, f32[224,1,128]{2,0,1:T(8,128)S(1)} %bitcast.14, f32[224,1,128]{2,0,1:T(8,128)S(1)} %get-tuple-element.33, f32[224,1,128]{2,0,1:T(8,128)S(1)} %get-tuple-element.32, f32[224,224]{1,0:T(8,128)S(1)} %copy-done), kind=kOutput, calls=%fused_computation.1 | convolution fusion | flops 352665600 | bytes 1183744 | tf_op jit(solution)/shard_map/crw,bc->rwb/dot_general | solution.py:269
  21.0 1.3 %collective-permute-start.3 = (f32[2,128,256]{2,1,0:T(8,128)S(1)}, f32[2,128,256]{2,1,0:T(8,128)}, u32[]{:S(2)}, u32[]{:S(2)}) collective-permute-start(f32[2,128,256]{2,1,0:T(8,128)S(1)} %get-tuple-element.30), channel_id=1, source_target_pairs={{2,0},{4,2},{6,4},{8,6},{10,8},{12,10},{14,12},{3,1},{5,3},{7,5},{... | collective-permute-start | bytes 786440 | tf_op jit(solution)/shard_map/ppermute | solution.py:26
  22.3 5.8 %collective-permute-start.1 = (f32[2,128,256]{2,1,0:T(8,128)S(1)}, f32[2,128,256]{2,1,0:T(8,128)}, u32[]{:S(2)}, u32[]{:S(2)}) collective-permute-start(f32[2,128,256]{2,1,0:T(8,128)S(1)} %get-tuple-element.31), channel_id=1, source_target_pairs={{0,2},{2,4},{4,6},{6,8},{8,10},{10,12},{12,14},{1,3},{3,5},{5,7},{... | collective-permute-start | bytes 786440 | tf_op jit(solution)/shard_map/ppermute | solution.py:26
  28.1 1.3 %collective-permute-start.4 = (f32[2,32,256]{2,1,0:T(8,128)S(1)}, f32[2,32,256]{2,1,0:T(8,128)S(1)}, u32[]{:S(2)}, u32[]{:S(2)}) collective-permute-start(f32[2,32,256]{2,1,0:T(8,128)S(1)} %get-tuple-element.28), channel_id=1, source_target_pairs={{2,1},{3,0},{4,3},{5,2},{6,5},{7,4},{8,7},{9,6},{10,9},{11,8},{12,... | collective-permute-start | bytes 196616 | tf_op jit(solution)/shard_map/ppermute | solution.py:249
  29.4 4.5 %collective-permute-start.2 = (f32[2,32,256]{2,1,0:T(8,128)S(1)}, f32[2,32,256]{2,1,0:T(8,128)S(1)}, u32[]{:S(2)}, u32[]{:S(2)}) collective-permute-start(f32[2,32,256]{2,1,0:T(8,128)S(1)} %get-tuple-element.29), channel_id=1, source_target_pairs={{0,3},{1,2},{2,5},{3,4},{4,7},{5,6},{6,9},{7,8},{8,11},{9,10},{10,... | collective-permute-start | bytes 196616 | tf_op jit(solution)/shard_map/ppermute | solution.py:249
  33.9 0.6 add_convert_fusion.flags
  34.5 0.0 collective-permute-done.4.next_halo
  34.5 0.0 copy-start.1
  34.5 6.5 %collective-permute-done.2.prev_halo = f32[2,32,256]{2,1,0:T(8,128)S(1)} collective-permute-done((f32[2,32,256]{2,1,0:T(8,128)S(1)}, f32[2,32,256]{2,1,0:T(8,128)S(1)}, u32[]{:S(2)}, u32[]{:S(2)}) %collective-permute-start.2) | collective-permute-done | bytes 65568 | tf_op jit(solution)/shard_map/ppermute | solution.py:249
  41.0 0.0 copy-start.2
  41.0 0.0 collective-permute-done.3.next_own
  41.0 0.0 collective-permute-done.1.prev_own
  41.0 0.0 copy-done.1
  41.0 0.6 copy-done.2
  41.7 0.0 collective-permute-done.halo
  41.7 11.5 %shard_map.29 = (f32[32,128,256]{2,1,0:T(8,128)}, f32[16,80,256]{2,1,0:T(8,128)}, f32[2,80,256]{2,1,0:T(8,128)}, f32[2,80,256]{2,1,0:T(8,128)}) custom-call(s32[3]{0:T(128)} %add_convert_fusion.flags, f32[32,128,256]{2,1,0:T(8,128)} %shard_map.28.own, f32[32,32,256]{2,1,0:T(8,128)} %collective-permute-done.halo, ...), custom_call_target="tpu_custom_call" | custom-call | tf_op jit(solution)/shard_map/pallas_call | solution.py:202
  53.1 5.0 %collective-permute-start.5 = (f32[2,80,256]{2,1,0:T(8,128)}, f32[2,80,256]{2,1,0:T(8,128)}, u32[]{:S(2)}, u32[]{:S(2)}) collective-permute-start(f32[2,80,256]{2,1,0:T(8,128)} %get-tuple-element.14), channel_id=1, source_target_pairs={{0,2},{2,4},{4,6},{6,8},{8,10},{10,12},{12,14},{1,3},{3,5},{5,7},{... | collective-permute-start | bytes 491528 | tf_op jit(solution)/shard_map/ppermute | solution.py:26
  58.1 1.3 %collective-permute-start.6 = (f32[2,80,256]{2,1,0:T(8,128)}, f32[2,80,256]{2,1,0:T(8,128)}, u32[]{:S(2)}, u32[]{:S(2)}) collective-permute-start(f32[2,80,256]{2,1,0:T(8,128)} %get-tuple-element.15), channel_id=1, source_target_pairs={{2,0},{4,2},{6,4},{8,6},{10,8},{12,10},{14,12},{3,1},{5,3},{7,5},{... | collective-permute-start | bytes 491528 | tf_op jit(solution)/shard_map/ppermute | solution.py:26
  59.4 5.6 %collective-permute-done.5.from_prev = f32[2,80,256]{2,1,0:T(8,128)} collective-permute-done((f32[2,80,256]{2,1,0:T(8,128)}, f32[2,80,256]{2,1,0:T(8,128)}, u32[]{:S(2)}, u32[]{:S(2)}) %collective-permute-start.5) | collective-permute-done | bytes 163872 | tf_op jit(solution)/shard_map/ppermute | solution.py:26
  65.0 1.2 %collective-permute-done.6.from_next = f32[2,80,256]{2,1,0:T(8,128)} collective-permute-done((f32[2,80,256]{2,1,0:T(8,128)}, f32[2,80,256]{2,1,0:T(8,128)}, u32[]{:S(2)}, u32[]{:S(2)}) %collective-permute-start.6) | collective-permute-done | bytes 163872 | tf_op jit(solution)/shard_map/ppermute | solution.py:26
  66.3 5.8 %shard_map.30 = (f32[32,128,256]{2,1,0:T(8,128)}, f32[8,40,256]{2,1,0:T(8,128)}, f32[2,40,256]{2,1,0:T(8,128)}, f32[2,40,256]{2,1,0:T(8,128)}) custom-call(s32[3]{0:T(128)} %add_convert_fusion.flags, f32[16,80,256]{2,1,0:T(8,128)} %get-tuple-element.13.x_ref, f32[2,80,256]{2,1,0:T(8,128)} %collective-permute-done.5.from_prev, ...), custom_call_target="tpu_custom_call", output_to_operand_aliasing={{0}: (4, {})} | custom-call | tf_op jit(solution)/shard_map/pallas_call | solution.py:202
  72.0 3.8 %collective-permute-start.7 = (f32[2,40,256]{2,1,0:T(8,128)}, f32[2,40,256]{2,1,0:T(8,128)}, u32[]{:S(2)}, u32[]{:S(2)}) collective-permute-start(f32[2,40,256]{2,1,0:T(8,128)} %get-tuple-element.18), channel_id=1, source_target_pairs={{0,2},{2,4},{4,6},{6,8},{8,10},{10,12},{12,14},{1,3},{3,5},{5,7},{... | collective-permute-start | bytes 245768 | tf_op jit(solution)/shard_map/ppermute | solution.py:26
  75.8 1.3 %collective-permute-start.8 = (f32[2,40,256]{2,1,0:T(8,128)}, f32[2,40,256]{2,1,0:T(8,128)}, u32[]{:S(2)}, u32[]{:S(2)}) collective-permute-start(f32[2,40,256]{2,1,0:T(8,128)} %get-tuple-element.19), channel_id=1, source_target_pairs={{2,0},{4,2},{6,4},{8,6},{10,8},{12,10},{14,12},{3,1},{5,3},{7,5},{... | collective-permute-start | bytes 245768 | tf_op jit(solution)/shard_map/ppermute | solution.py:26
  77.1 0.4 collective-permute-done.7.from_prev
  77.5 4.9 %collective-permute-done.8.from_next = f32[2,40,256]{2,1,0:T(8,128)} collective-permute-done((f32[2,40,256]{2,1,0:T(8,128)}, f32[2,40,256]{2,1,0:T(8,128)}, u32[]{:S(2)}, u32[]{:S(2)}) %collective-permute-start.8) | collective-permute-done | bytes 81952 | tf_op jit(solution)/shard_map/ppermute | solution.py:26
  82.4 7.0 %shard_map.31 = f32[224,32,128]{2,1,0:T(8,128)} custom-call(s32[3]{0:T(128)} %add_convert_fusion.flags, f32[8,40,256]{2,1,0:T(8,128)} %get-tuple-element.17.x_ref, f32[2,40,256]{2,1,0:T(8,128)} %collective-permute-done.7.from_prev, f32[2,40,256]{2,1,0:T(8,128)} %collective-permute-done.8.from_next, f32[32,128,256]{2,1,0:T(8,128)} %get-tuple-element.20.prev_out), custom_call_target="tpu_custom_call" | custom-call | tf_op jit(solution)/shard_map/pallas_call | solution.py:318
  (2 shorter events, 0.1 us)
Async XLA Ops:
  13.8 6.2 %copy-start = (f32[224,224]{1,0:T(8,128)S(1)}, f32[224,224]{1,0:T(8,128)}, u32[]{:S(2)}) copy-start(f32[224,224]{1,0:T(8,128)} %param.3) | copy-start | bytes 602116
  15.6 26.1 %collective-permute-start = (f32[32,32,256]{2,1,0:T(8,128)S(1)}, f32[32,32,256]{2,1,0:T(8,128)}, u32[]{:S(2)}, u32[]{:S(2)}) collective-permute-start(f32[32,32,256]{2,1,0:T(8,128)S(1)} %slice_select_fusion), channel_id=1, source_target_pairs={{0,1},{1,0},{2,3},{3,2},{4,5},{5,4},{6,7},{7,6},{8,9},{9,8},{10,11... | collective-permute-start | bytes 3145736 | tf_op jit(solution)/shard_map/ppermute | solution.py:238
  21.0 20.0 %collective-permute-start.3 = (f32[2,128,256]{2,1,0:T(8,128)S(1)}, f32[2,128,256]{2,1,0:T(8,128)}, u32[]{:S(2)}, u32[]{:S(2)}) collective-permute-start(f32[2,128,256]{2,1,0:T(8,128)S(1)} %get-tuple-element.30), channel_id=1, source_target_pairs={{2,0},{4,2},{6,4},{8,6},{10,8},{12,10},{14,12},{3,1},{5,3},{7,5},{... | collective-permute-start | bytes 786440 | tf_op jit(solution)/shard_map/ppermute | solution.py:26
  22.3 18.7 %collective-permute-start.1 = (f32[2,128,256]{2,1,0:T(8,128)S(1)}, f32[2,128,256]{2,1,0:T(8,128)}, u32[]{:S(2)}, u32[]{:S(2)}) collective-permute-start(f32[2,128,256]{2,1,0:T(8,128)S(1)} %get-tuple-element.31), channel_id=1, source_target_pairs={{0,2},{2,4},{4,6},{6,8},{8,10},{10,12},{12,14},{1,3},{3,5},{5,7},{... | collective-permute-start | bytes 786440 | tf_op jit(solution)/shard_map/ppermute | solution.py:26
  28.1 6.4 %collective-permute-start.4 = (f32[2,32,256]{2,1,0:T(8,128)S(1)}, f32[2,32,256]{2,1,0:T(8,128)S(1)}, u32[]{:S(2)}, u32[]{:S(2)}) collective-permute-start(f32[2,32,256]{2,1,0:T(8,128)S(1)} %get-tuple-element.28), channel_id=1, source_target_pairs={{2,1},{3,0},{4,3},{5,2},{6,5},{7,4},{8,7},{9,6},{10,9},{11,8},{12,... | collective-permute-start | bytes 196616 | tf_op jit(solution)/shard_map/ppermute | solution.py:249
  29.4 11.6 %collective-permute-start.2 = (f32[2,32,256]{2,1,0:T(8,128)S(1)}, f32[2,32,256]{2,1,0:T(8,128)S(1)}, u32[]{:S(2)}, u32[]{:S(2)}) collective-permute-start(f32[2,32,256]{2,1,0:T(8,128)S(1)} %get-tuple-element.29), channel_id=1, source_target_pairs={{0,3},{1,2},{2,5},{3,4},{4,7},{5,6},{6,9},{7,8},{8,11},{9,10},{10,... | collective-permute-start | bytes 196616 | tf_op jit(solution)/shard_map/ppermute | solution.py:249
  34.5 6.5 %copy-start.1 = (f32[2,32,256]{2,1,0:T(8,128)}, f32[2,32,256]{2,1,0:T(8,128)S(1)}, u32[]{:S(2)}) copy-start(f32[2,32,256]{2,1,0:T(8,128)S(1)} %collective-permute-done.4.next_halo) | copy-start | bytes 196612
  41.0 0.6 copy-start.2
  53.1 11.9 %collective-permute-start.5 = (f32[2,80,256]{2,1,0:T(8,128)}, f32[2,80,256]{2,1,0:T(8,128)}, u32[]{:S(2)}, u32[]{:S(2)}) collective-permute-start(f32[2,80,256]{2,1,0:T(8,128)} %get-tuple-element.14), channel_id=1, source_target_pairs={{0,2},{2,4},{4,6},{6,8},{8,10},{10,12},{12,14},{1,3},{3,5},{5,7},{... | collective-permute-start | bytes 491528 | tf_op jit(solution)/shard_map/ppermute | solution.py:26
  58.1 8.1 %collective-permute-start.6 = (f32[2,80,256]{2,1,0:T(8,128)}, f32[2,80,256]{2,1,0:T(8,128)}, u32[]{:S(2)}, u32[]{:S(2)}) collective-permute-start(f32[2,80,256]{2,1,0:T(8,128)} %get-tuple-element.15), channel_id=1, source_target_pairs={{2,0},{4,2},{6,4},{8,6},{10,8},{12,10},{14,12},{3,1},{5,3},{7,5},{... | collective-permute-start | bytes 491528 | tf_op jit(solution)/shard_map/ppermute | solution.py:26
  72.0 5.5 %collective-permute-start.7 = (f32[2,40,256]{2,1,0:T(8,128)}, f32[2,40,256]{2,1,0:T(8,128)}, u32[]{:S(2)}, u32[]{:S(2)}) collective-permute-start(f32[2,40,256]{2,1,0:T(8,128)} %get-tuple-element.18), channel_id=1, source_target_pairs={{0,2},{2,4},{4,6},{6,8},{8,10},{10,12},{12,14},{1,3},{3,5},{5,7},{... | collective-permute-start | bytes 245768 | tf_op jit(solution)/shard_map/ppermute | solution.py:26
  75.8 6.6 %collective-permute-start.8 = (f32[2,40,256]{2,1,0:T(8,128)}, f32[2,40,256]{2,1,0:T(8,128)}, u32[]{:S(2)}, u32[]{:S(2)}) collective-permute-start(f32[2,40,256]{2,1,0:T(8,128)} %get-tuple-element.19), channel_id=1, source_target_pairs={{2,0},{4,2},{6,4},{8,6},{10,8},{12,10},{14,12},{3,1},{5,3},{7,5},{... | collective-permute-start | bytes 245768 | tf_op jit(solution)/shard_map/ppermute | solution.py:26

commit v10 on v8

--- a/solution.py
+++ b/solution.py
@@ -1,5 +1,6 @@
 import functools
 
+import numpy as np
 import jax
 import jax.numpy as jnp
 from jax import lax
@@ -208,6 +209,70 @@
     )(flags, *arrays)
 
 
+def np_partials(x):
+    a1, b1 = alpha_one, beta_one
+    n = x.shape[0]
+    s_pen, d_pen, s_last, d_last = x[n - 4], x[n - 3], x[n - 2], x[n - 1]
+    to_next = np.stack([s_last + b1 * (d_pen + a1 * (s_pen + s_last)), d_last + a1 * s_last])
+    to_prev = np.stack([x[0], x[1] + a1 * (x[0] + x[2])])
+    return to_next, to_prev
+
+
+def np_lift(v, axis):
+    a1, b1, a2, b2 = alpha_one, beta_one, alpha_two, beta_two
+    v = np.moveaxis(v, axis, 0)
+    s, d = v[0::2].copy(), v[1::2].copy()
+
+    def nxt(u):
+        return np.concatenate([u[1:], u[-1:]])
+
+    def prv(u):
+        return np.concatenate([u[:1], u[:-1]])
+
+    d = d + a1 * (s + nxt(s))
+    s = s + b1 * (prv(d) + d)
+    d = d + a2 * (s + nxt(s))
+    s = s + b2 * (prv(d) + d)
+    return np.moveaxis(s / scale_k, 0, axis), np.moveaxis(d * scale_k, 0, axis)
+
+
+def np_ll(level, from_prev, from_next):
+    a1 = alpha_one
+    b, a = from_prev
+    s, dp = from_next
+    z = np.zeros_like(b)
+    ext = np.concatenate([np.stack([z, -a1 * b, b, a - a1 * b]), level,
+                          np.stack([s, dp - a1 * s, z, z])])
+    rows_s, _ = np_lift(ext, 0)
+    lo = EDGE // 2
+    rows_s = rows_s[lo : lo + level.shape[0] // 2]
+    ll, _ = np_lift(rows_s, 1)
+    return ll
+
+
+@functools.lru_cache(maxsize=None)
+def next_level_maps(rows, width):
+    zero_edge = np.zeros((2, width))
+    own = np.zeros((rows, width, 4, width // 2))
+    for r in range(rows):
+        for w in range(width):
+            unit = np.zeros((rows, width))
+            unit[r, w] = 1.0
+            ll = np_ll(unit, zero_edge, zero_edge)
+            tn, tp = np_partials(ll)
+            own[r, w] = np.concatenate([tn, tp])
+    from_below = np.zeros((2, width, 2, width // 2))
+    from_above = np.zeros((2, width, 2, width // 2))
+    zero = np.zeros((rows, width))
+    for p in range(2):
+        for w in range(width):
+            unit = np.zeros((2, width))
+            unit[p, w] = 1.0
+            from_below[p, w] = np_partials(np_ll(zero, zero_edge, unit))[0]
+            from_above[p, w] = np_partials(np_ll(zero, unit, zero_edge))[1]
+    return tuple(m.astype(np.float32) for m in (own, from_below, from_above))
+
+
 def to_core_mate(x):
     return lax.ppermute(x, "cols", [(0, 1), (1, 0)])
 
@@ -259,16 +324,25 @@
         first_kernel, flags,
         [own, halo, p_own, p_halo, n_own, n_halo],
         out_shape, rows, ext_width, {})
-    for lvl in range(1, LEVELS - 1):
-        from_prev = shifted(tn, "rows", 1)
-        from_next = shifted(tp, "rows", -1)
-        r, w = level.shape[0], level.shape[1]
-        out, level, tn, tp = level_call(
-            functools.partial(next_kernel, stride=2**lvl), flags,
-            [level, from_prev, from_next, out], out_shape, r, w, {4: 0})
-    from_prev = shifted(tn, "rows", 1)
-    from_next = shifted(tp, "rows", -1)
-    return last_call(flags, [level, from_prev, from_next, out], bands, 2 ** (LEVELS - 1))
+    assert LEVELS == 3
+    r, w = level.shape[0], level.shape[1]
+    own_map, below_map, above_map = next_level_maps(r, w)
+
+    def apply(x, m):
+        return jnp.einsum("rwb,rwqv->qvb", x, m, precision=lax.Precision.HIGHEST,
+                          preferred_element_type=jnp.float32)
+
+    ahead = apply(level, own_map)
+    send_next = jnp.concatenate([tn, ahead[:2]], axis=1)
+    send_prev = jnp.concatenate([tp, ahead[2:]], axis=1)
+    got_prev = shifted(send_next, "rows", 1)
+    got_next = shifted(send_prev, "rows", -1)
+    from_prev3 = got_prev[:, w:] + apply(tp, below_map)
+    from_next3 = got_next[:, w:] + apply(tn, above_map)
+    out, level, tn, tp = level_call(
+        functools.partial(next_kernel, stride=2), flags,
+        [level, got_prev[:, :w], got_next[:, :w], out], out_shape, r, w, {4: 0})
+    return last_call(flags, [level, from_prev3, from_next3, out], bands, 4)
 
 
 def last_call(flags, arrays, bands, stride):

time: 86.4 us -> 88.6 us (1.025)
  matrix products: 11.5 us -> 18.4 us
  starting transfers between devices: 24.5 us -> 18.8 us
  local copies, waits for them, and re-layouts: 5.81 us -> 8.64 us
  waiting for transfers between devices: 18.9 us -> 16.1 us
  other arithmetic: 0.84 us -> 1.8 us
    dot_general x0 -> x3, matrix products: none -> 6.9 us  [apply(): jnp.einsum('rwb,rwqv->qvb', x, m, precision=lax.Precision.HIGHEST, prefer...]
    ppermute x6 -> x4, starting transfers between devices: 18.4 us -> 12.7 us  [shifted(): return lax.ppermute(x, axis, pairs)]
    ppermute x6 -> x4, waiting for transfers between devices: 12.2 us -> 9.4 us  [shifted(): return lax.ppermute(x, axis, pairs)]
    unnamed x10 -> x16, local copies, waits for them, and re-layouts: 5.77 us -> 7.22 us
    slice x0 -> x3, local copies, waits for them, and re-layouts: none -> 1.38 us  [the longest x1 0.7 us: on_device(): got_next[:, :w]]
    concatenate x0 -> x2, other arithmetic: none -> 0.96 us  [the longest x1 0.94 us: on_device(): send_next = jnp.concatenate([tn, ahead[:2]], axis=1)]
  transfers between devices with their start and end apart: 9 -> 7, of which waited for: 5 -> 2; matrix products, arithmetic and copies ran while one was open for 4% -> 5% of each run, Pallas kernels for 0% -> 0%
where the time goes in v10:
time: 88.6 us; the launch traced here: 88.2 us
  Pallas kernels  24.3 us (27%)
  starting transfers between devices  18.8 us (21%)
  matrix products  18.4 us (21%)
  waiting for transfers between devices  16.1 us (18%)
  local copies, waits for them, and re-layouts  8.64 us (10%)
  other arithmetic  1.8 us (2%)
    pallas_call x2, Pallas kernels, level_call(): pl.pallas_call(kernel, grid_spec=grid_spec, out_shape=tuple((jax.ShapeDty...  17.3 us
    ppermute x4, starting transfers between devices, shifted(): return lax.ppermute(x, axis, pairs)  12.7 us
    dot_general x2, matrix products, mix(): jnp.einsum('crw,bc->rwb', x, weights, precision=lax.Precision.HIGHEST, pr...  11.5 us
    ppermute x4, waiting for transfers between devices, shifted(): return lax.ppermute(x, axis, pairs)  9.4 us
    unnamed x16, local copies, waits for them, and re-layouts  7.22 us
    pallas_call x1, Pallas kernels, last_call(): pl.pallas_call(functools.partial(last_kernel, stride=stride), grid_spec=g...  7.04 us
    dot_general x3, matrix products, apply(): jnp.einsum('rwb,rwqv->qvb', x, m, precision=lax.Precision.HIGHEST, prefer...  6.9 us
    ppermute x2, waiting for transfers between devices, diagonal(): return lax.ppermute(x, ('rows', 'cols'), pairs)  6.67 us
  transfers between devices with their start and end apart: 7, of which 2 were waited for; matrix products, arithmetic and copies ran while one was open for 5% of the time, Pallas kernels for 0%

profile of v10, /device:TPU:0, one launch (start us, length us, event | category | flops | bytes accessed | tf_op | source)
XLA Modules:
  0.0 88.2 jit_solution(10762664401624817841)
XLA Ops:
  0.0 1.1 %copy.7 = f32[224,224]{0,1:T(8,128)S(1)} copy(f32[224,224]{1,0:T(8,128)} %param.6) | data formatting | bytes 401408 | tf_op args[1]
  1.1 0.0 copy-start.1
  1.1 10.5 %convolution_bitcast_fusion.own = f32[32,128,256]{2,1,0:T(8,128)S(1)} fusion(f32[224,224]{0,1:T(8,128)S(1)} %copy.7, f32[224,32,128]{2,1,0:T(8,128)} %param.5), kind=kOutput, calls=%fused_computation | convolution fusion | flops 2818572288 | bytes 8065024 | tf_op jit(solution)/shard_map/crw,bc->rwb/dot_general | solution.py:308
  11.6 0.0 copy-start
  11.6 2.0 %copy-done = f32[32,128,256]{2,1,0:T(8,128)} copy-done((f32[32,128,256]{2,1,0:T(8,128)}, f32[32,128,256]{2,1,0:T(8,128)S(1)}, u32[]{:S(2)}) %copy-start) | copy-done | bytes 4194328
  13.6 0.1 slice_select_fusion
  13.7 0.5 collective-permute-start
  14.2 0.0 copy-done.1
  14.3 2.1 %copy.8 = f32[224,32,128]{2,0,1:T(8,128)S(1)} copy(f32[224,32,128]{2,1,0:T(8,128)S(1)} %copy-done.1) | data formatting | bytes 7340032 | tf_op args[0]
  16.4 0.1 fusion.24
  16.4 1.0 %fusion.5 = f32[4,128,256]{2,1,0:T(8,128)S(1)} fusion(f32[224,1,128]{2,0,1:T(8,128)S(1)} %get-tuple-element.18, f32[224,1,128]{2,0,1:T(8,128)S(1)} %get-tuple-element.19, f32[224,1,128]{2,0,1:T(8,128)S(1)} %get-tuple-element.20, f32[224,1,128]{2,0,1:T(8,128)S(1)} %get-tuple-element.17, f32[224,224]{0,1:T(8,128)S(1)} %copy.7), kind=kOutput, calls=%fused_computation.7 | convolution fusion | flops 352665600 | bytes 1183744 | tf_op jit(solution)/shard_map/crw,bc->rwb/dot_general | solution.py:308
  17.5 1.3 %collective-permute-start.3 = (f32[2,128,256]{2,1,0:T(8,128)S(1)}, f32[2,128,256]{2,1,0:T(8,128)}, u32[]{:S(2)}, u32[]{:S(2)}) collective-permute-start(f32[2,128,256]{2,1,0:T(8,128)S(1)} %get-tuple-element.23), channel_id=1, source_target_pairs={{2,0},{4,2},{6,4},{8,6},{10,8},{12,10},{14,12},{3,1},{5,3},{7,5},{... | collective-permute-start | bytes 786440 | tf_op jit(solution)/shard_map/ppermute | solution.py:27
  18.8 5.8 %collective-permute-start.1 = (f32[2,128,256]{2,1,0:T(8,128)S(1)}, f32[2,128,256]{2,1,0:T(8,128)}, u32[]{:S(2)}, u32[]{:S(2)}) collective-permute-start(f32[2,128,256]{2,1,0:T(8,128)S(1)} %get-tuple-element.24), channel_id=1, source_target_pairs={{0,2},{2,4},{4,6},{6,8},{8,10},{10,12},{12,14},{1,3},{3,5},{5,7},{... | collective-permute-start | bytes 786440 | tf_op jit(solution)/shard_map/ppermute | solution.py:27
  24.6 1.3 %collective-permute-start.4 = (f32[2,32,256]{2,1,0:T(8,128)S(1)}, f32[2,32,256]{2,1,0:T(8,128)S(1)}, u32[]{:S(2)}, u32[]{:S(2)}) collective-permute-start(f32[2,32,256]{2,1,0:T(8,128)S(1)} %get-tuple-element.21), channel_id=1, source_target_pairs={{2,1},{3,0},{4,3},{5,2},{6,5},{7,4},{8,7},{9,6},{10,9},{11,8},{12,... | collective-permute-start | bytes 196616 | tf_op jit(solution)/shard_map/ppermute | solution.py:288
  25.9 4.3 %collective-permute-start.2 = (f32[2,32,256]{2,1,0:T(8,128)S(1)}, f32[2,32,256]{2,1,0:T(8,128)S(1)}, u32[]{:S(2)}, u32[]{:S(2)}) collective-permute-start(f32[2,32,256]{2,1,0:T(8,128)S(1)} %get-tuple-element.22), channel_id=1, source_target_pairs={{0,3},{1,2},{2,5},{3,4},{4,7},{5,6},{6,9},{7,8},{8,11},{9,10},{10,... | collective-permute-start | bytes 196616 | tf_op jit(solution)/shard_map/ppermute | solution.py:288
  30.2 0.6 add_convert_fusion.flags
  30.8 0.0 collective-permute-done.4.next_halo
  30.8 0.0 copy-start.5
  30.9 6.7 %collective-permute-done.2.prev_halo = f32[2,32,256]{2,1,0:T(8,128)S(1)} collective-permute-done((f32[2,32,256]{2,1,0:T(8,128)S(1)}, f32[2,32,256]{2,1,0:T(8,128)S(1)}, u32[]{:S(2)}, u32[]{:S(2)}) %collective-permute-start.2) | collective-permute-done | bytes 65568 | tf_op jit(solution)/shard_map/ppermute | solution.py:288
  37.5 0.0 copy-start.6
  37.5 0.0 collective-permute-done.3.next_own
  37.5 0.0 collective-permute-done.1.prev_own
  37.5 0.0 copy-done.5
  37.5 0.6 copy-done.6
  38.1 0.0 collective-permute-done.halo
  38.1 11.5 %shard_map.55 = (f32[32,128,256]{2,1,0:T(8,128)}, f32[16,80,256]{2,1,0:T(8,128)}, f32[2,80,256]{2,1,0:T(8,128)}, f32[2,80,256]{2,1,0:T(8,128)}) custom-call(s32[3]{0:T(128)} %add_convert_fusion.flags, f32[32,128,256]{2,1,0:T(8,128)} %copy-done, f32[32,32,256]{2,1,0:T(8,128)} %collective-permute-done.halo, f32[2,128,256]{2,1,0:T(8,128)} %collective-permute-done.1.prev_own, ...), custom_call_target="tpu_custom_call" | custom-call | tf_op jit(solution)/shard_map/pallas_call | solution.py:203
  49.6 0.0 copy-start.2
  49.6 3.1 %fusion.2 = f32[4,40,256]{2,1,0:T(8,128)S(1)} fusion(f32[16,80,4,40]{1,3,0,2:T(8,128)} %constant.24.clone, f32[16,80,256]{2,1,0:T(8,128)} %get-tuple-element.11.x_ref), kind=kOutput, calls=%fused_computation.3 | convolution fusion | flops 629145600 | bytes 2293760 | tf_op jit(solution)/shard_map/rwb,rwqv->qvb/dot_general | solution.py:332
  52.7 0.9 %pad_maximum_fusion = f32[2,120,256]{2,1,0:T(8,128)S(1)} fusion(f32[2,40,256]{2,1,0:T(8,128)S(1)} %get-tuple-element.26, f32[2,80,256]{2,1,0:T(8,128)} %get-tuple-element.12), kind=kLoop, calls=%fused_computation.15 | loop fusion | flops 61440 | bytes 491520 | tf_op jit(solution)/shard_map/concatenate | solution.py:336
  53.7 4.3 %collective-permute-start.5 = (f32[2,120,256]{2,1,0:T(8,128)S(1)}, f32[2,120,256]{2,1,0:T(8,128)S(1)}, u32[]{:S(2)}, u32[]{:S(2)}) collective-permute-start(f32[2,120,256]{2,1,0:T(8,128)S(1)} %pad_maximum_fusion), channel_id=1, source_target_pairs={{0,2},{2,4},{4,6},{6,8},{8,10},{10,12},{12,14},{1,3},{3,5},{5,7},{... | collective-permute-start | bytes 737288 | tf_op jit(solution)/shard_map/ppermute | solution.py:27
  58.0 0.0 copy-done.2
  58.0 1.3 %collective-permute-start.6 = (f32[2,120,256]{2,1,0:T(8,128)S(1)}, f32[2,120,256]{2,1,0:T(8,128)S(1)}, u32[]{:S(2)}, u32[]{:S(2)}) collective-permute-start(f32[2,120,256]{2,1,0:T(8,128)S(1)} %pad_maximum_fusion.1), channel_id=1, source_target_pairs={{2,0},{4,2},{6,4},{8,6},{10,8},{12,10},{14,12},{3,1},{5,3},{7,5},{... | collective-permute-start | bytes 737288 | tf_op jit(solution)/shard_map/ppermute | solution.py:27
  59.3 9.4 %collective-permute-done.5 = f32[2,120,256]{2,1,0:T(8,128)S(1)} collective-permute-done((f32[2,120,256]{2,1,0:T(8,128)S(1)}, f32[2,120,256]{2,1,0:T(8,128)S(1)}, u32[]{:S(2)}, u32[]{:S(2)}) %collective-permute-start.5) | collective-permute-done | bytes 245792 | tf_op jit(solution)/shard_map/ppermute | solution.py:27
  68.7 0.0 copy-start.3
  68.7 0.7 copy-done.3
  69.4 0.7 slice.104.from_prev
  70.1 0.0 collective-permute-done.6
  70.1 0.0 copy-start.4
  70.1 0.7 copy-done.4
  70.8 0.7 slice.106.from_next
  71.5 5.8 %shard_map.56 = (f32[32,128,256]{2,1,0:T(8,128)}, f32[8,40,256]{2,1,0:T(8,128)}, f32[2,40,256]{2,1,0:T(8,128)}, f32[2,40,256]{2,1,0:T(8,128)}) custom-call(s32[3]{0:T(128)} %add_convert_fusion.flags, f32[16,80,256]{2,1,0:T(8,128)} %get-tuple-element.11.x_ref, f32[2,80,256]{2,1,0:T(8,128)} %slice.104.from_prev, ...), custom_call_target="tpu_custom_call", output_to_operand_aliasing={{0}: (4, {})} | custom-call | tf_op jit(solution)/shard_map/pallas_call | solution.py:203
  77.4 1.9 %slice_add_fusion.4.from_prev = f32[2,40,256]{2,1,0:T(8,128)} fusion(f32[2,120,256]{2,1,0:T(8,128)} %copy-done.3, f32[2,80,2,40]{1,3,0,2:T(8,128)} %constant.25.clone, f32[2,80,256]{2,1,0:T(8,128)} %get-tuple-element.13), kind=kOutput, calls=%fused_computation.33 | convolution fusion | flops 39342080 | bytes 378880 | tf_op jit(solution)/shard_map/rwb,rwqv->qvb/dot_general | solution.py:332
  79.3 1.9 %slice_add_fusion.3.from_next = f32[2,40,256]{2,1,0:T(8,128)} fusion(f32[2,120,256]{2,1,0:T(8,128)} %copy-done.4, f32[2,80,2,40]{1,3,0,2:T(8,128)} %constant.26.clone, f32[2,80,256]{2,1,0:T(8,128)} %get-tuple-element.12), kind=kOutput, calls=%fused_computation.32 | convolution fusion | flops 39342080 | bytes 378880 | tf_op jit(solution)/shard_map/rwb,rwqv->qvb/dot_general | solution.py:332
  81.2 7.0 %shard_map.57 = f32[224,32,128]{2,1,0:T(8,128)} custom-call(s32[3]{0:T(128)} %add_convert_fusion.flags, f32[8,40,256]{2,1,0:T(8,128)} %get-tuple-element.15.x_ref, f32[2,40,256]{2,1,0:T(8,128)} %slice_add_fusion.4.from_prev, f32[2,40,256]{2,1,0:T(8,128)} %slice_add_fusion.3.from_next, f32[32,128,256]{2,1,0:T(8,128)} %get-tuple-element.16.prev_out), custom_call_target="tpu_custom_call" | custom-call | tf_op jit(solution)/shard_map/pallas_call | solution.py:366
  (4 shorter events, 0.1 us)
Async XLA Ops:
  1.1 13.2 %copy-start.1 = (f32[224,32,128]{2,1,0:T(8,128)S(1)}, f32[224,32,128]{2,1,0:T(8,128)}, u32[]{:S(2)}) copy-start(f32[224,32,128]{2,1,0:T(8,128)} %param.5) | copy-start | bytes 11010052
  11.6 2.0 %copy-start = (f32[32,128,256]{2,1,0:T(8,128)}, f32[32,128,256]{2,1,0:T(8,128)S(1)}, u32[]{:S(2)}) copy-start(f32[32,128,256]{2,1,0:T(8,128)S(1)} %convolution_bitcast_fusion.own) | copy-start | bytes 12582916
  13.7 24.4 %collective-permute-start = (f32[32,32,256]{2,1,0:T(8,128)S(1)}, f32[32,32,256]{2,1,0:T(8,128)}, u32[]{:S(2)}, u32[]{:S(2)}) collective-permute-start(f32[32,32,256]{2,1,0:T(8,128)S(1)} %slice_select_fusion), channel_id=1, source_target_pairs={{0,1},{1,0},{2,3},{3,2},{4,5},{5,4},{6,7},{7,6},{8,9},{9,8},{10,11... | collective-permute-start | bytes 3145736 | tf_op jit(solution)/shard_map/ppermute | solution.py:277
  17.5 20.0 %collective-permute-start.3 = (f32[2,128,256]{2,1,0:T(8,128)S(1)}, f32[2,128,256]{2,1,0:T(8,128)}, u32[]{:S(2)}, u32[]{:S(2)}) collective-permute-start(f32[2,128,256]{2,1,0:T(8,128)S(1)} %get-tuple-element.23), channel_id=1, source_target_pairs={{2,0},{4,2},{6,4},{8,6},{10,8},{12,10},{14,12},{3,1},{5,3},{7,5},{... | collective-permute-start | bytes 786440 | tf_op jit(solution)/shard_map/ppermute | solution.py:27
  18.8 18.7 %collective-permute-start.1 = (f32[2,128,256]{2,1,0:T(8,128)S(1)}, f32[2,128,256]{2,1,0:T(8,128)}, u32[]{:S(2)}, u32[]{:S(2)}) collective-permute-start(f32[2,128,256]{2,1,0:T(8,128)S(1)} %get-tuple-element.24), channel_id=1, source_target_pairs={{0,2},{2,4},{4,6},{6,8},{8,10},{10,12},{12,14},{1,3},{3,5},{5,7},{... | collective-permute-start | bytes 786440 | tf_op jit(solution)/shard_map/ppermute | solution.py:27
  24.6 6.2 %collective-permute-start.4 = (f32[2,32,256]{2,1,0:T(8,128)S(1)}, f32[2,32,256]{2,1,0:T(8,128)S(1)}, u32[]{:S(2)}, u32[]{:S(2)}) collective-permute-start(f32[2,32,256]{2,1,0:T(8,128)S(1)} %get-tuple-element.21), channel_id=1, source_target_pairs={{2,1},{3,0},{4,3},{5,2},{6,5},{7,4},{8,7},{9,6},{10,9},{11,8},{12,... | collective-permute-start | bytes 196616 | tf_op jit(solution)/shard_map/ppermute | solution.py:288
  25.9 11.6 %collective-permute-start.2 = (f32[2,32,256]{2,1,0:T(8,128)S(1)}, f32[2,32,256]{2,1,0:T(8,128)S(1)}, u32[]{:S(2)}, u32[]{:S(2)}) collective-permute-start(f32[2,32,256]{2,1,0:T(8,128)S(1)} %get-tuple-element.22), channel_id=1, source_target_pairs={{0,3},{1,2},{2,5},{3,4},{4,7},{5,6},{6,9},{7,8},{8,11},{9,10},{10,... | collective-permute-start | bytes 196616 | tf_op jit(solution)/shard_map/ppermute | solution.py:288
  30.8 6.7 %copy-start.5 = (f32[2,32,256]{2,1,0:T(8,128)}, f32[2,32,256]{2,1,0:T(8,128)S(1)}, u32[]{:S(2)}) copy-start(f32[2,32,256]{2,1,0:T(8,128)S(1)} %collective-permute-done.4.next_halo) | copy-start | bytes 196612
  37.5 0.6 copy-start.6
  49.6 8.4 %copy-start.2 = (f32[2,80,256]{2,1,0:T(8,128)S(1)}, f32[2,80,256]{2,1,0:T(8,128)}, u32[]{:S(2)}) copy-start(f32[2,80,256]{2,1,0:T(8,128)} %get-tuple-element.13) | copy-start | bytes 491524
  53.7 15.1 %collective-permute-start.5 = (f32[2,120,256]{2,1,0:T(8,128)S(1)}, f32[2,120,256]{2,1,0:T(8,128)S(1)}, u32[]{:S(2)}, u32[]{:S(2)}) collective-permute-start(f32[2,120,256]{2,1,0:T(8,128)S(1)} %pad_maximum_fusion), channel_id=1, source_target_pairs={{0,2},{2,4},{4,6},{6,8},{8,10},{10,12},{12,14},{1,3},{3,5},{5,7},{... | collective-permute-start | bytes 737288 | tf_op jit(solution)/shard_map/ppermute | solution.py:27
  58.0 12.1 %collective-permute-start.6 = (f32[2,120,256]{2,1,0:T(8,128)S(1)}, f32[2,120,256]{2,1,0:T(8,128)S(1)}, u32[]{:S(2)}, u32[]{:S(2)}) collective-permute-start(f32[2,120,256]{2,1,0:T(8,128)S(1)} %pad_maximum_fusion.1), channel_id=1, source_target_pairs={{2,0},{4,2},{6,4},{8,6},{10,8},{12,10},{14,12},{3,1},{5,3},{7,5},{... | collective-permute-start | bytes 737288 | tf_op jit(solution)/shard_map/ppermute | solution.py:27
  68.7 0.7 copy-start.3
  70.1 0.7 copy-start.4

commit v11 on v10

--- a/solution.py
+++ b/solution.py
@@ -73,7 +73,8 @@
         ext[base : base + EDGE] = jnp.concatenate([s, dp - a1 * s, z, z], axis=0)
 
 
-def lift_block(flags, ext, half, out_ref, ll_ref, tn_ref, tp_ref, rows, width, stride):
+def lift_block(flags, ext, half, out_ref, ll_ref, tn_ref, tp_ref, rows, width, stride,
+               ahead_map=None):
     hr, hw = rows // 2, width // 2
     a1, b1, a2, b2 = alpha_one, beta_one, alpha_two, beta_two
     n = hr + EDGE
@@ -133,11 +134,22 @@
         if pr == 0:
             ll_ref[...] = e
             to_next, to_prev = partials(e, 0)
-            tn_ref[...] = to_next
-            tp_ref[...] = to_prev
-
-
-def first_kernel(flags, own, halo, prev_own, prev_halo, next_own, next_halo,
+            if ahead_map is None:
+                tn_ref[...] = to_next
+                tp_ref[...] = to_prev
+            else:
+                quarter = hw // 2
+                ahead = jnp.dot(ahead_map[...], e.reshape(hr * hw, LANES),
+                                precision=lax.Precision.HIGHEST,
+                                preferred_element_type=jnp.float32)
+                ahead = ahead.reshape(4, quarter, LANES)
+                tn_ref[:, :hw] = to_next
+                tn_ref[:, hw:] = ahead[:2]
+                tp_ref[:, :hw] = to_prev
+                tp_ref[:, hw:] = ahead[2:]
+
+
+def first_kernel(flags, own, halo, prev_own, prev_halo, next_own, next_halo, ahead_map,
                  out_ref, ll_ref, tn_ref, tp_ref, ext, half):
     rows, h = own.shape[0], halo.shape[1]
     width = own.shape[1] + h
@@ -158,7 +170,7 @@
                          jnp.concatenate([hh[...], o[...]], axis=1))
 
     fill_rows(ext, flags, joined(prev_own, prev_halo), joined(next_own, next_halo), rows)
-    lift_block(flags, ext, half, out_ref, ll_ref, tn_ref, tp_ref, rows, width, 1)
+    lift_block(flags, ext, half, out_ref, ll_ref, tn_ref, tp_ref, rows, width, 1, ahead_map)
 
 
 def next_kernel(flags, x_ref, from_prev, from_next, prev_out,
@@ -166,16 +178,25 @@
     rows, width = x_ref.shape[0], x_ref.shape[1]
     out_ref[...] = prev_out[...]
     ext[EDGE : EDGE + rows] = x_ref[...]
-    fill_rows(ext, flags, from_prev[...], from_next[...], rows)
+    fill_rows(ext, flags, from_prev[:, :width], from_next[:, :width], rows)
     lift_block(flags, ext, half, out_ref, ll_ref, tn_ref, tp_ref, rows, width, stride)
 
 
-def last_kernel(flags, x_ref, from_prev, from_next, prev_out,
-                final_ref, ext, half, full, ll, tn, tp, *, stride):
+def last_kernel(flags, x_ref, got_prev, got_next, sent_next, sent_prev, below_map, above_map,
+                prev_out, final_ref, ext, half, full, ll, tn, tp, *, stride):
     rows, width = x_ref.shape[0], x_ref.shape[1]
+    wide = 2 * width
+
+    def share(m, sent):
+        part = jnp.dot(m[...], sent[:, :wide].reshape(2 * wide, LANES),
+                       precision=lax.Precision.HIGHEST, preferred_element_type=jnp.float32)
+        return part.reshape(2, width, LANES)
+
     full[...] = prev_out[...]
     ext[EDGE : EDGE + rows] = x_ref[...]
-    fill_rows(ext, flags, from_prev[...], from_next[...], rows)
+    from_prev = got_prev[:, wide:] + share(below_map, sent_prev)
+    from_next = got_next[:, wide:] + share(above_map, sent_next)
+    fill_rows(ext, flags, from_prev, from_next, rows)
     lift_block(flags, ext, half, full, ll, tn, tp, rows, width, stride)
     for r in range(full.shape[0]):
         final_ref[:, r, :] = full[r].T
@@ -185,15 +206,19 @@
     return pl.BlockSpec(shape[:-1] + (LANES,), lambda h, f: (0,) * (len(shape) - 1) + (h,))
 
 
-def level_call(kernel, flags, arrays, out_shape, rows, width, aliases):
+def whole(a):
+    return pl.BlockSpec(a.shape, lambda h, f: (0,) * a.ndim)
+
+
+def level_call(kernel, flags, arrays, out_shape, rows, width, aliases, consts=(), ahead=False):
     bands = arrays[0].shape[-1]
     ll_shape = (rows // 2, width // 2, bands)
-    edge_shape = (2, width // 2, bands)
+    edge_shape = (2, width // 2 + (width // 4 if ahead else 0), bands)
     outs = (out_shape, ll_shape, edge_shape, edge_shape)
     grid_spec = pltpu.PrefetchScalarGridSpec(
         num_scalar_prefetch=1,
         grid=(bands // LANES,),
-        in_specs=[spec(a.shape) for a in arrays],
+        in_specs=[spec(a.shape) for a in arrays] + [whole(c) for c in consts],
         out_specs=tuple(spec(o) for o in outs),
         scratch_shapes=[
             pltpu.VMEM((rows + 2 * EDGE, width, LANES), jnp.float32),
@@ -206,7 +231,7 @@
         out_shape=tuple(jax.ShapeDtypeStruct(o, jnp.float32) for o in outs),
         input_output_aliases=aliases,
         compiler_params=pltpu.CompilerParams(vmem_limit_bytes=100 * 1024 * 1024),
-    )(flags, *arrays)
+    )(flags, *arrays, *consts)
 
 
 def np_partials(x):
@@ -320,39 +345,35 @@
     halo = to_core_mate(facing(own))
     ext_width = width + HALO
     out_shape = (rows, width, padded_bands)
+    assert LEVELS == 3
+    own_map, below_map, above_map = next_level_maps(rows // 2, ext_width // 2)
+    ahead_map = jnp.asarray(own_map.reshape(-1, own_map.shape[2] * own_map.shape[3]).T)
     out, level, tn, tp = level_call(
         first_kernel, flags,
         [own, halo, p_own, p_halo, n_own, n_halo],
-        out_shape, rows, ext_width, {})
-    assert LEVELS == 3
+        out_shape, rows, ext_width, {}, consts=(ahead_map,), ahead=True)
     r, w = level.shape[0], level.shape[1]
-    own_map, below_map, above_map = next_level_maps(r, w)
-
-    def apply(x, m):
-        return jnp.einsum("rwb,rwqv->qvb", x, m, precision=lax.Precision.HIGHEST,
-                          preferred_element_type=jnp.float32)
-
-    ahead = apply(level, own_map)
-    send_next = jnp.concatenate([tn, ahead[:2]], axis=1)
-    send_prev = jnp.concatenate([tp, ahead[2:]], axis=1)
-    got_prev = shifted(send_next, "rows", 1)
-    got_next = shifted(send_prev, "rows", -1)
-    from_prev3 = got_prev[:, w:] + apply(tp, below_map)
-    from_next3 = got_next[:, w:] + apply(tn, above_map)
+    got_prev = shifted(tn, "rows", 1)
+    got_next = shifted(tp, "rows", -1)
+    sent_next, sent_prev = tn, tp
     out, level, tn, tp = level_call(
         functools.partial(next_kernel, stride=2), flags,
-        [level, got_prev[:, :w], got_next[:, :w], out], out_shape, r, w, {4: 0})
-    return last_call(flags, [level, from_prev3, from_next3, out], bands, 4)
-
-
-def last_call(flags, arrays, bands, stride):
-    level, out = arrays[0], arrays[3]
+        [level, got_prev, got_next, out], out_shape, r, w, {4: 0})
+    below = jnp.asarray(below_map.reshape(-1, below_map.shape[2] * below_map.shape[3]).T)
+    above = jnp.asarray(above_map.reshape(-1, above_map.shape[2] * above_map.shape[3]).T)
+    return last_call(flags, [level, got_prev, got_next, sent_next, sent_prev, out],
+                     (below, above), bands, 4)
+
+
+def last_call(flags, arrays, consts, bands, stride):
+    level, out = arrays[0], arrays[-1]
+    arrays = arrays[:-1]
     rows, width = level.shape[0], level.shape[1]
     final_shape = (bands, out.shape[0], out.shape[1])
     grid_spec = pltpu.PrefetchScalarGridSpec(
         num_scalar_prefetch=1,
         grid=(out.shape[-1] // LANES,),
-        in_specs=[spec(a.shape) for a in arrays],
+        in_specs=[spec(a.shape) for a in arrays] + [whole(c) for c in consts] + [spec(out.shape)],
         out_specs=pl.BlockSpec((LANES,) + final_shape[1:], lambda h, f: (h, 0, 0)),
         scratch_shapes=[
             pltpu.VMEM((rows + 2 * EDGE, width, LANES), jnp.float32),
@@ -368,7 +389,7 @@
         grid_spec=grid_spec,
         out_shape=jax.ShapeDtypeStruct(final_shape, jnp.float32),
         compiler_params=pltpu.CompilerParams(vmem_limit_bytes=100 * 1024 * 1024),
-    )(flags, *arrays)
+    )(flags, *arrays, *consts, out)
 
 
 def solution(mesh):

time: 88.6 us -> 81.9 us (0.924)
  matrix products: 18.4 us -> 11.5 us
  Pallas kernels: 24.3 us -> 27.2 us
  local copies, waits for them, and re-layouts: 8.64 us -> 6.66 us
  other arithmetic: 1.8 us -> 0.81 us
  starting transfers between devices: 18.8 us -> 19.7 us
    dot_general x3 -> x0, matrix products: 6.9 us -> none  [apply(): jnp.einsum('rwb,rwqv->qvb', x, m, precision=lax.Precision.HIGHEST, prefer...]
    pallas_call x2, Pallas kernels: 17.3 us -> 19.4 us  [level_call(): pl.pallas_call(kernel, grid_spec=grid_spec, out_shape=tuple((jax.ShapeDty...]
    slice x3 -> x0, local copies, waits for them, and re-layouts: 1.38 us -> none  [the longest x1 0.7 us: on_device(): got_next[:, :w]]
    concatenate x2 -> x0, other arithmetic: 0.96 us -> none  [the longest x1 0.94 us: on_device(): send_next = jnp.concatenate([tn, ahead[:2]], axis=1)]
    unnamed x16 -> x14, local copies, waits for them, and re-layouts: 7.22 us -> 6.62 us
where the time goes in v11:
time: 81.9 us; the launch traced here: 81.6 us
  Pallas kernels  27.2 us (33%)
  starting transfers between devices  19.7 us (24%)
  waiting for transfers between devices  15.6 us (19%)
  matrix products  11.5 us (14%)
  local copies, waits for them, and re-layouts  6.66 us (8%)
    pallas_call x2, Pallas kernels, level_call(): pl.pallas_call(kernel, grid_spec=grid_spec, out_shape=tuple((jax.ShapeDty...  19.4 us
    ppermute x4, starting transfers between devices, shifted(): return lax.ppermute(x, axis, pairs)  12.9 us
    dot_general x2, matrix products, mix(): jnp.einsum('crw,bc->rwb', x, weights, precision=lax.Precision.HIGHEST, pr...  11.5 us
    ppermute x4, waiting for transfers between devices, shifted(): return lax.ppermute(x, axis, pairs)  9.06 us
    pallas_call x1, Pallas kernels, last_call(): pl.pallas_call(functools.partial(last_kernel, stride=stride), grid_spec=g...  7.82 us
    unnamed x14, local copies, waits for them, and re-layouts  6.62 us
    ppermute x2, waiting for transfers between devices, diagonal(): return lax.ppermute(x, ('rows', 'cols'), pairs)  6.52 us
    ppermute x2, starting transfers between devices, diagonal(): return lax.ppermute(x, ('rows', 'cols'), pairs)  6.26 us
  transfers between devices with their start and end apart: 7, of which 2 were waited for; matrix products, arithmetic and copies ran while one was open for 5% of the time, Pallas kernels for 0%

profile of v11, /device:TPU:0, one launch (start us, length us, event | category | flops | bytes accessed | tf_op | source)
XLA Modules:
  0.0 81.6 jit_solution(661020579057653440)
XLA Ops:
  0.0 1.1 %copy.7 = f32[224,224]{0,1:T(8,128)S(1)} copy(f32[224,224]{1,0:T(8,128)} %param.6) | data formatting | bytes 401408 | tf_op args[1]
  1.1 0.0 copy-start.1
  1.1 10.5 %convolution_bitcast_fusion.own = f32[32,128,256]{2,1,0:T(8,128)S(1)} fusion(f32[224,224]{0,1:T(8,128)S(1)} %copy.7, f32[224,32,128]{2,1,0:T(8,128)} %param.5), kind=kOutput, calls=%fused_computation | convolution fusion | flops 2818572288 | bytes 8065024 | tf_op jit(solution)/shard_map/crw,bc->rwb/dot_general | solution.py:333
  11.6 0.0 copy-start
  11.6 2.0 %copy-done = f32[32,128,256]{2,1,0:T(8,128)} copy-done((f32[32,128,256]{2,1,0:T(8,128)}, f32[32,128,256]{2,1,0:T(8,128)S(1)}, u32[]{:S(2)}) %copy-start) | copy-done | bytes 4194328
  13.6 0.1 slice_select_fusion
  13.7 0.5 collective-permute-start
  14.2 0.0 copy-done.1
  14.2 2.1 %copy.8 = f32[224,32,128]{2,0,1:T(8,128)S(1)} copy(f32[224,32,128]{2,1,0:T(8,128)S(1)} %copy-done.1) | data formatting | bytes 7340032 | tf_op args[0]
  16.4 0.1 fusion.17
  16.4 1.0 %fusion = f32[4,128,256]{2,1,0:T(8,128)S(1)} fusion(f32[224,1,128]{2,0,1:T(8,128)S(1)} %get-tuple-element.18, f32[224,1,128]{2,0,1:T(8,128)S(1)} %get-tuple-element.19, f32[224,1,128]{2,0,1:T(8,128)S(1)} %get-tuple-element.20, f32[224,1,128]{2,0,1:T(8,128)S(1)} %get-tuple-element.17, f32[224,224]{0,1:T(8,128)S(1)} %copy.7), kind=kOutput, calls=%fused_computation.2 | convolution fusion | flops 352665600 | bytes 1183744 | tf_op jit(solution)/shard_map/crw,bc->rwb/dot_general | solution.py:333
  17.5 1.3 %collective-permute-start.3 = (f32[2,128,256]{2,1,0:T(8,128)S(1)}, f32[2,128,256]{2,1,0:T(8,128)S(1)}, u32[]{:S(2)}, u32[]{:S(2)}) collective-permute-start(f32[2,128,256]{2,1,0:T(8,128)S(1)} %get-tuple-element.23), channel_id=1, source_target_pairs={{2,0},{4,2},{6,4},{8,6},{10,8},{12,10},{14,12},{3,1},{5,3},{7,5},{... | collective-permute-start | bytes 786440 | tf_op jit(solution)/shard_map/ppermute | solution.py:27
  18.8 5.3 %collective-permute-start.1 = (f32[2,128,256]{2,1,0:T(8,128)S(1)}, f32[2,128,256]{2,1,0:T(8,128)S(1)}, u32[]{:S(2)}, u32[]{:S(2)}) collective-permute-start(f32[2,128,256]{2,1,0:T(8,128)S(1)} %get-tuple-element.24), channel_id=1, source_target_pairs={{0,2},{2,4},{4,6},{6,8},{8,10},{10,12},{12,14},{1,3},{3,5},{5,7},{... | collective-permute-start | bytes 786440 | tf_op jit(solution)/shard_map/ppermute | solution.py:27
  24.1 1.3 %collective-permute-start.4 = (f32[2,32,256]{2,1,0:T(8,128)S(1)}, f32[2,32,256]{2,1,0:T(8,128)S(1)}, u32[]{:S(2)}, u32[]{:S(2)}) collective-permute-start(f32[2,32,256]{2,1,0:T(8,128)S(1)} %get-tuple-element.21), channel_id=1, source_target_pairs={{2,1},{3,0},{4,3},{5,2},{6,5},{7,4},{8,7},{9,6},{10,9},{11,8},{12,... | collective-permute-start | bytes 196616 | tf_op jit(solution)/shard_map/ppermute | solution.py:313
  25.4 5.0 %collective-permute-start.2 = (f32[2,32,256]{2,1,0:T(8,128)S(1)}, f32[2,32,256]{2,1,0:T(8,128)S(1)}, u32[]{:S(2)}, u32[]{:S(2)}) collective-permute-start(f32[2,32,256]{2,1,0:T(8,128)S(1)} %get-tuple-element.22), channel_id=1, source_target_pairs={{0,3},{1,2},{2,5},{3,4},{4,7},{5,6},{6,9},{7,8},{8,11},{9,10},{10,... | collective-permute-start | bytes 196616 | tf_op jit(solution)/shard_map/ppermute | solution.py:313
  30.4 0.6 add_convert_fusion.flags
  31.0 0.0 collective-permute-done.4.next_halo
  31.0 0.0 copy-start.4
  31.0 6.5 %collective-permute-done.2.prev_halo = f32[2,32,256]{2,1,0:T(8,128)S(1)} collective-permute-done((f32[2,32,256]{2,1,0:T(8,128)S(1)}, f32[2,32,256]{2,1,0:T(8,128)S(1)}, u32[]{:S(2)}, u32[]{:S(2)}) %collective-permute-start.2) | collective-permute-done | bytes 65568 | tf_op jit(solution)/shard_map/ppermute | solution.py:313
  37.5 0.0 copy-start.5
  37.5 0.0 collective-permute-done.3.next_own
  37.5 0.0 copy-start.2
  37.5 0.0 collective-permute-done.1.prev_own
  37.5 0.0 copy-done.4
  37.5 0.6 copy-done.5
  38.1 0.2 copy-done.2
  38.3 0.0 copy-start.3
  38.3 0.7 copy-done.3
  39.0 0.0 collective-permute-done.halo
  39.0 13.6 %shard_map.55 = (f32[32,128,256]{2,1,0:T(8,128)}, f32[16,80,256]{2,1,0:T(8,128)}, f32[2,120,256]{2,1,0:T(8,128)}, f32[2,120,256]{2,1,0:T(8,128)}) custom-call(s32[3]{0:T(128)} %add_convert_fusion.flags, f32[32,128,256]{2,1,0:T(8,128)} %copy-done, f32[32,32,256]{2,1,0:T(8,128)} %collective-permute-done.halo, f32[2,128,256]{2,1,0:T(8,128)} %copy-done.3, ...), custom_call_target="tpu_custom_call" | custom-call | tf_op jit(solution)/shard_map/pallas_call | solution.py:228
  52.6 5.0 %collective-permute-start.5 = (f32[2,120,256]{2,1,0:T(8,128)}, f32[2,120,256]{2,1,0:T(8,128)}, u32[]{:S(2)}, u32[]{:S(2)}) collective-permute-start(f32[2,120,256]{2,1,0:T(8,128)} %get-tuple-element.12.sent_next), channel_id=1, source_target_pairs={{0,2},{2,4},{4,6},{6,8},{8,10},{10,12},{12,14},{1,3},{3,5},{5,7},{... | collective-permute-start | bytes 737288 | tf_op jit(solution)/shard_map/ppermute | solution.py:27
  57.6 1.3 %collective-permute-start.6 = (f32[2,120,256]{2,1,0:T(8,128)}, f32[2,120,256]{2,1,0:T(8,128)}, u32[]{:S(2)}, u32[]{:S(2)}) collective-permute-start(f32[2,120,256]{2,1,0:T(8,128)} %get-tuple-element.13.sent_prev), channel_id=1, source_target_pairs={{2,0},{4,2},{6,4},{8,6},{10,8},{12,10},{14,12},{3,1},{5,3},{7,5},{... | collective-permute-start | bytes 737288 | tf_op jit(solution)/shard_map/ppermute | solution.py:27
  58.9 9.1 %collective-permute-done.5.from_prev.got_prev = f32[2,120,256]{2,1,0:T(8,128)} collective-permute-done((f32[2,120,256]{2,1,0:T(8,128)}, f32[2,120,256]{2,1,0:T(8,128)}, u32[]{:S(2)}, u32[]{:S(2)}) %collective-permute-start.5) | collective-permute-done | bytes 245792 | tf_op jit(solution)/shard_map/ppermute | solution.py:27
  67.9 0.0 collective-permute-done.6.from_next.got_next
  67.9 5.8 %shard_map.56 = (f32[32,128,256]{2,1,0:T(8,128)}, f32[8,40,256]{2,1,0:T(8,128)}, f32[2,40,256]{2,1,0:T(8,128)}, f32[2,40,256]{2,1,0:T(8,128)}) custom-call(s32[3]{0:T(128)} %add_convert_fusion.flags, f32[16,80,256]{2,1,0:T(8,128)} %get-tuple-element.11.x_ref, ...), custom_call_target="tpu_custom_call", output_to_operand_aliasing={{0}: (4, {})} | custom-call | tf_op jit(solution)/shard_map/pallas_call | solution.py:228
  73.8 7.8 %shard_map.57 = f32[224,32,128]{2,1,0:T(8,128)} custom-call(s32[3]{0:T(128)} %add_convert_fusion.flags, f32[8,40,256]{2,1,0:T(8,128)} %get-tuple-element.15.x_ref, f32[2,120,256]{2,1,0:T(8,128)} %collective-permute-done.5.from_prev.got_prev, f32[2,120,256]{2,1,0:T(8,128)} %collective-permute-done.6.from_next.got_next, ...), custom_call_target="tpu_custom_call" | custom-call | tf_op jit(solution)/shard_map/pallas_call | solution.py:387
  (2 shorter events, 0.1 us)
Async XLA Ops:
  1.1 13.2 %copy-start.1 = (f32[224,32,128]{2,1,0:T(8,128)S(1)}, f32[224,32,128]{2,1,0:T(8,128)}, u32[]{:S(2)}) copy-start(f32[224,32,128]{2,1,0:T(8,128)} %param.5) | copy-start | bytes 11010052
  11.6 2.0 %copy-start = (f32[32,128,256]{2,1,0:T(8,128)}, f32[32,128,256]{2,1,0:T(8,128)S(1)}, u32[]{:S(2)}) copy-start(f32[32,128,256]{2,1,0:T(8,128)S(1)} %convolution_bitcast_fusion.own) | copy-start | bytes 12582916
  13.7 25.3 %collective-permute-start = (f32[32,32,256]{2,1,0:T(8,128)S(1)}, f32[32,32,256]{2,1,0:T(8,128)}, u32[]{:S(2)}, u32[]{:S(2)}) collective-permute-start(f32[32,32,256]{2,1,0:T(8,128)S(1)} %slice_select_fusion), channel_id=1, source_target_pairs={{0,1},{1,0},{2,3},{3,2},{4,5},{5,4},{6,7},{7,6},{8,9},{9,8},{10,11... | collective-permute-start | bytes 3145736 | tf_op jit(solution)/shard_map/ppermute | solution.py:302
  17.5 20.0 %collective-permute-start.3 = (f32[2,128,256]{2,1,0:T(8,128)S(1)}, f32[2,128,256]{2,1,0:T(8,128)S(1)}, u32[]{:S(2)}, u32[]{:S(2)}) collective-permute-start(f32[2,128,256]{2,1,0:T(8,128)S(1)} %get-tuple-element.23), channel_id=1, source_target_pairs={{2,0},{4,2},{6,4},{8,6},{10,8},{12,10},{14,12},{3,1},{5,3},{7,5},{... | collective-permute-start | bytes 786440 | tf_op jit(solution)/shard_map/ppermute | solution.py:27
  18.8 18.7 %collective-permute-start.1 = (f32[2,128,256]{2,1,0:T(8,128)S(1)}, f32[2,128,256]{2,1,0:T(8,128)S(1)}, u32[]{:S(2)}, u32[]{:S(2)}) collective-permute-start(f32[2,128,256]{2,1,0:T(8,128)S(1)} %get-tuple-element.24), channel_id=1, source_target_pairs={{0,2},{2,4},{4,6},{6,8},{8,10},{10,12},{12,14},{1,3},{3,5},{5,7},{... | collective-permute-start | bytes 786440 | tf_op jit(solution)/shard_map/ppermute | solution.py:27
  24.1 6.9 %collective-permute-start.4 = (f32[2,32,256]{2,1,0:T(8,128)S(1)}, f32[2,32,256]{2,1,0:T(8,128)S(1)}, u32[]{:S(2)}, u32[]{:S(2)}) collective-permute-start(f32[2,32,256]{2,1,0:T(8,128)S(1)} %get-tuple-element.21), channel_id=1, source_target_pairs={{2,1},{3,0},{4,3},{5,2},{6,5},{7,4},{8,7},{9,6},{10,9},{11,8},{12,... | collective-permute-start | bytes 196616 | tf_op jit(solution)/shard_map/ppermute | solution.py:313
  25.4 12.1 %collective-permute-start.2 = (f32[2,32,256]{2,1,0:T(8,128)S(1)}, f32[2,32,256]{2,1,0:T(8,128)S(1)}, u32[]{:S(2)}, u32[]{:S(2)}) collective-permute-start(f32[2,32,256]{2,1,0:T(8,128)S(1)} %get-tuple-element.22), channel_id=1, source_target_pairs={{0,3},{1,2},{2,5},{3,4},{4,7},{5,6},{6,9},{7,8},{8,11},{9,10},{10,... | collective-permute-start | bytes 196616 | tf_op jit(solution)/shard_map/ppermute | solution.py:313
  31.0 6.5 %copy-start.4 = (f32[2,32,256]{2,1,0:T(8,128)}, f32[2,32,256]{2,1,0:T(8,128)S(1)}, u32[]{:S(2)}) copy-start(f32[2,32,256]{2,1,0:T(8,128)S(1)} %collective-permute-done.4.next_halo) | copy-start | bytes 196612
  37.5 0.6 copy-start.5
  37.5 0.8 copy-start.2
  38.3 0.7 copy-start.3
  52.6 15.4 %collective-permute-start.5 = (f32[2,120,256]{2,1,0:T(8,128)}, f32[2,120,256]{2,1,0:T(8,128)}, u32[]{:S(2)}, u32[]{:S(2)}) collective-permute-start(f32[2,120,256]{2,1,0:T(8,128)} %get-tuple-element.12.sent_next), channel_id=1, source_target_pairs={{0,2},{2,4},{4,6},{6,8},{8,10},{10,12},{12,14},{1,3},{3,5},{5,7},{... | collective-permute-start | bytes 737288 | tf_op jit(solution)/shard_map/ppermute | solution.py:27
  57.6 10.3 %collective-permute-start.6 = (f32[2,120,256]{2,1,0:T(8,128)}, f32[2,120,256]{2,1,0:T(8,128)}, u32[]{:S(2)}, u32[]{:S(2)}) collective-permute-start(f32[2,120,256]{2,1,0:T(8,128)} %get-tuple-element.13.sent_prev), channel_id=1, source_target_pairs={{2,0},{4,2},{6,4},{8,6},{10,8},{12,10},{14,12},{3,1},{5,3},{7,5},{... | collective-permute-start | bytes 737288 | tf_op jit(solution)/shard_map/ppermute | solution.py:27

commit v12 on v11

--- a/solution.py
+++ b/solution.py
@@ -173,17 +173,16 @@
     lift_block(flags, ext, half, out_ref, ll_ref, tn_ref, tp_ref, rows, width, 1, ahead_map)
 
 
-def next_kernel(flags, x_ref, from_prev, from_next, prev_out,
+def next_kernel(flags, x_ref, from_prev, from_next,
                 out_ref, ll_ref, tn_ref, tp_ref, ext, half, *, stride):
     rows, width = x_ref.shape[0], x_ref.shape[1]
-    out_ref[...] = prev_out[...]
     ext[EDGE : EDGE + rows] = x_ref[...]
     fill_rows(ext, flags, from_prev[:, :width], from_next[:, :width], rows)
     lift_block(flags, ext, half, out_ref, ll_ref, tn_ref, tp_ref, rows, width, stride)
 
 
 def last_kernel(flags, x_ref, got_prev, got_next, sent_next, sent_prev, below_map, above_map,
-                prev_out, final_ref, ext, half, full, ll, tn, tp, *, stride):
+                prev_out, middle, final_ref, ext, half, full, ll, tn, tp, *, stride):
     rows, width = x_ref.shape[0], x_ref.shape[1]
     wide = 2 * width
 
@@ -193,6 +192,8 @@
         return part.reshape(2, width, LANES)
 
     full[...] = prev_out[...]
+    mr, mw = middle.shape[0], middle.shape[1]
+    full[pl.ds(0, mr, stride=2), pl.ds(0, mw, stride=2), :] = middle[...]
     ext[EDGE : EDGE + rows] = x_ref[...]
     from_prev = got_prev[:, wide:] + share(below_map, sent_prev)
     from_next = got_next[:, wide:] + share(above_map, sent_next)
@@ -356,24 +357,25 @@
     got_prev = shifted(tn, "rows", 1)
     got_next = shifted(tp, "rows", -1)
     sent_next, sent_prev = tn, tp
-    out, level, tn, tp = level_call(
-        functools.partial(next_kernel, stride=2), flags,
-        [level, got_prev, got_next, out], out_shape, r, w, {4: 0})
+    middle, level, tn, tp = level_call(
+        functools.partial(next_kernel, stride=1), flags,
+        [level, got_prev, got_next], (rows // 2, width // 2, padded_bands), r, w, {})
     below = jnp.asarray(below_map.reshape(-1, below_map.shape[2] * below_map.shape[3]).T)
     above = jnp.asarray(above_map.reshape(-1, above_map.shape[2] * above_map.shape[3]).T)
-    return last_call(flags, [level, got_prev, got_next, sent_next, sent_prev, out],
+    return last_call(flags, [level, got_prev, got_next, sent_next, sent_prev, out, middle],
                      (below, above), bands, 4)
 
 
 def last_call(flags, arrays, consts, bands, stride):
-    level, out = arrays[0], arrays[-1]
-    arrays = arrays[:-1]
+    level, out, middle = arrays[0], arrays[-2], arrays[-1]
+    arrays = arrays[:-2]
     rows, width = level.shape[0], level.shape[1]
     final_shape = (bands, out.shape[0], out.shape[1])
     grid_spec = pltpu.PrefetchScalarGridSpec(
         num_scalar_prefetch=1,
         grid=(out.shape[-1] // LANES,),
-        in_specs=[spec(a.shape) for a in arrays] + [whole(c) for c in consts] + [spec(out.shape)],
+        in_specs=[spec(a.shape) for a in arrays] + [whole(c) for c in consts]
+        + [spec(out.shape), spec(middle.shape)],
         out_specs=pl.BlockSpec((LANES,) + final_shape[1:], lambda h, f: (h, 0, 0)),
         scratch_shapes=[
             pltpu.VMEM((rows + 2 * EDGE, width, LANES), jnp.float32),
@@ -389,7 +391,7 @@
         grid_spec=grid_spec,
         out_shape=jax.ShapeDtypeStruct(final_shape, jnp.float32),
         compiler_params=pltpu.CompilerParams(vmem_limit_bytes=100 * 1024 * 1024),
-    )(flags, *arrays, *consts, out)
+    )(flags, *arrays, *consts, out, middle)
 
 
 def solution(mesh):

time: 81.9 us -> 81.1 us (level)
    pallas_call x2, Pallas kernels: 19.4 us -> 17.8 us  [level_call(): pl.pallas_call(kernel, grid_spec=grid_spec, out_shape=tuple((jax.ShapeDty...]
where the time goes in v12:
time: 81.1 us; the launch traced here: 80.8 us
  Pallas kernels  26.4 us (33%)
  starting transfers between devices  19.6 us (24%)
  waiting for transfers between devices  15.6 us (19%)
  matrix products  11.5 us (14%)
  local copies, waits for them, and re-layouts  6.66 us (8%)
    pallas_call x2, Pallas kernels, level_call(): pl.pallas_call(kernel, grid_spec=grid_spec, out_shape=tuple((jax.ShapeDty...  17.8 us
    ppermute x4, starting transfers between devices, shifted(): return lax.ppermute(x, axis, pairs)  12.9 us
    dot_general x2, matrix products, mix(): jnp.einsum('crw,bc->rwb', x, weights, precision=lax.Precision.HIGHEST, pr...  11.5 us
    ppermute x4, waiting for transfers between devices, shifted(): return lax.ppermute(x, axis, pairs)  9.08 us
    pallas_call x1, Pallas kernels, last_call(): pl.pallas_call(functools.partial(last_kernel, stride=stride), grid_spec=g...  8.62 us
    unnamed x14, local copies, waits for them, and re-layouts  6.62 us
    ppermute x2, waiting for transfers between devices, diagonal(): return lax.ppermute(x, ('rows', 'cols'), pairs)  6.52 us
    ppermute x2, starting transfers between devices, diagonal(): return lax.ppermute(x, ('rows', 'cols'), pairs)  6.26 us
  transfers between devices with their start and end apart: 7, of which 2 were waited for; matrix products, arithmetic and copies ran while one was open for 5% of the time, Pallas kernels for 0%

profile of v12, /device:TPU:0, one launch (start us, length us, event | category | flops | bytes accessed | tf_op | source)
XLA Modules:
  0.0 80.8 jit_solution(9132054229575573963)
XLA Ops:
  0.0 1.1 %copy.6 = f32[224,224]{0,1:T(8,128)S(1)} copy(f32[224,224]{1,0:T(8,128)} %param.6) | data formatting | bytes 401408 | tf_op args[1]
  1.1 0.0 copy-start.1
  1.1 10.5 %convolution_bitcast_fusion.own = f32[32,128,256]{2,1,0:T(8,128)S(1)} fusion(f32[224,224]{0,1:T(8,128)S(1)} %copy.6, f32[224,32,128]{2,1,0:T(8,128)} %param.5), kind=kOutput, calls=%fused_computation | convolution fusion | flops 2818572288 | bytes 8065024 | tf_op jit(solution)/shard_map/crw,bc->rwb/dot_general | solution.py:334
  11.6 0.0 copy-start
  11.6 2.0 %copy-done = f32[32,128,256]{2,1,0:T(8,128)} copy-done((f32[32,128,256]{2,1,0:T(8,128)}, f32[32,128,256]{2,1,0:T(8,128)S(1)}, u32[]{:S(2)}) %copy-start) | copy-done | bytes 4194328
  13.6 0.1 slice_select_fusion
  13.7 0.5 collective-permute-start
  14.2 0.0 copy-done.1
  14.2 2.1 %copy.7 = f32[224,32,128]{2,0,1:T(8,128)S(1)} copy(f32[224,32,128]{2,1,0:T(8,128)S(1)} %copy-done.1) | data formatting | bytes 7340032 | tf_op args[0]
  16.4 0.1 fusion.17
  16.4 1.0 %fusion = f32[4,128,256]{2,1,0:T(8,128)S(1)} fusion(f32[224,1,128]{2,0,1:T(8,128)S(1)} %get-tuple-element.18, f32[224,1,128]{2,0,1:T(8,128)S(1)} %get-tuple-element.19, f32[224,1,128]{2,0,1:T(8,128)S(1)} %get-tuple-element.20, f32[224,1,128]{2,0,1:T(8,128)S(1)} %get-tuple-element.17, f32[224,224]{0,1:T(8,128)S(1)} %copy.6), kind=kOutput, calls=%fused_computation.2 | convolution fusion | flops 352665600 | bytes 1183744 | tf_op jit(solution)/shard_map/crw,bc->rwb/dot_general | solution.py:334
  17.5 1.3 %collective-permute-start.3 = (f32[2,128,256]{2,1,0:T(8,128)S(1)}, f32[2,128,256]{2,1,0:T(8,128)S(1)}, u32[]{:S(2)}, u32[]{:S(2)}) collective-permute-start(f32[2,128,256]{2,1,0:T(8,128)S(1)} %get-tuple-element.23), channel_id=1, source_target_pairs={{2,0},{4,2},{6,4},{8,6},{10,8},{12,10},{14,12},{3,1},{5,3},{7,5},{... | collective-permute-start | bytes 786440 | tf_op jit(solution)/shard_map/ppermute | solution.py:27
  18.8 5.3 %collective-permute-start.1 = (f32[2,128,256]{2,1,0:T(8,128)S(1)}, f32[2,128,256]{2,1,0:T(8,128)S(1)}, u32[]{:S(2)}, u32[]{:S(2)}) collective-permute-start(f32[2,128,256]{2,1,0:T(8,128)S(1)} %get-tuple-element.24), channel_id=1, source_target_pairs={{0,2},{2,4},{4,6},{6,8},{8,10},{10,12},{12,14},{1,3},{3,5},{5,7},{... | collective-permute-start | bytes 786440 | tf_op jit(solution)/shard_map/ppermute | solution.py:27
  24.1 1.3 %collective-permute-start.4 = (f32[2,32,256]{2,1,0:T(8,128)S(1)}, f32[2,32,256]{2,1,0:T(8,128)S(1)}, u32[]{:S(2)}, u32[]{:S(2)}) collective-permute-start(f32[2,32,256]{2,1,0:T(8,128)S(1)} %get-tuple-element.21), channel_id=1, source_target_pairs={{2,1},{3,0},{4,3},{5,2},{6,5},{7,4},{8,7},{9,6},{10,9},{11,8},{12,... | collective-permute-start | bytes 196616 | tf_op jit(solution)/shard_map/ppermute | solution.py:314
  25.4 5.0 %collective-permute-start.2 = (f32[2,32,256]{2,1,0:T(8,128)S(1)}, f32[2,32,256]{2,1,0:T(8,128)S(1)}, u32[]{:S(2)}, u32[]{:S(2)}) collective-permute-start(f32[2,32,256]{2,1,0:T(8,128)S(1)} %get-tuple-element.22), channel_id=1, source_target_pairs={{0,3},{1,2},{2,5},{3,4},{4,7},{5,6},{6,9},{7,8},{8,11},{9,10},{10,... | collective-permute-start | bytes 196616 | tf_op jit(solution)/shard_map/ppermute | solution.py:314
  30.4 0.6 add_convert_fusion.flags
  31.0 0.0 collective-permute-done.4.next_halo
  31.0 0.0 copy-start.4
  31.0 6.5 %collective-permute-done.2.prev_halo = f32[2,32,256]{2,1,0:T(8,128)S(1)} collective-permute-done((f32[2,32,256]{2,1,0:T(8,128)S(1)}, f32[2,32,256]{2,1,0:T(8,128)S(1)}, u32[]{:S(2)}, u32[]{:S(2)}) %collective-permute-start.2) | collective-permute-done | bytes 65568 | tf_op jit(solution)/shard_map/ppermute | solution.py:314
  37.5 0.0 copy-start.5
  37.5 0.0 collective-permute-done.3.next_own
  37.5 0.0 copy-start.2
  37.5 0.0 collective-permute-done.1.prev_own
  37.5 0.0 copy-done.4
  37.5 0.6 copy-done.5
  38.1 0.2 copy-done.2
  38.3 0.0 copy-start.3
  38.3 0.7 copy-done.3
  39.0 0.0 collective-permute-done.halo
  39.0 13.6 %shard_map.55 = (f32[32,128,256]{2,1,0:T(8,128)}, f32[16,80,256]{2,1,0:T(8,128)}, f32[2,120,256]{2,1,0:T(8,128)}, f32[2,120,256]{2,1,0:T(8,128)}) custom-call(s32[3]{0:T(128)} %add_convert_fusion.flags, f32[32,128,256]{2,1,0:T(8,128)} %copy-done, f32[32,32,256]{2,1,0:T(8,128)} %collective-permute-done.halo, f32[2,128,256]{2,1,0:T(8,128)} %copy-done.3, ...), custom_call_target="tpu_custom_call" | custom-call | tf_op jit(solution)/shard_map/pallas_call | solution.py:229
  52.6 5.0 %collective-permute-start.5 = (f32[2,120,256]{2,1,0:T(8,128)}, f32[2,120,256]{2,1,0:T(8,128)}, u32[]{:S(2)}, u32[]{:S(2)}) collective-permute-start(f32[2,120,256]{2,1,0:T(8,128)} %get-tuple-element.12.sent_next), channel_id=1, source_target_pairs={{0,2},{2,4},{4,6},{6,8},{8,10},{10,12},{12,14},{1,3},{3,5},{5,7},{... | collective-permute-start | bytes 737288 | tf_op jit(solution)/shard_map/ppermute | solution.py:27
  57.6 1.3 %collective-permute-start.6 = (f32[2,120,256]{2,1,0:T(8,128)}, f32[2,120,256]{2,1,0:T(8,128)}, u32[]{:S(2)}, u32[]{:S(2)}) collective-permute-start(f32[2,120,256]{2,1,0:T(8,128)} %get-tuple-element.13.sent_prev), channel_id=1, source_target_pairs={{2,0},{4,2},{6,4},{8,6},{10,8},{12,10},{14,12},{3,1},{5,3},{7,5},{... | collective-permute-start | bytes 737288 | tf_op jit(solution)/shard_map/ppermute | solution.py:27
  58.9 9.1 %collective-permute-done.5.from_prev.got_prev = f32[2,120,256]{2,1,0:T(8,128)} collective-permute-done((f32[2,120,256]{2,1,0:T(8,128)}, f32[2,120,256]{2,1,0:T(8,128)}, u32[]{:S(2)}, u32[]{:S(2)}) %collective-permute-start.5) | collective-permute-done | bytes 245792 | tf_op jit(solution)/shard_map/ppermute | solution.py:27
  67.9 0.0 collective-permute-done.6.from_next.got_next
  67.9 4.3 %shard_map.56 = (f32[16,64,256]{2,1,0:T(8,128)}, f32[8,40,256]{2,1,0:T(8,128)}, f32[2,40,256]{2,1,0:T(8,128)}, f32[2,40,256]{2,1,0:T(8,128)}) custom-call(s32[3]{0:T(128)} %add_convert_fusion.flags, f32[16,80,256]{2,1,0:T(8,128)} %get-tuple-element.11.x_ref, f32[2,120,256]{2,1,0:T(8,128)} %collective-permute-done.5.from_prev.got_prev, ...), custom_call_target="tpu_custom_call" | custom-call | tf_op jit(solution)/shard_map/pallas_call | solution.py:229
  72.2 8.6 %shard_map.57 = f32[224,32,128]{2,1,0:T(8,128)} custom-call(s32[3]{0:T(128)} %add_convert_fusion.flags, f32[8,40,256]{2,1,0:T(8,128)} %get-tuple-element.14.x_ref, f32[2,120,256]{2,1,0:T(8,128)} %collective-permute-done.5.from_prev.got_prev, f32[2,120,256]{2,1,0:T(8,128)} %collective-permute-done.6.from_next.got_next, ...), custom_call_target="tpu_custom_call" | custom-call | tf_op jit(solution)/shard_map/pallas_call | solution.py:389
  (2 shorter events, 0.1 us)
Async XLA Ops:
  1.1 13.2 %copy-start.1 = (f32[224,32,128]{2,1,0:T(8,128)S(1)}, f32[224,32,128]{2,1,0:T(8,128)}, u32[]{:S(2)}) copy-start(f32[224,32,128]{2,1,0:T(8,128)} %param.5) | copy-start | bytes 11010052
  11.6 2.0 %copy-start = (f32[32,128,256]{2,1,0:T(8,128)}, f32[32,128,256]{2,1,0:T(8,128)S(1)}, u32[]{:S(2)}) copy-start(f32[32,128,256]{2,1,0:T(8,128)S(1)} %convolution_bitcast_fusion.own) | copy-start | bytes 12582916
  13.7 25.3 %collective-permute-start = (f32[32,32,256]{2,1,0:T(8,128)S(1)}, f32[32,32,256]{2,1,0:T(8,128)}, u32[]{:S(2)}, u32[]{:S(2)}) collective-permute-start(f32[32,32,256]{2,1,0:T(8,128)S(1)} %slice_select_fusion), channel_id=1, source_target_pairs={{0,1},{1,0},{2,3},{3,2},{4,5},{5,4},{6,7},{7,6},{8,9},{9,8},{10,11... | collective-permute-start | bytes 3145736 | tf_op jit(solution)/shard_map/ppermute | solution.py:303
  17.5 20.0 %collective-permute-start.3 = (f32[2,128,256]{2,1,0:T(8,128)S(1)}, f32[2,128,256]{2,1,0:T(8,128)S(1)}, u32[]{:S(2)}, u32[]{:S(2)}) collective-permute-start(f32[2,128,256]{2,1,0:T(8,128)S(1)} %get-tuple-element.23), channel_id=1, source_target_pairs={{2,0},{4,2},{6,4},{8,6},{10,8},{12,10},{14,12},{3,1},{5,3},{7,5},{... | collective-permute-start | bytes 786440 | tf_op jit(solution)/shard_map/ppermute | solution.py:27
  18.8 18.7 %collective-permute-start.1 = (f32[2,128,256]{2,1,0:T(8,128)S(1)}, f32[2,128,256]{2,1,0:T(8,128)S(1)}, u32[]{:S(2)}, u32[]{:S(2)}) collective-permute-start(f32[2,128,256]{2,1,0:T(8,128)S(1)} %get-tuple-element.24), channel_id=1, source_target_pairs={{0,2},{2,4},{4,6},{6,8},{8,10},{10,12},{12,14},{1,3},{3,5},{5,7},{... | collective-permute-start | bytes 786440 | tf_op jit(solution)/shard_map/ppermute | solution.py:27
  24.1 6.9 %collective-permute-start.4 = (f32[2,32,256]{2,1,0:T(8,128)S(1)}, f32[2,32,256]{2,1,0:T(8,128)S(1)}, u32[]{:S(2)}, u32[]{:S(2)}) collective-permute-start(f32[2,32,256]{2,1,0:T(8,128)S(1)} %get-tuple-element.21), channel_id=1, source_target_pairs={{2,1},{3,0},{4,3},{5,2},{6,5},{7,4},{8,7},{9,6},{10,9},{11,8},{12,... | collective-permute-start | bytes 196616 | tf_op jit(solution)/shard_map/ppermute | solution.py:314
  25.4 12.1 %collective-permute-start.2 = (f32[2,32,256]{2,1,0:T(8,128)S(1)}, f32[2,32,256]{2,1,0:T(8,128)S(1)}, u32[]{:S(2)}, u32[]{:S(2)}) collective-permute-start(f32[2,32,256]{2,1,0:T(8,128)S(1)} %get-tuple-element.22), channel_id=1, source_target_pairs={{0,3},{1,2},{2,5},{3,4},{4,7},{5,6},{6,9},{7,8},{8,11},{9,10},{10,... | collective-permute-start | bytes 196616 | tf_op jit(solution)/shard_map/ppermute | solution.py:314
  31.0 6.5 %copy-start.4 = (f32[2,32,256]{2,1,0:T(8,128)}, f32[2,32,256]{2,1,0:T(8,128)S(1)}, u32[]{:S(2)}) copy-start(f32[2,32,256]{2,1,0:T(8,128)S(1)} %collective-permute-done.4.next_halo) | copy-start | bytes 196612
  37.5 0.6 copy-start.5
  37.5 0.8 copy-start.2
  38.3 0.7 copy-start.3
  52.6 15.4 %collective-permute-start.5 = (f32[2,120,256]{2,1,0:T(8,128)}, f32[2,120,256]{2,1,0:T(8,128)}, u32[]{:S(2)}, u32[]{:S(2)}) collective-permute-start(f32[2,120,256]{2,1,0:T(8,128)} %get-tuple-element.12.sent_next), channel_id=1, source_target_pairs={{0,2},{2,4},{4,6},{6,8},{8,10},{10,12},{12,14},{1,3},{3,5},{5,7},{... | collective-permute-start | bytes 737288 | tf_op jit(solution)/shard_map/ppermute | solution.py:27
  57.6 10.4 %collective-permute-start.6 = (f32[2,120,256]{2,1,0:T(8,128)}, f32[2,120,256]{2,1,0:T(8,128)}, u32[]{:S(2)}, u32[]{:S(2)}) collective-permute-start(f32[2,120,256]{2,1,0:T(8,128)} %get-tuple-element.13.sent_prev), channel_id=1, source_target_pairs={{2,0},{4,2},{6,4},{8,6},{10,8},{12,10},{14,12},{3,1},{5,3},{7,5},{... | collective-permute-start | bytes 737288 | tf_op jit(solution)/shard_map/ppermute | solution.py:27

commit v13 on v12

--- a/solution.py
+++ b/solution.py
@@ -334,15 +334,12 @@
         return jnp.einsum("crw,bc->rwb", x, weights, precision=lax.Precision.HIGHEST,
                           preferred_element_type=jnp.float32)
 
-    rad_next, rad_prev = partials(radiance, 1)
-    mixed_parts = mix(jnp.concatenate([rad_next, rad_prev], axis=1))
-    mixed_next, mixed_prev = mixed_parts[:2], mixed_parts[2:]
+    own = mix(radiance)
+    mixed_next, mixed_prev = partials(own, 0)
     p_own = shifted(mixed_next, "rows", 1)
     n_own = shifted(mixed_prev, "rows", -1)
     p_halo = diagonal(facing(mixed_next), 1)
     n_halo = diagonal(facing(mixed_prev), -1)
-
-    own = mix(radiance)
     halo = to_core_mate(facing(own))
     ext_width = width + HALO
     out_shape = (rows, width, padded_bands)

time: 81.1 us -> 77.5 us (0.956)
  the two profiles are of different devices: /device:TPU:0 before, /device:TPU:25 now
where the time goes in v13:
time: 77.5 us; the launch traced here: 77.1 us
  Pallas kernels  26.5 us (34%)
  starting transfers between devices  19.7 us (25%)
  waiting for transfers between devices  16 us (21%)
  matrix products  10.4 us (13%)
  local copies, waits for them, and re-layouts  3.49 us (5%)
  other arithmetic  0.93 us (1%)
    pallas_call x2, Pallas kernels, level_call(): pl.pallas_call(kernel, grid_spec=grid_spec, out_shape=tuple((jax.ShapeDty...  17.8 us
    ppermute x4, starting transfers between devices, shifted(): return lax.ppermute(x, axis, pairs)  12.4 us
    dot_general x1, matrix products, mix(): jnp.einsum('crw,bc->rwb', x, weights, precision=lax.Precision.HIGHEST, pr...  10.4 us
    ppermute x4, waiting for transfers between devices, shifted(): return lax.ppermute(x, axis, pairs)  10.1 us
    pallas_call x1, Pallas kernels, last_call(): pl.pallas_call(functools.partial(last_kernel, stride=stride), grid_spec=g...  8.64 us
    ppermute x2, starting transfers between devices, diagonal(): return lax.ppermute(x, ('rows', 'cols'), pairs)  6.64 us
    ppermute x2, waiting for transfers between devices, diagonal(): return lax.ppermute(x, ('rows', 'cols'), pairs)  5.91 us
    unnamed x11, local copies, waits for them, and re-layouts  3.49 us
  transfers between devices with their start and end apart: 7, of which 3 were waited for; matrix products, arithmetic and copies ran while one was open for 1% of the time, Pallas kernels for 0%

profile of v13, /device:TPU:25, one launch (start us, length us, event | category | flops | bytes accessed | tf_op | source)
XLA Modules:
  0.0 77.1 jit_solution(11574252041348322108)
XLA Ops:
  0.0 1.1 %copy.6 = f32[224,224]{0,1:T(8,128)S(1)} copy(f32[224,224]{1,0:T(8,128)} %param.6) | data formatting | bytes 401408 | tf_op args[1]
  1.1 10.4 %fusion.2.own = f32[32,128,256]{2,1,0:T(8,128)S(1)} fusion(f32[224,32,128]{2,1,0:T(8,128)} %param.5, f32[224,224]{0,1:T(8,128)S(1)} %copy.6), kind=kOutput, calls=%fused_computation.2 | convolution fusion | flops 2818572288 | bytes 8065024 | tf_op jit(solution)/shard_map/crw,bc->rwb/dot_general | solution.py:334
  11.5 0.0 copy-start
  11.5 0.2 slice_select_fusion
  11.7 0.7 collective-permute-start
  12.4 1.0 %copy-done = f32[32,128,256]{2,1,0:T(8,128)} copy-done((f32[32,128,256]{2,1,0:T(8,128)}, f32[32,128,256]{2,1,0:T(8,128)S(1)}, u32[]{:S(2)}) %copy-start) | copy-done | bytes 4194328
  13.4 0.1 fusion.20
  13.5 3.1 %collective-permute-start.1 = (f32[2,128,256]{2,1,0:T(8,128)S(1)}, f32[2,128,256]{2,1,0:T(8,128)S(1)}, u32[]{:S(2)}, u32[]{:S(2)}) collective-permute-start(f32[2,128,256]{2,1,0:T(8,128)S(1)} %pad_maximum_fusion), channel_id=1, source_target_pairs={{0,2},{2,4},{4,6},{6,8},{8,10},{10,12},{12,14},{1,3},{3,5},{5,7},{... | collective-permute-start | bytes 786440 | tf_op jit(solution)/shard_map/ppermute | solution.py:27
  16.7 3.0 %collective-permute-start.3 = (f32[2,128,256]{2,1,0:T(8,128)S(1)}, f32[2,128,256]{2,1,0:T(8,128)S(1)}, u32[]{:S(2)}, u32[]{:S(2)}) collective-permute-start(f32[2,128,256]{2,1,0:T(8,128)S(1)} %pad_maximum_fusion.1), channel_id=1, source_target_pairs={{2,0},{4,2},{6,4},{8,6},{10,8},{12,10},{14,12},{3,1},{5,3},{7,5},{... | collective-permute-start | bytes 786440 | tf_op jit(solution)/shard_map/ppermute | solution.py:27
  19.8 3.4 %collective-permute-start.2 = (f32[2,32,256]{2,1,0:T(8,128)S(1)}, f32[2,32,256]{2,1,0:T(8,128)S(1)}, u32[]{:S(2)}, u32[]{:S(2)}) collective-permute-start(f32[2,32,256]{2,1,0:T(8,128)S(1)} %fusion.17), channel_id=1, source_target_pairs={{0,3},{1,2},{2,5},{3,4},{4,7},{5,6},{6,9},{7,8},{8,11},{9,10},{10,... | collective-permute-start | bytes 196616 | tf_op jit(solution)/shard_map/ppermute | solution.py:314
  23.2 3.3 %collective-permute-start.4 = (f32[2,32,256]{2,1,0:T(8,128)S(1)}, f32[2,32,256]{2,1,0:T(8,128)S(1)}, u32[]{:S(2)}, u32[]{:S(2)}) collective-permute-start(f32[2,32,256]{2,1,0:T(8,128)S(1)} %fusion.14), channel_id=1, source_target_pairs={{2,1},{3,0},{4,3},{5,2},{6,5},{7,4},{8,7},{9,6},{10,9},{11,8},{12,... | collective-permute-start | bytes 196616 | tf_op jit(solution)/shard_map/ppermute | solution.py:314
  26.5 0.6 add_convert_fusion.flags
  27.1 0.0 collective-permute-done.2.prev_halo
  27.1 0.0 copy-start.3
  27.1 5.9 %collective-permute-done.4.next_halo = f32[2,32,256]{2,1,0:T(8,128)S(1)} collective-permute-done((f32[2,32,256]{2,1,0:T(8,128)S(1)}, f32[2,32,256]{2,1,0:T(8,128)S(1)}, u32[]{:S(2)}, u32[]{:S(2)}) %collective-permute-start.4) | collective-permute-done | bytes 65568 | tf_op jit(solution)/shard_map/ppermute | solution.py:314
  33.0 0.0 copy-start.4
  33.0 0.0 collective-permute-done.1.prev_own
  33.0 0.0 copy-start.1
  33.0 0.0 collective-permute-done.3.next_own
  33.0 0.0 copy-done.3
  33.0 0.6 copy-done.4
  33.6 0.1 copy-done.1
  33.7 0.0 copy-start.2
  33.7 0.7 copy-done.2
  34.4 0.0 collective-permute-done.halo
  34.4 13.6 %shard_map.55 = (f32[32,128,256]{2,1,0:T(8,128)}, f32[16,80,256]{2,1,0:T(8,128)}, f32[2,120,256]{2,1,0:T(8,128)}, f32[2,120,256]{2,1,0:T(8,128)}) custom-call(s32[3]{0:T(128)} %add_convert_fusion.flags, f32[32,128,256]{2,1,0:T(8,128)} %copy-done, f32[32,32,256]{2,1,0:T(8,128)} %collective-permute-done.halo, f32[2,128,256]{2,1,0:T(8,128)} %copy-done.1, ...), custom_call_target="tpu_custom_call" | custom-call | tf_op jit(solution)/shard_map/pallas_call | solution.py:229
  48.0 1.9 %collective-permute-start.5 = (f32[2,120,256]{2,1,0:T(8,128)}, f32[2,120,256]{2,1,0:T(8,128)}, u32[]{:S(2)}, u32[]{:S(2)}) collective-permute-start(f32[2,120,256]{2,1,0:T(8,128)} %get-tuple-element.12.sent_next), channel_id=1, source_target_pairs={{0,2},{2,4},{4,6},{6,8},{8,10},{10,12},{12,14},{1,3},{3,5},{5,7},{... | collective-permute-start | bytes 737288 | tf_op jit(solution)/shard_map/ppermute | solution.py:27
  49.9 4.3 %collective-permute-start.6 = (f32[2,120,256]{2,1,0:T(8,128)}, f32[2,120,256]{2,1,0:T(8,128)}, u32[]{:S(2)}, u32[]{:S(2)}) collective-permute-start(f32[2,120,256]{2,1,0:T(8,128)} %get-tuple-element.13.sent_prev), channel_id=1, source_target_pairs={{2,0},{4,2},{6,4},{8,6},{10,8},{12,10},{14,12},{3,1},{5,3},{7,5},{... | collective-permute-start | bytes 737288 | tf_op jit(solution)/shard_map/ppermute | solution.py:27
  54.2 4.1 %collective-permute-done.5.from_prev.got_prev = f32[2,120,256]{2,1,0:T(8,128)} collective-permute-done((f32[2,120,256]{2,1,0:T(8,128)}, f32[2,120,256]{2,1,0:T(8,128)}, u32[]{:S(2)}, u32[]{:S(2)}) %collective-permute-start.5) | collective-permute-done | bytes 245792 | tf_op jit(solution)/shard_map/ppermute | solution.py:27
  58.3 6.0 %collective-permute-done.6.from_next.got_next = f32[2,120,256]{2,1,0:T(8,128)} collective-permute-done((f32[2,120,256]{2,1,0:T(8,128)}, f32[2,120,256]{2,1,0:T(8,128)}, u32[]{:S(2)}, u32[]{:S(2)}) %collective-permute-start.6) | collective-permute-done | bytes 245792 | tf_op jit(solution)/shard_map/ppermute | solution.py:27
  64.3 4.2 %shard_map.56 = (f32[16,64,256]{2,1,0:T(8,128)}, f32[8,40,256]{2,1,0:T(8,128)}, f32[2,40,256]{2,1,0:T(8,128)}, f32[2,40,256]{2,1,0:T(8,128)}) custom-call(s32[3]{0:T(128)} %add_convert_fusion.flags, f32[16,80,256]{2,1,0:T(8,128)} %get-tuple-element.11.x_ref, f32[2,120,256]{2,1,0:T(8,128)} %collective-permute-done.5.from_prev.got_prev, ...), custom_call_target="tpu_custom_call" | custom-call | tf_op jit(solution)/shard_map/pallas_call | solution.py:229
  68.5 8.6 %shard_map.57 = f32[224,32,128]{2,1,0:T(8,128)} custom-call(s32[3]{0:T(128)} %add_convert_fusion.flags, f32[8,40,256]{2,1,0:T(8,128)} %get-tuple-element.14.x_ref, f32[2,120,256]{2,1,0:T(8,128)} %collective-permute-done.5.from_prev.got_prev, f32[2,120,256]{2,1,0:T(8,128)} %collective-permute-done.6.from_next.got_next, ...), custom_call_target="tpu_custom_call" | custom-call | tf_op jit(solution)/shard_map/pallas_call | solution.py:386
  (4 shorter events, 0.1 us)
Async XLA Ops:
  11.5 2.0 %copy-start = (f32[32,128,256]{2,1,0:T(8,128)}, f32[32,128,256]{2,1,0:T(8,128)S(1)}, u32[]{:S(2)}) copy-start(f32[32,128,256]{2,1,0:T(8,128)S(1)} %fusion.2.own) | copy-start | bytes 12582916
  11.7 22.7 %collective-permute-start = (f32[32,32,256]{2,1,0:T(8,128)S(1)}, f32[32,32,256]{2,1,0:T(8,128)}, u32[]{:S(2)}, u32[]{:S(2)}) collective-permute-start(f32[32,32,256]{2,1,0:T(8,128)S(1)} %slice_select_fusion), channel_id=1, source_target_pairs={{0,1},{1,0},{2,3},{3,2},{4,5},{5,4},{6,7},{7,6},{8,9},{9,8},{10,11... | collective-permute-start | bytes 3145736 | tf_op jit(solution)/shard_map/ppermute | solution.py:303
  13.5 19.5 %collective-permute-start.1 = (f32[2,128,256]{2,1,0:T(8,128)S(1)}, f32[2,128,256]{2,1,0:T(8,128)S(1)}, u32[]{:S(2)}, u32[]{:S(2)}) collective-permute-start(f32[2,128,256]{2,1,0:T(8,128)S(1)} %pad_maximum_fusion), channel_id=1, source_target_pairs={{0,2},{2,4},{4,6},{6,8},{8,10},{10,12},{12,14},{1,3},{3,5},{5,7},{... | collective-permute-start | bytes 786440 | tf_op jit(solution)/shard_map/ppermute | solution.py:27
  16.7 16.3 %collective-permute-start.3 = (f32[2,128,256]{2,1,0:T(8,128)S(1)}, f32[2,128,256]{2,1,0:T(8,128)S(1)}, u32[]{:S(2)}, u32[]{:S(2)}) collective-permute-start(f32[2,128,256]{2,1,0:T(8,128)S(1)} %pad_maximum_fusion.1), channel_id=1, source_target_pairs={{2,0},{4,2},{6,4},{8,6},{10,8},{12,10},{14,12},{3,1},{5,3},{7,5},{... | collective-permute-start | bytes 786440 | tf_op jit(solution)/shard_map/ppermute | solution.py:27
  19.8 7.3 %collective-permute-start.2 = (f32[2,32,256]{2,1,0:T(8,128)S(1)}, f32[2,32,256]{2,1,0:T(8,128)S(1)}, u32[]{:S(2)}, u32[]{:S(2)}) collective-permute-start(f32[2,32,256]{2,1,0:T(8,128)S(1)} %fusion.17), channel_id=1, source_target_pairs={{0,3},{1,2},{2,5},{3,4},{4,7},{5,6},{6,9},{7,8},{8,11},{9,10},{10,... | collective-permute-start | bytes 196616 | tf_op jit(solution)/shard_map/ppermute | solution.py:314
  23.2 9.8 %collective-permute-start.4 = (f32[2,32,256]{2,1,0:T(8,128)S(1)}, f32[2,32,256]{2,1,0:T(8,128)S(1)}, u32[]{:S(2)}, u32[]{:S(2)}) collective-permute-start(f32[2,32,256]{2,1,0:T(8,128)S(1)} %fusion.14), channel_id=1, source_target_pairs={{2,1},{3,0},{4,3},{5,2},{6,5},{7,4},{8,7},{9,6},{10,9},{11,8},{12,... | collective-permute-start | bytes 196616 | tf_op jit(solution)/shard_map/ppermute | solution.py:314
  27.1 5.9 %copy-start.3 = (f32[2,32,256]{2,1,0:T(8,128)}, f32[2,32,256]{2,1,0:T(8,128)S(1)}, u32[]{:S(2)}) copy-start(f32[2,32,256]{2,1,0:T(8,128)S(1)} %collective-permute-done.2.prev_halo) | copy-start | bytes 196612
  33.0 0.6 copy-start.4
  33.0 0.7 copy-start.1
  33.7 0.7 copy-start.2
  48.0 10.3 %collective-permute-start.5 = (f32[2,120,256]{2,1,0:T(8,128)}, f32[2,120,256]{2,1,0:T(8,128)}, u32[]{:S(2)}, u32[]{:S(2)}) collective-permute-start(f32[2,120,256]{2,1,0:T(8,128)} %get-tuple-element.12.sent_next), channel_id=1, source_target_pairs={{0,2},{2,4},{4,6},{6,8},{8,10},{10,12},{12,14},{1,3},{3,5},{5,7},{... | collective-permute-start | bytes 737288 | tf_op jit(solution)/shard_map/ppermute | solution.py:27
  49.9 14.3 %collective-permute-start.6 = (f32[2,120,256]{2,1,0:T(8,128)}, f32[2,120,256]{2,1,0:T(8,128)}, u32[]{:S(2)}, u32[]{:S(2)}) collective-permute-start(f32[2,120,256]{2,1,0:T(8,128)} %get-tuple-element.13.sent_prev), channel_id=1, source_target_pairs={{2,0},{4,2},{6,4},{8,6},{10,8},{12,10},{14,12},{3,1},{5,3},{7,5},{... | collective-permute-start | bytes 737288 | tf_op jit(solution)/shard_map/ppermute | solution.py:27

commit v14 on v13

--- a/solution.py
+++ b/solution.py
@@ -211,10 +211,11 @@
     return pl.BlockSpec(a.shape, lambda h, f: (0,) * a.ndim)
 
 
-def level_call(kernel, flags, arrays, out_shape, rows, width, aliases, consts=(), ahead=False):
+def level_call(kernel, flags, arrays, out_shape, rows, width, aliases, consts=(), ahead=False,
+               edge_bands=None):
     bands = arrays[0].shape[-1]
     ll_shape = (rows // 2, width // 2, bands)
-    edge_shape = (2, width // 2 + (width // 4 if ahead else 0), bands)
+    edge_shape = (2, width // 2 + (width // 4 if ahead else 0), edge_bands or bands)
     outs = (out_shape, ll_shape, edge_shape, edge_shape)
     grid_spec = pltpu.PrefetchScalarGridSpec(
         num_scalar_prefetch=1,
@@ -336,11 +337,15 @@
 
     own = mix(radiance)
     mixed_next, mixed_prev = partials(own, 0)
-    p_own = shifted(mixed_next, "rows", 1)
-    n_own = shifted(mixed_prev, "rows", -1)
-    p_halo = diagonal(facing(mixed_next), 1)
-    n_halo = diagonal(facing(mixed_prev), -1)
-    halo = to_core_mate(facing(own))
+
+    def real(x):
+        return x[..., :bands]
+
+    p_own = shifted(real(mixed_next), "rows", 1)
+    n_own = shifted(real(mixed_prev), "rows", -1)
+    p_halo = diagonal(real(facing(mixed_next)), 1)
+    n_halo = diagonal(real(facing(mixed_prev)), -1)
+    halo = to_core_mate(real(facing(own)))
     ext_width = width + HALO
     out_shape = (rows, width, padded_bands)
     assert LEVELS == 3
@@ -349,7 +354,7 @@
     out, level, tn, tp = level_call(
         first_kernel, flags,
         [own, halo, p_own, p_halo, n_own, n_halo],
-        out_shape, rows, ext_width, {}, consts=(ahead_map,), ahead=True)
+        out_shape, rows, ext_width, {}, consts=(ahead_map,), ahead=True, edge_bands=bands)
     r, w = level.shape[0], level.shape[1]
     got_prev = shifted(tn, "rows", 1)
     got_next = shifted(tp, "rows", -1)

time: 77.5 us -> 80.8 us (1.043)
  the two profiles are of different devices: /device:TPU:25 before, /device:TPU:11 now
where the time goes in v14:
time: 80.8 us; the launch traced here: 80.4 us
  Pallas kernels  26.4 us (33%)
  starting transfers between devices  18.9 us (23%)
  waiting for transfers between devices  18.4 us (23%)
  matrix products  10.4 us (13%)
  local copies, waits for them, and re-layouts  4.01 us (5%)
  other arithmetic  2.16 us (3%)
    pallas_call x2, Pallas kernels, level_call(): pl.pallas_call(kernel, grid_spec=grid_spec, out_shape=tuple((jax.ShapeDty...  17.8 us
    ppermute x4, waiting for transfers between devices, shifted(): return lax.ppermute(x, axis, pairs)  13.2 us
    ppermute x4, starting transfers between devices, shifted(): return lax.ppermute(x, axis, pairs)  12.4 us
    dot_general x1, matrix products, mix(): jnp.einsum('crw,bc->rwb', x, weights, precision=lax.Precision.HIGHEST, pr...  10.4 us
    pallas_call x1, Pallas kernels, last_call(): pl.pallas_call(functools.partial(last_kernel, stride=stride), grid_spec=g...  8.64 us
    ppermute x2, starting transfers between devices, diagonal(): return lax.ppermute(x, ('rows', 'cols'), pairs)  5.81 us
    ppermute x2, waiting for transfers between devices, diagonal(): return lax.ppermute(x, ('rows', 'cols'), pairs)  5.16 us
    unnamed x11, local copies, waits for them, and re-layouts  3.75 us
  transfers between devices with their start and end apart: 7, of which 4 were waited for; matrix products, arithmetic and copies ran while one was open for 2% of the time, Pallas kernels for 0%

profile of v14, /device:TPU:11, one launch (start us, length us, event | category | flops | bytes accessed | tf_op | source)
XLA Modules:
  0.0 80.4 jit_solution(12201849263464381628)
XLA Ops:
  0.0 1.1 %copy.6 = f32[224,224]{0,1:T(8,128)S(1)} copy(f32[224,224]{1,0:T(8,128)} %param.6) | data formatting | bytes 401408 | tf_op args[1]
  1.1 10.4 %fusion.2.own = f32[32,128,256]{2,1,0:T(8,128)S(1)} fusion(f32[224,32,128]{2,1,0:T(8,128)} %param.5, f32[224,224]{0,1:T(8,128)S(1)} %copy.6), kind=kOutput, calls=%fused_computation.2 | convolution fusion | flops 2818572288 | bytes 8065024 | tf_op jit(solution)/shard_map/crw,bc->rwb/dot_general | solution.py:335
  11.5 0.0 copy-start
  11.5 2.0 %copy-done = f32[32,128,256]{2,1,0:T(8,128)} copy-done((f32[32,128,256]{2,1,0:T(8,128)}, f32[32,128,256]{2,1,0:T(8,128)S(1)}, u32[]{:S(2)}) %copy-start) | copy-done | bytes 4194328
  13.4 0.2 fusion.18
  13.7 0.2 slice_select_fusion
  13.9 0.7 collective-permute-start
  14.6 1.3 %fusion.10 = (f32[1,128,256]{2,1,0:T(8,128)S(1)}, f32[1,128,256]{2,1,0:T(8,128)S(1)}, f32[1,128,256]{2,1,0:T(8,128)S(1)}, f32[1,128,256]{2,1,0:T(8,128)S(1)}) fusion(f32[32,128,256]{2,1,0:T(8,128)} %copy-done), kind=kLoop, calls=%fused_computation.18 | loop fusion | flops 327680 | bytes 1441792 | tf_op jit(solution)/shard_map/add | solution.py:42
  16.0 2.9 %collective-permute-start.4 = (f32[2,32,224]{2,1,0:T(8,128)S(1)}, f32[2,32,224]{2,1,0:T(8,128)S(1)}, u32[]{:S(2)}, u32[]{:S(2)}) collective-permute-start(f32[2,32,224]{2,1,0:T(8,128)S(1)} %fusion.15), channel_id=1, source_target_pairs={{2,1},{3,0},{4,3},{5,2},{6,5},{7,4},{8,7},{9,6},{10,9},{11,8},{12,... | collective-permute-start | bytes 172040 | tf_op jit(solution)/shard_map/ppermute | solution.py:315
  18.9 2.2 %collective-permute-start.1 = (f32[2,128,224]{2,1,0:T(8,128)S(1)}, f32[2,128,224]{2,1,0:T(8,128)S(1)}, u32[]{:S(2)}, u32[]{:S(2)}) collective-permute-start(f32[2,128,224]{2,1,0:T(8,128)S(1)} %fusion.6), channel_id=1, source_target_pairs={{0,2},{2,4},{4,6},{6,8},{8,10},{10,12},{12,14},{1,3},{3,5},{5,7},{... | collective-permute-start | bytes 688136 | tf_op jit(solution)/shard_map/ppermute | solution.py:27
  21.2 3.9 %collective-permute-start.3 = (f32[2,128,224]{2,1,0:T(8,128)S(1)}, f32[2,128,224]{2,1,0:T(8,128)S(1)}, u32[]{:S(2)}, u32[]{:S(2)}) collective-permute-start(f32[2,128,224]{2,1,0:T(8,128)S(1)} %fusion.5), channel_id=1, source_target_pairs={{2,0},{4,2},{6,4},{8,6},{10,8},{12,10},{14,12},{3,1},{5,3},{7,5},{... | collective-permute-start | bytes 688136 | tf_op jit(solution)/shard_map/ppermute | solution.py:27
  25.2 2.9 %collective-permute-start.2 = (f32[2,32,224]{2,1,0:T(8,128)S(1)}, f32[2,32,224]{2,1,0:T(8,128)S(1)}, u32[]{:S(2)}, u32[]{:S(2)}) collective-permute-start(f32[2,32,224]{2,1,0:T(8,128)S(1)} %fusion.16), channel_id=1, source_target_pairs={{0,3},{1,2},{2,5},{3,4},{4,7},{5,6},{6,9},{7,8},{8,11},{9,10},{10,... | collective-permute-start | bytes 172040 | tf_op jit(solution)/shard_map/ppermute | solution.py:315
  28.1 0.6 add_convert_fusion.flags
  28.7 0.0 collective-permute-done.4.next_halo
  28.7 0.0 copy-start.3
  28.7 5.2 %collective-permute-done.2.prev_halo = f32[2,32,224]{2,1,0:T(8,128)S(1)} collective-permute-done((f32[2,32,224]{2,1,0:T(8,128)S(1)}, f32[2,32,224]{2,1,0:T(8,128)S(1)}, u32[]{:S(2)}, u32[]{:S(2)}) %collective-permute-start.2) | collective-permute-done | bytes 57376 | tf_op jit(solution)/shard_map/ppermute | solution.py:315
  33.8 0.0 copy-start.4
  33.9 0.0 collective-permute-done.1.prev_own
  33.9 0.0 copy-start.1
  33.9 3.1 %collective-permute-done.3.next_own = f32[2,128,224]{2,1,0:T(8,128)S(1)} collective-permute-done((f32[2,128,224]{2,1,0:T(8,128)S(1)}, f32[2,128,224]{2,1,0:T(8,128)S(1)}, u32[]{:S(2)}, u32[]{:S(2)}) %collective-permute-start.3) | collective-permute-done | bytes 229408 | tf_op jit(solution)/shard_map/ppermute | solution.py:27
  37.0 0.0 copy-done.3
  37.0 0.0 copy-done.4
  37.0 0.0 copy-done.1
  37.0 0.0 copy-start.2
  37.0 0.7 copy-done.2
  37.7 0.0 collective-permute-done.halo
  37.7 13.6 %shard_map.55 = (f32[32,128,256]{2,1,0:T(8,128)}, f32[16,80,256]{2,1,0:T(8,128)}, f32[2,120,224]{2,1,0:T(8,128)}, f32[2,120,224]{2,1,0:T(8,128)}) custom-call(s32[3]{0:T(128)} %add_convert_fusion.flags, f32[32,128,256]{2,1,0:T(8,128)} %copy-done, f32[32,32,224]{2,1,0:T(8,128)} %collective-permute-done.halo, f32[2,128,224]{2,1,0:T(8,128)} %copy-done.1, ...), custom_call_target="tpu_custom_call" | custom-call | tf_op jit(solution)/shard_map/pallas_call | solution.py:230
  51.3 2.0 %collective-permute-start.5 = (f32[2,120,224]{2,1,0:T(8,128)}, f32[2,120,224]{2,1,0:T(8,128)}, u32[]{:S(2)}, u32[]{:S(2)}) collective-permute-start(f32[2,120,224]{2,1,0:T(8,128)} %get-tuple-element.12.sent_next), channel_id=1, source_target_pairs={{0,2},{2,4},{4,6},{6,8},{8,10},{10,12},{12,14},{1,3},{3,5},{5,7},{... | collective-permute-start | bytes 645128 | tf_op jit(solution)/shard_map/ppermute | solution.py:27
  53.3 4.2 %collective-permute-start.6 = (f32[2,120,224]{2,1,0:T(8,128)}, f32[2,120,224]{2,1,0:T(8,128)}, u32[]{:S(2)}, u32[]{:S(2)}) collective-permute-start(f32[2,120,224]{2,1,0:T(8,128)} %get-tuple-element.13.sent_prev), channel_id=1, source_target_pairs={{2,0},{4,2},{6,4},{8,6},{10,8},{12,10},{14,12},{3,1},{5,3},{7,5},{... | collective-permute-start | bytes 645128 | tf_op jit(solution)/shard_map/ppermute | solution.py:27
  57.5 4.0 %collective-permute-done.5.from_prev.got_prev = f32[2,120,224]{2,1,0:T(8,128)} collective-permute-done((f32[2,120,224]{2,1,0:T(8,128)}, f32[2,120,224]{2,1,0:T(8,128)}, u32[]{:S(2)}, u32[]{:S(2)}) %collective-permute-start.5) | collective-permute-done | bytes 215072 | tf_op jit(solution)/shard_map/ppermute | solution.py:27
  61.5 6.1 %collective-permute-done.6.from_next.got_next = f32[2,120,224]{2,1,0:T(8,128)} collective-permute-done((f32[2,120,224]{2,1,0:T(8,128)}, f32[2,120,224]{2,1,0:T(8,128)}, u32[]{:S(2)}, u32[]{:S(2)}) %collective-permute-start.6) | collective-permute-done | bytes 215072 | tf_op jit(solution)/shard_map/ppermute | solution.py:27
  67.6 4.2 %shard_map.56 = (f32[16,64,256]{2,1,0:T(8,128)}, f32[8,40,256]{2,1,0:T(8,128)}, f32[2,40,256]{2,1,0:T(8,128)}, f32[2,40,256]{2,1,0:T(8,128)}) custom-call(s32[3]{0:T(128)} %add_convert_fusion.flags, f32[16,80,256]{2,1,0:T(8,128)} %get-tuple-element.11.x_ref, f32[2,120,224]{2,1,0:T(8,128)} %collective-permute-done.5.from_prev.got_prev, ...), custom_call_target="tpu_custom_call" | custom-call | tf_op jit(solution)/shard_map/pallas_call | solution.py:230
  71.8 8.6 %shard_map.57 = f32[224,32,128]{2,1,0:T(8,128)} custom-call(s32[3]{0:T(128)} %add_convert_fusion.flags, f32[8,40,256]{2,1,0:T(8,128)} %get-tuple-element.14.x_ref, f32[2,120,224]{2,1,0:T(8,128)} %collective-permute-done.5.from_prev.got_prev, f32[2,120,224]{2,1,0:T(8,128)} %collective-permute-done.6.from_next.got_next, ...), custom_call_target="tpu_custom_call" | custom-call | tf_op jit(solution)/shard_map/pallas_call | solution.py:391
  (6 shorter events, 0.1 us)
Async XLA Ops:
  11.5 2.0 %copy-start = (f32[32,128,256]{2,1,0:T(8,128)}, f32[32,128,256]{2,1,0:T(8,128)S(1)}, u32[]{:S(2)}) copy-start(f32[32,128,256]{2,1,0:T(8,128)S(1)} %fusion.2.own) | copy-start | bytes 12582916
  13.9 23.9 %collective-permute-start = (f32[32,32,224]{2,1,0:T(8,128)S(1)}, f32[32,32,224]{2,1,0:T(8,128)}, u32[]{:S(2)}, u32[]{:S(2)}) collective-permute-start(f32[32,32,224]{2,1,0:T(8,128)S(1)} %slice_select_fusion), channel_id=1, source_target_pairs={{0,1},{1,0},{2,3},{3,2},{4,5},{5,4},{6,7},{7,6},{8,9},{9,8},{10,11... | collective-permute-start | bytes 2752520 | tf_op jit(solution)/shard_map/ppermute | solution.py:304
  16.0 12.7 %collective-permute-start.4 = (f32[2,32,224]{2,1,0:T(8,128)S(1)}, f32[2,32,224]{2,1,0:T(8,128)S(1)}, u32[]{:S(2)}, u32[]{:S(2)}) collective-permute-start(f32[2,32,224]{2,1,0:T(8,128)S(1)} %fusion.15), channel_id=1, source_target_pairs={{2,1},{3,0},{4,3},{5,2},{6,5},{7,4},{8,7},{9,6},{10,9},{11,8},{12,... | collective-permute-start | bytes 172040 | tf_op jit(solution)/shard_map/ppermute | solution.py:315
  18.9 14.9 %collective-permute-start.1 = (f32[2,128,224]{2,1,0:T(8,128)S(1)}, f32[2,128,224]{2,1,0:T(8,128)S(1)}, u32[]{:S(2)}, u32[]{:S(2)}) collective-permute-start(f32[2,128,224]{2,1,0:T(8,128)S(1)} %fusion.6), channel_id=1, source_target_pairs={{0,2},{2,4},{4,6},{6,8},{8,10},{10,12},{12,14},{1,3},{3,5},{5,7},{... | collective-permute-start | bytes 688136 | tf_op jit(solution)/shard_map/ppermute | solution.py:27
  21.2 15.8 %collective-permute-start.3 = (f32[2,128,224]{2,1,0:T(8,128)S(1)}, f32[2,128,224]{2,1,0:T(8,128)S(1)}, u32[]{:S(2)}, u32[]{:S(2)}) collective-permute-start(f32[2,128,224]{2,1,0:T(8,128)S(1)} %fusion.5), channel_id=1, source_target_pairs={{2,0},{4,2},{6,4},{8,6},{10,8},{12,10},{14,12},{3,1},{5,3},{7,5},{... | collective-permute-start | bytes 688136 | tf_op jit(solution)/shard_map/ppermute | solution.py:27
  25.2 8.6 %collective-permute-start.2 = (f32[2,32,224]{2,1,0:T(8,128)S(1)}, f32[2,32,224]{2,1,0:T(8,128)S(1)}, u32[]{:S(2)}, u32[]{:S(2)}) collective-permute-start(f32[2,32,224]{2,1,0:T(8,128)S(1)} %fusion.16), channel_id=1, source_target_pairs={{0,3},{1,2},{2,5},{3,4},{4,7},{5,6},{6,9},{7,8},{8,11},{9,10},{10,... | collective-permute-start | bytes 172040 | tf_op jit(solution)/shard_map/ppermute | solution.py:315
  28.7 8.3 %copy-start.3 = (f32[2,32,224]{2,1,0:T(8,128)}, f32[2,32,224]{2,1,0:T(8,128)S(1)}, u32[]{:S(2)}) copy-start(f32[2,32,224]{2,1,0:T(8,128)S(1)} %collective-permute-done.4.next_halo) | copy-start | bytes 172036
  33.8 3.1 %copy-start.4 = (f32[2,32,224]{2,1,0:T(8,128)}, f32[2,32,224]{2,1,0:T(8,128)S(1)}, u32[]{:S(2)}) copy-start(f32[2,32,224]{2,1,0:T(8,128)S(1)} %collective-permute-done.2.prev_halo) | copy-start | bytes 172036
  33.9 3.1 %copy-start.1 = (f32[2,128,224]{2,1,0:T(8,128)}, f32[2,128,224]{2,1,0:T(8,128)S(1)}, u32[]{:S(2)}) copy-start(f32[2,128,224]{2,1,0:T(8,128)S(1)} %collective-permute-done.1.prev_own) | copy-start | bytes 688132
  37.0 0.7 copy-start.2
  51.3 10.2 %collective-permute-start.5 = (f32[2,120,224]{2,1,0:T(8,128)}, f32[2,120,224]{2,1,0:T(8,128)}, u32[]{:S(2)}, u32[]{:S(2)}) collective-permute-start(f32[2,120,224]{2,1,0:T(8,128)} %get-tuple-element.12.sent_next), channel_id=1, source_target_pairs={{0,2},{2,4},{4,6},{6,8},{8,10},{10,12},{12,14},{1,3},{3,5},{5,7},{... | collective-permute-start | bytes 645128 | tf_op jit(solution)/shard_map/ppermute | solution.py:27
  53.3 14.2 %collective-permute-start.6 = (f32[2,120,224]{2,1,0:T(8,128)}, f32[2,120,224]{2,1,0:T(8,128)}, u32[]{:S(2)}, u32[]{:S(2)}) collective-permute-start(f32[2,120,224]{2,1,0:T(8,128)} %get-tuple-element.13.sent_prev), channel_id=1, source_target_pairs={{2,0},{4,2},{6,4},{8,6},{10,8},{12,10},{14,12},{3,1},{5,3},{7,5},{... | collective-permute-start | bytes 645128 | tf_op jit(solution)/shard_map/ppermute | solution.py:27

commit v15 on v13

--- a/solution.py
+++ b/solution.py
@@ -139,14 +139,18 @@
                 tp_ref[...] = to_prev
             else:
                 quarter = hw // 2
-                ahead = jnp.dot(ahead_map[...], e.reshape(hr * hw, LANES),
-                                precision=lax.Precision.HIGHEST,
-                                preferred_element_type=jnp.float32)
-                ahead = ahead.reshape(4, quarter, LANES)
+                used = hr - EDGE
+                flat = e.reshape(hr * hw, LANES)
+                ahead_next = jnp.dot(ahead_map[0: 2 * quarter, EDGE * hw :], flat[EDGE * hw :],
+                                     precision=lax.Precision.HIGHEST,
+                                     preferred_element_type=jnp.float32)
+                ahead_prev = jnp.dot(ahead_map[2 * quarter :, : used * hw], flat[: used * hw],
+                                     precision=lax.Precision.HIGHEST,
+                                     preferred_element_type=jnp.float32)
                 tn_ref[:, :hw] = to_next
-                tn_ref[:, hw:] = ahead[:2]
+                tn_ref[:, hw:] = ahead_next.reshape(2, quarter, LANES)
                 tp_ref[:, :hw] = to_prev
-                tp_ref[:, hw:] = ahead[2:]
+                tp_ref[:, hw:] = ahead_prev.reshape(2, quarter, LANES)
 
 
 def first_kernel(flags, own, halo, prev_own, prev_halo, next_own, next_halo, ahead_map,
@@ -182,7 +186,7 @@
 
 
 def last_kernel(flags, x_ref, got_prev, got_next, sent_next, sent_prev, below_map, above_map,
-                prev_out, middle, final_ref, ext, half, full, ll, tn, tp, *, stride):
+                prev_out, middle, final_ref, ext, half, ll, tn, tp, *, stride):
     rows, width = x_ref.shape[0], x_ref.shape[1]
     wide = 2 * width
 
@@ -191,7 +195,7 @@
                        precision=lax.Precision.HIGHEST, preferred_element_type=jnp.float32)
         return part.reshape(2, width, LANES)
 
-    full[...] = prev_out[...]
+    full = prev_out
     mr, mw = middle.shape[0], middle.shape[1]
     full[pl.ds(0, mr, stride=2), pl.ds(0, mw, stride=2), :] = middle[...]
     ext[EDGE : EDGE + rows] = x_ref[...]
@@ -377,7 +381,6 @@
         scratch_shapes=[
             pltpu.VMEM((rows + 2 * EDGE, width, LANES), jnp.float32),
             pltpu.VMEM((2, rows // 2, width, LANES), jnp.float32),
-            pltpu.VMEM(out.shape[:-1] + (LANES,), jnp.float32),
             pltpu.VMEM((rows // 2, width // 2, LANES), jnp.float32),
             pltpu.VMEM((2, width // 2, LANES), jnp.float32),
             pltpu.VMEM((2, width // 2, LANES), jnp.float32),

time: 77.5 us -> 77 us (level)
  no operation moved by 1% of the time
where the time goes in v15:
time: 77 us; the launch traced here: 76.6 us
  Pallas kernels  26 us (34%)
  starting transfers between devices  19.7 us (26%)
  waiting for transfers between devices  16 us (21%)
  matrix products  10.4 us (14%)
  local copies, waits for them, and re-layouts  3.49 us (5%)
  other arithmetic  0.93 us (1%)
    pallas_call x2, Pallas kernels, level_call(): pl.pallas_call(kernel, grid_spec=grid_spec, out_shape=tuple((jax.ShapeDty...  17.6 us
    ppermute x4, starting transfers between devices, shifted(): return lax.ppermute(x, axis, pairs)  12.4 us
    dot_general x1, matrix products, mix(): jnp.einsum('crw,bc->rwb', x, weights, precision=lax.Precision.HIGHEST, pr...  10.4 us
    ppermute x4, waiting for transfers between devices, shifted(): return lax.ppermute(x, axis, pairs)  10.1 us
    pallas_call x1, Pallas kernels, last_call(): pl.pallas_call(functools.partial(last_kernel, stride=stride), grid_spec=g...  8.38 us
    ppermute x2, starting transfers between devices, diagonal(): return lax.ppermute(x, ('rows', 'cols'), pairs)  6.64 us
    ppermute x2, waiting for transfers between devices, diagonal(): return lax.ppermute(x, ('rows', 'cols'), pairs)  5.91 us
    unnamed x11, local copies, waits for them, and re-layouts  3.49 us
  transfers between devices with their start and end apart: 7, of which 3 were waited for; matrix products, arithmetic and copies ran while one was open for 1% of the time, Pallas kernels for 0%

profile of v15, /device:TPU:25, one launch (start us, length us, event | category | flops | bytes accessed | tf_op | source)
XLA Modules:
  0.0 76.6 jit_solution(8402648205198655329)
XLA Ops:
  0.0 1.1 %copy.6 = f32[224,224]{0,1:T(8,128)S(1)} copy(f32[224,224]{1,0:T(8,128)} %param.6) | data formatting | bytes 401408 | tf_op args[1]
  1.1 10.4 %fusion.2.own = f32[32,128,256]{2,1,0:T(8,128)S(1)} fusion(f32[224,32,128]{2,1,0:T(8,128)} %param.5, f32[224,224]{0,1:T(8,128)S(1)} %copy.6), kind=kOutput, calls=%fused_computation.2 | convolution fusion | flops 2818572288 | bytes 8065024 | tf_op jit(solution)/shard_map/crw,bc->rwb/dot_general | solution.py:338
  11.5 0.0 copy-start
  11.5 0.2 slice_select_fusion
  11.7 0.7 collective-permute-start
  12.4 1.0 %copy-done = f32[32,128,256]{2,1,0:T(8,128)} copy-done((f32[32,128,256]{2,1,0:T(8,128)}, f32[32,128,256]{2,1,0:T(8,128)S(1)}, u32[]{:S(2)}) %copy-start) | copy-done | bytes 4194328
  13.4 0.1 fusion.20
  13.5 3.1 %collective-permute-start.1 = (f32[2,128,256]{2,1,0:T(8,128)S(1)}, f32[2,128,256]{2,1,0:T(8,128)S(1)}, u32[]{:S(2)}, u32[]{:S(2)}) collective-permute-start(f32[2,128,256]{2,1,0:T(8,128)S(1)} %pad_maximum_fusion), channel_id=1, source_target_pairs={{0,2},{2,4},{4,6},{6,8},{8,10},{10,12},{12,14},{1,3},{3,5},{5,7},{... | collective-permute-start | bytes 786440 | tf_op jit(solution)/shard_map/ppermute | solution.py:27
  16.7 3.0 %collective-permute-start.3 = (f32[2,128,256]{2,1,0:T(8,128)S(1)}, f32[2,128,256]{2,1,0:T(8,128)S(1)}, u32[]{:S(2)}, u32[]{:S(2)}) collective-permute-start(f32[2,128,256]{2,1,0:T(8,128)S(1)} %pad_maximum_fusion.1), channel_id=1, source_target_pairs={{2,0},{4,2},{6,4},{8,6},{10,8},{12,10},{14,12},{3,1},{5,3},{7,5},{... | collective-permute-start | bytes 786440 | tf_op jit(solution)/shard_map/ppermute | solution.py:27
  19.8 3.4 %collective-permute-start.2 = (f32[2,32,256]{2,1,0:T(8,128)S(1)}, f32[2,32,256]{2,1,0:T(8,128)S(1)}, u32[]{:S(2)}, u32[]{:S(2)}) collective-permute-start(f32[2,32,256]{2,1,0:T(8,128)S(1)} %fusion.17), channel_id=1, source_target_pairs={{0,3},{1,2},{2,5},{3,4},{4,7},{5,6},{6,9},{7,8},{8,11},{9,10},{10,... | collective-permute-start | bytes 196616 | tf_op jit(solution)/shard_map/ppermute | solution.py:318
  23.2 3.3 %collective-permute-start.4 = (f32[2,32,256]{2,1,0:T(8,128)S(1)}, f32[2,32,256]{2,1,0:T(8,128)S(1)}, u32[]{:S(2)}, u32[]{:S(2)}) collective-permute-start(f32[2,32,256]{2,1,0:T(8,128)S(1)} %fusion.14), channel_id=1, source_target_pairs={{2,1},{3,0},{4,3},{5,2},{6,5},{7,4},{8,7},{9,6},{10,9},{11,8},{12,... | collective-permute-start | bytes 196616 | tf_op jit(solution)/shard_map/ppermute | solution.py:318
  26.5 0.6 add_convert_fusion.flags
  27.1 0.0 collective-permute-done.2.prev_halo
  27.1 0.0 copy-start.3
  27.1 5.9 %collective-permute-done.4.next_halo = f32[2,32,256]{2,1,0:T(8,128)S(1)} collective-permute-done((f32[2,32,256]{2,1,0:T(8,128)S(1)}, f32[2,32,256]{2,1,0:T(8,128)S(1)}, u32[]{:S(2)}, u32[]{:S(2)}) %collective-permute-start.4) | collective-permute-done | bytes 65568 | tf_op jit(solution)/shard_map/ppermute | solution.py:318
  33.0 0.0 copy-start.4
  33.0 0.0 collective-permute-done.1.prev_own
  33.0 0.0 copy-start.1
  33.0 0.0 collective-permute-done.3.next_own
  33.0 0.0 copy-done.3
  33.0 0.6 copy-done.4
  33.6 0.1 copy-done.1
  33.7 0.0 copy-start.2
  33.7 0.7 copy-done.2
  34.4 0.0 collective-permute-done.halo
  34.4 13.4 %shard_map.55 = (f32[32,128,256]{2,1,0:T(8,128)}, f32[16,80,256]{2,1,0:T(8,128)}, f32[2,120,256]{2,1,0:T(8,128)}, f32[2,120,256]{2,1,0:T(8,128)}) custom-call(s32[3]{0:T(128)} %add_convert_fusion.flags, f32[32,128,256]{2,1,0:T(8,128)} %copy-done, f32[32,32,256]{2,1,0:T(8,128)} %collective-permute-done.halo, f32[2,128,256]{2,1,0:T(8,128)} %copy-done.1, ...), custom_call_target="tpu_custom_call" | custom-call | tf_op jit(solution)/shard_map/pallas_call | solution.py:233
  47.8 1.9 %collective-permute-start.5 = (f32[2,120,256]{2,1,0:T(8,128)}, f32[2,120,256]{2,1,0:T(8,128)}, u32[]{:S(2)}, u32[]{:S(2)}) collective-permute-start(f32[2,120,256]{2,1,0:T(8,128)} %get-tuple-element.12.sent_next), channel_id=1, source_target_pairs={{0,2},{2,4},{4,6},{6,8},{8,10},{10,12},{12,14},{1,3},{3,5},{5,7},{... | collective-permute-start | bytes 737288 | tf_op jit(solution)/shard_map/ppermute | solution.py:27
  49.7 4.3 %collective-permute-start.6 = (f32[2,120,256]{2,1,0:T(8,128)}, f32[2,120,256]{2,1,0:T(8,128)}, u32[]{:S(2)}, u32[]{:S(2)}) collective-permute-start(f32[2,120,256]{2,1,0:T(8,128)} %get-tuple-element.13.sent_prev), channel_id=1, source_target_pairs={{2,0},{4,2},{6,4},{8,6},{10,8},{12,10},{14,12},{3,1},{5,3},{7,5},{... | collective-permute-start | bytes 737288 | tf_op jit(solution)/shard_map/ppermute | solution.py:27
  54.0 4.1 %collective-permute-done.5.from_prev.got_prev = f32[2,120,256]{2,1,0:T(8,128)} collective-permute-done((f32[2,120,256]{2,1,0:T(8,128)}, f32[2,120,256]{2,1,0:T(8,128)}, u32[]{:S(2)}, u32[]{:S(2)}) %collective-permute-start.5) | collective-permute-done | bytes 245792 | tf_op jit(solution)/shard_map/ppermute | solution.py:27
  58.1 6.0 %collective-permute-done.6.from_next.got_next = f32[2,120,256]{2,1,0:T(8,128)} collective-permute-done((f32[2,120,256]{2,1,0:T(8,128)}, f32[2,120,256]{2,1,0:T(8,128)}, u32[]{:S(2)}, u32[]{:S(2)}) %collective-permute-start.6) | collective-permute-done | bytes 245792 | tf_op jit(solution)/shard_map/ppermute | solution.py:27
  64.0 4.2 %shard_map.56 = (f32[16,64,256]{2,1,0:T(8,128)}, f32[8,40,256]{2,1,0:T(8,128)}, f32[2,40,256]{2,1,0:T(8,128)}, f32[2,40,256]{2,1,0:T(8,128)}) custom-call(s32[3]{0:T(128)} %add_convert_fusion.flags, f32[16,80,256]{2,1,0:T(8,128)} %get-tuple-element.11.x_ref, f32[2,120,256]{2,1,0:T(8,128)} %collective-permute-done.5.from_prev.got_prev, ...), custom_call_target="tpu_custom_call" | custom-call | tf_op jit(solution)/shard_map/pallas_call | solution.py:233
  68.3 8.4 %shard_map.57 = f32[224,32,128]{2,1,0:T(8,128)} custom-call(s32[3]{0:T(128)} %add_convert_fusion.flags, f32[8,40,256]{2,1,0:T(8,128)} %get-tuple-element.14.x_ref, f32[2,120,256]{2,1,0:T(8,128)} %collective-permute-done.5.from_prev.got_prev, f32[2,120,256]{2,1,0:T(8,128)} %collective-permute-done.6.from_next.got_next, ...), custom_call_target="tpu_custom_call" | custom-call | tf_op jit(solution)/shard_map/pallas_call | solution.py:389
  (4 shorter events, 0.1 us)
Async XLA Ops:
  11.5 2.0 %copy-start = (f32[32,128,256]{2,1,0:T(8,128)}, f32[32,128,256]{2,1,0:T(8,128)S(1)}, u32[]{:S(2)}) copy-start(f32[32,128,256]{2,1,0:T(8,128)S(1)} %fusion.2.own) | copy-start | bytes 12582916
  11.7 22.7 %collective-permute-start = (f32[32,32,256]{2,1,0:T(8,128)S(1)}, f32[32,32,256]{2,1,0:T(8,128)}, u32[]{:S(2)}, u32[]{:S(2)}) collective-permute-start(f32[32,32,256]{2,1,0:T(8,128)S(1)} %slice_select_fusion), channel_id=1, source_target_pairs={{0,1},{1,0},{2,3},{3,2},{4,5},{5,4},{6,7},{7,6},{8,9},{9,8},{10,11... | collective-permute-start | bytes 3145736 | tf_op jit(solution)/shard_map/ppermute | solution.py:307
  13.5 19.5 %collective-permute-start.1 = (f32[2,128,256]{2,1,0:T(8,128)S(1)}, f32[2,128,256]{2,1,0:T(8,128)S(1)}, u32[]{:S(2)}, u32[]{:S(2)}) collective-permute-start(f32[2,128,256]{2,1,0:T(8,128)S(1)} %pad_maximum_fusion), channel_id=1, source_target_pairs={{0,2},{2,4},{4,6},{6,8},{8,10},{10,12},{12,14},{1,3},{3,5},{5,7},{... | collective-permute-start | bytes 786440 | tf_op jit(solution)/shard_map/ppermute | solution.py:27
  16.7 16.3 %collective-permute-start.3 = (f32[2,128,256]{2,1,0:T(8,128)S(1)}, f32[2,128,256]{2,1,0:T(8,128)S(1)}, u32[]{:S(2)}, u32[]{:S(2)}) collective-permute-start(f32[2,128,256]{2,1,0:T(8,128)S(1)} %pad_maximum_fusion.1), channel_id=1, source_target_pairs={{2,0},{4,2},{6,4},{8,6},{10,8},{12,10},{14,12},{3,1},{5,3},{7,5},{... | collective-permute-start | bytes 786440 | tf_op jit(solution)/shard_map/ppermute | solution.py:27
  19.8 7.3 %collective-permute-start.2 = (f32[2,32,256]{2,1,0:T(8,128)S(1)}, f32[2,32,256]{2,1,0:T(8,128)S(1)}, u32[]{:S(2)}, u32[]{:S(2)}) collective-permute-start(f32[2,32,256]{2,1,0:T(8,128)S(1)} %fusion.17), channel_id=1, source_target_pairs={{0,3},{1,2},{2,5},{3,4},{4,7},{5,6},{6,9},{7,8},{8,11},{9,10},{10,... | collective-permute-start | bytes 196616 | tf_op jit(solution)/shard_map/ppermute | solution.py:318
  23.2 9.8 %collective-permute-start.4 = (f32[2,32,256]{2,1,0:T(8,128)S(1)}, f32[2,32,256]{2,1,0:T(8,128)S(1)}, u32[]{:S(2)}, u32[]{:S(2)}) collective-permute-start(f32[2,32,256]{2,1,0:T(8,128)S(1)} %fusion.14), channel_id=1, source_target_pairs={{2,1},{3,0},{4,3},{5,2},{6,5},{7,4},{8,7},{9,6},{10,9},{11,8},{12,... | collective-permute-start | bytes 196616 | tf_op jit(solution)/shard_map/ppermute | solution.py:318
  27.1 5.9 %copy-start.3 = (f32[2,32,256]{2,1,0:T(8,128)}, f32[2,32,256]{2,1,0:T(8,128)S(1)}, u32[]{:S(2)}) copy-start(f32[2,32,256]{2,1,0:T(8,128)S(1)} %collective-permute-done.2.prev_halo) | copy-start | bytes 196612
  33.0 0.6 copy-start.4
  33.0 0.7 copy-start.1
  33.7 0.7 copy-start.2
  47.8 10.3 %collective-permute-start.5 = (f32[2,120,256]{2,1,0:T(8,128)}, f32[2,120,256]{2,1,0:T(8,128)}, u32[]{:S(2)}, u32[]{:S(2)}) collective-permute-start(f32[2,120,256]{2,1,0:T(8,128)} %get-tuple-element.12.sent_next), channel_id=1, source_target_pairs={{0,2},{2,4},{4,6},{6,8},{8,10},{10,12},{12,14},{1,3},{3,5},{5,7},{... | collective-permute-start | bytes 737288 | tf_op jit(solution)/shard_map/ppermute | solution.py:27
  49.7 14.3 %collective-permute-start.6 = (f32[2,120,256]{2,1,0:T(8,128)}, f32[2,120,256]{2,1,0:T(8,128)}, u32[]{:S(2)}, u32[]{:S(2)}) collective-permute-start(f32[2,120,256]{2,1,0:T(8,128)} %get-tuple-element.13.sent_prev), channel_id=1, source_target_pairs={{2,0},{4,2},{6,4},{8,6},{10,8},{12,10},{14,12},{3,1},{5,3},{7,5},{... | collective-permute-start | bytes 737288 | tf_op jit(solution)/shard_map/ppermute | solution.py:27

commit v16 on v15

--- a/solution.py
+++ b/solution.py
@@ -203,8 +203,7 @@
     from_next = got_next[:, wide:] + share(above_map, sent_next)
     fill_rows(ext, flags, from_prev, from_next, rows)
     lift_block(flags, ext, half, full, ll, tn, tp, rows, width, stride)
-    for r in range(full.shape[0]):
-        final_ref[:, r, :] = full[r].T
+    final_ref[...] = jnp.transpose(full[...], (2, 0, 1))
 
 
 def spec(shape):

time: 77 us -> 75.8 us (0.984)
  the two profiles are of different devices: /device:TPU:25 before, /device:TPU:11 now
where the time goes in v16:
time: 75.8 us; the launch traced here: 75.4 us
  Pallas kernels  24.8 us (33%)
  starting transfers between devices  19.7 us (26%)
  waiting for transfers between devices  16 us (21%)
  matrix products  10.4 us (14%)
  local copies, waits for them, and re-layouts  3.48 us (5%)
  other arithmetic  0.93 us (1%)
    pallas_call x2, Pallas kernels, level_call(): pl.pallas_call(kernel, grid_spec=grid_spec, out_shape=tuple((jax.ShapeDty...  17.6 us
    ppermute x4, starting transfers between devices, shifted(): return lax.ppermute(x, axis, pairs)  12.4 us
    dot_general x1, matrix products, mix(): jnp.einsum('crw,bc->rwb', x, weights, precision=lax.Precision.HIGHEST, pr...  10.4 us
    ppermute x4, waiting for transfers between devices, shifted(): return lax.ppermute(x, axis, pairs)  10.1 us
    pallas_call x1, Pallas kernels, last_call(): pl.pallas_call(functools.partial(last_kernel, stride=stride), grid_spec=g...  7.18 us
    ppermute x2, starting transfers between devices, diagonal(): return lax.ppermute(x, ('rows', 'cols'), pairs)  6.64 us
    ppermute x2, waiting for transfers between devices, diagonal(): return lax.ppermute(x, ('rows', 'cols'), pairs)  5.91 us
    unnamed x11, local copies, waits for them, and re-layouts  3.48 us
  transfers between devices with their start and end apart: 7, of which 4 were waited for; matrix products, arithmetic and copies ran while one was open for 1% of the time, Pallas kernels for 0%

profile of v16, /device:TPU:11, one launch (start us, length us, event | category | flops | bytes accessed | tf_op | source)
XLA Modules:
  0.0 75.4 jit_solution(5567437039949534060)
XLA Ops:
  0.0 1.1 %copy.6 = f32[224,224]{0,1:T(8,128)S(1)} copy(f32[224,224]{1,0:T(8,128)} %param.6) | data formatting | bytes 401408 | tf_op args[1]
  1.1 10.4 %fusion.2.own = f32[32,128,256]{2,1,0:T(8,128)S(1)} fusion(f32[224,32,128]{2,1,0:T(8,128)} %param.5, f32[224,224]{0,1:T(8,128)S(1)} %copy.6), kind=kOutput, calls=%fused_computation.2 | convolution fusion | flops 2818572288 | bytes 8065024 | tf_op jit(solution)/shard_map/crw,bc->rwb/dot_general | solution.py:337
  11.5 0.0 copy-start
  11.5 0.2 slice_select_fusion
  11.7 0.7 collective-permute-start
  12.4 1.0 %copy-done = f32[32,128,256]{2,1,0:T(8,128)} copy-done((f32[32,128,256]{2,1,0:T(8,128)}, f32[32,128,256]{2,1,0:T(8,128)S(1)}, u32[]{:S(2)}) %copy-start) | copy-done | bytes 4194328
  13.4 0.1 fusion.20
  13.5 3.1 %collective-permute-start.1 = (f32[2,128,256]{2,1,0:T(8,128)S(1)}, f32[2,128,256]{2,1,0:T(8,128)S(1)}, u32[]{:S(2)}, u32[]{:S(2)}) collective-permute-start(f32[2,128,256]{2,1,0:T(8,128)S(1)} %pad_maximum_fusion), channel_id=1, source_target_pairs={{0,2},{2,4},{4,6},{6,8},{8,10},{10,12},{12,14},{1,3},{3,5},{5,7},{... | collective-permute-start | bytes 786440 | tf_op jit(solution)/shard_map/ppermute | solution.py:27
  16.7 3.0 %collective-permute-start.3 = (f32[2,128,256]{2,1,0:T(8,128)S(1)}, f32[2,128,256]{2,1,0:T(8,128)S(1)}, u32[]{:S(2)}, u32[]{:S(2)}) collective-permute-start(f32[2,128,256]{2,1,0:T(8,128)S(1)} %pad_maximum_fusion.1), channel_id=1, source_target_pairs={{2,0},{4,2},{6,4},{8,6},{10,8},{12,10},{14,12},{3,1},{5,3},{7,5},{... | collective-permute-start | bytes 786440 | tf_op jit(solution)/shard_map/ppermute | solution.py:27
  19.8 3.4 %collective-permute-start.2 = (f32[2,32,256]{2,1,0:T(8,128)S(1)}, f32[2,32,256]{2,1,0:T(8,128)S(1)}, u32[]{:S(2)}, u32[]{:S(2)}) collective-permute-start(f32[2,32,256]{2,1,0:T(8,128)S(1)} %fusion.17), channel_id=1, source_target_pairs={{0,3},{1,2},{2,5},{3,4},{4,7},{5,6},{6,9},{7,8},{8,11},{9,10},{10,... | collective-permute-start | bytes 196616 | tf_op jit(solution)/shard_map/ppermute | solution.py:317
  23.2 3.3 %collective-permute-start.4 = (f32[2,32,256]{2,1,0:T(8,128)S(1)}, f32[2,32,256]{2,1,0:T(8,128)S(1)}, u32[]{:S(2)}, u32[]{:S(2)}) collective-permute-start(f32[2,32,256]{2,1,0:T(8,128)S(1)} %fusion.14), channel_id=1, source_target_pairs={{2,1},{3,0},{4,3},{5,2},{6,5},{7,4},{8,7},{9,6},{10,9},{11,8},{12,... | collective-permute-start | bytes 196616 | tf_op jit(solution)/shard_map/ppermute | solution.py:317
  26.5 0.6 add_convert_fusion.flags
  27.1 2.2 %collective-permute-done.2.prev_halo = f32[2,32,256]{2,1,0:T(8,128)S(1)} collective-permute-done((f32[2,32,256]{2,1,0:T(8,128)S(1)}, f32[2,32,256]{2,1,0:T(8,128)S(1)}, u32[]{:S(2)}, u32[]{:S(2)}) %collective-permute-start.2) | collective-permute-done | bytes 65568 | tf_op jit(solution)/shard_map/ppermute | solution.py:317
  29.2 0.0 copy-start.3
  29.2 3.8 %collective-permute-done.4.next_halo = f32[2,32,256]{2,1,0:T(8,128)S(1)} collective-permute-done((f32[2,32,256]{2,1,0:T(8,128)S(1)}, f32[2,32,256]{2,1,0:T(8,128)S(1)}, u32[]{:S(2)}, u32[]{:S(2)}) %collective-permute-start.4) | collective-permute-done | bytes 65568 | tf_op jit(solution)/shard_map/ppermute | solution.py:317
  33.0 0.0 copy-start.4
  33.0 0.0 collective-permute-done.1.prev_own
  33.0 0.0 copy-start.1
  33.0 0.0 collective-permute-done.3.next_own
  33.0 0.0 copy-done.3
  33.0 0.6 copy-done.4
  33.6 0.1 copy-done.1
  33.7 0.0 copy-start.2
  33.7 0.7 copy-done.2
  34.4 0.0 collective-permute-done.halo
  34.4 13.4 %shard_map.55 = (f32[32,128,256]{2,1,0:T(8,128)}, f32[16,80,256]{2,1,0:T(8,128)}, f32[2,120,256]{2,1,0:T(8,128)}, f32[2,120,256]{2,1,0:T(8,128)}) custom-call(s32[3]{0:T(128)} %add_convert_fusion.flags, f32[32,128,256]{2,1,0:T(8,128)} %copy-done, f32[32,32,256]{2,1,0:T(8,128)} %collective-permute-done.halo, f32[2,128,256]{2,1,0:T(8,128)} %copy-done.1, ...), custom_call_target="tpu_custom_call" | custom-call | tf_op jit(solution)/shard_map/pallas_call | solution.py:232
  47.8 2.1 %collective-permute-start.5 = (f32[2,120,256]{2,1,0:T(8,128)}, f32[2,120,256]{2,1,0:T(8,128)}, u32[]{:S(2)}, u32[]{:S(2)}) collective-permute-start(f32[2,120,256]{2,1,0:T(8,128)} %get-tuple-element.12.sent_next), channel_id=1, source_target_pairs={{0,2},{2,4},{4,6},{6,8},{8,10},{10,12},{12,14},{1,3},{3,5},{5,7},{... | collective-permute-start | bytes 737288 | tf_op jit(solution)/shard_map/ppermute | solution.py:27
  49.8 4.1 %collective-permute-start.6 = (f32[2,120,256]{2,1,0:T(8,128)}, f32[2,120,256]{2,1,0:T(8,128)}, u32[]{:S(2)}, u32[]{:S(2)}) collective-permute-start(f32[2,120,256]{2,1,0:T(8,128)} %get-tuple-element.13.sent_prev), channel_id=1, source_target_pairs={{2,0},{4,2},{6,4},{8,6},{10,8},{12,10},{14,12},{3,1},{5,3},{7,5},{... | collective-permute-start | bytes 737288 | tf_op jit(solution)/shard_map/ppermute | solution.py:27
  54.0 4.1 %collective-permute-done.5.from_prev.got_prev = f32[2,120,256]{2,1,0:T(8,128)} collective-permute-done((f32[2,120,256]{2,1,0:T(8,128)}, f32[2,120,256]{2,1,0:T(8,128)}, u32[]{:S(2)}, u32[]{:S(2)}) %collective-permute-start.5) | collective-permute-done | bytes 245792 | tf_op jit(solution)/shard_map/ppermute | solution.py:27
  58.0 6.0 %collective-permute-done.6.from_next.got_next = f32[2,120,256]{2,1,0:T(8,128)} collective-permute-done((f32[2,120,256]{2,1,0:T(8,128)}, f32[2,120,256]{2,1,0:T(8,128)}, u32[]{:S(2)}, u32[]{:S(2)}) %collective-permute-start.6) | collective-permute-done | bytes 245792 | tf_op jit(solution)/shard_map/ppermute | solution.py:27
  64.0 4.2 %shard_map.56 = (f32[16,64,256]{2,1,0:T(8,128)}, f32[8,40,256]{2,1,0:T(8,128)}, f32[2,40,256]{2,1,0:T(8,128)}, f32[2,40,256]{2,1,0:T(8,128)}) custom-call(s32[3]{0:T(128)} %add_convert_fusion.flags, f32[16,80,256]{2,1,0:T(8,128)} %get-tuple-element.11.x_ref, f32[2,120,256]{2,1,0:T(8,128)} %collective-permute-done.5.from_prev.got_prev, ...), custom_call_target="tpu_custom_call" | custom-call | tf_op jit(solution)/shard_map/pallas_call | solution.py:232
  68.3 7.2 %shard_map.57 = f32[224,32,128]{2,1,0:T(8,128)} custom-call(s32[3]{0:T(128)} %add_convert_fusion.flags, f32[8,40,256]{2,1,0:T(8,128)} %get-tuple-element.14.x_ref, f32[2,120,256]{2,1,0:T(8,128)} %collective-permute-done.5.from_prev.got_prev, f32[2,120,256]{2,1,0:T(8,128)} %collective-permute-done.6.from_next.got_next, ...), custom_call_target="tpu_custom_call" | custom-call | tf_op jit(solution)/shard_map/pallas_call | solution.py:388
  (4 shorter events, 0.1 us)
Async XLA Ops:
  11.5 2.0 %copy-start = (f32[32,128,256]{2,1,0:T(8,128)}, f32[32,128,256]{2,1,0:T(8,128)S(1)}, u32[]{:S(2)}) copy-start(f32[32,128,256]{2,1,0:T(8,128)S(1)} %fusion.2.own) | copy-start | bytes 12582916
  11.7 22.7 %collective-permute-start = (f32[32,32,256]{2,1,0:T(8,128)S(1)}, f32[32,32,256]{2,1,0:T(8,128)}, u32[]{:S(2)}, u32[]{:S(2)}) collective-permute-start(f32[32,32,256]{2,1,0:T(8,128)S(1)} %slice_select_fusion), channel_id=1, source_target_pairs={{0,1},{1,0},{2,3},{3,2},{4,5},{5,4},{6,7},{7,6},{8,9},{9,8},{10,11... | collective-permute-start | bytes 3145736 | tf_op jit(solution)/shard_map/ppermute | solution.py:306
  13.5 19.5 %collective-permute-start.1 = (f32[2,128,256]{2,1,0:T(8,128)S(1)}, f32[2,128,256]{2,1,0:T(8,128)S(1)}, u32[]{:S(2)}, u32[]{:S(2)}) collective-permute-start(f32[2,128,256]{2,1,0:T(8,128)S(1)} %pad_maximum_fusion), channel_id=1, source_target_pairs={{0,2},{2,4},{4,6},{6,8},{8,10},{10,12},{12,14},{1,3},{3,5},{5,7},{... | collective-permute-start | bytes 786440 | tf_op jit(solution)/shard_map/ppermute | solution.py:27
  16.7 16.3 %collective-permute-start.3 = (f32[2,128,256]{2,1,0:T(8,128)S(1)}, f32[2,128,256]{2,1,0:T(8,128)S(1)}, u32[]{:S(2)}, u32[]{:S(2)}) collective-permute-start(f32[2,128,256]{2,1,0:T(8,128)S(1)} %pad_maximum_fusion.1), channel_id=1, source_target_pairs={{2,0},{4,2},{6,4},{8,6},{10,8},{12,10},{14,12},{3,1},{5,3},{7,5},{... | collective-permute-start | bytes 786440 | tf_op jit(solution)/shard_map/ppermute | solution.py:27
  19.8 9.4 %collective-permute-start.2 = (f32[2,32,256]{2,1,0:T(8,128)S(1)}, f32[2,32,256]{2,1,0:T(8,128)S(1)}, u32[]{:S(2)}, u32[]{:S(2)}) collective-permute-start(f32[2,32,256]{2,1,0:T(8,128)S(1)} %fusion.17), channel_id=1, source_target_pairs={{0,3},{1,2},{2,5},{3,4},{4,7},{5,6},{6,9},{7,8},{8,11},{9,10},{10,... | collective-permute-start | bytes 196616 | tf_op jit(solution)/shard_map/ppermute | solution.py:317
  23.2 9.8 %collective-permute-start.4 = (f32[2,32,256]{2,1,0:T(8,128)S(1)}, f32[2,32,256]{2,1,0:T(8,128)S(1)}, u32[]{:S(2)}, u32[]{:S(2)}) collective-permute-start(f32[2,32,256]{2,1,0:T(8,128)S(1)} %fusion.14), channel_id=1, source_target_pairs={{2,1},{3,0},{4,3},{5,2},{6,5},{7,4},{8,7},{9,6},{10,9},{11,8},{12,... | collective-permute-start | bytes 196616 | tf_op jit(solution)/shard_map/ppermute | solution.py:317
  29.2 3.8 %copy-start.3 = (f32[2,32,256]{2,1,0:T(8,128)}, f32[2,32,256]{2,1,0:T(8,128)S(1)}, u32[]{:S(2)}) copy-start(f32[2,32,256]{2,1,0:T(8,128)S(1)} %collective-permute-done.2.prev_halo) | copy-start | bytes 196612
  33.0 0.6 copy-start.4
  33.0 0.7 copy-start.1
  33.7 0.7 copy-start.2
  47.8 10.3 %collective-permute-start.5 = (f32[2,120,256]{2,1,0:T(8,128)}, f32[2,120,256]{2,1,0:T(8,128)}, u32[]{:S(2)}, u32[]{:S(2)}) collective-permute-start(f32[2,120,256]{2,1,0:T(8,128)} %get-tuple-element.12.sent_next), channel_id=1, source_target_pairs={{0,2},{2,4},{4,6},{6,8},{8,10},{10,12},{12,14},{1,3},{3,5},{5,7},{... | collective-permute-start | bytes 737288 | tf_op jit(solution)/shard_map/ppermute | solution.py:27
  49.8 14.2 %collective-permute-start.6 = (f32[2,120,256]{2,1,0:T(8,128)}, f32[2,120,256]{2,1,0:T(8,128)}, u32[]{:S(2)}, u32[]{:S(2)}) collective-permute-start(f32[2,120,256]{2,1,0:T(8,128)} %get-tuple-element.13.sent_prev), channel_id=1, source_target_pairs={{2,0},{4,2},{6,4},{8,6},{10,8},{12,10},{14,12},{3,1},{5,3},{7,5},{... | collective-permute-start | bytes 737288 | tf_op jit(solution)/shard_map/ppermute | solution.py:27

commit v17 on v16

--- a/solution.py
+++ b/solution.py
@@ -111,15 +111,22 @@
     def store(pr, e, o):
         rows_at = pl.ds(pr * stride, hr, stride=step)
 
+        def put(lo):
+            ee, oo = e[:, lo : lo + own_hw], o[:, lo : lo + own_hw]
+            if stride == 1:
+                both = jnp.stack([ee, oo], axis=2).reshape(hr, 2 * own_hw, LANES)
+                out_ref[rows_at] = both
+            else:
+                out_ref[rows_at, pl.ds(0, own_hw, stride=step), :] = ee
+                out_ref[rows_at, pl.ds(stride, own_hw, stride=step), :] = oo
+
         @pl.when(on_left)
         def _():
-            out_ref[rows_at, pl.ds(0, own_hw, stride=step), :] = e[:, :own_hw]
-            out_ref[rows_at, pl.ds(stride, own_hw, stride=step), :] = o[:, :own_hw]
+            put(0)
 
         @pl.when(jnp.logical_not(on_left))
         def _():
-            out_ref[rows_at, pl.ds(0, own_hw, stride=step), :] = e[:, hw - own_hw :]
-            out_ref[rows_at, pl.ds(stride, own_hw, stride=step), :] = o[:, hw - own_hw :]
+            put(hw - own_hw)
 
     for pr in range(2):
         e = half[pr, :, pl.ds(0, hw, stride=2), :]

time: 75.8 us -> 80 us (1.055)
  the two profiles are of different devices: /device:TPU:11 before, /device:TPU:9 now
where the time goes in v17:
time: 80 us; the launch traced here: 79.7 us
  Pallas kernels  29 us (36%)
  starting transfers between devices  19.7 us (25%)
  waiting for transfers between devices  16 us (20%)
  matrix products  10.4 us (13%)
  local copies, waits for them, and re-layouts  3.49 us (4%)
  other arithmetic  0.93 us (1%)
    pallas_call x2, Pallas kernels, level_call(): pl.pallas_call(kernel, grid_spec=grid_spec, out_shape=tuple((jax.ShapeDty...  21.8 us
    ppermute x4, starting transfers between devices, shifted(): return lax.ppermute(x, axis, pairs)  12.4 us
    dot_general x1, matrix products, mix(): jnp.einsum('crw,bc->rwb', x, weights, precision=lax.Precision.HIGHEST, pr...  10.4 us
    ppermute x4, waiting for transfers between devices, shifted(): return lax.ppermute(x, axis, pairs)  10.1 us
    pallas_call x1, Pallas kernels, last_call(): pl.pallas_call(functools.partial(last_kernel, stride=stride), grid_spec=g...  7.18 us
    ppermute x2, starting transfers between devices, diagonal(): return lax.ppermute(x, ('rows', 'cols'), pairs)  6.64 us
    ppermute x2, waiting for transfers between devices, diagonal(): return lax.ppermute(x, ('rows', 'cols'), pairs)  5.91 us
    unnamed x11, local copies, waits for them, and re-layouts  3.49 us
  transfers between devices with their start and end apart: 7, of which 4 were waited for; matrix products, arithmetic and copies ran while one was open for 1% of the time, Pallas kernels for 0%

profile of v17, /device:TPU:9, one launch (start us, length us, event | category | flops | bytes accessed | tf_op | source)
XLA Modules:
  0.0 79.7 jit_solution(13707264211110782865)
XLA Ops:
  0.0 1.1 %copy.6 = f32[224,224]{0,1:T(8,128)S(1)} copy(f32[224,224]{1,0:T(8,128)} %param.6) | data formatting | bytes 401408 | tf_op args[1]
  1.1 10.4 %fusion.2.own = f32[32,128,256]{2,1,0:T(8,128)S(1)} fusion(f32[224,32,128]{2,1,0:T(8,128)} %param.5, f32[224,224]{0,1:T(8,128)S(1)} %copy.6), kind=kOutput, calls=%fused_computation.2 | convolution fusion | flops 2818572288 | bytes 8065024 | tf_op jit(solution)/shard_map/crw,bc->rwb/dot_general | solution.py:344
  11.5 0.0 copy-start
  11.5 0.2 slice_select_fusion
  11.7 0.7 collective-permute-start
  12.4 1.0 %copy-done = f32[32,128,256]{2,1,0:T(8,128)} copy-done((f32[32,128,256]{2,1,0:T(8,128)}, f32[32,128,256]{2,1,0:T(8,128)S(1)}, u32[]{:S(2)}) %copy-start) | copy-done | bytes 4194328
  13.4 0.1 fusion.20
  13.5 3.1 %collective-permute-start.1 = (f32[2,128,256]{2,1,0:T(8,128)S(1)}, f32[2,128,256]{2,1,0:T(8,128)S(1)}, u32[]{:S(2)}, u32[]{:S(2)}) collective-permute-start(f32[2,128,256]{2,1,0:T(8,128)S(1)} %pad_maximum_fusion), channel_id=1, source_target_pairs={{0,2},{2,4},{4,6},{6,8},{8,10},{10,12},{12,14},{1,3},{3,5},{5,7},{... | collective-permute-start | bytes 786440 | tf_op jit(solution)/shard_map/ppermute | solution.py:27
  16.7 3.0 %collective-permute-start.3 = (f32[2,128,256]{2,1,0:T(8,128)S(1)}, f32[2,128,256]{2,1,0:T(8,128)S(1)}, u32[]{:S(2)}, u32[]{:S(2)}) collective-permute-start(f32[2,128,256]{2,1,0:T(8,128)S(1)} %pad_maximum_fusion.1), channel_id=1, source_target_pairs={{2,0},{4,2},{6,4},{8,6},{10,8},{12,10},{14,12},{3,1},{5,3},{7,5},{... | collective-permute-start | bytes 786440 | tf_op jit(solution)/shard_map/ppermute | solution.py:27
  19.8 3.4 %collective-permute-start.2 = (f32[2,32,256]{2,1,0:T(8,128)S(1)}, f32[2,32,256]{2,1,0:T(8,128)S(1)}, u32[]{:S(2)}, u32[]{:S(2)}) collective-permute-start(f32[2,32,256]{2,1,0:T(8,128)S(1)} %fusion.17), channel_id=1, source_target_pairs={{0,3},{1,2},{2,5},{3,4},{4,7},{5,6},{6,9},{7,8},{8,11},{9,10},{10,... | collective-permute-start | bytes 196616 | tf_op jit(solution)/shard_map/ppermute | solution.py:324
  23.2 3.3 %collective-permute-start.4 = (f32[2,32,256]{2,1,0:T(8,128)S(1)}, f32[2,32,256]{2,1,0:T(8,128)S(1)}, u32[]{:S(2)}, u32[]{:S(2)}) collective-permute-start(f32[2,32,256]{2,1,0:T(8,128)S(1)} %fusion.14), channel_id=1, source_target_pairs={{2,1},{3,0},{4,3},{5,2},{6,5},{7,4},{8,7},{9,6},{10,9},{11,8},{12,... | collective-permute-start | bytes 196616 | tf_op jit(solution)/shard_map/ppermute | solution.py:324
  26.5 0.6 add_convert_fusion.flags
  27.1 2.2 %collective-permute-done.2.prev_halo = f32[2,32,256]{2,1,0:T(8,128)S(1)} collective-permute-done((f32[2,32,256]{2,1,0:T(8,128)S(1)}, f32[2,32,256]{2,1,0:T(8,128)S(1)}, u32[]{:S(2)}, u32[]{:S(2)}) %collective-permute-start.2) | collective-permute-done | bytes 65568 | tf_op jit(solution)/shard_map/ppermute | solution.py:324
  29.2 0.0 copy-start.3
  29.2 3.8 %collective-permute-done.4.next_halo = f32[2,32,256]{2,1,0:T(8,128)S(1)} collective-permute-done((f32[2,32,256]{2,1,0:T(8,128)S(1)}, f32[2,32,256]{2,1,0:T(8,128)S(1)}, u32[]{:S(2)}, u32[]{:S(2)}) %collective-permute-start.4) | collective-permute-done | bytes 65568 | tf_op jit(solution)/shard_map/ppermute | solution.py:324
  33.0 0.0 copy-start.4
  33.0 0.0 collective-permute-done.1.prev_own
  33.0 0.0 copy-start.1
  33.0 0.0 collective-permute-done.3.next_own
  33.0 0.0 copy-done.3
  33.0 0.6 copy-done.4
  33.6 0.1 copy-done.1
  33.7 0.0 copy-start.2
  33.7 0.7 copy-done.2
  34.4 0.0 collective-permute-done.halo
  34.4 16.7 %shard_map.55 = (f32[32,128,256]{2,1,0:T(8,128)}, f32[16,80,256]{2,1,0:T(8,128)}, f32[2,120,256]{2,1,0:T(8,128)}, f32[2,120,256]{2,1,0:T(8,128)}) custom-call(s32[3]{0:T(128)} %add_convert_fusion.flags, f32[32,128,256]{2,1,0:T(8,128)} %copy-done, f32[32,32,256]{2,1,0:T(8,128)} %collective-permute-done.halo, f32[2,128,256]{2,1,0:T(8,128)} %copy-done.1, ...), custom_call_target="tpu_custom_call" | custom-call | tf_op jit(solution)/shard_map/pallas_call | solution.py:239
  51.1 2.1 %collective-permute-start.5 = (f32[2,120,256]{2,1,0:T(8,128)}, f32[2,120,256]{2,1,0:T(8,128)}, u32[]{:S(2)}, u32[]{:S(2)}) collective-permute-start(f32[2,120,256]{2,1,0:T(8,128)} %get-tuple-element.12.sent_next), channel_id=1, source_target_pairs={{0,2},{2,4},{4,6},{6,8},{8,10},{10,12},{12,14},{1,3},{3,5},{5,7},{... | collective-permute-start | bytes 737288 | tf_op jit(solution)/shard_map/ppermute | solution.py:27
  53.2 4.1 %collective-permute-start.6 = (f32[2,120,256]{2,1,0:T(8,128)}, f32[2,120,256]{2,1,0:T(8,128)}, u32[]{:S(2)}, u32[]{:S(2)}) collective-permute-start(f32[2,120,256]{2,1,0:T(8,128)} %get-tuple-element.13.sent_prev), channel_id=1, source_target_pairs={{2,0},{4,2},{6,4},{8,6},{10,8},{12,10},{14,12},{3,1},{5,3},{7,5},{... | collective-permute-start | bytes 737288 | tf_op jit(solution)/shard_map/ppermute | solution.py:27
  57.3 4.1 %collective-permute-done.5.from_prev.got_prev = f32[2,120,256]{2,1,0:T(8,128)} collective-permute-done((f32[2,120,256]{2,1,0:T(8,128)}, f32[2,120,256]{2,1,0:T(8,128)}, u32[]{:S(2)}, u32[]{:S(2)}) %collective-permute-start.5) | collective-permute-done | bytes 245792 | tf_op jit(solution)/shard_map/ppermute | solution.py:27
  61.4 6.0 %collective-permute-done.6.from_next.got_next = f32[2,120,256]{2,1,0:T(8,128)} collective-permute-done((f32[2,120,256]{2,1,0:T(8,128)}, f32[2,120,256]{2,1,0:T(8,128)}, u32[]{:S(2)}, u32[]{:S(2)}) %collective-permute-start.6) | collective-permute-done | bytes 245792 | tf_op jit(solution)/shard_map/ppermute | solution.py:27
  67.4 5.1 %shard_map.56 = (f32[16,64,256]{2,1,0:T(8,128)}, f32[8,40,256]{2,1,0:T(8,128)}, f32[2,40,256]{2,1,0:T(8,128)}, f32[2,40,256]{2,1,0:T(8,128)}) custom-call(s32[3]{0:T(128)} %add_convert_fusion.flags, f32[16,80,256]{2,1,0:T(8,128)} %get-tuple-element.11.x_ref, f32[2,120,256]{2,1,0:T(8,128)} %collective-permute-done.5.from_prev.got_prev, ...), custom_call_target="tpu_custom_call" | custom-call | tf_op jit(solution)/shard_map/pallas_call | solution.py:239
  72.5 7.2 %shard_map.57 = f32[224,32,128]{2,1,0:T(8,128)} custom-call(s32[3]{0:T(128)} %add_convert_fusion.flags, f32[8,40,256]{2,1,0:T(8,128)} %get-tuple-element.14.x_ref, f32[2,120,256]{2,1,0:T(8,128)} %collective-permute-done.5.from_prev.got_prev, f32[2,120,256]{2,1,0:T(8,128)} %collective-permute-done.6.from_next.got_next, ...), custom_call_target="tpu_custom_call" | custom-call | tf_op jit(solution)/shard_map/pallas_call | solution.py:395
  (4 shorter events, 0.1 us)
Async XLA Ops:
  11.5 2.0 %copy-start = (f32[32,128,256]{2,1,0:T(8,128)}, f32[32,128,256]{2,1,0:T(8,128)S(1)}, u32[]{:S(2)}) copy-start(f32[32,128,256]{2,1,0:T(8,128)S(1)} %fusion.2.own) | copy-start | bytes 12582916
  11.7 22.7 %collective-permute-start = (f32[32,32,256]{2,1,0:T(8,128)S(1)}, f32[32,32,256]{2,1,0:T(8,128)}, u32[]{:S(2)}, u32[]{:S(2)}) collective-permute-start(f32[32,32,256]{2,1,0:T(8,128)S(1)} %slice_select_fusion), channel_id=1, source_target_pairs={{0,1},{1,0},{2,3},{3,2},{4,5},{5,4},{6,7},{7,6},{8,9},{9,8},{10,11... | collective-permute-start | bytes 3145736 | tf_op jit(solution)/shard_map/ppermute | solution.py:313
  13.5 19.5 %collective-permute-start.1 = (f32[2,128,256]{2,1,0:T(8,128)S(1)}, f32[2,128,256]{2,1,0:T(8,128)S(1)}, u32[]{:S(2)}, u32[]{:S(2)}) collective-permute-start(f32[2,128,256]{2,1,0:T(8,128)S(1)} %pad_maximum_fusion), channel_id=1, source_target_pairs={{0,2},{2,4},{4,6},{6,8},{8,10},{10,12},{12,14},{1,3},{3,5},{5,7},{... | collective-permute-start | bytes 786440 | tf_op jit(solution)/shard_map/ppermute | solution.py:27
  16.7 16.3 %collective-permute-start.3 = (f32[2,128,256]{2,1,0:T(8,128)S(1)}, f32[2,128,256]{2,1,0:T(8,128)S(1)}, u32[]{:S(2)}, u32[]{:S(2)}) collective-permute-start(f32[2,128,256]{2,1,0:T(8,128)S(1)} %pad_maximum_fusion.1), channel_id=1, source_target_pairs={{2,0},{4,2},{6,4},{8,6},{10,8},{12,10},{14,12},{3,1},{5,3},{7,5},{... | collective-permute-start | bytes 786440 | tf_op jit(solution)/shard_map/ppermute | solution.py:27
  19.8 9.4 %collective-permute-start.2 = (f32[2,32,256]{2,1,0:T(8,128)S(1)}, f32[2,32,256]{2,1,0:T(8,128)S(1)}, u32[]{:S(2)}, u32[]{:S(2)}) collective-permute-start(f32[2,32,256]{2,1,0:T(8,128)S(1)} %fusion.17), channel_id=1, source_target_pairs={{0,3},{1,2},{2,5},{3,4},{4,7},{5,6},{6,9},{7,8},{8,11},{9,10},{10,... | collective-permute-start | bytes 196616 | tf_op jit(solution)/shard_map/ppermute | solution.py:324
  23.2 9.8 %collective-permute-start.4 = (f32[2,32,256]{2,1,0:T(8,128)S(1)}, f32[2,32,256]{2,1,0:T(8,128)S(1)}, u32[]{:S(2)}, u32[]{:S(2)}) collective-permute-start(f32[2,32,256]{2,1,0:T(8,128)S(1)} %fusion.14), channel_id=1, source_target_pairs={{2,1},{3,0},{4,3},{5,2},{6,5},{7,4},{8,7},{9,6},{10,9},{11,8},{12,... | collective-permute-start | bytes 196616 | tf_op jit(solution)/shard_map/ppermute | solution.py:324
  29.2 3.8 %copy-start.3 = (f32[2,32,256]{2,1,0:T(8,128)}, f32[2,32,256]{2,1,0:T(8,128)S(1)}, u32[]{:S(2)}) copy-start(f32[2,32,256]{2,1,0:T(8,128)S(1)} %collective-permute-done.2.prev_halo) | copy-start | bytes 196612
  33.0 0.6 copy-start.4
  33.0 0.7 copy-start.1
  33.7 0.7 copy-start.2
  51.1 10.3 %collective-permute-start.5 = (f32[2,120,256]{2,1,0:T(8,128)}, f32[2,120,256]{2,1,0:T(8,128)}, u32[]{:S(2)}, u32[]{:S(2)}) collective-permute-start(f32[2,120,256]{2,1,0:T(8,128)} %get-tuple-element.12.sent_next), channel_id=1, source_target_pairs={{0,2},{2,4},{4,6},{6,8},{8,10},{10,12},{12,14},{1,3},{3,5},{5,7},{... | collective-permute-start | bytes 737288 | tf_op jit(solution)/shard_map/ppermute | solution.py:27
  53.2 14.2 %collective-permute-start.6 = (f32[2,120,256]{2,1,0:T(8,128)}, f32[2,120,256]{2,1,0:T(8,128)}, u32[]{:S(2)}, u32[]{:S(2)}) collective-permute-start(f32[2,120,256]{2,1,0:T(8,128)} %get-tuple-element.13.sent_prev), channel_id=1, source_target_pairs={{2,0},{4,2},{6,4},{8,6},{10,8},{12,10},{14,12},{3,1},{5,3},{7,5},{... | collective-permute-start | bytes 737288 | tf_op jit(solution)/shard_map/ppermute | solution.py:27

commit v18 on v16

--- a/solution.py
+++ b/solution.py
@@ -133,6 +133,8 @@
         store(pr, e, o)
         if pr == 0:
             ll_ref[...] = e
+            if tn_ref is None:
+                continue
             to_next, to_prev = partials(e, 0)
             if ahead_map is None:
                 tn_ref[...] = to_next
@@ -178,7 +180,8 @@
 
 
 def next_kernel(flags, x_ref, from_prev, from_next,
-                out_ref, ll_ref, tn_ref, tp_ref, ext, half, *, stride):
+                out_ref, ll_ref, ext, half, *, stride):
+    tn_ref = tp_ref = None
     rows, width = x_ref.shape[0], x_ref.shape[1]
     ext[EDGE : EDGE + rows] = x_ref[...]
     fill_rows(ext, flags, from_prev[:, :width], from_next[:, :width], rows)
@@ -214,11 +217,12 @@
     return pl.BlockSpec(a.shape, lambda h, f: (0,) * a.ndim)
 
 
-def level_call(kernel, flags, arrays, out_shape, rows, width, aliases, consts=(), ahead=False):
+def level_call(kernel, flags, arrays, out_shape, rows, width, aliases, consts=(), ahead=False,
+               edges=True):
     bands = arrays[0].shape[-1]
     ll_shape = (rows // 2, width // 2, bands)
     edge_shape = (2, width // 2 + (width // 4 if ahead else 0), bands)
-    outs = (out_shape, ll_shape, edge_shape, edge_shape)
+    outs = (out_shape, ll_shape, edge_shape, edge_shape) if edges else (out_shape, ll_shape)
     grid_spec = pltpu.PrefetchScalarGridSpec(
         num_scalar_prefetch=1,
         grid=(bands // LANES,),
@@ -357,9 +361,10 @@
     got_prev = shifted(tn, "rows", 1)
     got_next = shifted(tp, "rows", -1)
     sent_next, sent_prev = tn, tp
-    middle, level, tn, tp = level_call(
+    middle, level = level_call(
         functools.partial(next_kernel, stride=1), flags,
-        [level, got_prev, got_next], (rows // 2, width // 2, padded_bands), r, w, {})
+        [level, got_prev, got_next], (rows // 2, width // 2, padded_bands), r, w, {},
+        edges=False)
     below = jnp.asarray(below_map.reshape(-1, below_map.shape[2] * below_map.shape[3]).T)
     above = jnp.asarray(above_map.reshape(-1, above_map.shape[2] * above_map.shape[3]).T)
     return last_call(flags, [level, got_prev, got_next, sent_next, sent_prev, out, middle],

time: 75.8 us -> 75.7 us (level)
  no operation moved by 1% of the time
where the time goes in v18:
time: 75.7 us; the launch traced here: 75.4 us
  Pallas kernels  24.7 us (33%)
  starting transfers between devices  19.7 us (26%)
  waiting for transfers between devices  16 us (21%)
  matrix products  10.4 us (14%)
  local copies, waits for them, and re-layouts  3.48 us (5%)
  other arithmetic  0.93 us (1%)
    pallas_call x2, Pallas kernels, level_call(): pl.pallas_call(kernel, grid_spec=grid_spec, out_shape=tuple((jax.ShapeDty...  17.5 us
    ppermute x4, starting transfers between devices, shifted(): return lax.ppermute(x, axis, pairs)  12.4 us
    dot_general x1, matrix products, mix(): jnp.einsum('crw,bc->rwb', x, weights, precision=lax.Precision.HIGHEST, pr...  10.4 us
    ppermute x4, waiting for transfers between devices, shifted(): return lax.ppermute(x, axis, pairs)  10.1 us
    pallas_call x1, Pallas kernels, last_call(): pl.pallas_call(functools.partial(last_kernel, stride=stride), grid_spec=g...  7.18 us
    ppermute x2, starting transfers between devices, diagonal(): return lax.ppermute(x, ('rows', 'cols'), pairs)  6.64 us
    ppermute x2, waiting for transfers between devices, diagonal(): return lax.ppermute(x, ('rows', 'cols'), pairs)  5.91 us
    unnamed x11, local copies, waits for them, and re-layouts  3.48 us
  transfers between devices with their start and end apart: 7, of which 4 were waited for; matrix products, arithmetic and copies ran while one was open for 1% of the time, Pallas kernels for 0%

profile of v18, /device:TPU:11, one launch (start us, length us, event | category | flops | bytes accessed | tf_op | source)
XLA Modules:
  0.0 75.4 jit_solution(16949127656063070949)
XLA Ops:
  0.0 1.1 %copy.6 = f32[224,224]{0,1:T(8,128)S(1)} copy(f32[224,224]{1,0:T(8,128)} %param.6) | data formatting | bytes 401408 | tf_op args[1]
  1.1 10.4 %fusion.2.own = f32[32,128,256]{2,1,0:T(8,128)S(1)} fusion(f32[224,32,128]{2,1,0:T(8,128)} %param.5, f32[224,224]{0,1:T(8,128)S(1)} %copy.6), kind=kOutput, calls=%fused_computation.2 | convolution fusion | flops 2818572288 | bytes 8065024 | tf_op jit(solution)/shard_map/crw,bc->rwb/dot_general | solution.py:341
  11.5 0.0 copy-start
  11.5 0.2 slice_select_fusion
  11.7 0.7 collective-permute-start
  12.4 1.0 %copy-done = f32[32,128,256]{2,1,0:T(8,128)} copy-done((f32[32,128,256]{2,1,0:T(8,128)}, f32[32,128,256]{2,1,0:T(8,128)S(1)}, u32[]{:S(2)}) %copy-start) | copy-done | bytes 4194328
  13.4 0.1 fusion.20
  13.5 3.1 %collective-permute-start.1 = (f32[2,128,256]{2,1,0:T(8,128)S(1)}, f32[2,128,256]{2,1,0:T(8,128)S(1)}, u32[]{:S(2)}, u32[]{:S(2)}) collective-permute-start(f32[2,128,256]{2,1,0:T(8,128)S(1)} %pad_maximum_fusion), channel_id=1, source_target_pairs={{0,2},{2,4},{4,6},{6,8},{8,10},{10,12},{12,14},{1,3},{3,5},{5,7},{... | collective-permute-start | bytes 786440 | tf_op jit(solution)/shard_map/ppermute | solution.py:27
  16.7 3.0 %collective-permute-start.3 = (f32[2,128,256]{2,1,0:T(8,128)S(1)}, f32[2,128,256]{2,1,0:T(8,128)S(1)}, u32[]{:S(2)}, u32[]{:S(2)}) collective-permute-start(f32[2,128,256]{2,1,0:T(8,128)S(1)} %pad_maximum_fusion.1), channel_id=1, source_target_pairs={{2,0},{4,2},{6,4},{8,6},{10,8},{12,10},{14,12},{3,1},{5,3},{7,5},{... | collective-permute-start | bytes 786440 | tf_op jit(solution)/shard_map/ppermute | solution.py:27
  19.8 3.4 %collective-permute-start.2 = (f32[2,32,256]{2,1,0:T(8,128)S(1)}, f32[2,32,256]{2,1,0:T(8,128)S(1)}, u32[]{:S(2)}, u32[]{:S(2)}) collective-permute-start(f32[2,32,256]{2,1,0:T(8,128)S(1)} %fusion.17), channel_id=1, source_target_pairs={{0,3},{1,2},{2,5},{3,4},{4,7},{5,6},{6,9},{7,8},{8,11},{9,10},{10,... | collective-permute-start | bytes 196616 | tf_op jit(solution)/shard_map/ppermute | solution.py:321
  23.2 3.3 %collective-permute-start.4 = (f32[2,32,256]{2,1,0:T(8,128)S(1)}, f32[2,32,256]{2,1,0:T(8,128)S(1)}, u32[]{:S(2)}, u32[]{:S(2)}) collective-permute-start(f32[2,32,256]{2,1,0:T(8,128)S(1)} %fusion.14), channel_id=1, source_target_pairs={{2,1},{3,0},{4,3},{5,2},{6,5},{7,4},{8,7},{9,6},{10,9},{11,8},{12,... | collective-permute-start | bytes 196616 | tf_op jit(solution)/shard_map/ppermute | solution.py:321
  26.5 0.6 add_convert_fusion.flags
  27.1 2.2 %collective-permute-done.2.prev_halo = f32[2,32,256]{2,1,0:T(8,128)S(1)} collective-permute-done((f32[2,32,256]{2,1,0:T(8,128)S(1)}, f32[2,32,256]{2,1,0:T(8,128)S(1)}, u32[]{:S(2)}, u32[]{:S(2)}) %collective-permute-start.2) | collective-permute-done | bytes 65568 | tf_op jit(solution)/shard_map/ppermute | solution.py:321
  29.2 0.0 copy-start.3
  29.2 3.8 %collective-permute-done.4.next_halo = f32[2,32,256]{2,1,0:T(8,128)S(1)} collective-permute-done((f32[2,32,256]{2,1,0:T(8,128)S(1)}, f32[2,32,256]{2,1,0:T(8,128)S(1)}, u32[]{:S(2)}, u32[]{:S(2)}) %collective-permute-start.4) | collective-permute-done | bytes 65568 | tf_op jit(solution)/shard_map/ppermute | solution.py:321
  33.0 0.0 copy-start.4
  33.0 0.0 collective-permute-done.1.prev_own
  33.0 0.0 copy-start.1
  33.0 0.0 collective-permute-done.3.next_own
  33.0 0.0 copy-done.3
  33.0 0.6 copy-done.4
  33.6 0.1 copy-done.1
  33.7 0.0 copy-start.2
  33.7 0.7 copy-done.2
  34.4 0.0 collective-permute-done.halo
  34.4 13.4 %shard_map.55 = (f32[32,128,256]{2,1,0:T(8,128)}, f32[16,80,256]{2,1,0:T(8,128)}, f32[2,120,256]{2,1,0:T(8,128)}, f32[2,120,256]{2,1,0:T(8,128)}) custom-call(s32[3]{0:T(128)} %add_convert_fusion.flags, f32[32,128,256]{2,1,0:T(8,128)} %copy-done, f32[32,32,256]{2,1,0:T(8,128)} %collective-permute-done.halo, f32[2,128,256]{2,1,0:T(8,128)} %copy-done.1, ...), custom_call_target="tpu_custom_call" | custom-call | tf_op jit(solution)/shard_map/pallas_call | solution.py:236
  47.8 2.1 %collective-permute-start.5 = (f32[2,120,256]{2,1,0:T(8,128)}, f32[2,120,256]{2,1,0:T(8,128)}, u32[]{:S(2)}, u32[]{:S(2)}) collective-permute-start(f32[2,120,256]{2,1,0:T(8,128)} %get-tuple-element.12.sent_next), channel_id=1, source_target_pairs={{0,2},{2,4},{4,6},{6,8},{8,10},{10,12},{12,14},{1,3},{3,5},{5,7},{... | collective-permute-start | bytes 737288 | tf_op jit(solution)/shard_map/ppermute | solution.py:27
  49.8 4.1 %collective-permute-start.6 = (f32[2,120,256]{2,1,0:T(8,128)}, f32[2,120,256]{2,1,0:T(8,128)}, u32[]{:S(2)}, u32[]{:S(2)}) collective-permute-start(f32[2,120,256]{2,1,0:T(8,128)} %get-tuple-element.13.sent_prev), channel_id=1, source_target_pairs={{2,0},{4,2},{6,4},{8,6},{10,8},{12,10},{14,12},{3,1},{5,3},{7,5},{... | collective-permute-start | bytes 737288 | tf_op jit(solution)/shard_map/ppermute | solution.py:27
  54.0 4.1 %collective-permute-done.5.from_prev.got_prev = f32[2,120,256]{2,1,0:T(8,128)} collective-permute-done((f32[2,120,256]{2,1,0:T(8,128)}, f32[2,120,256]{2,1,0:T(8,128)}, u32[]{:S(2)}, u32[]{:S(2)}) %collective-permute-start.5) | collective-permute-done | bytes 245792 | tf_op jit(solution)/shard_map/ppermute | solution.py:27
  58.0 6.0 %collective-permute-done.6.from_next.got_next = f32[2,120,256]{2,1,0:T(8,128)} collective-permute-done((f32[2,120,256]{2,1,0:T(8,128)}, f32[2,120,256]{2,1,0:T(8,128)}, u32[]{:S(2)}, u32[]{:S(2)}) %collective-permute-start.6) | collective-permute-done | bytes 245792 | tf_op jit(solution)/shard_map/ppermute | solution.py:27
  64.0 4.1 %shard_map.56 = (f32[16,64,256]{2,1,0:T(8,128)}, f32[8,40,256]{2,1,0:T(8,128)}) custom-call(s32[3]{0:T(128)} %add_convert_fusion.flags, f32[16,80,256]{2,1,0:T(8,128)} %get-tuple-element.11.x_ref, f32[2,120,256]{2,1,0:T(8,128)} %collective-permute-done.5.from_prev.got_prev, f32[2,120,256]{2,1,0:T(8,128)} %collective-permute-done.6.from_next.got_next), custom_call_target="tpu_custom_call" | custom-call | tf_op jit(solution)/shard_map/pallas_call | solution.py:236
  68.2 7.2 %shard_map.57 = f32[224,32,128]{2,1,0:T(8,128)} custom-call(s32[3]{0:T(128)} %add_convert_fusion.flags, f32[8,40,256]{2,1,0:T(8,128)} %get-tuple-element.14.x_ref, f32[2,120,256]{2,1,0:T(8,128)} %collective-permute-done.5.from_prev.got_prev, f32[2,120,256]{2,1,0:T(8,128)} %collective-permute-done.6.from_next.got_next, ...), custom_call_target="tpu_custom_call" | custom-call | tf_op jit(solution)/shard_map/pallas_call | solution.py:393
  (4 shorter events, 0.1 us)
Async XLA Ops:
  11.5 2.0 %copy-start = (f32[32,128,256]{2,1,0:T(8,128)}, f32[32,128,256]{2,1,0:T(8,128)S(1)}, u32[]{:S(2)}) copy-start(f32[32,128,256]{2,1,0:T(8,128)S(1)} %fusion.2.own) | copy-start | bytes 12582916
  11.7 22.7 %collective-permute-start = (f32[32,32,256]{2,1,0:T(8,128)S(1)}, f32[32,32,256]{2,1,0:T(8,128)}, u32[]{:S(2)}, u32[]{:S(2)}) collective-permute-start(f32[32,32,256]{2,1,0:T(8,128)S(1)} %slice_select_fusion), channel_id=1, source_target_pairs={{0,1},{1,0},{2,3},{3,2},{4,5},{5,4},{6,7},{7,6},{8,9},{9,8},{10,11... | collective-permute-start | bytes 3145736 | tf_op jit(solution)/shard_map/ppermute | solution.py:310
  13.5 19.5 %collective-permute-start.1 = (f32[2,128,256]{2,1,0:T(8,128)S(1)}, f32[2,128,256]{2,1,0:T(8,128)S(1)}, u32[]{:S(2)}, u32[]{:S(2)}) collective-permute-start(f32[2,128,256]{2,1,0:T(8,128)S(1)} %pad_maximum_fusion), channel_id=1, source_target_pairs={{0,2},{2,4},{4,6},{6,8},{8,10},{10,12},{12,14},{1,3},{3,5},{5,7},{... | collective-permute-start | bytes 786440 | tf_op jit(solution)/shard_map/ppermute | solution.py:27
  16.7 16.3 %collective-permute-start.3 = (f32[2,128,256]{2,1,0:T(8,128)S(1)}, f32[2,128,256]{2,1,0:T(8,128)S(1)}, u32[]{:S(2)}, u32[]{:S(2)}) collective-permute-start(f32[2,128,256]{2,1,0:T(8,128)S(1)} %pad_maximum_fusion.1), channel_id=1, source_target_pairs={{2,0},{4,2},{6,4},{8,6},{10,8},{12,10},{14,12},{3,1},{5,3},{7,5},{... | collective-permute-start | bytes 786440 | tf_op jit(solution)/shard_map/ppermute | solution.py:27
  19.8 9.4 %collective-permute-start.2 = (f32[2,32,256]{2,1,0:T(8,128)S(1)}, f32[2,32,256]{2,1,0:T(8,128)S(1)}, u32[]{:S(2)}, u32[]{:S(2)}) collective-permute-start(f32[2,32,256]{2,1,0:T(8,128)S(1)} %fusion.17), channel_id=1, source_target_pairs={{0,3},{1,2},{2,5},{3,4},{4,7},{5,6},{6,9},{7,8},{8,11},{9,10},{10,... | collective-permute-start | bytes 196616 | tf_op jit(solution)/shard_map/ppermute | solution.py:321
  23.2 9.8 %collective-permute-start.4 = (f32[2,32,256]{2,1,0:T(8,128)S(1)}, f32[2,32,256]{2,1,0:T(8,128)S(1)}, u32[]{:S(2)}, u32[]{:S(2)}) collective-permute-start(f32[2,32,256]{2,1,0:T(8,128)S(1)} %fusion.14), channel_id=1, source_target_pairs={{2,1},{3,0},{4,3},{5,2},{6,5},{7,4},{8,7},{9,6},{10,9},{11,8},{12,... | collective-permute-start | bytes 196616 | tf_op jit(solution)/shard_map/ppermute | solution.py:321
  29.2 3.8 %copy-start.3 = (f32[2,32,256]{2,1,0:T(8,128)}, f32[2,32,256]{2,1,0:T(8,128)S(1)}, u32[]{:S(2)}) copy-start(f32[2,32,256]{2,1,0:T(8,128)S(1)} %collective-permute-done.2.prev_halo) | copy-start | bytes 196612
  33.0 0.6 copy-start.4
  33.0 0.7 copy-start.1
  33.7 0.7 copy-start.2
  47.8 10.3 %collective-permute-start.5 = (f32[2,120,256]{2,1,0:T(8,128)}, f32[2,120,256]{2,1,0:T(8,128)}, u32[]{:S(2)}, u32[]{:S(2)}) collective-permute-start(f32[2,120,256]{2,1,0:T(8,128)} %get-tuple-element.12.sent_next), channel_id=1, source_target_pairs={{0,2},{2,4},{4,6},{6,8},{8,10},{10,12},{12,14},{1,3},{3,5},{5,7},{... | collective-permute-start | bytes 737288 | tf_op jit(solution)/shard_map/ppermute | solution.py:27
  49.8 14.2 %collective-permute-start.6 = (f32[2,120,256]{2,1,0:T(8,128)}, f32[2,120,256]{2,1,0:T(8,128)}, u32[]{:S(2)}, u32[]{:S(2)}) collective-permute-start(f32[2,120,256]{2,1,0:T(8,128)} %get-tuple-element.13.sent_prev), channel_id=1, source_target_pairs={{2,0},{4,2},{6,4},{8,6},{10,8},{12,10},{14,12},{3,1},{5,3},{7,5},{... | collective-permute-start | bytes 737288 | tf_op jit(solution)/shard_map/ppermute | solution.py:27
